TPU v7x, 128 devices: a whole 4x4x4 slice. The times are simulated.
128 devices in a mesh: section: 2 (over x_hi), expert: 16 (over z, y), tensor: 4 (over x_lo, core).
Axes of the slice: x: 4 (x_hi: 2, x_lo: 2; x = x_hi * 2 + x_lo), y: 4, z: 4, core: 2. Of those that a mesh axis runs over, the one named last changes fastest.
Arguments:
- tokens: bfloat16 [2, 1024, 3072], P(None, 'expert', 'tensor'), may hold values from -6 to 6
- norm_gain: float32 [2, 3072], P('section', 'tensor'), may hold values from 0.1 to 1.9
- expert_ids: int32 [2, 2, 1024, 2], P('section', None, 'expert'), may hold values from 0 to 7, all different within a row; in each aligned block of 64 rows (0 to 63, 64 to 127, ..., all dimensions but the last counted through in order) at most 24 rows name the same one
- gate_weights: float32 [2, 2, 1024, 2], P('section', None, 'expert'), may hold values from 0.1 to 0.9
- w_up: bfloat16 [2, 16, 3072, 4096], P('section', 'expert', None, 'tensor'), may hold values from -0.109375 to 0.109375
- w_down: bfloat16 [2, 16, 4096, 3072], P('section', 'expert', 'tensor'), may hold values from -0.0625 to 0.0625
Outputs:
- layer_states: bfloat16 [2, 2, 1024, 3072], P('section', None, 'expert', 'tensor')
Inputs may be any that keep to these rules, and one draw needn't show every extreme that they name: `expert_ids`: the two ids of a token differ. In each layer and microbatch, among the 64 tokens of one index of expert, no expert is named by more than 24 of them, a bound that some block reaches.
All inputs are finite; a program needn't handle non-finite values.
Results may differ from a plain program's by a relative error of at most 0.0052.
Values may be sent and summed in bfloat16 or wider, within the bound.
No kernel may reach another device: no remote copies, remote signals or barrier semaphores. Data moves between devices by JAX's collectives and lax.ppermute only.
A program may use at most 64 MiB of HBM per device.

v0:
```python
import jax
import jax.numpy as jnp
from jax import lax
from jax.sharding import PartitionSpec as P

D = 3072
EXPERTS = 8


def from_behind(block, axis, distance):
    devices = range(lax.axis_size(axis))
    route = [(i - distance, i) for i in devices if i - distance in devices]
    return lax.ppermute(block, axis, route)


def shards(tokens, norm_gain, expert_ids, gate_weights, w_up, w_down):
    segments = lax.axis_size("section")
    n_exp = lax.axis_size("expert")
    segment_pos = lax.axis_index("section")
    micro = tokens.shape[0]
    rows_here = tokens.shape[1]
    width_here = tokens.shape[2]
    capacity = max(3 * rows_here // 8, 2 * rows_here // EXPERTS)
    gain = norm_gain[0]
    up_local = w_up[0]
    down_local = w_down[0]
    local_count = up_local.shape[0]
    copies = n_exp * local_count // EXPERTS
    collected = jnp.zeros((micro, rows_here, width_here), jnp.bfloat16)
    carried = jnp.zeros((rows_here, width_here), jnp.bfloat16)
    total_steps = micro + segments - 1
    for step in range(total_steps):
        which = step - segment_pos
        which_safe = jnp.clip(which, 0, micro - 1)
        entering = tokens[min(step, micro - 1)]
        current = jnp.where(segment_pos == 0, entering, carried)
        routes = lax.dynamic_index_in_dim(expert_ids[0], which_safe, 0, keepdims=False)
        weights = lax.dynamic_index_in_dim(gate_weights[0], which_safe, 0, keepdims=False)
        xf = current.astype(jnp.float32)
        sums = lax.psum(jnp.sum(xf * xf, axis=1), "tensor")
        normed = (xf * lax.rsqrt(sums / D + 1e-05)[:, None] * gain[None, :]).astype(jnp.bfloat16)
        source_rows = lax.all_gather(normed, "tensor", axis=1, tiled=True)
        row_width = source_rows.shape[1]
        flat = routes.reshape(-1)
        onehot = (flat[:, None] == jnp.arange(EXPERTS, dtype=jnp.int32)[None, :]).astype(jnp.int32)
        slot = jnp.sum((jnp.cumsum(onehot, axis=0) - onehot) * onehot, axis=1)
        dest = flat * capacity + slot
        source = (
            jnp.full((EXPERTS * capacity,), -1, jnp.int32)
            .at[dest]
            .set(jnp.arange(2 * rows_here, dtype=jnp.int32) // 2)
        )
        filled = source >= 0
        outgoing = jnp.where(
            filled[:, None],
            jnp.take(source_rows, jnp.maximum(source, 0), axis=0),
            jnp.zeros((), jnp.bfloat16),
        )
        outgoing = outgoing.reshape(EXPERTS, capacity, row_width)
        outgoing = jnp.repeat(outgoing, copies, axis=0).reshape(
            n_exp, local_count, capacity, row_width
        )
        summed_up = jnp.einsum(
            "sekd,edf->sekf",
            lax.all_to_all(outgoing, "expert", split_axis=0, concat_axis=0, tiled=True),
            up_local,
            preferred_element_type=jnp.float32,
        )
        hidden = jax.nn.silu(summed_up).astype(jnp.bfloat16)
        partial_out = jnp.einsum(
            "sekf,efd->sekd", hidden, down_local, preferred_element_type=jnp.float32
        )
        result = lax.psum_scatter(partial_out, "tensor", scatter_dimension=3, tiled=True)
        returned = lax.all_to_all(result, "expert", split_axis=0, concat_axis=0, tiled=True)
        summed = jnp.sum(returned.reshape(EXPERTS, copies, capacity, width_here), axis=1).astype(
            jnp.bfloat16
        )
        picked = jnp.take(summed.reshape(-1, width_here), dest, axis=0).astype(jnp.float32)
        picked = picked.reshape(rows_here, 2, width_here)
        mixed = xf + jnp.sum(picked * weights[:, :, None], axis=1)
        produced = mixed.astype(jnp.bfloat16)
        chosen = (jnp.arange(micro, dtype=jnp.int32) == which)[:, None, None]
        collected = jnp.where(chosen, produced[None], collected)
        if step + 1 < total_steps:
            carried = from_behind(produced, "section", 1)
    return collected[None]


def solution(mesh):
    placed = (
        P(None, "expert", "tensor"),
        P("section", "tensor"),
        P("section", None, "expert", None),
        P("section", None, "expert", None),
        P("section", "expert", None, "tensor"),
        P("section", "expert", "tensor", None),
    )
    return jax.shard_map(
        shards,
        mesh=mesh,
        in_specs=placed,
        out_specs=P("section", None, "expert", "tensor"),
        check_vma=False,
    )
```

profile of v0, /device:TPU:6, one launch (start us, length us, event | category | flops | bytes accessed | tf_op | source)
XLA Modules:
  0.0 444.7 jit_solution(9581021212160880358)
XLA Ops:
  11.2 6.2 %psum.21 = f32[64]{0:T(128)S(1)} all-reduce(f32[64]{0:T(128)S(1)} %fusion.66), channel_id=1, replica_groups=mesh['section'=2,'expert'=16,'tensor'=4] {'tensor'}, use_global_device_ids=true, to_apply=%region_4.5 | all-reduce | flops 64 | bytes 512 | tf_op jit(solution)/shard_map/psum | solution.py:40
  19.1 6.2 %all_gather.9 = bf16[64,3072]{1,0:T(8,128)(2,1)S(1)} all-gather(bf16[64,768]{1,0:T(8,128)(2,1)S(1)} %fusion.68), channel_id=1, replica_groups=mesh['section'=2,'expert'=16,'tensor'=4] {'tensor'}, dimensions={1}, use_global_device_ids=true | all-gather | bytes 491520 | tf_op jit(solution)/shard_map/all_gather | solution.py:42
  27.1 39.8 %all_to_all.30 = bf16[16,1,24,3072]{3,2,1,0:T(8,128)(2,1)S(1)} all-to-all(bf16[16,1,24,3072]{3,2,1,0:T(8,128)(2,1)S(1)} %bitcast.228), channel_id=1, replica_groups=mesh['section'=2,'expert'=16,'tensor'=4] {'expert'}, dimensions={0} | all-to-all | bytes 4718592 | tf_op jit(solution)/shard_map/all_to_all | solution.py:65
  67.0 5.7 %fusion.40 = bf16[16,24,1024]{2,1,0:T(8,128)(2,1)S(1)} fusion(bf16[1,1,3072,1024]{3,2,1,0:T(8,128)(2,1)} %param.14, bf16[16,1,24,3072]{3,2,1,0:T(8,128)(2,1)S(1)} %all_to_all.30), kind=kOutput, calls=%fused_computation.45 | convolution fusion | flops 2417885184 | bytes 9437184 | tf_op jit(solution)/shard_map/sekd,edf->sekf/dot_general | solution.py:63
  77.0 46.9 %reduce-scatter.4.cloned.1.call-done = f32[16,1,24,768]{3,2,0,1:T(8,128)} async-done(((f32[16,1,24,3072]{3,2,0,1:T(8,128)}), f32[16,1,24,768]{3,2,0,1:T(8,128)}) %reduce-scatter.4.cloned.1.call-update) | async-done | bytes 1179664 | tf_op jit(solution)/shard_map/reduce_scatter | solution.py:73
  123.9 7.0 %all-to-all-start.1 = ((f32[16,1,24,768]{3,2,1,0:T(8,128)}), f32[16,1,24,768]{3,2,1,0:T(8,128)S(1)}, u32[]{:S(2)}, u32[]{:S(2)}) async-start(f32[16,1,24,768]{3,2,1,0:T(8,128)} %bitcast.238), calls=%async_computation.2 | async-start | bytes 2359296 | tf_op jit(solution)/shard_map/all_to_all | solution.py:74
  132.1 18.5 %all-to-all-done.1 = f32[16,1,24,768]{3,2,1,0:T(8,128)S(1)} async-done(((f32[16,1,24,768]{3,2,1,0:T(8,128)}), f32[16,1,24,768]{3,2,1,0:T(8,128)S(1)}, u32[]{:S(2)}, u32[]{:S(2)}) %all-to-all-start.1) | async-done | bytes 1179680 | tf_op jit(solution)/shard_map/all_to_all | solution.py:74
  153.8 6.7 %collective-permute-done = bf16[64,768]{1,0:T(8,128)(2,1)S(1)} collective-permute-done((bf16[64,768]{1,0:T(8,128)(2,1)S(1)}, bf16[64,768]{1,0:T(8,128)(2,1)S(1)}, u32[]{:S(2)}, u32[]{:S(2)}) %collective-permute-start) | collective-permute-done | bytes 98336 | tf_op jit(solution)/shard_map/ppermute | solution.py:13
  160.7 5.7 %psum.22 = f32[64]{0:T(128)S(1)} all-reduce(f32[64]{0:T(128)S(1)} %get-tuple-element.17), channel_id=1, replica_groups=mesh['section'=2,'expert'=16,'tensor'=4] {'tensor'}, use_global_device_ids=true, to_apply=%region_12.15 | all-reduce | flops 64 | bytes 512 | tf_op jit(solution)/shard_map/psum | solution.py:40
  166.4 6.1 %all_gather.10 = bf16[64,3072]{1,0:T(8,128)(2,1)S(1)} all-gather(bf16[64,768]{1,0:T(8,128)(2,1)S(1)} %fusion.73), channel_id=1, replica_groups=mesh['section'=2,'expert'=16,'tensor'=4] {'tensor'}, dimensions={1}, use_global_device_ids=true | all-gather | bytes 491520 | tf_op jit(solution)/shard_map/all_gather | solution.py:42
  174.4 35.1 %all_to_all.31 = bf16[16,1,24,3072]{3,2,1,0:T(8,128)(2,1)S(1)} all-to-all(bf16[16,1,24,3072]{3,2,1,0:T(8,128)(2,1)S(1)} %bitcast.229), channel_id=1, replica_groups=mesh['section'=2,'expert'=16,'tensor'=4] {'expert'}, dimensions={0} | all-to-all | bytes 4718592 | tf_op jit(solution)/shard_map/all_to_all | solution.py:65
  209.5 5.7 %fusion.49 = bf16[16,24,1024]{2,1,0:T(8,128)(2,1)S(1)} fusion(bf16[1,1,3072,1024]{3,2,1,0:T(8,128)(2,1)} %param.14, bf16[16,1,24,3072]{3,2,1,0:T(8,128)(2,1)S(1)} %all_to_all.31), kind=kOutput, calls=%fused_computation.46 | convolution fusion | flops 2417885184 | bytes 9437184 | tf_op jit(solution)/shard_map/sekd,edf->sekf/dot_general | solution.py:63
  215.2 4.3 fusion.15
  220.4 46.0 %reduce-scatter.6.cloned.1.call-done = f32[16,1,24,768]{3,2,0,1:T(8,128)} async-done(((f32[16,1,24,3072]{3,2,0,1:T(8,128)}), f32[16,1,24,768]{3,2,0,1:T(8,128)}) %reduce-scatter.6.cloned.1.call-update) | async-done | bytes 1179664 | tf_op jit(solution)/shard_map/reduce_scatter | solution.py:73
  266.4 7.0 %all-to-all-start.3 = ((f32[16,1,24,768]{3,2,1,0:T(8,128)}), f32[16,1,24,768]{3,2,1,0:T(8,128)S(1)}, u32[]{:S(2)}, u32[]{:S(2)}) async-start(f32[16,1,24,768]{3,2,1,0:T(8,128)} %bitcast.237), calls=%async_computation.5 | async-start | bytes 2359296 | tf_op jit(solution)/shard_map/all_to_all | solution.py:74
  274.7 18.4 %all-to-all-done.3 = f32[16,1,24,768]{3,2,1,0:T(8,128)S(1)} async-done(((f32[16,1,24,768]{3,2,1,0:T(8,128)}), f32[16,1,24,768]{3,2,1,0:T(8,128)S(1)}, u32[]{:S(2)}, u32[]{:S(2)}) %all-to-all-start.3) | async-done | bytes 1179680 | tf_op jit(solution)/shard_map/all_to_all | solution.py:74
  296.3 6.7 %collective-permute-done.1 = bf16[64,768]{1,0:T(8,128)(2,1)S(1)} collective-permute-done((bf16[64,768]{1,0:T(8,128)(2,1)S(1)}, bf16[64,768]{1,0:T(8,128)(2,1)S(1)}, u32[]{:S(2)}, u32[]{:S(2)}) %collective-permute-start.1) | collective-permute-done | bytes 98336 | tf_op jit(solution)/shard_map/ppermute | solution.py:13
  303.1 5.7 %psum.23 = f32[64]{0:T(128)S(1)} all-reduce(f32[64]{0:T(128)S(1)} %get-tuple-element.11), channel_id=1, replica_groups=mesh['section'=2,'expert'=16,'tensor'=4] {'tensor'}, use_global_device_ids=true, to_apply=%region_20.23 | all-reduce | flops 64 | bytes 512 | tf_op jit(solution)/shard_map/psum | solution.py:40
  308.9 6.1 %all_gather.11 = bf16[64,3072]{1,0:T(8,128)(2,1)S(1)} all-gather(bf16[64,768]{1,0:T(8,128)(2,1)S(1)} %fusion.77), channel_id=1, replica_groups=mesh['section'=2,'expert'=16,'tensor'=4] {'tensor'}, dimensions={1}, use_global_device_ids=true | all-gather | bytes 491520 | tf_op jit(solution)/shard_map/all_gather | solution.py:42
  316.9 35.1 %all_to_all.32 = bf16[16,1,24,3072]{3,2,1,0:T(8,128)(2,1)S(1)} all-to-all(bf16[16,1,24,3072]{3,2,1,0:T(8,128)(2,1)S(1)} %bitcast.230), channel_id=1, replica_groups=mesh['section'=2,'expert'=16,'tensor'=4] {'expert'}, dimensions={0} | all-to-all | bytes 4718592 | tf_op jit(solution)/shard_map/all_to_all | solution.py:65
  351.9 5.7 %fusion.58 = bf16[16,24,1024]{2,1,0:T(8,128)(2,1)S(1)} fusion(bf16[1,1,3072,1024]{3,2,1,0:T(8,128)(2,1)} %param.14, bf16[16,1,24,3072]{3,2,1,0:T(8,128)(2,1)S(1)} %all_to_all.32), kind=kOutput, calls=%fused_computation.47 | convolution fusion | flops 2417885184 | bytes 9437184 | tf_op jit(solution)/shard_map/sekd,edf->sekf/dot_general | solution.py:63
  362.0 46.9 %reduce-scatter.8.cloned.1.call-done = f32[16,1,24,768]{3,2,0,1:T(8,128)} async-done(((f32[16,1,24,3072]{3,2,0,1:T(8,128)}), f32[16,1,24,768]{3,2,0,1:T(8,128)}) %reduce-scatter.8.cloned.1.call-update) | async-done | bytes 1179664 | tf_op jit(solution)/shard_map/reduce_scatter | solution.py:73
  408.9 7.0 %all-to-all-start.5 = ((f32[16,1,24,768]{3,2,1,0:T(8,128)}), f32[16,1,24,768]{3,2,1,0:T(8,128)S(1)}, u32[]{:S(2)}, u32[]{:S(2)}) async-start(f32[16,1,24,768]{3,2,1,0:T(8,128)} %bitcast.239), calls=%async_computation.8 | async-start | bytes 2359296 | tf_op jit(solution)/shard_map/all_to_all | solution.py:74
  416.1 19.5 %all-to-all-done.5 = f32[16,1,24,768]{3,2,1,0:T(8,128)S(1)} async-done(((f32[16,1,24,768]{3,2,1,0:T(8,128)}), f32[16,1,24,768]{3,2,1,0:T(8,128)S(1)}, u32[]{:S(2)}, u32[]{:S(2)}) %all-to-all-start.5) | async-done | bytes 1179680 | tf_op jit(solution)/shard_map/all_to_all | solution.py:74
  (117 shorter events, 33.0 us)
Async XLA Ops:
  6.5 117.4 %reduce-scatter.4.cloned.1.call-start = ((), (), s32[]{:S(2)}) async-start(), calls=%async_computation.9 | async-start | bytes 5898240 | tf_op jit(solution)/shard_map/reduce_scatter | solution.py:73
  27.1 45.6 %slice-start = ((s8[6291456]{0:T(1024)(128)(4,1)}), s8[4194304]{0:T(1024)(128)(4,1)S(1)}, s32[]{:S(2)}) async-start(s8[6291456]{0:T(1024)(128)(4,1)} %bitcast.240), calls=%async_computation.12 | async-start | bytes 8388608
  67.0 5.7 %slice-start.1 = ((s8[6291456]{0:T(1024)(128)(4,1)}), s8[2097152]{0:T(1024)(128)(4,1)S(1)}, s32[]{:S(2)}) async-start(s8[6291456]{0:T(1024)(128)(4,1)} %bitcast.240), calls=%async_computation.13 | async-start | bytes 4194304
  77.0 53.9 %copy-start.1 = (f32[1,2,64,2]{2,3,1,0:T(2,128)S(1)}, f32[1,2,64,2]{2,3,1,0:T(2,128)}, u32[]{:S(2)}) copy-start(f32[1,2,64,2]{2,3,1,0:T(2,128)} %param.13) | copy-start | bytes 3076
  123.9 26.7 %all-to-all-start.1 = ((f32[16,1,24,768]{3,2,1,0:T(8,128)}), f32[16,1,24,768]{3,2,1,0:T(8,128)S(1)}, u32[]{:S(2)}, u32[]{:S(2)}) async-start(f32[16,1,24,768]{3,2,1,0:T(8,128)} %bitcast.238), calls=%async_computation.2 | async-start | bytes 2359296 | tf_op jit(solution)/shard_map/all_to_all | solution.py:74
  130.9 135.5 %reduce-scatter.6.cloned.1.call-start = ((), (), s32[]{:S(2)}) async-start(), calls=%async_computation.10 | async-start | bytes 5898240 | tf_op jit(solution)/shard_map/reduce_scatter | solution.py:73
  150.7 1.8 copy-start
  152.5 8.0 %collective-permute-start = (bf16[64,768]{1,0:T(8,128)(2,1)S(1)}, bf16[64,768]{1,0:T(8,128)(2,1)S(1)}, u32[]{:S(2)}, u32[]{:S(2)}) collective-permute-start(bf16[64,768]{1,0:T(8,128)(2,1)S(1)} %fusion.69), channel_id=1, source_target_pairs={{0,64},{1,65},{2,66},{3,67},{4,68},{5,69},{6,70},{7,71},{8,72},{9,... | collective-permute-start | bytes 294920 | tf_op jit(solution)/shard_map/ppermute | solution.py:13
  174.4 40.8 %slice-start.2 = ((s8[6291456]{0:T(1024)(128)(4,1)}), s8[4194304]{0:T(1024)(128)(4,1)S(1)}, s32[]{:S(2)}) async-start(s8[6291456]{0:T(1024)(128)(4,1)} %bitcast.242), calls=%async_computation.14 | async-start | bytes 8388608
  209.5 5.7 %slice-start.3 = ((s8[6291456]{0:T(1024)(128)(4,1)}), s8[2097152]{0:T(1024)(128)(4,1)S(1)}, s32[]{:S(2)}) async-start(s8[6291456]{0:T(1024)(128)(4,1)} %bitcast.242), calls=%async_computation.15 | async-start | bytes 4194304
  266.4 26.7 %all-to-all-start.3 = ((f32[16,1,24,768]{3,2,1,0:T(8,128)}), f32[16,1,24,768]{3,2,1,0:T(8,128)S(1)}, u32[]{:S(2)}, u32[]{:S(2)}) async-start(f32[16,1,24,768]{3,2,1,0:T(8,128)} %bitcast.237), calls=%async_computation.5 | async-start | bytes 2359296 | tf_op jit(solution)/shard_map/all_to_all | solution.py:74
  273.4 135.5 %reduce-scatter.8.cloned.1.call-start = ((), (), s32[]{:S(2)}) async-start(), calls=%async_computation.11 | async-start | bytes 5898240 | tf_op jit(solution)/shard_map/reduce_scatter | solution.py:73
  295.0 8.0 %collective-permute-start.1 = (bf16[64,768]{1,0:T(8,128)(2,1)S(1)}, bf16[64,768]{1,0:T(8,128)(2,1)S(1)}, u32[]{:S(2)}, u32[]{:S(2)}) collective-permute-start(bf16[64,768]{1,0:T(8,128)(2,1)S(1)} %fusion.74), channel_id=1, source_target_pairs={{0,64},{1,65},{2,66},{3,67},{4,68},{5,69},{6,70},{7,71},{8,72},{9,... | collective-permute-start | bytes 294920 | tf_op jit(solution)/shard_map/ppermute | solution.py:13
  316.9 40.8 %slice-start.4 = ((s8[6291456]{0:T(1024)(128)(4,1)}), s8[4194304]{0:T(1024)(128)(4,1)S(1)}, s32[]{:S(2)}) async-start(s8[6291456]{0:T(1024)(128)(4,1)} %bitcast.244), calls=%async_computation.16 | async-start | bytes 8388608
  351.9 5.7 %slice-start.5 = ((s8[6291456]{0:T(1024)(128)(4,1)}), s8[2097152]{0:T(1024)(128)(4,1)S(1)}, s32[]{:S(2)}) async-start(s8[6291456]{0:T(1024)(128)(4,1)} %bitcast.244), calls=%async_computation.17 | async-start | bytes 4194304
  408.9 26.7 %all-to-all-start.5 = ((f32[16,1,24,768]{3,2,1,0:T(8,128)}), f32[16,1,24,768]{3,2,1,0:T(8,128)S(1)}, u32[]{:S(2)}, u32[]{:S(2)}) async-start(f32[16,1,24,768]{3,2,1,0:T(8,128)} %bitcast.239), calls=%async_computation.8 | async-start | bytes 2359296 | tf_op jit(solution)/shard_map/all_to_all | solution.py:74
Sparse Core Ops, SparseCore 0:
  77.2 46.7 reduce-scatter.3
  219.7 46.7 reduce-scatter.5
  362.1 46.7 reduce-scatter.7
where the time goes:
time: 446 us; the launch traced here: 445 us
  waiting for transfers between devices  210 us (47%)
  blocking collectives  146 us (33%)
  matrix products  30 us (7%)
  starting transfers between devices  23.6 us (5%)
  between operations  13.7 us (3%)
  local copies, waits for them, and re-layouts  12.7 us (3%)
  other arithmetic  8.98 us (2%)
    reduce_scatter x3, waiting for transfers between devices, shards(): lax.psum_scatter(partial_out, 'tensor', scatter_dimension=3, tiled=True)  140 us
    all_to_all x3, blocking collectives, shards(): lax.all_to_all(outgoing, 'expert', split_axis=0, concat_axis=0, tiled=True)  110 us
    all_to_all x3, waiting for transfers between devices, shards(): lax.all_to_all(result, 'expert', split_axis=0, concat_axis=0, tiled=True)  56.5 us
    all_to_all x3, starting transfers between devices, shards(): lax.all_to_all(result, 'expert', split_axis=0, concat_axis=0, tiled=True)  20.9 us
    all_gather x3, blocking collectives, shards(): source_rows = lax.all_gather(normed, 'tensor', axis=1, tiled=True)  18.5 us
    psum x3, blocking collectives, shards(): sums = lax.psum(jnp.sum(xf * xf, axis=1), 'tensor')  17.6 us
    dot_general x3, matrix products, shards(): jnp.einsum('sekd,edf->sekf', lax.all_to_all(outgoing, 'expert', split_axi...  17.1 us
    ppermute x2, waiting for transfers between devices, from_behind(): return lax.ppermute(block, axis, route)  13.4 us
  transfers between devices with their start and end apart: 8, of which 8 were waited for; matrix products, arithmetic and copies ran while one was open for 1% of the time, Pallas kernels for 0%

commit v1 on v0

v1 whole, which is shorter than its diff:
```python
import jax
import jax.numpy as jnp
from jax import lax
from jax.sharding import PartitionSpec as P

D = 3072
EXPERTS = 8


def from_behind(block, axis, distance):
    devices = range(lax.axis_size(axis))
    route = [(i - distance, i) for i in devices if i - distance in devices]
    return lax.ppermute(block, axis, route)


def swap(block, axis, bit):
    n = lax.axis_size(axis)
    return lax.ppermute(block, axis, [(i, i ^ bit) for i in range(n)])


def shards(tokens, norm_gain, expert_ids, gate_weights, w_up, w_down):
    segments = lax.axis_size("section")
    n_exp = lax.axis_size("expert")
    segment_pos = lax.axis_index("section")
    t_pos = lax.axis_index("tensor")
    x_lo = t_pos // 2
    core = t_pos % 2
    micro = tokens.shape[0]
    rows_here = tokens.shape[1]
    quarter = tokens.shape[2]
    capacity = max(3 * rows_here // 8, 2 * rows_here // EXPERTS)
    gain_full = lax.all_gather(norm_gain[0], "tensor", axis=0, tiled=True)
    up_local = w_up[0]
    down_local = w_down[0]
    local_count = up_local.shape[0]
    copies = n_exp * local_count // EXPERTS
    collected = jnp.zeros((micro, rows_here, quarter), jnp.bfloat16)
    carried = jnp.zeros((rows_here, quarter), jnp.bfloat16)
    total_steps = micro + segments - 1
    x_first = x_lo == 0
    core_first = core == 0
    for step in range(total_steps):
        which = step - segment_pos
        which_safe = jnp.clip(which, 0, micro - 1)
        entering = tokens[min(step, micro - 1)]
        current = jnp.where(segment_pos == 0, entering, carried)
        routes = lax.dynamic_index_in_dim(expert_ids[0], which_safe, 0, keepdims=False)
        weights = lax.dynamic_index_in_dim(gate_weights[0], which_safe, 0, keepdims=False)
        xf = current.astype(jnp.float32)
        other = swap(current, "tensor", 2)
        half_rows = jnp.where(
            x_first,
            jnp.concatenate([current, other], axis=1),
            jnp.concatenate([other, current], axis=1),
        )
        flat = routes.reshape(-1)
        onehot = (flat[:, None] == jnp.arange(EXPERTS, dtype=jnp.int32)[None, :]).astype(jnp.int32)
        slot = jnp.sum((jnp.cumsum(onehot, axis=0) - onehot) * onehot, axis=1)
        dest = flat * capacity + slot
        source = (
            jnp.full((EXPERTS * capacity,), -1, jnp.int32)
            .at[dest]
            .set(jnp.arange(2 * rows_here, dtype=jnp.int32) // 2)
        )
        filled = source >= 0
        outgoing = jnp.where(
            filled[:, None],
            jnp.take(half_rows, jnp.maximum(source, 0), axis=0),
            jnp.zeros((), jnp.bfloat16),
        )
        outgoing = outgoing.reshape(EXPERTS, capacity, 2 * quarter)
        outgoing = jnp.repeat(outgoing, copies, axis=0).reshape(
            n_exp, local_count, capacity, 2 * quarter
        )
        mine = lax.all_to_all(outgoing, "expert", split_axis=0, concat_axis=0, tiled=True)
        theirs = swap(mine, "tensor", 1)
        lo_q = lambda a: a[..., :quarter]
        hi_q = lambda a: a[..., quarter:]
        first = jnp.where(core_first, mine, theirs)
        second = jnp.where(core_first, theirs, mine)
        rows = jnp.concatenate([lo_q(first), lo_q(second), hi_q(first), hi_q(second)], axis=-1)
        rf = rows.astype(jnp.float32)
        sums = jnp.sum(rf * rf, axis=-1)
        normed = (rf * lax.rsqrt(sums / D + 1e-05)[..., None] * gain_full).astype(jnp.bfloat16)
        summed_up = jnp.einsum(
            "sekd,edf->sekf", normed, up_local, preferred_element_type=jnp.float32
        )
        hidden = jax.nn.silu(summed_up).astype(jnp.bfloat16)
        partial_out = jnp.einsum(
            "sekf,efd->sekd", hidden, down_local, preferred_element_type=jnp.float32
        )
        pq = [partial_out[..., q * quarter:(q + 1) * quarter] for q in range(4)]
        keep = jnp.where(
            core_first,
            jnp.concatenate([pq[0], pq[2]], axis=-1),
            jnp.concatenate([pq[1], pq[3]], axis=-1),
        )
        give = jnp.where(
            core_first,
            jnp.concatenate([pq[1], pq[3]], axis=-1),
            jnp.concatenate([pq[0], pq[2]], axis=-1),
        )
        got = swap(give.astype(jnp.bfloat16), "tensor", 1)
        chip_sum = (keep + got.astype(jnp.float32)).astype(jnp.bfloat16)
        returned = lax.all_to_all(chip_sum, "expert", split_axis=0, concat_axis=0, tiled=True)
        summed = jnp.sum(
            returned.reshape(EXPERTS, copies, capacity, 2 * quarter).astype(jnp.float32), axis=1
        )
        picked = jnp.take(summed.reshape(-1, 2 * quarter), dest, axis=0)
        picked = picked.reshape(rows_here, 2, 2 * quarter)
        y_half = jnp.sum(picked * weights[:, :, None], axis=1)
        y_keep = jnp.where(x_first, y_half[:, :quarter], y_half[:, quarter:])
        y_give = jnp.where(x_first, y_half[:, quarter:], y_half[:, :quarter])
        y_got = swap(y_give, "tensor", 2)
        mixed = xf + (y_keep + y_got)
        produced = mixed.astype(jnp.bfloat16)
        chosen = (jnp.arange(micro, dtype=jnp.int32) == which)[:, None, None]
        collected = jnp.where(chosen, produced[None], collected)
        if step + 1 < total_steps:
            carried = from_behind(produced, "section", 1)
    return collected[None]


def solution(mesh):
    placed = (
        P(None, "expert", "tensor"),
        P("section", "tensor"),
        P("section", None, "expert", None),
        P("section", None, "expert", None),
        P("section", "expert", None, "tensor"),
        P("section", "expert", "tensor", None),
    )
    return jax.shard_map(
        shards,
        mesh=mesh,
        in_specs=placed,
        out_specs=P("section", None, "expert", "tensor"),
        check_vma=False,
    )
```

time: 446 us -> 252 us (0.57)
  waiting for transfers between devices: 210 us -> 106 us
  blocking collectives: 146 us -> 68.8 us
  matrix products: 30 us -> 16.4 us
  between operations: 13.7 us -> 0.75 us
  other arithmetic: 8.98 us -> 16.4 us
  local copies, waits for them, and re-layouts: 12.7 us -> 20.1 us
    reduce_scatter x3 -> x0, waiting for transfers between devices: 140 us -> none  [shards(): lax.psum_scatter(partial_out, 'tensor', scatter_dimension=3, tiled=True)]
    all_to_all x3, blocking collectives: 110 us -> 63.7 us  [shards(): lax.all_to_all(outgoing, 'expert', split_axis=0, concat_axis=0, tiled=True)]
    ppermute x0 -> x12, waiting for transfers between devices: none -> 34.6 us  [swap(): return lax.ppermute(block, axis, [(i, i ^ bit) for i in range(n)])]
    psum x3 -> x0, blocking collectives: 17.6 us -> none  [shards(): sums = lax.psum(jnp.sum(xf * xf, axis=1), 'tensor')]
    all_gather x3 -> x1, blocking collectives: 18.5 us -> 5.17 us  [shards(): gain_full = lax.all_gather(norm_gain[0], 'tensor', axis=0, tiled=True)]
    all_to_all x3, starting transfers between devices: 20.9 us -> 11.5 us  [shards(): lax.all_to_all(chip_sum, 'expert', split_axis=0, concat_axis=0, tiled=True)]
    dot_general x3, matrix products: 17.1 us -> 8.07 us  [shards(): jnp.einsum('sekd,edf->sekf', normed, up_local, preferred_element_type=jnp...]
    ppermute x0 -> x12, starting transfers between devices: none -> 8.21 us  [swap(): return lax.ppermute(block, axis, [(i, i ^ bit) for i in range(n)])]
  transfers between devices with their start and end apart: 8 -> 17, of which waited for: 8 -> 16; matrix products, arithmetic and copies ran while one was open for 1% -> 3% of each run, Pallas kernels for 0% -> 0%
where the time goes in v1:
time: 252 us; the launch traced here: 251 us
  waiting for transfers between devices  106 us (42%)
  blocking collectives  68.8 us (27%)
  starting transfers between devices  22.3 us (9%)
  local copies, waits for them, and re-layouts  20.1 us (8%)
  other arithmetic  16.4 us (7%)
  matrix products  16.4 us (7%)
    all_to_all x3, blocking collectives, shards(): lax.all_to_all(outgoing, 'expert', split_axis=0, concat_axis=0, tiled=True)  63.7 us
    all_to_all x3, waiting for transfers between devices, shards(): lax.all_to_all(chip_sum, 'expert', split_axis=0, concat_axis=0, tiled=True)  57.7 us
    ppermute x12, waiting for transfers between devices, swap(): return lax.ppermute(block, axis, [(i, i ^ bit) for i in range(n)])  34.6 us
    ppermute x2, waiting for transfers between devices, from_behind(): return lax.ppermute(block, axis, route)  14.2 us
    all_to_all x3, starting transfers between devices, shards(): lax.all_to_all(chip_sum, 'expert', split_axis=0, concat_axis=0, tiled=True)  11.5 us
    dot_general x3, matrix products, shards(): jnp.einsum('sekf,efd->sekd', hidden, down_local, preferred_element_type=j...  8.34 us
    ppermute x12, starting transfers between devices, swap(): return lax.ppermute(block, axis, [(i, i ^ bit) for i in range(n)])  8.21 us
    dot_general x3, matrix products, shards(): jnp.einsum('sekd,edf->sekf', normed, up_local, preferred_element_type=jnp...  8.07 us
  transfers between devices with their start and end apart: 17, of which 16 were waited for; matrix products, arithmetic and copies ran while one was open for 3% of the time, Pallas kernels for 0%

profile of v1, /device:TPU:6, one launch (start us, length us, event | category | flops | bytes accessed | tf_op | source)
XLA Modules:
  0.0 251.3 jit_solution(2905733946833905288)
XLA Ops:
  7.0 26.0 %all_to_all.30 = bf16[16,1,24,1536]{3,2,1,0:T(8,128)(2,1)S(1)} all-to-all(bf16[16,1,24,1536]{3,2,1,0:T(8,128)(2,1)S(1)} %bitcast.230), channel_id=1, replica_groups=mesh['section'=2,'expert'=16,'tensor'=4] {'expert'}, dimensions={0} | all-to-all | bytes 2359296 | tf_op jit(solution)/shard_map/all_to_all | solution.py:75
  33.0 5.2 %all-gather = f32[1,3072]{1,0:T(1,128)S(1)} all-gather(f32[1,768]{1,0:T(1,128)S(1)} %copy-done.2), channel_id=2, replica_groups=mesh['section'=2,'expert'=16,'tensor'=4] {'tensor'}, dimensions={1}, use_global_device_ids=true | all-gather | bytes 15360 | tf_op jit(solution)/shard_map/all_gather | solution.py:32
  43.8 2.8 %fusion.12 = f32[16,1,24,3072]{3,2,0,1:T(8,128)S(1)} fusion(bf16[1,1,1024,3072]{3,2,1,0:T(8,128)(2,1)S(1)} %bitcast.246, f32[16,24,1024]{2,1,0:T(8,128)S(1)} %fusion.10), kind=kOutput, calls=%fused_computation.27 | convolution fusion | flops 2417885184 | bytes 12582912 | tf_op jit(solution)/shard_map/sekf,efd->sekd/dot_general | solution.py:89
  51.7 3.8 %all-to-all-start.1 = ((bf16[16,1,24,1536]{3,2,1,0:T(8,128)(2,1)}), bf16[16,1,24,1536]{3,2,1,0:T(8,128)(2,1)S(1)}, u32[]{:S(2)}, u32[]{:S(2)}) async-start(bf16[16,1,24,1536]{3,2,1,0:T(8,128)(2,1)} %fusion.60), calls=%async_computation.1 | async-start | bytes 2359296 | tf_op jit(solution)/shard_map/all_to_all | solution.py:105
  56.9 19.7 %all-to-all-done.1 = bf16[16,1,24,1536]{3,2,1,0:T(8,128)(2,1)S(1)} async-done(((bf16[16,1,24,1536]{3,2,1,0:T(8,128)(2,1)}), bf16[16,1,24,1536]{3,2,1,0:T(8,128)(2,1)S(1)}, u32[]{:S(2)}, u32[]{:S(2)}) %all-to-all-start.1) | async-done | bytes 1179680 | tf_op jit(solution)/shard_map/all_to_all | solution.py:105
  80.6 5.1 %collective-permute-done.3 = f32[64,768]{1,0:T(8,128)S(1)} collective-permute-done((f32[64,768]{1,0:T(8,128)S(1)}, f32[64,768]{1,0:T(8,128)S(1)}, u32[]{:S(2)}, u32[]{:S(2)}) %collective-permute-start.3) | collective-permute-done | bytes 196640 | tf_op jit(solution)/shard_map/ppermute | solution.py:18
  87.1 6.8 %collective-permute-done.4 = bf16[64,768]{1,0:T(8,128)(2,1)S(1)} collective-permute-done((bf16[64,768]{1,0:T(8,128)(2,1)S(1)}, bf16[64,768]{1,0:T(8,128)(2,1)S(1)}, u32[]{:S(2)}, u32[]{:S(2)}) %collective-permute-start.4) | collective-permute-done | bytes 98336 | tf_op jit(solution)/shard_map/ppermute | solution.py:13
  95.6 3.1 %collective-permute-done.5 = bf16[64,768]{1,0:T(8,128)(2,1)S(1)} collective-permute-done((bf16[64,768]{1,0:T(8,128)(2,1)S(1)}, bf16[64,768]{1,0:T(8,128)(2,1)S(1)}, u32[]{:S(2)}, u32[]{:S(2)}) %collective-permute-start.5) | collective-permute-done | bytes 98336 | tf_op jit(solution)/shard_map/ppermute | solution.py:18
  100.0 18.8 %all_to_all.31 = bf16[16,1,24,1536]{3,2,1,0:T(8,128)(2,1)S(1)} all-to-all(bf16[16,1,24,1536]{3,2,1,0:T(8,128)(2,1)S(1)} %bitcast.231), channel_id=1, replica_groups=mesh['section'=2,'expert'=16,'tensor'=4] {'expert'}, dimensions={0} | all-to-all | bytes 2359296 | tf_op jit(solution)/shard_map/all_to_all | solution.py:75
  118.8 2.8 %collective-permute-done.6 = bf16[16,1,24,1536]{3,2,0,1:T(8,128)(2,1)S(1)} collective-permute-done((bf16[16,1,24,1536]{3,2,0,1:T(8,128)(2,1)S(1)}, bf16[16,1,24,1536]{3,2,0,1:T(8,128)(2,1)S(1)}, u32[]{:S(2)}, u32[]{:S(2)}) %collective-permute-start.6) | collective-permute-done | bytes 1179680 | tf_op jit(solution)/shard_map/ppermute | solution.py:18
  127.3 2.8 %fusion.15 = f32[16,1,24,3072]{3,2,0,1:T(8,128)S(1)} fusion(bf16[1,1,1024,3072]{3,2,1,0:T(8,128)(2,1)S(1)} %bitcast.248, f32[16,24,1024]{2,1,0:T(8,128)S(1)} %fusion.8), kind=kOutput, calls=%fused_computation.28 | convolution fusion | flops 2417885184 | bytes 12582912 | tf_op jit(solution)/shard_map/sekf,efd->sekd/dot_general | solution.py:89
  131.0 2.7 %collective-permute-done.7 = bf16[16,1,24,1536]{3,2,0,1:T(8,128)(2,1)S(1)} collective-permute-done((bf16[16,1,24,1536]{3,2,0,1:T(8,128)(2,1)S(1)}, bf16[16,1,24,1536]{3,2,0,1:T(8,128)(2,1)S(1)}, u32[]{:S(2)}, u32[]{:S(2)}) %collective-permute-start.7) | collective-permute-done | bytes 1179680 | tf_op jit(solution)/shard_map/ppermute | solution.py:18
  135.2 3.7 %all-to-all-start.3 = ((bf16[16,1,24,1536]{3,2,1,0:T(8,128)(2,1)}), bf16[16,1,24,1536]{3,2,1,0:T(8,128)(2,1)S(1)}, u32[]{:S(2)}, u32[]{:S(2)}) async-start(bf16[16,1,24,1536]{3,2,1,0:T(8,128)(2,1)} %fusion.61), calls=%async_computation.3 | async-start | bytes 2359296 | tf_op jit(solution)/shard_map/all_to_all | solution.py:105
  141.1 18.1 %all-to-all-done.3 = bf16[16,1,24,1536]{3,2,1,0:T(8,128)(2,1)S(1)} async-done(((bf16[16,1,24,1536]{3,2,1,0:T(8,128)(2,1)}), bf16[16,1,24,1536]{3,2,1,0:T(8,128)(2,1)S(1)}, u32[]{:S(2)}, u32[]{:S(2)}) %all-to-all-start.3) | async-done | bytes 1179680 | tf_op jit(solution)/shard_map/all_to_all | solution.py:105
  163.4 4.4 %collective-permute-done.8 = f32[64,768]{1,0:T(8,128)S(1)} collective-permute-done((f32[64,768]{1,0:T(8,128)S(1)}, f32[64,768]{1,0:T(8,128)S(1)}, u32[]{:S(2)}, u32[]{:S(2)}) %collective-permute-start.8) | collective-permute-done | bytes 196640 | tf_op jit(solution)/shard_map/ppermute | solution.py:18
  169.2 7.3 %collective-permute-done.9 = bf16[64,768]{1,0:T(8,128)(2,1)S(1)} collective-permute-done((bf16[64,768]{1,0:T(8,128)(2,1)S(1)}, bf16[64,768]{1,0:T(8,128)(2,1)S(1)}, u32[]{:S(2)}, u32[]{:S(2)}) %collective-permute-start.9) | collective-permute-done | bytes 98336 | tf_op jit(solution)/shard_map/ppermute | solution.py:13
  177.2 4.0 %collective-permute-done.10 = bf16[64,768]{1,0:T(8,128)(2,1)S(1)} collective-permute-done((bf16[64,768]{1,0:T(8,128)(2,1)S(1)}, bf16[64,768]{1,0:T(8,128)(2,1)S(1)}, u32[]{:S(2)}, u32[]{:S(2)}) %collective-permute-start.10) | collective-permute-done | bytes 98336 | tf_op jit(solution)/shard_map/ppermute | solution.py:18
  182.6 18.9 %all_to_all.32 = bf16[16,1,24,1536]{3,2,1,0:T(8,128)(2,1)S(1)} all-to-all(bf16[16,1,24,1536]{3,2,1,0:T(8,128)(2,1)S(1)} %bitcast.232), channel_id=1, replica_groups=mesh['section'=2,'expert'=16,'tensor'=4] {'expert'}, dimensions={0} | all-to-all | bytes 2359296 | tf_op jit(solution)/shard_map/all_to_all | solution.py:75
  201.5 2.8 %collective-permute-done.11 = bf16[16,1,24,1536]{3,2,0,1:T(8,128)(2,1)S(1)} collective-permute-done((bf16[16,1,24,1536]{3,2,0,1:T(8,128)(2,1)S(1)}, bf16[16,1,24,1536]{3,2,0,1:T(8,128)(2,1)S(1)}, u32[]{:S(2)}, u32[]{:S(2)}) %collective-permute-start.11) | collective-permute-done | bytes 1179680 | tf_op jit(solution)/shard_map/ppermute | solution.py:18
  210.0 2.8 %fusion.18 = f32[16,1,24,3072]{3,2,0,1:T(8,128)S(1)} fusion(bf16[1,1,1024,3072]{3,2,1,0:T(8,128)(2,1)S(1)} %bitcast.250, f32[16,24,1024]{2,1,0:T(8,128)S(1)} %fusion.6), kind=kOutput, calls=%fused_computation.29 | convolution fusion | flops 2417885184 | bytes 12582912 | tf_op jit(solution)/shard_map/sekf,efd->sekd/dot_general | solution.py:89
  213.7 2.7 %collective-permute-done.12 = bf16[16,1,24,1536]{3,2,0,1:T(8,128)(2,1)S(1)} collective-permute-done((bf16[16,1,24,1536]{3,2,0,1:T(8,128)(2,1)S(1)}, bf16[16,1,24,1536]{3,2,0,1:T(8,128)(2,1)S(1)}, u32[]{:S(2)}, u32[]{:S(2)}) %collective-permute-start.12) | collective-permute-done | bytes 1179680 | tf_op jit(solution)/shard_map/ppermute | solution.py:18
  217.8 4.0 %all-to-all-start.5 = ((bf16[16,1,24,1536]{3,2,1,0:T(8,128)(2,1)}), bf16[16,1,24,1536]{3,2,1,0:T(8,128)(2,1)S(1)}, u32[]{:S(2)}, u32[]{:S(2)}) async-start(bf16[16,1,24,1536]{3,2,1,0:T(8,128)(2,1)} %fusion.62), calls=%async_computation.5 | async-start | bytes 2359296 | tf_op jit(solution)/shard_map/all_to_all | solution.py:105
  221.9 20.0 %all-to-all-done.5 = bf16[16,1,24,1536]{3,2,1,0:T(8,128)(2,1)S(1)} async-done(((bf16[16,1,24,1536]{3,2,1,0:T(8,128)(2,1)}), bf16[16,1,24,1536]{3,2,1,0:T(8,128)(2,1)S(1)}, u32[]{:S(2)}, u32[]{:S(2)}) %all-to-all-start.5) | async-done | bytes 1179680 | tf_op jit(solution)/shard_map/all_to_all | solution.py:105
  246.1 4.3 %collective-permute-done.13 = f32[64,768]{1,0:T(8,128)S(1)} collective-permute-done((f32[64,768]{1,0:T(8,128)S(1)}, f32[64,768]{1,0:T(8,128)S(1)}, u32[]{:S(2)}, u32[]{:S(2)}) %collective-permute-start.13) | collective-permute-done | bytes 196640 | tf_op jit(solution)/shard_map/ppermute | solution.py:18
  (166 shorter events, 58.0 us)
Async XLA Ops:
  0.9 4.7 %collective-permute-start = (bf16[64,768]{1,0:T(8,128)(2,1)S(1)}, bf16[64,768]{1,0:T(8,128)(2,1)S(1)}, u32[]{:S(2)}, u32[]{:S(2)}) collective-permute-start(bf16[64,768]{1,0:T(8,128)(2,1)S(1)} %select_bitcast_fusion), channel_id=1, source_target_pairs={{0,2},{1,3},{2,0},{3,1},{4,6},{5,7},{6,4},{7,5},{8,10},{9,11},{10,... | collective-permute-start | bytes 294920 | tf_op jit(solution)/shard_map/ppermute | solution.py:18
  6.9 26.1 %copy-start.2 = (f32[1,768]{1,0:T(1,128)S(1)}, f32[1,768]{1,0:T(1,128)}, u32[]{:S(2)}) copy-start(f32[1,768]{1,0:T(1,128)} %param.11) | copy-start | bytes 9220
  33.0 5.2 %collective-permute-start.1 = (bf16[16,1,24,1536]{3,2,0,1:T(8,128)(2,1)S(1)}, bf16[16,1,24,1536]{3,2,0,1:T(8,128)(2,1)S(1)}, u32[]{:S(2)}, u32[]{:S(2)}) collective-permute-start(bf16[16,1,24,1536]{3,2,0,1:T(8,128)(2,1)S(1)} %bitcast.224), channel_id=1, source_target_pairs={{0,1},{1,0},{2,3},{3,2},{4,5},{5,4},{6,7},{7,6},{8,9},{9,8},{10,11... | collective-permute-start | bytes 3538952 | tf_op jit(solution)/shard_map/ppermute | solution.py:18
  38.4 2.7 %slice-start.1 = ((s8[6291456]{0:T(1024)(128)(4,1)}), s8[2097152]{0:T(1024)(128)(4,1)S(1)}, s32[]{:S(2)}) async-start(s8[6291456]{0:T(1024)(128)(4,1)} %bitcast.239), calls=%async_computation.7 | async-start | bytes 4194304
  38.7 5.1 %slice-start.6 = ((s8[6291456]{0:T(1024)(128)(4,1)}), s8[4194304]{0:T(1024)(128)(4,1)S(1)}, s32[]{:S(2)}) async-start(s8[6291456]{0:T(1024)(128)(4,1)} %bitcast.245), calls=%async_computation.12 | async-start | bytes 8388608
  47.4 2.9 %collective-permute-start.2 = (bf16[16,1,24,1536]{3,2,0,1:T(8,128)(2,1)S(1)}, bf16[16,1,24,1536]{3,2,0,1:T(8,128)(2,1)S(1)}, u32[]{:S(2)}, u32[]{:S(2)}) collective-permute-start(bf16[16,1,24,1536]{3,2,0,1:T(8,128)(2,1)S(1)} %select_convert_fusion.2), channel_id=1, source_target_pairs={{0,1},{1,0},{2,3},{3,2},{4,5},{5,4},{6,7},{7,6},{8,9},{9,8},{10,11... | collective-permute-start | bytes 3538952 | tf_op jit(solution)/shard_map/ppermute | solution.py:18
  51.7 3.8 %copy-start.1 = (f32[1,2,64,2]{2,3,1,0:T(2,128)S(1)}, f32[1,2,64,2]{2,3,1,0:T(2,128)}, u32[]{:S(2)}) copy-start(f32[1,2,64,2]{2,3,1,0:T(2,128)} %param.13) | copy-start | bytes 3076
  51.7 24.8 %all-to-all-start.1 = ((bf16[16,1,24,1536]{3,2,1,0:T(8,128)(2,1)}), bf16[16,1,24,1536]{3,2,1,0:T(8,128)(2,1)S(1)}, u32[]{:S(2)}, u32[]{:S(2)}) async-start(bf16[16,1,24,1536]{3,2,1,0:T(8,128)(2,1)} %fusion.60), calls=%async_computation.1 | async-start | bytes 2359296 | tf_op jit(solution)/shard_map/all_to_all | solution.py:105
  77.6 8.1 %copy-start = (bf16[2,64,768]{2,1,0:T(8,128)(2,1)S(1)}, bf16[2,64,768]{2,1,0:T(8,128)(2,1)}, u32[]{:S(2)}) copy-start(bf16[2,64,768]{2,1,0:T(8,128)(2,1)} %param.10) | copy-start | bytes 589828
  79.4 6.4 %collective-permute-start.3 = (f32[64,768]{1,0:T(8,128)S(1)}, f32[64,768]{1,0:T(8,128)S(1)}, u32[]{:S(2)}, u32[]{:S(2)}) collective-permute-start(f32[64,768]{1,0:T(8,128)S(1)} %slice_select_fusion.2), channel_id=1, source_target_pairs={{0,2},{1,3},{2,0},{3,1},{4,6},{5,7},{6,4},{7,5},{8,10},{9,11},{10,... | collective-permute-start | bytes 589832 | tf_op jit(solution)/shard_map/ppermute | solution.py:18
  85.8 8.1 %collective-permute-start.4 = (bf16[64,768]{1,0:T(8,128)(2,1)S(1)}, bf16[64,768]{1,0:T(8,128)(2,1)S(1)}, u32[]{:S(2)}, u32[]{:S(2)}) collective-permute-start(bf16[64,768]{1,0:T(8,128)(2,1)S(1)} %add_convert_fusion.5), channel_id=1, source_target_pairs={{0,64},{1,65},{2,66},{3,67},{4,68},{5,69},{6,70},{7,71},{8,72},{9,... | collective-permute-start | bytes 294920 | tf_op jit(solution)/shard_map/ppermute | solution.py:13
  94.0 4.7 %collective-permute-start.5 = (bf16[64,768]{1,0:T(8,128)(2,1)S(1)}, bf16[64,768]{1,0:T(8,128)(2,1)S(1)}, u32[]{:S(2)}, u32[]{:S(2)}) collective-permute-start(bf16[64,768]{1,0:T(8,128)(2,1)S(1)} %bitcast_select_fusion.1), channel_id=1, source_target_pairs={{0,2},{1,3},{2,0},{3,1},{4,6},{5,7},{6,4},{7,5},{8,10},{9,11},{10,... | collective-permute-start | bytes 294920 | tf_op jit(solution)/shard_map/ppermute | solution.py:18
  118.8 2.8 %collective-permute-start.6 = (bf16[16,1,24,1536]{3,2,0,1:T(8,128)(2,1)S(1)}, bf16[16,1,24,1536]{3,2,0,1:T(8,128)(2,1)S(1)}, u32[]{:S(2)}, u32[]{:S(2)}) collective-permute-start(bf16[16,1,24,1536]{3,2,0,1:T(8,128)(2,1)S(1)} %bitcast.225), channel_id=1, source_target_pairs={{0,1},{1,0},{2,3},{3,2},{4,5},{5,4},{6,7},{7,6},{8,9},{9,8},{10,11... | collective-permute-start | bytes 3538952 | tf_op jit(solution)/shard_map/ppermute | solution.py:18
  122.1 5.1 %slice-start.8 = ((s8[6291456]{0:T(1024)(128)(4,1)}), s8[4194304]{0:T(1024)(128)(4,1)S(1)}, s32[]{:S(2)}) async-start(s8[6291456]{0:T(1024)(128)(4,1)} %bitcast.247), calls=%async_computation.14 | async-start | bytes 8388608
  130.8 2.9 %collective-permute-start.7 = (bf16[16,1,24,1536]{3,2,0,1:T(8,128)(2,1)S(1)}, bf16[16,1,24,1536]{3,2,0,1:T(8,128)(2,1)S(1)}, u32[]{:S(2)}, u32[]{:S(2)}) collective-permute-start(bf16[16,1,24,1536]{3,2,0,1:T(8,128)(2,1)S(1)} %select_convert_fusion.1), channel_id=1, source_target_pairs={{0,1},{1,0},{2,3},{3,2},{4,5},{5,4},{6,7},{7,6},{8,9},{9,8},{10,11... | collective-permute-start | bytes 3538952 | tf_op jit(solution)/shard_map/ppermute | solution.py:18
  135.2 24.0 %all-to-all-start.3 = ((bf16[16,1,24,1536]{3,2,1,0:T(8,128)(2,1)}), bf16[16,1,24,1536]{3,2,1,0:T(8,128)(2,1)S(1)}, u32[]{:S(2)}, u32[]{:S(2)}) async-start(bf16[16,1,24,1536]{3,2,1,0:T(8,128)(2,1)} %fusion.61), calls=%async_computation.3 | async-start | bytes 2359296 | tf_op jit(solution)/shard_map/all_to_all | solution.py:105
  162.0 5.8 %collective-permute-start.8 = (f32[64,768]{1,0:T(8,128)S(1)}, f32[64,768]{1,0:T(8,128)S(1)}, u32[]{:S(2)}, u32[]{:S(2)}) collective-permute-start(f32[64,768]{1,0:T(8,128)S(1)} %slice_select_fusion.1), channel_id=1, source_target_pairs={{0,2},{1,3},{2,0},{3,1},{4,6},{5,7},{6,4},{7,5},{8,10},{9,11},{10,... | collective-permute-start | bytes 589832 | tf_op jit(solution)/shard_map/ppermute | solution.py:18
  167.8 8.6 %collective-permute-start.9 = (bf16[64,768]{1,0:T(8,128)(2,1)S(1)}, bf16[64,768]{1,0:T(8,128)(2,1)S(1)}, u32[]{:S(2)}, u32[]{:S(2)}) collective-permute-start(bf16[64,768]{1,0:T(8,128)(2,1)S(1)} %add_convert_fusion.4), channel_id=1, source_target_pairs={{0,64},{1,65},{2,66},{3,67},{4,68},{5,69},{6,70},{7,71},{8,72},{9,... | collective-permute-start | bytes 294920 | tf_op jit(solution)/shard_map/ppermute | solution.py:13
  176.5 4.7 %collective-permute-start.10 = (bf16[64,768]{1,0:T(8,128)(2,1)S(1)}, bf16[64,768]{1,0:T(8,128)(2,1)S(1)}, u32[]{:S(2)}, u32[]{:S(2)}) collective-permute-start(bf16[64,768]{1,0:T(8,128)(2,1)S(1)} %bitcast_select_fusion), channel_id=1, source_target_pairs={{0,2},{1,3},{2,0},{3,1},{4,6},{5,7},{6,4},{7,5},{8,10},{9,11},{10,... | collective-permute-start | bytes 294920 | tf_op jit(solution)/shard_map/ppermute | solution.py:18
  201.5 2.8 %collective-permute-start.11 = (bf16[16,1,24,1536]{3,2,0,1:T(8,128)(2,1)S(1)}, bf16[16,1,24,1536]{3,2,0,1:T(8,128)(2,1)S(1)}, u32[]{:S(2)}, u32[]{:S(2)}) collective-permute-start(bf16[16,1,24,1536]{3,2,0,1:T(8,128)(2,1)S(1)} %bitcast.226), channel_id=1, source_target_pairs={{0,1},{1,0},{2,3},{3,2},{4,5},{5,4},{6,7},{7,6},{8,9},{9,8},{10,11... | collective-permute-start | bytes 3538952 | tf_op jit(solution)/shard_map/ppermute | solution.py:18
  204.7 5.3 %slice-start.10 = ((s8[6291456]{0:T(1024)(128)(4,1)}), s8[4194304]{0:T(1024)(128)(4,1)S(1)}, s32[]{:S(2)}) async-start(s8[6291456]{0:T(1024)(128)(4,1)} %bitcast.249), calls=%async_computation.16 | async-start | bytes 8388608
  213.5 2.9 %collective-permute-start.12 = (bf16[16,1,24,1536]{3,2,0,1:T(8,128)(2,1)S(1)}, bf16[16,1,24,1536]{3,2,0,1:T(8,128)(2,1)S(1)}, u32[]{:S(2)}, u32[]{:S(2)}) collective-permute-start(bf16[16,1,24,1536]{3,2,0,1:T(8,128)(2,1)S(1)} %select_convert_fusion), channel_id=1, source_target_pairs={{0,1},{1,0},{2,3},{3,2},{4,5},{5,4},{6,7},{7,6},{8,9},{9,8},{10,11... | collective-permute-start | bytes 3538952 | tf_op jit(solution)/shard_map/ppermute | solution.py:18
  217.8 24.0 %all-to-all-start.5 = ((bf16[16,1,24,1536]{3,2,1,0:T(8,128)(2,1)}), bf16[16,1,24,1536]{3,2,1,0:T(8,128)(2,1)S(1)}, u32[]{:S(2)}, u32[]{:S(2)}) async-start(bf16[16,1,24,1536]{3,2,1,0:T(8,128)(2,1)} %fusion.62), calls=%async_computation.5 | async-start | bytes 2359296 | tf_op jit(solution)/shard_map/all_to_all | solution.py:105
  244.7 5.8 %collective-permute-start.13 = (f32[64,768]{1,0:T(8,128)S(1)}, f32[64,768]{1,0:T(8,128)S(1)}, u32[]{:S(2)}, u32[]{:S(2)}) collective-permute-start(f32[64,768]{1,0:T(8,128)S(1)} %slice_select_fusion), channel_id=1, source_target_pairs={{0,2},{1,3},{2,0},{3,1},{4,6},{5,7},{6,4},{7,5},{8,10},{9,11},{10,... | collective-permute-start | bytes 589832 | tf_op jit(solution)/shard_map/ppermute | solution.py:18
  (8 other events, 20.2 us)

commit v2 on v1

--- a/solution.py
+++ b/solution.py
@@ -29,30 +29,38 @@
     rows_here = tokens.shape[1]
     quarter = tokens.shape[2]
     capacity = max(3 * rows_here // 8, 2 * rows_here // EXPERTS)
-    gain_full = lax.all_gather(norm_gain[0], "tensor", axis=0, tiled=True)
+    gain = norm_gain[0]
+    gain_from = [gain, swap(gain, "tensor", 1), swap(gain, "tensor", 2), swap(gain, "tensor", 3)]
+    gain_full = jnp.concatenate(
+        [
+            jnp.where(t_pos == q, gain_from[0],
+                      jnp.where(t_pos ^ 1 == q, gain_from[1],
+                                jnp.where(t_pos ^ 2 == q, gain_from[2], gain_from[3])))
+            for q in range(4)
+        ]
+    )
     up_local = w_up[0]
     down_local = w_down[0]
     local_count = up_local.shape[0]
     copies = n_exp * local_count // EXPERTS
     collected = jnp.zeros((micro, rows_here, quarter), jnp.bfloat16)
-    carried = jnp.zeros((rows_here, quarter), jnp.bfloat16)
+    carried = jnp.zeros((rows_here, 2 * quarter), jnp.bfloat16)
     total_steps = micro + segments - 1
     x_first = x_lo == 0
     core_first = core == 0
+    tokens_other = swap(tokens, "tensor", 2)
+    tokens_half = jnp.where(
+        x_first,
+        jnp.concatenate([tokens, tokens_other], axis=2),
+        jnp.concatenate([tokens_other, tokens], axis=2),
+    )
     for step in range(total_steps):
         which = step - segment_pos
         which_safe = jnp.clip(which, 0, micro - 1)
-        entering = tokens[min(step, micro - 1)]
-        current = jnp.where(segment_pos == 0, entering, carried)
+        entering = tokens_half[min(step, micro - 1)]
+        half_rows = jnp.where(segment_pos == 0, entering, carried)
         routes = lax.dynamic_index_in_dim(expert_ids[0], which_safe, 0, keepdims=False)
         weights = lax.dynamic_index_in_dim(gate_weights[0], which_safe, 0, keepdims=False)
-        xf = current.astype(jnp.float32)
-        other = swap(current, "tensor", 2)
-        half_rows = jnp.where(
-            x_first,
-            jnp.concatenate([current, other], axis=1),
-            jnp.concatenate([other, current], axis=1),
-        )
         flat = routes.reshape(-1)
         onehot = (flat[:, None] == jnp.arange(EXPERTS, dtype=jnp.int32)[None, :]).astype(jnp.int32)
         slot = jnp.sum((jnp.cumsum(onehot, axis=0) - onehot) * onehot, axis=1)
@@ -109,15 +117,13 @@
         picked = jnp.take(summed.reshape(-1, 2 * quarter), dest, axis=0)
         picked = picked.reshape(rows_here, 2, 2 * quarter)
         y_half = jnp.sum(picked * weights[:, :, None], axis=1)
-        y_keep = jnp.where(x_first, y_half[:, :quarter], y_half[:, quarter:])
-        y_give = jnp.where(x_first, y_half[:, quarter:], y_half[:, :quarter])
-        y_got = swap(y_give, "tensor", 2)
-        mixed = xf + (y_keep + y_got)
-        produced = mixed.astype(jnp.bfloat16)
+        y_got = swap(y_half, "tensor", 2)
+        produced_half = (half_rows.astype(jnp.float32) + (y_half + y_got)).astype(jnp.bfloat16)
+        produced = jnp.where(x_first, produced_half[:, :quarter], produced_half[:, quarter:])
         chosen = (jnp.arange(micro, dtype=jnp.int32) == which)[:, None, None]
         collected = jnp.where(chosen, produced[None], collected)
         if step + 1 < total_steps:
-            carried = from_behind(produced, "section", 1)
+            carried = from_behind(produced_half, "section", 1)
     return collected[None]
 
 

time: 252 us -> 262 us (1.040)
  waiting for transfers between devices: 106 us -> 117 us
    ppermute x12 -> x13, waiting for transfers between devices: 34.6 us -> 42.8 us  [swap(): return lax.ppermute(block, axis, [(i, i ^ bit) for i in range(n)])]
    all_gather x1 -> x0, blocking collectives: 5.17 us -> none  [shards(): gain_full = lax.all_gather(norm_gain[0], 'tensor', axis=0, tiled=True)]
    all_to_all x3, blocking collectives: 63.7 us -> 68.8 us  [shards(): lax.all_to_all(outgoing, 'expert', split_axis=0, concat_axis=0, tiled=True)]
    ppermute x12 -> x13, starting transfers between devices: 8.21 us -> 7.32 us  [swap(): return lax.ppermute(block, axis, [(i, i ^ bit) for i in range(n)])]
    unnamed x30 -> x28, local copies, waits for them, and re-layouts: 5.3 us -> 5.29 us
  transfers between devices with their start and end apart: 17 -> 18, of which waited for: 16 -> 17; matrix products, arithmetic and copies ran while one was open for 3% -> 3% of each run, Pallas kernels for 0% -> 0%
where the time goes in v2:
time: 262 us; the launch traced here: 261 us
  waiting for transfers between devices  117 us (45%)
  blocking collectives  68.8 us (26%)
  starting transfers between devices  21.8 us (8%)
  local copies, waits for them, and re-layouts  19.7 us (8%)
  other arithmetic  16.5 us (6%)
  matrix products  16.4 us (6%)
    all_to_all x3, blocking collectives, shards(): lax.all_to_all(outgoing, 'expert', split_axis=0, concat_axis=0, tiled=True)  68.8 us
    all_to_all x3, waiting for transfers between devices, shards(): lax.all_to_all(chip_sum, 'expert', split_axis=0, concat_axis=0, tiled=True)  59 us
    ppermute x13, waiting for transfers between devices, swap(): return lax.ppermute(block, axis, [(i, i ^ bit) for i in range(n)])  42.8 us
    ppermute x2, waiting for transfers between devices, from_behind(): return lax.ppermute(block, axis, route)  15.5 us
    all_to_all x3, starting transfers between devices, shards(): lax.all_to_all(chip_sum, 'expert', split_axis=0, concat_axis=0, tiled=True)  11.9 us
    dot_general x3, matrix products, shards(): jnp.einsum('sekf,efd->sekd', hidden, down_local, preferred_element_type=j...  8.36 us
    dot_general x3, matrix products, shards(): jnp.einsum('sekd,edf->sekf', normed, up_local, preferred_element_type=jnp...  8.07 us
    ppermute x13, starting transfers between devices, swap(): return lax.ppermute(block, axis, [(i, i ^ bit) for i in range(n)])  7.32 us
  transfers between devices with their start and end apart: 18, of which 17 were waited for; matrix products, arithmetic and copies ran while one was open for 3% of the time, Pallas kernels for 0%

profile of v2, /device:TPU:6, one launch (start us, length us, event | category | flops | bytes accessed | tf_op | source)
XLA Modules:
  0.0 261.3 jit_solution(2557414067744237110)
XLA Ops:
  9.4 25.6 %all_to_all.30 = bf16[16,1,24,1536]{3,2,1,0:T(8,128)(2,1)S(1)} all-to-all(bf16[16,1,24,1536]{3,2,1,0:T(8,128)(2,1)S(1)} %bitcast.232), channel_id=1, replica_groups=mesh['section'=2,'expert'=16,'tensor'=4] {'expert'}, dimensions={0} | all-to-all | bytes 2359296 | tf_op jit(solution)/shard_map/all_to_all | solution.py:83
  42.5 2.7 %fusion.10 = f32[16,24,1024]{2,1,0:T(8,128)S(1)} fusion(bf16[1,1,3072,1024]{3,2,1,0:T(8,128)(2,1)S(1)} %bitcast.239, bf16[16,24,768]{2,1,0:T(8,128)(2,1)S(1)} %get-tuple-element.59, bf16[16,24,768]{2,1,0:T(8,128)(2,1)S(1)} %get-tuple-element.55, bf16[16,24,768]{2,1,0:T(8,128)(2,1)S(1)} %get-tuple-element.58, ...), kind=kOutput, calls=%fused_computation.19 | convolution fusion | flops 2428895232 | bytes 10237440 | tf_op jit(solution)/shard_map/sekd,edf->sekf/dot_general | solution.py:93
  45.2 2.8 %fusion.12 = f32[16,1,24,3072]{3,2,0,1:T(8,128)S(1)} fusion(bf16[1,1,1024,3072]{3,2,1,0:T(8,128)(2,1)S(1)} %bitcast.245, f32[16,24,1024]{2,1,0:T(8,128)S(1)} %fusion.10), kind=kOutput, calls=%fused_computation.27 | convolution fusion | flops 2417885184 | bytes 12582912 | tf_op jit(solution)/shard_map/sekf,efd->sekd/dot_general | solution.py:97
  48.9 2.7 %collective-permute-done.5 = bf16[16,1,24,1536]{3,2,0,1:T(8,128)(2,1)S(1)} collective-permute-done((bf16[16,1,24,1536]{3,2,0,1:T(8,128)(2,1)S(1)}, bf16[16,1,24,1536]{3,2,0,1:T(8,128)(2,1)S(1)}, u32[]{:S(2)}, u32[]{:S(2)}) %collective-permute-start.5) | collective-permute-done | bytes 1179680 | tf_op jit(solution)/shard_map/ppermute | solution.py:18
  53.0 4.0 %all-to-all-start.1 = ((bf16[16,1,24,1536]{3,2,1,0:T(8,128)(2,1)}), bf16[16,1,24,1536]{3,2,1,0:T(8,128)(2,1)S(1)}, u32[]{:S(2)}, u32[]{:S(2)}) async-start(bf16[16,1,24,1536]{3,2,1,0:T(8,128)(2,1)} %fusion.60), calls=%async_computation.1 | async-start | bytes 2359296 | tf_op jit(solution)/shard_map/all_to_all | solution.py:113
  57.2 20.0 %all-to-all-done.1 = bf16[16,1,24,1536]{3,2,1,0:T(8,128)(2,1)S(1)} async-done(((bf16[16,1,24,1536]{3,2,1,0:T(8,128)(2,1)}), bf16[16,1,24,1536]{3,2,1,0:T(8,128)(2,1)S(1)}, u32[]{:S(2)}, u32[]{:S(2)}) %all-to-all-start.1) | async-done | bytes 1179680 | tf_op jit(solution)/shard_map/all_to_all | solution.py:113
  82.3 7.7 %collective-permute-done.6 = f32[64,1536]{1,0:T(8,128)S(1)} collective-permute-done((f32[64,1536]{1,0:T(8,128)S(1)}, f32[64,1536]{1,0:T(8,128)S(1)}, u32[]{:S(2)}, u32[]{:S(2)}) %collective-permute-start.6) | collective-permute-done | bytes 393248 | tf_op jit(solution)/shard_map/ppermute | solution.py:18
  91.4 7.8 %collective-permute-done.7 = bf16[64,1536]{1,0:T(8,128)(2,1)S(1)} collective-permute-done((bf16[64,1536]{1,0:T(8,128)(2,1)S(1)}, bf16[64,1536]{1,0:T(8,128)(2,1)S(1)}, u32[]{:S(2)}, u32[]{:S(2)}) %collective-permute-start.7) | collective-permute-done | bytes 196640 | tf_op jit(solution)/shard_map/ppermute | solution.py:13
  100.5 21.6 %all_to_all.31 = bf16[16,1,24,1536]{3,2,1,0:T(8,128)(2,1)S(1)} all-to-all(bf16[16,1,24,1536]{3,2,1,0:T(8,128)(2,1)S(1)} %bitcast.233), channel_id=1, replica_groups=mesh['section'=2,'expert'=16,'tensor'=4] {'expert'}, dimensions={0} | all-to-all | bytes 2359296 | tf_op jit(solution)/shard_map/all_to_all | solution.py:83
  122.0 2.8 %collective-permute-done.8 = bf16[16,1,24,1536]{3,2,0,1:T(8,128)(2,1)S(1)} collective-permute-done((bf16[16,1,24,1536]{3,2,0,1:T(8,128)(2,1)S(1)}, bf16[16,1,24,1536]{3,2,0,1:T(8,128)(2,1)S(1)}, u32[]{:S(2)}, u32[]{:S(2)}) %collective-permute-start.8) | collective-permute-done | bytes 1179680 | tf_op jit(solution)/shard_map/ppermute | solution.py:18
  127.8 2.7 %fusion.8 = f32[16,24,1024]{2,1,0:T(8,128)S(1)} fusion(bf16[1,1,3072,1024]{3,2,1,0:T(8,128)(2,1)S(1)} %bitcast.241, bf16[16,24,768]{2,1,0:T(8,128)(2,1)S(1)} %get-tuple-element.51, bf16[16,24,768]{2,1,0:T(8,128)(2,1)S(1)} %get-tuple-element.47, bf16[16,24,768]{2,1,0:T(8,128)(2,1)S(1)} %get-tuple-element.50, bf16[16,24,768]{2,1,0:T(8,128)(2,1)S(1)} %get-tuple-element.46, ...), kind=kOutput, calls=%fused_computation.17 | convolution fusion | flops 2428895232 | bytes 10237440 | tf_op jit(solution)/shard_map/sekd,edf->sekf/dot_general | solution.py:93
  130.5 2.8 %fusion.15 = f32[16,1,24,3072]{3,2,0,1:T(8,128)S(1)} fusion(bf16[1,1,1024,3072]{3,2,1,0:T(8,128)(2,1)S(1)} %bitcast.247, f32[16,24,1024]{2,1,0:T(8,128)S(1)} %fusion.8), kind=kOutput, calls=%fused_computation.28 | convolution fusion | flops 2417885184 | bytes 12582912 | tf_op jit(solution)/shard_map/sekf,efd->sekd/dot_general | solution.py:97
  134.3 2.7 %collective-permute-done.9 = bf16[16,1,24,1536]{3,2,0,1:T(8,128)(2,1)S(1)} collective-permute-done((bf16[16,1,24,1536]{3,2,0,1:T(8,128)(2,1)S(1)}, bf16[16,1,24,1536]{3,2,0,1:T(8,128)(2,1)S(1)}, u32[]{:S(2)}, u32[]{:S(2)}) %collective-permute-start.9) | collective-permute-done | bytes 1179680 | tf_op jit(solution)/shard_map/ppermute | solution.py:18
  138.4 3.9 %all-to-all-start.3 = ((bf16[16,1,24,1536]{3,2,1,0:T(8,128)(2,1)}), bf16[16,1,24,1536]{3,2,1,0:T(8,128)(2,1)S(1)}, u32[]{:S(2)}, u32[]{:S(2)}) async-start(bf16[16,1,24,1536]{3,2,1,0:T(8,128)(2,1)} %fusion.61), calls=%async_computation.3 | async-start | bytes 2359296 | tf_op jit(solution)/shard_map/all_to_all | solution.py:113
  143.4 19.1 %all-to-all-done.3 = bf16[16,1,24,1536]{3,2,1,0:T(8,128)(2,1)S(1)} async-done(((bf16[16,1,24,1536]{3,2,1,0:T(8,128)(2,1)}), bf16[16,1,24,1536]{3,2,1,0:T(8,128)(2,1)S(1)}, u32[]{:S(2)}, u32[]{:S(2)}) %all-to-all-start.3) | async-done | bytes 1179680 | tf_op jit(solution)/shard_map/all_to_all | solution.py:113
  167.5 7.7 %collective-permute-done.10 = f32[64,1536]{1,0:T(8,128)S(1)} collective-permute-done((f32[64,1536]{1,0:T(8,128)S(1)}, f32[64,1536]{1,0:T(8,128)S(1)}, u32[]{:S(2)}, u32[]{:S(2)}) %collective-permute-start.10) | collective-permute-done | bytes 393248 | tf_op jit(solution)/shard_map/ppermute | solution.py:18
  176.6 7.8 %collective-permute-done.11 = bf16[64,1536]{1,0:T(8,128)(2,1)S(1)} collective-permute-done((bf16[64,1536]{1,0:T(8,128)(2,1)S(1)}, bf16[64,1536]{1,0:T(8,128)(2,1)S(1)}, u32[]{:S(2)}, u32[]{:S(2)}) %collective-permute-start.11) | collective-permute-done | bytes 196640 | tf_op jit(solution)/shard_map/ppermute | solution.py:13
  185.7 21.6 %all_to_all.32 = bf16[16,1,24,1536]{3,2,1,0:T(8,128)(2,1)S(1)} all-to-all(bf16[16,1,24,1536]{3,2,1,0:T(8,128)(2,1)S(1)} %bitcast.234), channel_id=1, replica_groups=mesh['section'=2,'expert'=16,'tensor'=4] {'expert'}, dimensions={0} | all-to-all | bytes 2359296 | tf_op jit(solution)/shard_map/all_to_all | solution.py:83
  207.3 2.8 %collective-permute-done.12 = bf16[16,1,24,1536]{3,2,0,1:T(8,128)(2,1)S(1)} collective-permute-done((bf16[16,1,24,1536]{3,2,0,1:T(8,128)(2,1)S(1)}, bf16[16,1,24,1536]{3,2,0,1:T(8,128)(2,1)S(1)}, u32[]{:S(2)}, u32[]{:S(2)}) %collective-permute-start.12) | collective-permute-done | bytes 1179680 | tf_op jit(solution)/shard_map/ppermute | solution.py:18
  215.8 2.8 %fusion.18 = f32[16,1,24,3072]{3,2,0,1:T(8,128)S(1)} fusion(bf16[1,1,1024,3072]{3,2,1,0:T(8,128)(2,1)S(1)} %bitcast.249, f32[16,24,1024]{2,1,0:T(8,128)S(1)} %fusion.6), kind=kOutput, calls=%fused_computation.29 | convolution fusion | flops 2417885184 | bytes 12582912 | tf_op jit(solution)/shard_map/sekf,efd->sekd/dot_general | solution.py:97
  219.5 2.7 %collective-permute-done.13 = bf16[16,1,24,1536]{3,2,0,1:T(8,128)(2,1)S(1)} collective-permute-done((bf16[16,1,24,1536]{3,2,0,1:T(8,128)(2,1)S(1)}, bf16[16,1,24,1536]{3,2,0,1:T(8,128)(2,1)S(1)}, u32[]{:S(2)}, u32[]{:S(2)}) %collective-permute-start.13) | collective-permute-done | bytes 1179680 | tf_op jit(solution)/shard_map/ppermute | solution.py:18
  223.6 4.0 %all-to-all-start.5 = ((bf16[16,1,24,1536]{3,2,1,0:T(8,128)(2,1)}), bf16[16,1,24,1536]{3,2,1,0:T(8,128)(2,1)S(1)}, u32[]{:S(2)}, u32[]{:S(2)}) async-start(bf16[16,1,24,1536]{3,2,1,0:T(8,128)(2,1)} %fusion.62), calls=%async_computation.5 | async-start | bytes 2359296 | tf_op jit(solution)/shard_map/all_to_all | solution.py:113
  227.7 19.9 %all-to-all-done.5 = bf16[16,1,24,1536]{3,2,1,0:T(8,128)(2,1)S(1)} async-done(((bf16[16,1,24,1536]{3,2,1,0:T(8,128)(2,1)}), bf16[16,1,24,1536]{3,2,1,0:T(8,128)(2,1)S(1)}, u32[]{:S(2)}, u32[]{:S(2)}) %all-to-all-start.5) | async-done | bytes 1179680 | tf_op jit(solution)/shard_map/all_to_all | solution.py:113
  251.7 8.7 %collective-permute-done.14 = f32[64,1536]{1,0:T(8,128)S(1)} collective-permute-done((f32[64,1536]{1,0:T(8,128)S(1)}, f32[64,1536]{1,0:T(8,128)S(1)}, u32[]{:S(2)}, u32[]{:S(2)}) %collective-permute-start.14) | collective-permute-done | bytes 393248 | tf_op jit(solution)/shard_map/ppermute | solution.py:18
  (166 shorter events, 53.6 us)
Async XLA Ops:
  0.0 6.9 %collective-permute-start = (bf16[2,64,768]{2,1,0:T(8,128)(2,1)}, bf16[2,64,768]{2,1,0:T(8,128)(2,1)S(1)}, u32[]{:S(2)}, u32[]{:S(2)}) collective-permute-start(bf16[2,64,768]{2,1,0:T(8,128)(2,1)} %param.10), channel_id=1, source_target_pairs={{0,2},{1,3},{2,0},{3,1},{4,6},{5,7},{6,4},{7,5},{8,10},{9,11},{10,... | collective-permute-start | bytes 589832 | tf_op jit(solution)/shard_map/ppermute | solution.py:18
  9.3 25.7 %copy-start.1 = (f32[1,768]{1,0:T(1,128)S(1)}, f32[1,768]{1,0:T(1,128)}, u32[]{:S(2)}) copy-start(f32[1,768]{1,0:T(1,128)} %param.11) | copy-start | bytes 9220
  35.0 4.5 %collective-permute-start.1 = (bf16[16,1,24,1536]{3,2,0,1:T(8,128)(2,1)S(1)}, bf16[16,1,24,1536]{3,2,0,1:T(8,128)(2,1)S(1)}, u32[]{:S(2)}, u32[]{:S(2)}) collective-permute-start(bf16[16,1,24,1536]{3,2,0,1:T(8,128)(2,1)S(1)} %bitcast.226), channel_id=1, source_target_pairs={{0,1},{1,0},{2,3},{3,2},{4,5},{5,4},{6,7},{7,6},{8,9},{9,8},{10,11... | collective-permute-start | bytes 3538952 | tf_op jit(solution)/shard_map/ppermute | solution.py:18
  35.0 2.8 %collective-permute-start.2 = (f32[768]{0:T(1024)S(1)}, f32[768]{0:T(1024)S(1)}, u32[]{:S(2)}, u32[]{:S(2)}) collective-permute-start(f32[768]{0:T(1024)S(1)} %reduce.3), channel_id=1, source_target_pairs={{0,1},{1,0},{2,3},{3,2},{4,5},{5,4},{6,7},{7,6},{8,9},{9,8},{10,11... | collective-permute-start | bytes 9224 | tf_op jit(solution)/shard_map/ppermute | solution.py:18
  35.6 3.6 %collective-permute-start.3 = (f32[768]{0:T(1024)S(1)}, f32[768]{0:T(1024)S(1)}, u32[]{:S(2)}, u32[]{:S(2)}) collective-permute-start(f32[768]{0:T(1024)S(1)} %reduce.3), channel_id=1, source_target_pairs={{0,2},{1,3},{2,0},{3,1},{4,6},{5,7},{6,4},{7,5},{8,10},{9,11},{10,... | collective-permute-start | bytes 9224 | tf_op jit(solution)/shard_map/ppermute | solution.py:18
  36.5 3.1 %collective-permute-start.4 = (f32[768]{0:T(1024)S(1)}, f32[768]{0:T(1024)S(1)}, u32[]{:S(2)}, u32[]{:S(2)}) collective-permute-start(f32[768]{0:T(1024)S(1)} %reduce.3), channel_id=1, source_target_pairs={{0,3},{1,2},{2,1},{3,0},{4,7},{5,6},{6,5},{7,4},{8,11},{9,10},{10,... | collective-permute-start | bytes 9224 | tf_op jit(solution)/shard_map/ppermute | solution.py:18
  40.1 5.1 %slice-start.6 = ((s8[6291456]{0:T(1024)(128)(4,1)}), s8[4194304]{0:T(1024)(128)(4,1)S(1)}, s32[]{:S(2)}) async-start(s8[6291456]{0:T(1024)(128)(4,1)} %bitcast.244), calls=%async_computation.12 | async-start | bytes 8388608
  48.7 2.9 %collective-permute-start.5 = (bf16[16,1,24,1536]{3,2,0,1:T(8,128)(2,1)S(1)}, bf16[16,1,24,1536]{3,2,0,1:T(8,128)(2,1)S(1)}, u32[]{:S(2)}, u32[]{:S(2)}) collective-permute-start(bf16[16,1,24,1536]{3,2,0,1:T(8,128)(2,1)S(1)} %select_convert_fusion.2), channel_id=1, source_target_pairs={{0,1},{1,0},{2,3},{3,2},{4,5},{5,4},{6,7},{7,6},{8,9},{9,8},{10,11... | collective-permute-start | bytes 3538952 | tf_op jit(solution)/shard_map/ppermute | solution.py:18
  53.0 4.0 %copy-start = (f32[1,2,64,2]{2,3,1,0:T(2,128)S(1)}, f32[1,2,64,2]{2,3,1,0:T(2,128)}, u32[]{:S(2)}) copy-start(f32[1,2,64,2]{2,3,1,0:T(2,128)} %param.13) | copy-start | bytes 3076
  53.0 24.2 %all-to-all-start.1 = ((bf16[16,1,24,1536]{3,2,1,0:T(8,128)(2,1)}), bf16[16,1,24,1536]{3,2,1,0:T(8,128)(2,1)S(1)}, u32[]{:S(2)}, u32[]{:S(2)}) async-start(bf16[16,1,24,1536]{3,2,1,0:T(8,128)(2,1)} %fusion.60), calls=%async_computation.1 | async-start | bytes 2359296 | tf_op jit(solution)/shard_map/all_to_all | solution.py:113
  80.0 10.0 %collective-permute-start.6 = (f32[64,1536]{1,0:T(8,128)S(1)}, f32[64,1536]{1,0:T(8,128)S(1)}, u32[]{:S(2)}, u32[]{:S(2)}) collective-permute-start(f32[64,1536]{1,0:T(8,128)S(1)} %multiply_reduce_fusion.5), channel_id=1, source_target_pairs={{0,2},{1,3},{2,0},{3,1},{4,6},{5,7},{6,4},{7,5},{8,10},{9,11},{10,... | collective-permute-start | bytes 1179656 | tf_op jit(solution)/shard_map/ppermute | solution.py:18
  90.0 9.1 %collective-permute-start.7 = (bf16[64,1536]{1,0:T(8,128)(2,1)S(1)}, bf16[64,1536]{1,0:T(8,128)(2,1)S(1)}, u32[]{:S(2)}, u32[]{:S(2)}) collective-permute-start(bf16[64,1536]{1,0:T(8,128)(2,1)S(1)} %add_convert_fusion.5), channel_id=1, source_target_pairs={{0,64},{1,65},{2,66},{3,67},{4,68},{5,69},{6,70},{7,71},{8,72},{9,... | collective-permute-start | bytes 589832 | tf_op jit(solution)/shard_map/ppermute | solution.py:13
  122.0 2.8 %collective-permute-start.8 = (bf16[16,1,24,1536]{3,2,0,1:T(8,128)(2,1)S(1)}, bf16[16,1,24,1536]{3,2,0,1:T(8,128)(2,1)S(1)}, u32[]{:S(2)}, u32[]{:S(2)}) collective-permute-start(bf16[16,1,24,1536]{3,2,0,1:T(8,128)(2,1)S(1)} %bitcast.227), channel_id=1, source_target_pairs={{0,1},{1,0},{2,3},{3,2},{4,5},{5,4},{6,7},{7,6},{8,9},{9,8},{10,11... | collective-permute-start | bytes 3538952 | tf_op jit(solution)/shard_map/ppermute | solution.py:18
  125.0 2.7 %slice-start.3 = ((s8[6291456]{0:T(1024)(128)(4,1)}), s8[2097152]{0:T(1024)(128)(4,1)S(1)}, s32[]{:S(2)}) async-start(s8[6291456]{0:T(1024)(128)(4,1)} %bitcast.240), calls=%async_computation.9 | async-start | bytes 4194304
  125.4 5.1 %slice-start.8 = ((s8[6291456]{0:T(1024)(128)(4,1)}), s8[4194304]{0:T(1024)(128)(4,1)S(1)}, s32[]{:S(2)}) async-start(s8[6291456]{0:T(1024)(128)(4,1)} %bitcast.246), calls=%async_computation.14 | async-start | bytes 8388608
  134.0 2.9 %collective-permute-start.9 = (bf16[16,1,24,1536]{3,2,0,1:T(8,128)(2,1)S(1)}, bf16[16,1,24,1536]{3,2,0,1:T(8,128)(2,1)S(1)}, u32[]{:S(2)}, u32[]{:S(2)}) collective-permute-start(bf16[16,1,24,1536]{3,2,0,1:T(8,128)(2,1)S(1)} %select_convert_fusion.1), channel_id=1, source_target_pairs={{0,1},{1,0},{2,3},{3,2},{4,5},{5,4},{6,7},{7,6},{8,9},{9,8},{10,11... | collective-permute-start | bytes 3538952 | tf_op jit(solution)/shard_map/ppermute | solution.py:18
  138.4 24.0 %all-to-all-start.3 = ((bf16[16,1,24,1536]{3,2,1,0:T(8,128)(2,1)}), bf16[16,1,24,1536]{3,2,1,0:T(8,128)(2,1)S(1)}, u32[]{:S(2)}, u32[]{:S(2)}) async-start(bf16[16,1,24,1536]{3,2,1,0:T(8,128)(2,1)} %fusion.61), calls=%async_computation.3 | async-start | bytes 2359296 | tf_op jit(solution)/shard_map/all_to_all | solution.py:113
  165.2 10.0 %collective-permute-start.10 = (f32[64,1536]{1,0:T(8,128)S(1)}, f32[64,1536]{1,0:T(8,128)S(1)}, u32[]{:S(2)}, u32[]{:S(2)}) collective-permute-start(f32[64,1536]{1,0:T(8,128)S(1)} %multiply_reduce_fusion.4), channel_id=1, source_target_pairs={{0,2},{1,3},{2,0},{3,1},{4,6},{5,7},{6,4},{7,5},{8,10},{9,11},{10,... | collective-permute-start | bytes 1179656 | tf_op jit(solution)/shard_map/ppermute | solution.py:18
  175.3 9.1 %collective-permute-start.11 = (bf16[64,1536]{1,0:T(8,128)(2,1)S(1)}, bf16[64,1536]{1,0:T(8,128)(2,1)S(1)}, u32[]{:S(2)}, u32[]{:S(2)}) collective-permute-start(bf16[64,1536]{1,0:T(8,128)(2,1)S(1)} %add_convert_fusion.4), channel_id=1, source_target_pairs={{0,64},{1,65},{2,66},{3,67},{4,68},{5,69},{6,70},{7,71},{8,72},{9,... | collective-permute-start | bytes 589832 | tf_op jit(solution)/shard_map/ppermute | solution.py:13
  207.3 2.8 %collective-permute-start.12 = (bf16[16,1,24,1536]{3,2,0,1:T(8,128)(2,1)S(1)}, bf16[16,1,24,1536]{3,2,0,1:T(8,128)(2,1)S(1)}, u32[]{:S(2)}, u32[]{:S(2)}) collective-permute-start(bf16[16,1,24,1536]{3,2,0,1:T(8,128)(2,1)S(1)} %bitcast.228), channel_id=1, source_target_pairs={{0,1},{1,0},{2,3},{3,2},{4,5},{5,4},{6,7},{7,6},{8,9},{9,8},{10,11... | collective-permute-start | bytes 3538952 | tf_op jit(solution)/shard_map/ppermute | solution.py:18
  210.5 5.3 %slice-start.10 = ((s8[6291456]{0:T(1024)(128)(4,1)}), s8[4194304]{0:T(1024)(128)(4,1)S(1)}, s32[]{:S(2)}) async-start(s8[6291456]{0:T(1024)(128)(4,1)} %bitcast.248), calls=%async_computation.16 | async-start | bytes 8388608
  219.3 2.9 %collective-permute-start.13 = (bf16[16,1,24,1536]{3,2,0,1:T(8,128)(2,1)S(1)}, bf16[16,1,24,1536]{3,2,0,1:T(8,128)(2,1)S(1)}, u32[]{:S(2)}, u32[]{:S(2)}) collective-permute-start(bf16[16,1,24,1536]{3,2,0,1:T(8,128)(2,1)S(1)} %select_convert_fusion), channel_id=1, source_target_pairs={{0,1},{1,0},{2,3},{3,2},{4,5},{5,4},{6,7},{7,6},{8,9},{9,8},{10,11... | collective-permute-start | bytes 3538952 | tf_op jit(solution)/shard_map/ppermute | solution.py:18
  223.6 24.0 %all-to-all-start.5 = ((bf16[16,1,24,1536]{3,2,1,0:T(8,128)(2,1)}), bf16[16,1,24,1536]{3,2,1,0:T(8,128)(2,1)S(1)}, u32[]{:S(2)}, u32[]{:S(2)}) async-start(bf16[16,1,24,1536]{3,2,1,0:T(8,128)(2,1)} %fusion.62), calls=%async_computation.5 | async-start | bytes 2359296 | tf_op jit(solution)/shard_map/all_to_all | solution.py:113
  250.4 10.0 %collective-permute-start.14 = (f32[64,1536]{1,0:T(8,128)S(1)}, f32[64,1536]{1,0:T(8,128)S(1)}, u32[]{:S(2)}, u32[]{:S(2)}) collective-permute-start(f32[64,1536]{1,0:T(8,128)S(1)} %multiply_reduce_fusion.3), channel_id=1, source_target_pairs={{0,2},{1,3},{2,0},{3,1},{4,6},{5,7},{6,4},{7,5},{8,10},{9,11},{10,... | collective-permute-start | bytes 1179656 | tf_op jit(solution)/shard_map/ppermute | solution.py:18
  (8 other events, 20.2 us)

commit v3 on v2

--- a/solution.py
+++ b/solution.py
@@ -44,32 +44,40 @@
     local_count = up_local.shape[0]
     copies = n_exp * local_count // EXPERTS
     collected = jnp.zeros((micro, rows_here, quarter), jnp.bfloat16)
-    carried = jnp.zeros((rows_here, 2 * quarter), jnp.bfloat16)
     total_steps = micro + segments - 1
     x_first = x_lo == 0
     core_first = core == 0
-    tokens_other = swap(tokens, "tensor", 2)
-    tokens_half = jnp.where(
-        x_first,
-        jnp.concatenate([tokens, tokens_other], axis=2),
-        jnp.concatenate([tokens_other, tokens], axis=2),
+
+    def to_half(own, other):
+        return jnp.where(
+            x_first,
+            jnp.concatenate([own, other], axis=-1),
+            jnp.concatenate([other, own], axis=-1),
+        )
+
+    tokens_half = to_half(tokens, swap(tokens, "tensor", 2))
+    routes_all = expert_ids[0].reshape(micro, -1)
+    onehot_all = (routes_all[..., None] == jnp.arange(EXPERTS, dtype=jnp.int32)).astype(jnp.int32)
+    slot_all = jnp.sum((jnp.cumsum(onehot_all, axis=1) - onehot_all) * onehot_all, axis=2)
+    dest_all = routes_all * capacity + slot_all
+    source_all = (
+        jnp.full((micro, EXPERTS * capacity), -1, jnp.int32)
+        .at[jnp.arange(micro)[:, None], dest_all]
+        .set(jnp.broadcast_to(jnp.arange(2 * rows_here, dtype=jnp.int32) // 2, dest_all.shape))
     )
+    n_t = lax.axis_size("tensor")
+    cross_route = [
+        (s * n_t + t, (s + 1) * n_t + (t ^ 2)) for s in range(segments - 1) for t in range(n_t)
+    ]
+    carried = jnp.zeros((rows_here, 2 * quarter), jnp.bfloat16)
     for step in range(total_steps):
         which = step - segment_pos
         which_safe = jnp.clip(which, 0, micro - 1)
         entering = tokens_half[min(step, micro - 1)]
         half_rows = jnp.where(segment_pos == 0, entering, carried)
-        routes = lax.dynamic_index_in_dim(expert_ids[0], which_safe, 0, keepdims=False)
         weights = lax.dynamic_index_in_dim(gate_weights[0], which_safe, 0, keepdims=False)
-        flat = routes.reshape(-1)
-        onehot = (flat[:, None] == jnp.arange(EXPERTS, dtype=jnp.int32)[None, :]).astype(jnp.int32)
-        slot = jnp.sum((jnp.cumsum(onehot, axis=0) - onehot) * onehot, axis=1)
-        dest = flat * capacity + slot
-        source = (
-            jnp.full((EXPERTS * capacity,), -1, jnp.int32)
-            .at[dest]
-            .set(jnp.arange(2 * rows_here, dtype=jnp.int32) // 2)
-        )
+        dest = lax.dynamic_index_in_dim(dest_all, which_safe, 0, keepdims=False)
+        source = lax.dynamic_index_in_dim(source_all, which_safe, 0, keepdims=False)
         filled = source >= 0
         outgoing = jnp.where(
             filled[:, None],
@@ -117,13 +125,19 @@
         picked = jnp.take(summed.reshape(-1, 2 * quarter), dest, axis=0)
         picked = picked.reshape(rows_here, 2, 2 * quarter)
         y_half = jnp.sum(picked * weights[:, :, None], axis=1)
-        y_got = swap(y_half, "tensor", 2)
-        produced_half = (half_rows.astype(jnp.float32) + (y_half + y_got)).astype(jnp.bfloat16)
-        produced = jnp.where(x_first, produced_half[:, :quarter], produced_half[:, quarter:])
+        y_keep = jnp.where(x_first, y_half[:, :quarter], y_half[:, quarter:])
+        y_give = jnp.where(x_first, y_half[:, quarter:], y_half[:, :quarter])
+        y_got = swap(y_give, "tensor", 2)
+        xf = jnp.where(x_first, half_rows[:, :quarter], half_rows[:, quarter:]).astype(jnp.float32)
+        mixed = xf + (y_keep + y_got)
+        produced = mixed.astype(jnp.bfloat16)
         chosen = (jnp.arange(micro, dtype=jnp.int32) == which)[:, None, None]
         collected = jnp.where(chosen, produced[None], collected)
         if step + 1 < total_steps:
-            carried = from_behind(produced_half, "section", 1)
+            carried = to_half(
+                from_behind(produced, "section", 1),
+                lax.ppermute(produced, ("section", "tensor"), cross_route),
+            )
     return collected[None]
 
 

time: 262 us -> 260 us (level)
  waiting for transfers between devices: 117 us -> 105 us
  local copies, waits for them, and re-layouts: 19.7 us -> 29 us
    ppermute x13, waiting for transfers between devices: 42.8 us -> 31.9 us  [swap(): return lax.ppermute(block, axis, [(i, i ^ bit) for i in range(n)])]
    scatter x3 -> x1, local copies, waits for them, and re-layouts: 2.93 us -> 12.5 us  [shards(): source_all = jnp.full((micro, EXPERTS * capacity), -1, jnp.int32).at[jnp....]
    ppermute x2, waiting for transfers between devices: 15.5 us -> 10.8 us  [from_behind(): return lax.ppermute(block, axis, route)]
    unnamed x28 -> x31, local copies, waits for them, and re-layouts: 5.29 us -> 6.07 us
  transfers between devices with their start and end apart: 18 -> 20, of which waited for: 17 -> 18; matrix products, arithmetic and copies ran while one was open for 3% -> 6% of each run, Pallas kernels for 0% -> 0%
where the time goes in v3:
time: 260 us; the launch traced here: 259 us
  waiting for transfers between devices  105 us (40%)
  blocking collectives  70.7 us (27%)
  local copies, waits for them, and re-layouts  29 us (11%)
  starting transfers between devices  22.7 us (9%)
  matrix products  16.4 us (6%)
  other arithmetic  15 us (6%)
    all_to_all x3, blocking collectives, shards(): lax.all_to_all(outgoing, 'expert', split_axis=0, concat_axis=0, tiled=True)  70.7 us
    all_to_all x3, waiting for transfers between devices, shards(): lax.all_to_all(chip_sum, 'expert', split_axis=0, concat_axis=0, tiled=True)  60 us
    ppermute x13, waiting for transfers between devices, swap(): return lax.ppermute(block, axis, [(i, i ^ bit) for i in range(n)])  31.9 us
    scatter x1, local copies, waits for them, and re-layouts, shards(): source_all = jnp.full((micro, EXPERTS * capacity), -1, jnp.int32).at[jnp....  12.5 us
    all_to_all x3, starting transfers between devices, shards(): lax.all_to_all(chip_sum, 'expert', split_axis=0, concat_axis=0, tiled=True)  11.9 us
    ppermute x2, waiting for transfers between devices, from_behind(): return lax.ppermute(block, axis, route)  10.8 us
    dot_general x3, matrix products, shards(): jnp.einsum('sekf,efd->sekd', hidden, down_local, preferred_element_type=j...  8.37 us
    dot_general x3, matrix products, shards(): jnp.einsum('sekd,edf->sekf', normed, up_local, preferred_element_type=jnp...  8.07 us
  transfers between devices with their start and end apart: 20, of which 18 were waited for; matrix products, arithmetic and copies ran while one was open for 6% of the time, Pallas kernels for 0%

profile of v3, /device:TPU:6, one launch (start us, length us, event | category | flops | bytes accessed | tf_op | source)
XLA Modules:
  0.0 259.5 jit_solution(3072009747604705478)
XLA Ops:
  3.2 12.5 %scatter_fusion = s32[2,192]{1,0:T(2,128)S(1)} fusion(s32[2,192]{1,0:T(2,128)S(1)} %broadcast_in_dim.128, s32[256]{0:T(256)S(1)} %fusion.75, s32[256]{0:T(256)S(1)} %broadcast_bitcast_fusion), kind=kCustom, calls=%fused_computation.6 | custom fusion | bytes 5120 | tf_op jit(solution)/shard_map/scatter | solution.py:66
  17.3 26.1 %all_to_all.30 = bf16[16,1,24,1536]{3,2,1,0:T(8,128)(2,1)S(1)} all-to-all(bf16[16,1,24,1536]{3,2,1,0:T(8,128)(2,1)S(1)} %bitcast.230), channel_id=1, replica_groups=mesh['section'=2,'expert'=16,'tensor'=4] {'expert'}, dimensions={0} | all-to-all | bytes 2359296 | tf_op jit(solution)/shard_map/all_to_all | solution.py:91
  54.0 2.8 %fusion.12 = f32[16,1,24,3072]{3,2,0,1:T(8,128)S(1)} fusion(bf16[1,1,1024,3072]{3,2,1,0:T(8,128)(2,1)S(1)} %bitcast.249, f32[16,24,1024]{2,1,0:T(8,128)S(1)} %fusion.10), kind=kOutput, calls=%fused_computation.25 | convolution fusion | flops 2417885184 | bytes 12582912 | tf_op jit(solution)/shard_map/sekf,efd->sekd/dot_general | solution.py:105
  57.7 2.7 %collective-permute-done.5 = bf16[16,1,24,1536]{3,2,0,1:T(8,128)(2,1)S(1)} collective-permute-done((bf16[16,1,24,1536]{3,2,0,1:T(8,128)(2,1)S(1)}, bf16[16,1,24,1536]{3,2,0,1:T(8,128)(2,1)S(1)}, u32[]{:S(2)}, u32[]{:S(2)}) %collective-permute-start.5) | collective-permute-done | bytes 1179680 | tf_op jit(solution)/shard_map/ppermute | solution.py:18
  62.0 4.0 %all-to-all-start.1 = ((bf16[16,1,24,1536]{3,2,1,0:T(8,128)(2,1)}), bf16[16,1,24,1536]{3,2,1,0:T(8,128)(2,1)S(1)}, u32[]{:S(2)}, u32[]{:S(2)}) async-start(bf16[16,1,24,1536]{3,2,1,0:T(8,128)(2,1)} %fusion.60), calls=%async_computation.1 | async-start | bytes 2359296 | tf_op jit(solution)/shard_map/all_to_all | solution.py:121
  66.2 20.0 %all-to-all-done.1 = bf16[16,1,24,1536]{3,2,1,0:T(8,128)(2,1)S(1)} async-done(((bf16[16,1,24,1536]{3,2,1,0:T(8,128)(2,1)}), bf16[16,1,24,1536]{3,2,1,0:T(8,128)(2,1)S(1)}, u32[]{:S(2)}, u32[]{:S(2)}) %all-to-all-start.1) | async-done | bytes 1179680 | tf_op jit(solution)/shard_map/all_to_all | solution.py:121
  89.9 4.9 %collective-permute-done.6 = f32[64,768]{1,0:T(8,128)S(1)} collective-permute-done((f32[64,768]{1,0:T(8,128)S(1)}, f32[64,768]{1,0:T(8,128)S(1)}, u32[]{:S(2)}, u32[]{:S(2)}) %collective-permute-start.6) | collective-permute-done | bytes 196640 | tf_op jit(solution)/shard_map/ppermute | solution.py:18
  97.4 5.4 %collective-permute-done.7 = bf16[64,768]{1,0:T(8,128)(2,1)S(1)} collective-permute-done((bf16[64,768]{1,0:T(8,128)(2,1)S(1)}, bf16[64,768]{1,0:T(8,128)(2,1)S(1)}, u32[]{:S(2)}, u32[]{:S(2)}) %collective-permute-start.7) | collective-permute-done | bytes 98336 | tf_op jit(solution)/shard_map/ppermute | solution.py:13
  105.5 22.3 %all_to_all.31 = bf16[16,1,24,1536]{3,2,1,0:T(8,128)(2,1)S(1)} all-to-all(bf16[16,1,24,1536]{3,2,1,0:T(8,128)(2,1)S(1)} %bitcast.231), channel_id=1, replica_groups=mesh['section'=2,'expert'=16,'tensor'=4] {'expert'}, dimensions={0} | all-to-all | bytes 2359296 | tf_op jit(solution)/shard_map/all_to_all | solution.py:91
  127.8 2.8 %collective-permute-done.9 = bf16[16,1,24,1536]{3,2,0,1:T(8,128)(2,1)S(1)} collective-permute-done((bf16[16,1,24,1536]{3,2,0,1:T(8,128)(2,1)S(1)}, bf16[16,1,24,1536]{3,2,0,1:T(8,128)(2,1)S(1)}, u32[]{:S(2)}, u32[]{:S(2)}) %collective-permute-start.9) | collective-permute-done | bytes 1179680 | tf_op jit(solution)/shard_map/ppermute | solution.py:18
  133.5 2.7 %fusion.8 = f32[16,24,1024]{2,1,0:T(8,128)S(1)} fusion(bf16[1,1,3072,1024]{3,2,1,0:T(8,128)(2,1)S(1)} %bitcast.245, bf16[16,24,768]{2,1,0:T(8,128)(2,1)S(1)} %get-tuple-element.48, bf16[16,24,768]{2,1,0:T(8,128)(2,1)S(1)} %get-tuple-element.44, bf16[16,24,768]{2,1,0:T(8,128)(2,1)S(1)} %get-tuple-element.47, bf16[16,24,768]{2,1,0:T(8,128)(2,1)S(1)} %get-tuple-element.43, ...), kind=kOutput, calls=%fused_computation.15 | convolution fusion | flops 2428895232 | bytes 10237440 | tf_op jit(solution)/shard_map/sekd,edf->sekf/dot_general | solution.py:101
  136.3 2.8 %fusion.15 = f32[16,1,24,3072]{3,2,0,1:T(8,128)S(1)} fusion(bf16[1,1,1024,3072]{3,2,1,0:T(8,128)(2,1)S(1)} %bitcast.251, f32[16,24,1024]{2,1,0:T(8,128)S(1)} %fusion.8), kind=kOutput, calls=%fused_computation.26 | convolution fusion | flops 2417885184 | bytes 12582912 | tf_op jit(solution)/shard_map/sekf,efd->sekd/dot_general | solution.py:105
  140.0 2.7 %collective-permute-done.10 = bf16[16,1,24,1536]{3,2,0,1:T(8,128)(2,1)S(1)} collective-permute-done((bf16[16,1,24,1536]{3,2,0,1:T(8,128)(2,1)S(1)}, bf16[16,1,24,1536]{3,2,0,1:T(8,128)(2,1)S(1)}, u32[]{:S(2)}, u32[]{:S(2)}) %collective-permute-start.10) | collective-permute-done | bytes 1179680 | tf_op jit(solution)/shard_map/ppermute | solution.py:18
  144.2 3.9 %all-to-all-start.3 = ((bf16[16,1,24,1536]{3,2,1,0:T(8,128)(2,1)}), bf16[16,1,24,1536]{3,2,1,0:T(8,128)(2,1)S(1)}, u32[]{:S(2)}, u32[]{:S(2)}) async-start(bf16[16,1,24,1536]{3,2,1,0:T(8,128)(2,1)} %fusion.61), calls=%async_computation.3 | async-start | bytes 2359296 | tf_op jit(solution)/shard_map/all_to_all | solution.py:121
  148.3 20.0 %all-to-all-done.3 = bf16[16,1,24,1536]{3,2,1,0:T(8,128)(2,1)S(1)} async-done(((bf16[16,1,24,1536]{3,2,1,0:T(8,128)(2,1)}), bf16[16,1,24,1536]{3,2,1,0:T(8,128)(2,1)S(1)}, u32[]{:S(2)}, u32[]{:S(2)}) %all-to-all-start.3) | async-done | bytes 1179680 | tf_op jit(solution)/shard_map/all_to_all | solution.py:121
  171.7 5.2 %collective-permute-done.11 = f32[64,768]{1,0:T(8,128)S(1)} collective-permute-done((f32[64,768]{1,0:T(8,128)S(1)}, f32[64,768]{1,0:T(8,128)S(1)}, u32[]{:S(2)}, u32[]{:S(2)}) %collective-permute-start.11) | collective-permute-done | bytes 196640 | tf_op jit(solution)/shard_map/ppermute | solution.py:18
  179.5 5.4 %collective-permute-done.12 = bf16[64,768]{1,0:T(8,128)(2,1)S(1)} collective-permute-done((bf16[64,768]{1,0:T(8,128)(2,1)S(1)}, bf16[64,768]{1,0:T(8,128)(2,1)S(1)}, u32[]{:S(2)}, u32[]{:S(2)}) %collective-permute-start.12) | collective-permute-done | bytes 98336 | tf_op jit(solution)/shard_map/ppermute | solution.py:13
  187.4 22.3 %all_to_all.32 = bf16[16,1,24,1536]{3,2,1,0:T(8,128)(2,1)S(1)} all-to-all(bf16[16,1,24,1536]{3,2,1,0:T(8,128)(2,1)S(1)} %bitcast.232), channel_id=1, replica_groups=mesh['section'=2,'expert'=16,'tensor'=4] {'expert'}, dimensions={0} | all-to-all | bytes 2359296 | tf_op jit(solution)/shard_map/all_to_all | solution.py:91
  209.7 2.8 %collective-permute-done.14 = bf16[16,1,24,1536]{3,2,0,1:T(8,128)(2,1)S(1)} collective-permute-done((bf16[16,1,24,1536]{3,2,0,1:T(8,128)(2,1)S(1)}, bf16[16,1,24,1536]{3,2,0,1:T(8,128)(2,1)S(1)}, u32[]{:S(2)}, u32[]{:S(2)}) %collective-permute-start.14) | collective-permute-done | bytes 1179680 | tf_op jit(solution)/shard_map/ppermute | solution.py:18
  218.2 2.8 %fusion.18 = f32[16,1,24,3072]{3,2,0,1:T(8,128)S(1)} fusion(bf16[1,1,1024,3072]{3,2,1,0:T(8,128)(2,1)S(1)} %bitcast.253, f32[16,24,1024]{2,1,0:T(8,128)S(1)} %fusion.6), kind=kOutput, calls=%fused_computation.27 | convolution fusion | flops 2417885184 | bytes 12582912 | tf_op jit(solution)/shard_map/sekf,efd->sekd/dot_general | solution.py:105
  221.9 2.7 %collective-permute-done.15 = bf16[16,1,24,1536]{3,2,0,1:T(8,128)(2,1)S(1)} collective-permute-done((bf16[16,1,24,1536]{3,2,0,1:T(8,128)(2,1)S(1)}, bf16[16,1,24,1536]{3,2,0,1:T(8,128)(2,1)S(1)}, u32[]{:S(2)}, u32[]{:S(2)}) %collective-permute-start.15) | collective-permute-done | bytes 1179680 | tf_op jit(solution)/shard_map/ppermute | solution.py:18
  226.0 4.0 %all-to-all-start.5 = ((bf16[16,1,24,1536]{3,2,1,0:T(8,128)(2,1)}), bf16[16,1,24,1536]{3,2,1,0:T(8,128)(2,1)S(1)}, u32[]{:S(2)}, u32[]{:S(2)}) async-start(bf16[16,1,24,1536]{3,2,1,0:T(8,128)(2,1)} %fusion.62), calls=%async_computation.5 | async-start | bytes 2359296 | tf_op jit(solution)/shard_map/all_to_all | solution.py:121
  230.1 20.0 %all-to-all-done.5 = bf16[16,1,24,1536]{3,2,1,0:T(8,128)(2,1)S(1)} async-done(((bf16[16,1,24,1536]{3,2,1,0:T(8,128)(2,1)}), bf16[16,1,24,1536]{3,2,1,0:T(8,128)(2,1)S(1)}, u32[]{:S(2)}, u32[]{:S(2)}) %all-to-all-start.5) | async-done | bytes 1179680 | tf_op jit(solution)/shard_map/all_to_all | solution.py:121
  253.5 5.2 %collective-permute-done.16 = f32[64,768]{1,0:T(8,128)S(1)} collective-permute-done((f32[64,768]{1,0:T(8,128)S(1)}, f32[64,768]{1,0:T(8,128)S(1)}, u32[]{:S(2)}, u32[]{:S(2)}) %collective-permute-start.16) | collective-permute-done | bytes 196640 | tf_op jit(solution)/shard_map/ppermute | solution.py:18
  (157 shorter events, 52.8 us)
Async XLA Ops:
  0.0 15.8 %copy-start = (bf16[2,64,768]{2,1,0:T(8,128)(2,1)S(1)}, bf16[2,64,768]{2,1,0:T(8,128)(2,1)}, u32[]{:S(2)}) copy-start(bf16[2,64,768]{2,1,0:T(8,128)(2,1)} %param.10) | copy-start | bytes 589828
  0.0 15.8 %collective-permute-start = (bf16[2,64,768]{2,1,0:T(8,128)(2,1)}, bf16[2,64,768]{2,1,0:T(8,128)(2,1)S(1)}, u32[]{:S(2)}, u32[]{:S(2)}) collective-permute-start(bf16[2,64,768]{2,1,0:T(8,128)(2,1)} %param.10), channel_id=1, source_target_pairs={{0,2},{1,3},{2,0},{3,1},{4,6},{5,7},{6,4},{7,5},{8,10},{9,11},{10,... | collective-permute-start | bytes 589832 | tf_op jit(solution)/shard_map/ppermute | solution.py:18
  17.2 26.2 %copy-start.2 = (f32[1,768]{1,0:T(1,128)S(1)}, f32[1,768]{1,0:T(1,128)}, u32[]{:S(2)}) copy-start(f32[1,768]{1,0:T(1,128)} %param.11) | copy-start | bytes 9220
  43.4 4.9 %collective-permute-start.1 = (bf16[16,1,24,1536]{3,2,0,1:T(8,128)(2,1)S(1)}, bf16[16,1,24,1536]{3,2,0,1:T(8,128)(2,1)S(1)}, u32[]{:S(2)}, u32[]{:S(2)}) collective-permute-start(bf16[16,1,24,1536]{3,2,0,1:T(8,128)(2,1)S(1)} %bitcast.224), channel_id=1, source_target_pairs={{0,1},{1,0},{2,3},{3,2},{4,5},{5,4},{6,7},{7,6},{8,9},{9,8},{10,11... | collective-permute-start | bytes 3538952 | tf_op jit(solution)/shard_map/ppermute | solution.py:18
  43.5 2.8 %collective-permute-start.2 = (f32[768]{0:T(1024)S(1)}, f32[768]{0:T(1024)S(1)}, u32[]{:S(2)}, u32[]{:S(2)}) collective-permute-start(f32[768]{0:T(1024)S(1)} %reduce.4), channel_id=1, source_target_pairs={{0,1},{1,0},{2,3},{3,2},{4,5},{5,4},{6,7},{7,6},{8,9},{9,8},{10,11... | collective-permute-start | bytes 9224 | tf_op jit(solution)/shard_map/ppermute | solution.py:18
  44.1 3.6 %collective-permute-start.3 = (f32[768]{0:T(1024)S(1)}, f32[768]{0:T(1024)S(1)}, u32[]{:S(2)}, u32[]{:S(2)}) collective-permute-start(f32[768]{0:T(1024)S(1)} %reduce.4), channel_id=1, source_target_pairs={{0,2},{1,3},{2,0},{3,1},{4,6},{5,7},{6,4},{7,5},{8,10},{9,11},{10,... | collective-permute-start | bytes 9224 | tf_op jit(solution)/shard_map/ppermute | solution.py:18
  45.3 3.1 %collective-permute-start.4 = (f32[768]{0:T(1024)S(1)}, f32[768]{0:T(1024)S(1)}, u32[]{:S(2)}, u32[]{:S(2)}) collective-permute-start(f32[768]{0:T(1024)S(1)} %reduce.4), channel_id=1, source_target_pairs={{0,3},{1,2},{2,1},{3,0},{4,7},{5,6},{6,5},{7,4},{8,11},{9,10},{10,... | collective-permute-start | bytes 9224 | tf_op jit(solution)/shard_map/ppermute | solution.py:18
  57.5 2.9 %collective-permute-start.5 = (bf16[16,1,24,1536]{3,2,0,1:T(8,128)(2,1)S(1)}, bf16[16,1,24,1536]{3,2,0,1:T(8,128)(2,1)S(1)}, u32[]{:S(2)}, u32[]{:S(2)}) collective-permute-start(bf16[16,1,24,1536]{3,2,0,1:T(8,128)(2,1)S(1)} %select_convert_fusion.2), channel_id=1, source_target_pairs={{0,1},{1,0},{2,3},{3,2},{4,5},{5,4},{6,7},{7,6},{8,9},{9,8},{10,11... | collective-permute-start | bytes 3538952 | tf_op jit(solution)/shard_map/ppermute | solution.py:18
  62.0 24.2 %all-to-all-start.1 = ((bf16[16,1,24,1536]{3,2,1,0:T(8,128)(2,1)}), bf16[16,1,24,1536]{3,2,1,0:T(8,128)(2,1)S(1)}, u32[]{:S(2)}, u32[]{:S(2)}) async-start(bf16[16,1,24,1536]{3,2,1,0:T(8,128)(2,1)} %fusion.60), calls=%async_computation.1 | async-start | bytes 2359296 | tf_op jit(solution)/shard_map/all_to_all | solution.py:121
  88.9 5.8 %collective-permute-start.6 = (f32[64,768]{1,0:T(8,128)S(1)}, f32[64,768]{1,0:T(8,128)S(1)}, u32[]{:S(2)}, u32[]{:S(2)}) collective-permute-start(f32[64,768]{1,0:T(8,128)S(1)} %slice_select_fusion.3), channel_id=1, source_target_pairs={{0,2},{1,3},{2,0},{3,1},{4,6},{5,7},{6,4},{7,5},{8,10},{9,11},{10,... | collective-permute-start | bytes 589832 | tf_op jit(solution)/shard_map/ppermute | solution.py:18
  94.8 8.0 %collective-permute-start.7 = (bf16[64,768]{1,0:T(8,128)(2,1)S(1)}, bf16[64,768]{1,0:T(8,128)(2,1)S(1)}, u32[]{:S(2)}, u32[]{:S(2)}) collective-permute-start(bf16[64,768]{1,0:T(8,128)(2,1)S(1)} %add_convert_fusion.5), channel_id=1, source_target_pairs={{0,64},{1,65},{2,66},{3,67},{4,68},{5,69},{6,70},{7,71},{8,72},{9,... | collective-permute-start | bytes 294920 | tf_op jit(solution)/shard_map/ppermute | solution.py:13
  96.1 8.0 %collective-permute-start.8 = (bf16[64,768]{1,0:T(8,128)(2,1)S(1)}, bf16[64,768]{1,0:T(8,128)(2,1)S(1)}, u32[]{:S(2)}, u32[]{:S(2)}) collective-permute-start(bf16[64,768]{1,0:T(8,128)(2,1)S(1)} %add_convert_fusion.5), channel_id=1, source_target_pairs={{0,66},{1,67},{2,64},{3,65},{4,70},{5,71},{6,68},{7,69},{8,74},{9,... | collective-permute-start | bytes 294920 | tf_op jit(solution)/shard_map/ppermute | solution.py:139
  127.8 2.8 %collective-permute-start.9 = (bf16[16,1,24,1536]{3,2,0,1:T(8,128)(2,1)S(1)}, bf16[16,1,24,1536]{3,2,0,1:T(8,128)(2,1)S(1)}, u32[]{:S(2)}, u32[]{:S(2)}) collective-permute-start(bf16[16,1,24,1536]{3,2,0,1:T(8,128)(2,1)S(1)} %bitcast.225), channel_id=1, source_target_pairs={{0,1},{1,0},{2,3},{3,2},{4,5},{5,4},{6,7},{7,6},{8,9},{9,8},{10,11... | collective-permute-start | bytes 3538952 | tf_op jit(solution)/shard_map/ppermute | solution.py:18
  131.1 5.1 %slice-start.8 = ((s8[6291456]{0:T(1024)(128)(4,1)}), s8[4194304]{0:T(1024)(128)(4,1)S(1)}, s32[]{:S(2)}) async-start(s8[6291456]{0:T(1024)(128)(4,1)} %bitcast.250), calls=%async_computation.14 | async-start | bytes 8388608
  139.8 2.9 %collective-permute-start.10 = (bf16[16,1,24,1536]{3,2,0,1:T(8,128)(2,1)S(1)}, bf16[16,1,24,1536]{3,2,0,1:T(8,128)(2,1)S(1)}, u32[]{:S(2)}, u32[]{:S(2)}) collective-permute-start(bf16[16,1,24,1536]{3,2,0,1:T(8,128)(2,1)S(1)} %select_convert_fusion.1), channel_id=1, source_target_pairs={{0,1},{1,0},{2,3},{3,2},{4,5},{5,4},{6,7},{7,6},{8,9},{9,8},{10,11... | collective-permute-start | bytes 3538952 | tf_op jit(solution)/shard_map/ppermute | solution.py:18
  144.2 24.0 %all-to-all-start.3 = ((bf16[16,1,24,1536]{3,2,1,0:T(8,128)(2,1)}), bf16[16,1,24,1536]{3,2,1,0:T(8,128)(2,1)S(1)}, u32[]{:S(2)}, u32[]{:S(2)}) async-start(bf16[16,1,24,1536]{3,2,1,0:T(8,128)(2,1)} %fusion.61), calls=%async_computation.3 | async-start | bytes 2359296 | tf_op jit(solution)/shard_map/all_to_all | solution.py:121
  171.1 5.8 %collective-permute-start.11 = (f32[64,768]{1,0:T(8,128)S(1)}, f32[64,768]{1,0:T(8,128)S(1)}, u32[]{:S(2)}, u32[]{:S(2)}) collective-permute-start(f32[64,768]{1,0:T(8,128)S(1)} %slice_select_fusion.2), channel_id=1, source_target_pairs={{0,2},{1,3},{2,0},{3,1},{4,6},{5,7},{6,4},{7,5},{8,10},{9,11},{10,... | collective-permute-start | bytes 589832 | tf_op jit(solution)/shard_map/ppermute | solution.py:18
  176.9 8.0 %collective-permute-start.12 = (bf16[64,768]{1,0:T(8,128)(2,1)S(1)}, bf16[64,768]{1,0:T(8,128)(2,1)S(1)}, u32[]{:S(2)}, u32[]{:S(2)}) collective-permute-start(bf16[64,768]{1,0:T(8,128)(2,1)S(1)} %add_convert_fusion.4), channel_id=1, source_target_pairs={{0,64},{1,65},{2,66},{3,67},{4,68},{5,69},{6,70},{7,71},{8,72},{9,... | collective-permute-start | bytes 294920 | tf_op jit(solution)/shard_map/ppermute | solution.py:13
  178.2 7.8 %collective-permute-start.13 = (bf16[64,768]{1,0:T(8,128)(2,1)S(1)}, bf16[64,768]{1,0:T(8,128)(2,1)S(1)}, u32[]{:S(2)}, u32[]{:S(2)}) collective-permute-start(bf16[64,768]{1,0:T(8,128)(2,1)S(1)} %add_convert_fusion.4), channel_id=1, source_target_pairs={{0,66},{1,67},{2,64},{3,65},{4,70},{5,71},{6,68},{7,69},{8,74},{9,... | collective-permute-start | bytes 294920 | tf_op jit(solution)/shard_map/ppermute | solution.py:139
  209.7 2.8 %collective-permute-start.14 = (bf16[16,1,24,1536]{3,2,0,1:T(8,128)(2,1)S(1)}, bf16[16,1,24,1536]{3,2,0,1:T(8,128)(2,1)S(1)}, u32[]{:S(2)}, u32[]{:S(2)}) collective-permute-start(bf16[16,1,24,1536]{3,2,0,1:T(8,128)(2,1)S(1)} %bitcast.226), channel_id=1, source_target_pairs={{0,1},{1,0},{2,3},{3,2},{4,5},{5,4},{6,7},{7,6},{8,9},{9,8},{10,11... | collective-permute-start | bytes 3538952 | tf_op jit(solution)/shard_map/ppermute | solution.py:18
  212.9 5.3 %slice-start.10 = ((s8[6291456]{0:T(1024)(128)(4,1)}), s8[4194304]{0:T(1024)(128)(4,1)S(1)}, s32[]{:S(2)}) async-start(s8[6291456]{0:T(1024)(128)(4,1)} %bitcast.252), calls=%async_computation.16 | async-start | bytes 8388608
  221.7 2.9 %collective-permute-start.15 = (bf16[16,1,24,1536]{3,2,0,1:T(8,128)(2,1)S(1)}, bf16[16,1,24,1536]{3,2,0,1:T(8,128)(2,1)S(1)}, u32[]{:S(2)}, u32[]{:S(2)}) collective-permute-start(bf16[16,1,24,1536]{3,2,0,1:T(8,128)(2,1)S(1)} %select_convert_fusion), channel_id=1, source_target_pairs={{0,1},{1,0},{2,3},{3,2},{4,5},{5,4},{6,7},{7,6},{8,9},{9,8},{10,11... | collective-permute-start | bytes 3538952 | tf_op jit(solution)/shard_map/ppermute | solution.py:18
  226.0 24.0 %all-to-all-start.5 = ((bf16[16,1,24,1536]{3,2,1,0:T(8,128)(2,1)}), bf16[16,1,24,1536]{3,2,1,0:T(8,128)(2,1)S(1)}, u32[]{:S(2)}, u32[]{:S(2)}) async-start(bf16[16,1,24,1536]{3,2,1,0:T(8,128)(2,1)} %fusion.62), calls=%async_computation.5 | async-start | bytes 2359296 | tf_op jit(solution)/shard_map/all_to_all | solution.py:121
  252.9 5.8 %collective-permute-start.16 = (f32[64,768]{1,0:T(8,128)S(1)}, f32[64,768]{1,0:T(8,128)S(1)}, u32[]{:S(2)}, u32[]{:S(2)}) collective-permute-start(f32[64,768]{1,0:T(8,128)S(1)} %slice_select_fusion.1), channel_id=1, source_target_pairs={{0,2},{1,3},{2,0},{3,1},{4,6},{5,7},{6,4},{7,5},{8,10},{9,11},{10,... | collective-permute-start | bytes 589832 | tf_op jit(solution)/shard_map/ppermute | solution.py:18
  (11 other events, 32.1 us)

commit v4 on v3

--- a/solution.py
+++ b/solution.py
@@ -60,10 +60,13 @@
     onehot_all = (routes_all[..., None] == jnp.arange(EXPERTS, dtype=jnp.int32)).astype(jnp.int32)
     slot_all = jnp.sum((jnp.cumsum(onehot_all, axis=1) - onehot_all) * onehot_all, axis=2)
     dest_all = routes_all * capacity + slot_all
-    source_all = (
-        jnp.full((micro, EXPERTS * capacity), -1, jnp.int32)
-        .at[jnp.arange(micro)[:, None], dest_all]
-        .set(jnp.broadcast_to(jnp.arange(2 * rows_here, dtype=jnp.int32) // 2, dest_all.shape))
+    source_all = jnp.stack(
+        [
+            jnp.full((EXPERTS * capacity,), -1, jnp.int32)
+            .at[dest_all[m]]
+            .set(jnp.arange(2 * rows_here, dtype=jnp.int32) // 2)
+            for m in range(micro)
+        ]
     )
     n_t = lax.axis_size("tensor")
     cross_route = [

time: 260 us -> 252 us (0.969)
  local copies, waits for them, and re-layouts: 29 us -> 18.2 us
    scatter x1 -> x2, local copies, waits for them, and re-layouts: 12.5 us -> 1.95 us  [shards(): source_all = jnp.stack([jnp.full((EXPERTS * capacity,), -1, jnp.int32).at...]
    unnamed x31 -> x29, local copies, waits for them, and re-layouts: 6.07 us -> 6.06 us
  transfers between devices with their start and end apart: 20 -> 20, of which waited for: 18 -> 19; matrix products, arithmetic and copies ran while one was open for 6% -> 2% of each run, Pallas kernels for 0% -> 0%
where the time goes in v4:
time: 252 us; the launch traced here: 251 us
  waiting for transfers between devices  107 us (42%)
  blocking collectives  70.2 us (28%)
  starting transfers between devices  23 us (9%)
  local copies, waits for them, and re-layouts  18.2 us (7%)
  matrix products  16.4 us (7%)
  other arithmetic  15.4 us (6%)
    all_to_all x3, blocking collectives, shards(): lax.all_to_all(outgoing, 'expert', split_axis=0, concat_axis=0, tiled=True)  70.2 us
    all_to_all x3, waiting for transfers between devices, shards(): lax.all_to_all(chip_sum, 'expert', split_axis=0, concat_axis=0, tiled=True)  60 us
    ppermute x13, waiting for transfers between devices, swap(): return lax.ppermute(block, axis, [(i, i ^ bit) for i in range(n)])  33.7 us
    all_to_all x3, starting transfers between devices, shards(): lax.all_to_all(chip_sum, 'expert', split_axis=0, concat_axis=0, tiled=True)  11.9 us
    ppermute x2, waiting for transfers between devices, from_behind(): return lax.ppermute(block, axis, route)  10.8 us
    dot_general x3, matrix products, shards(): jnp.einsum('sekf,efd->sekd', hidden, down_local, preferred_element_type=j...  8.37 us
    dot_general x3, matrix products, shards(): jnp.einsum('sekd,edf->sekf', normed, up_local, preferred_element_type=jnp...  8.07 us
    unnamed x29, local copies, waits for them, and re-layouts  6.06 us
  transfers between devices with their start and end apart: 20, of which 19 were waited for; matrix products, arithmetic and copies ran while one was open for 2% of the time, Pallas kernels for 0%

profile of v4, /device:TPU:6, one launch (start us, length us, event | category | flops | bytes accessed | tf_op | source)
XLA Modules:
  0.0 251.1 jit_solution(438382910782003699)
XLA Ops:
  9.4 25.6 %all_to_all.30 = bf16[16,1,24,1536]{3,2,1,0:T(8,128)(2,1)S(1)} all-to-all(bf16[16,1,24,1536]{3,2,1,0:T(8,128)(2,1)S(1)} %bitcast.230), channel_id=1, replica_groups=mesh['section'=2,'expert'=16,'tensor'=4] {'expert'}, dimensions={0} | all-to-all | bytes 2359296 | tf_op jit(solution)/shard_map/all_to_all | solution.py:94
  42.5 2.7 %fusion.10 = f32[16,24,1024]{2,1,0:T(8,128)S(1)} fusion(bf16[1,1,3072,1024]{3,2,1,0:T(8,128)(2,1)S(1)} %bitcast.245, bf16[16,24,768]{2,1,0:T(8,128)(2,1)S(1)} %get-tuple-element.81, bf16[16,24,768]{2,1,0:T(8,128)(2,1)S(1)} %get-tuple-element.55, bf16[16,24,768]{2,1,0:T(8,128)(2,1)S(1)} %get-tuple-element.82, ...), kind=kOutput, calls=%fused_computation.18 | convolution fusion | flops 2428895232 | bytes 10237440 | tf_op jit(solution)/shard_map/sekd,edf->sekf/dot_general | solution.py:104
  45.2 2.8 %fusion.12 = f32[16,1,24,3072]{3,2,0,1:T(8,128)S(1)} fusion(bf16[1,1,1024,3072]{3,2,1,0:T(8,128)(2,1)S(1)} %bitcast.251, f32[16,24,1024]{2,1,0:T(8,128)S(1)} %fusion.10), kind=kOutput, calls=%fused_computation.26 | convolution fusion | flops 2417885184 | bytes 12582912 | tf_op jit(solution)/shard_map/sekf,efd->sekd/dot_general | solution.py:108
  48.9 2.7 %collective-permute-done.5 = bf16[16,1,24,1536]{3,2,0,1:T(8,128)(2,1)S(1)} collective-permute-done((bf16[16,1,24,1536]{3,2,0,1:T(8,128)(2,1)S(1)}, bf16[16,1,24,1536]{3,2,0,1:T(8,128)(2,1)S(1)}, u32[]{:S(2)}, u32[]{:S(2)}) %collective-permute-start.5) | collective-permute-done | bytes 1179680 | tf_op jit(solution)/shard_map/ppermute | solution.py:18
  53.2 4.0 %all-to-all-start.1 = ((bf16[16,1,24,1536]{3,2,1,0:T(8,128)(2,1)}), bf16[16,1,24,1536]{3,2,1,0:T(8,128)(2,1)S(1)}, u32[]{:S(2)}, u32[]{:S(2)}) async-start(bf16[16,1,24,1536]{3,2,1,0:T(8,128)(2,1)} %fusion.60), calls=%async_computation.1 | async-start | bytes 2359296 | tf_op jit(solution)/shard_map/all_to_all | solution.py:124
  57.4 20.0 %all-to-all-done.1 = bf16[16,1,24,1536]{3,2,1,0:T(8,128)(2,1)S(1)} async-done(((bf16[16,1,24,1536]{3,2,1,0:T(8,128)(2,1)}), bf16[16,1,24,1536]{3,2,1,0:T(8,128)(2,1)S(1)}, u32[]{:S(2)}, u32[]{:S(2)}) %all-to-all-start.1) | async-done | bytes 1179680 | tf_op jit(solution)/shard_map/all_to_all | solution.py:124
  81.4 4.5 %collective-permute-done.6 = f32[64,768]{1,0:T(8,128)S(1)} collective-permute-done((f32[64,768]{1,0:T(8,128)S(1)}, f32[64,768]{1,0:T(8,128)S(1)}, u32[]{:S(2)}, u32[]{:S(2)}) %collective-permute-start.6) | collective-permute-done | bytes 196640 | tf_op jit(solution)/shard_map/ppermute | solution.py:18
  88.6 5.4 %collective-permute-done.7 = bf16[64,768]{1,0:T(8,128)(2,1)S(1)} collective-permute-done((bf16[64,768]{1,0:T(8,128)(2,1)S(1)}, bf16[64,768]{1,0:T(8,128)(2,1)S(1)}, u32[]{:S(2)}, u32[]{:S(2)}) %collective-permute-start.7) | collective-permute-done | bytes 98336 | tf_op jit(solution)/shard_map/ppermute | solution.py:13
  97.1 22.3 %all_to_all.31 = bf16[16,1,24,1536]{3,2,1,0:T(8,128)(2,1)S(1)} all-to-all(bf16[16,1,24,1536]{3,2,1,0:T(8,128)(2,1)S(1)} %bitcast.231), channel_id=1, replica_groups=mesh['section'=2,'expert'=16,'tensor'=4] {'expert'}, dimensions={0} | all-to-all | bytes 2359296 | tf_op jit(solution)/shard_map/all_to_all | solution.py:94
  119.4 2.8 %collective-permute-done.9 = bf16[16,1,24,1536]{3,2,0,1:T(8,128)(2,1)S(1)} collective-permute-done((bf16[16,1,24,1536]{3,2,0,1:T(8,128)(2,1)S(1)}, bf16[16,1,24,1536]{3,2,0,1:T(8,128)(2,1)S(1)}, u32[]{:S(2)}, u32[]{:S(2)}) %collective-permute-start.9) | collective-permute-done | bytes 1179680 | tf_op jit(solution)/shard_map/ppermute | solution.py:18
  125.1 2.7 %fusion.8 = f32[16,24,1024]{2,1,0:T(8,128)S(1)} fusion(bf16[1,1,3072,1024]{3,2,1,0:T(8,128)(2,1)S(1)} %bitcast.247, bf16[16,24,768]{2,1,0:T(8,128)(2,1)S(1)} %get-tuple-element.51, bf16[16,24,768]{2,1,0:T(8,128)(2,1)S(1)} %get-tuple-element.47, bf16[16,24,768]{2,1,0:T(8,128)(2,1)S(1)} %get-tuple-element.50, bf16[16,24,768]{2,1,0:T(8,128)(2,1)S(1)} %get-tuple-element.46, ...), kind=kOutput, calls=%fused_computation.16 | convolution fusion | flops 2428895232 | bytes 10237440 | tf_op jit(solution)/shard_map/sekd,edf->sekf/dot_general | solution.py:104
  127.8 2.8 %fusion.15 = f32[16,1,24,3072]{3,2,0,1:T(8,128)S(1)} fusion(bf16[1,1,1024,3072]{3,2,1,0:T(8,128)(2,1)S(1)} %bitcast.253, f32[16,24,1024]{2,1,0:T(8,128)S(1)} %fusion.8), kind=kOutput, calls=%fused_computation.27 | convolution fusion | flops 2417885184 | bytes 12582912 | tf_op jit(solution)/shard_map/sekf,efd->sekd/dot_general | solution.py:108
  131.6 2.7 %collective-permute-done.10 = bf16[16,1,24,1536]{3,2,0,1:T(8,128)(2,1)S(1)} collective-permute-done((bf16[16,1,24,1536]{3,2,0,1:T(8,128)(2,1)S(1)}, bf16[16,1,24,1536]{3,2,0,1:T(8,128)(2,1)S(1)}, u32[]{:S(2)}, u32[]{:S(2)}) %collective-permute-start.10) | collective-permute-done | bytes 1179680 | tf_op jit(solution)/shard_map/ppermute | solution.py:18
  135.8 3.9 %all-to-all-start.3 = ((bf16[16,1,24,1536]{3,2,1,0:T(8,128)(2,1)}), bf16[16,1,24,1536]{3,2,1,0:T(8,128)(2,1)S(1)}, u32[]{:S(2)}, u32[]{:S(2)}) async-start(bf16[16,1,24,1536]{3,2,1,0:T(8,128)(2,1)} %fusion.61), calls=%async_computation.3 | async-start | bytes 2359296 | tf_op jit(solution)/shard_map/all_to_all | solution.py:124
  139.8 20.0 %all-to-all-done.3 = bf16[16,1,24,1536]{3,2,1,0:T(8,128)(2,1)S(1)} async-done(((bf16[16,1,24,1536]{3,2,1,0:T(8,128)(2,1)}), bf16[16,1,24,1536]{3,2,1,0:T(8,128)(2,1)S(1)}, u32[]{:S(2)}, u32[]{:S(2)}) %all-to-all-start.3) | async-done | bytes 1179680 | tf_op jit(solution)/shard_map/all_to_all | solution.py:124
  163.3 5.2 %collective-permute-done.11 = f32[64,768]{1,0:T(8,128)S(1)} collective-permute-done((f32[64,768]{1,0:T(8,128)S(1)}, f32[64,768]{1,0:T(8,128)S(1)}, u32[]{:S(2)}, u32[]{:S(2)}) %collective-permute-start.11) | collective-permute-done | bytes 196640 | tf_op jit(solution)/shard_map/ppermute | solution.py:18
  171.1 5.4 %collective-permute-done.12 = bf16[64,768]{1,0:T(8,128)(2,1)S(1)} collective-permute-done((bf16[64,768]{1,0:T(8,128)(2,1)S(1)}, bf16[64,768]{1,0:T(8,128)(2,1)S(1)}, u32[]{:S(2)}, u32[]{:S(2)}) %collective-permute-start.12) | collective-permute-done | bytes 98336 | tf_op jit(solution)/shard_map/ppermute | solution.py:13
  179.0 22.3 %all_to_all.32 = bf16[16,1,24,1536]{3,2,1,0:T(8,128)(2,1)S(1)} all-to-all(bf16[16,1,24,1536]{3,2,1,0:T(8,128)(2,1)S(1)} %bitcast.232), channel_id=1, replica_groups=mesh['section'=2,'expert'=16,'tensor'=4] {'expert'}, dimensions={0} | all-to-all | bytes 2359296 | tf_op jit(solution)/shard_map/all_to_all | solution.py:94
  201.3 2.8 %collective-permute-done.14 = bf16[16,1,24,1536]{3,2,0,1:T(8,128)(2,1)S(1)} collective-permute-done((bf16[16,1,24,1536]{3,2,0,1:T(8,128)(2,1)S(1)}, bf16[16,1,24,1536]{3,2,0,1:T(8,128)(2,1)S(1)}, u32[]{:S(2)}, u32[]{:S(2)}) %collective-permute-start.14) | collective-permute-done | bytes 1179680 | tf_op jit(solution)/shard_map/ppermute | solution.py:18
  209.7 2.8 %fusion.18 = f32[16,1,24,3072]{3,2,0,1:T(8,128)S(1)} fusion(bf16[1,1,1024,3072]{3,2,1,0:T(8,128)(2,1)S(1)} %bitcast.255, f32[16,24,1024]{2,1,0:T(8,128)S(1)} %fusion.6), kind=kOutput, calls=%fused_computation.28 | convolution fusion | flops 2417885184 | bytes 12582912 | tf_op jit(solution)/shard_map/sekf,efd->sekd/dot_general | solution.py:108
  213.5 2.7 %collective-permute-done.15 = bf16[16,1,24,1536]{3,2,0,1:T(8,128)(2,1)S(1)} collective-permute-done((bf16[16,1,24,1536]{3,2,0,1:T(8,128)(2,1)S(1)}, bf16[16,1,24,1536]{3,2,0,1:T(8,128)(2,1)S(1)}, u32[]{:S(2)}, u32[]{:S(2)}) %collective-permute-start.15) | collective-permute-done | bytes 1179680 | tf_op jit(solution)/shard_map/ppermute | solution.py:18
  217.6 4.0 %all-to-all-start.5 = ((bf16[16,1,24,1536]{3,2,1,0:T(8,128)(2,1)}), bf16[16,1,24,1536]{3,2,1,0:T(8,128)(2,1)S(1)}, u32[]{:S(2)}, u32[]{:S(2)}) async-start(bf16[16,1,24,1536]{3,2,1,0:T(8,128)(2,1)} %fusion.62), calls=%async_computation.5 | async-start | bytes 2359296 | tf_op jit(solution)/shard_map/all_to_all | solution.py:124
  221.7 20.0 %all-to-all-done.5 = bf16[16,1,24,1536]{3,2,1,0:T(8,128)(2,1)S(1)} async-done(((bf16[16,1,24,1536]{3,2,1,0:T(8,128)(2,1)}), bf16[16,1,24,1536]{3,2,1,0:T(8,128)(2,1)S(1)}, u32[]{:S(2)}, u32[]{:S(2)}) %all-to-all-start.5) | async-done | bytes 1179680 | tf_op jit(solution)/shard_map/all_to_all | solution.py:124
  245.1 5.2 %collective-permute-done.16 = f32[64,768]{1,0:T(8,128)S(1)} collective-permute-done((f32[64,768]{1,0:T(8,128)S(1)}, f32[64,768]{1,0:T(8,128)S(1)}, u32[]{:S(2)}, u32[]{:S(2)}) %collective-permute-start.16) | collective-permute-done | bytes 196640 | tf_op jit(solution)/shard_map/ppermute | solution.py:18
  (152 shorter events, 55.0 us)
Async XLA Ops:
  0.0 6.9 %collective-permute-start = (bf16[2,64,768]{2,1,0:T(8,128)(2,1)}, bf16[2,64,768]{2,1,0:T(8,128)(2,1)S(1)}, u32[]{:S(2)}, u32[]{:S(2)}) collective-permute-start(bf16[2,64,768]{2,1,0:T(8,128)(2,1)} %param.10), channel_id=1, source_target_pairs={{0,2},{1,3},{2,0},{3,1},{4,6},{5,7},{6,4},{7,5},{8,10},{9,11},{10,... | collective-permute-start | bytes 589832 | tf_op jit(solution)/shard_map/ppermute | solution.py:18
  9.3 25.8 %copy-start.1 = (f32[1,768]{1,0:T(1,128)S(1)}, f32[1,768]{1,0:T(1,128)}, u32[]{:S(2)}) copy-start(f32[1,768]{1,0:T(1,128)} %param.11) | copy-start | bytes 9220
  35.0 4.5 %collective-permute-start.1 = (bf16[16,1,24,1536]{3,2,0,1:T(8,128)(2,1)S(1)}, bf16[16,1,24,1536]{3,2,0,1:T(8,128)(2,1)S(1)}, u32[]{:S(2)}, u32[]{:S(2)}) collective-permute-start(bf16[16,1,24,1536]{3,2,0,1:T(8,128)(2,1)S(1)} %bitcast.224), channel_id=1, source_target_pairs={{0,1},{1,0},{2,3},{3,2},{4,5},{5,4},{6,7},{7,6},{8,9},{9,8},{10,11... | collective-permute-start | bytes 3538952 | tf_op jit(solution)/shard_map/ppermute | solution.py:18
  35.0 2.8 %collective-permute-start.2 = (f32[768]{0:T(1024)S(1)}, f32[768]{0:T(1024)S(1)}, u32[]{:S(2)}, u32[]{:S(2)}) collective-permute-start(f32[768]{0:T(1024)S(1)} %reduce.4), channel_id=1, source_target_pairs={{0,1},{1,0},{2,3},{3,2},{4,5},{5,4},{6,7},{7,6},{8,9},{9,8},{10,11... | collective-permute-start | bytes 9224 | tf_op jit(solution)/shard_map/ppermute | solution.py:18
  35.6 3.6 %collective-permute-start.3 = (f32[768]{0:T(1024)S(1)}, f32[768]{0:T(1024)S(1)}, u32[]{:S(2)}, u32[]{:S(2)}) collective-permute-start(f32[768]{0:T(1024)S(1)} %reduce.4), channel_id=1, source_target_pairs={{0,2},{1,3},{2,0},{3,1},{4,6},{5,7},{6,4},{7,5},{8,10},{9,11},{10,... | collective-permute-start | bytes 9224 | tf_op jit(solution)/shard_map/ppermute | solution.py:18
  36.5 3.1 %collective-permute-start.4 = (f32[768]{0:T(1024)S(1)}, f32[768]{0:T(1024)S(1)}, u32[]{:S(2)}, u32[]{:S(2)}) collective-permute-start(f32[768]{0:T(1024)S(1)} %reduce.4), channel_id=1, source_target_pairs={{0,3},{1,2},{2,1},{3,0},{4,7},{5,6},{6,5},{7,4},{8,11},{9,10},{10,... | collective-permute-start | bytes 9224 | tf_op jit(solution)/shard_map/ppermute | solution.py:18
  40.1 5.1 %slice-start.6 = ((s8[6291456]{0:T(1024)(128)(4,1)}), s8[4194304]{0:T(1024)(128)(4,1)S(1)}, s32[]{:S(2)}) async-start(s8[6291456]{0:T(1024)(128)(4,1)} %bitcast.250), calls=%async_computation.12 | async-start | bytes 8388608
  48.7 2.9 %collective-permute-start.5 = (bf16[16,1,24,1536]{3,2,0,1:T(8,128)(2,1)S(1)}, bf16[16,1,24,1536]{3,2,0,1:T(8,128)(2,1)S(1)}, u32[]{:S(2)}, u32[]{:S(2)}) collective-permute-start(bf16[16,1,24,1536]{3,2,0,1:T(8,128)(2,1)S(1)} %select_convert_fusion.2), channel_id=1, source_target_pairs={{0,1},{1,0},{2,3},{3,2},{4,5},{5,4},{6,7},{7,6},{8,9},{9,8},{10,11... | collective-permute-start | bytes 3538952 | tf_op jit(solution)/shard_map/ppermute | solution.py:18
  53.2 24.2 %all-to-all-start.1 = ((bf16[16,1,24,1536]{3,2,1,0:T(8,128)(2,1)}), bf16[16,1,24,1536]{3,2,1,0:T(8,128)(2,1)S(1)}, u32[]{:S(2)}, u32[]{:S(2)}) async-start(bf16[16,1,24,1536]{3,2,1,0:T(8,128)(2,1)} %fusion.60), calls=%async_computation.1 | async-start | bytes 2359296 | tf_op jit(solution)/shard_map/all_to_all | solution.py:124
  80.2 5.8 %collective-permute-start.6 = (f32[64,768]{1,0:T(8,128)S(1)}, f32[64,768]{1,0:T(8,128)S(1)}, u32[]{:S(2)}, u32[]{:S(2)}) collective-permute-start(f32[64,768]{1,0:T(8,128)S(1)} %slice_select_fusion.3), channel_id=1, source_target_pairs={{0,2},{1,3},{2,0},{3,1},{4,6},{5,7},{6,4},{7,5},{8,10},{9,11},{10,... | collective-permute-start | bytes 589832 | tf_op jit(solution)/shard_map/ppermute | solution.py:18
  86.0 8.0 %collective-permute-start.7 = (bf16[64,768]{1,0:T(8,128)(2,1)S(1)}, bf16[64,768]{1,0:T(8,128)(2,1)S(1)}, u32[]{:S(2)}, u32[]{:S(2)}) collective-permute-start(bf16[64,768]{1,0:T(8,128)(2,1)S(1)} %add_convert_fusion.5), channel_id=1, source_target_pairs={{0,64},{1,65},{2,66},{3,67},{4,68},{5,69},{6,70},{7,71},{8,72},{9,... | collective-permute-start | bytes 294920 | tf_op jit(solution)/shard_map/ppermute | solution.py:13
  87.3 8.4 %collective-permute-start.8 = (bf16[64,768]{1,0:T(8,128)(2,1)S(1)}, bf16[64,768]{1,0:T(8,128)(2,1)S(1)}, u32[]{:S(2)}, u32[]{:S(2)}) collective-permute-start(bf16[64,768]{1,0:T(8,128)(2,1)S(1)} %add_convert_fusion.5), channel_id=1, source_target_pairs={{0,66},{1,67},{2,64},{3,65},{4,70},{5,71},{6,68},{7,69},{8,74},{9,... | collective-permute-start | bytes 294920 | tf_op jit(solution)/shard_map/ppermute | solution.py:142
  119.4 2.8 %collective-permute-start.9 = (bf16[16,1,24,1536]{3,2,0,1:T(8,128)(2,1)S(1)}, bf16[16,1,24,1536]{3,2,0,1:T(8,128)(2,1)S(1)}, u32[]{:S(2)}, u32[]{:S(2)}) collective-permute-start(bf16[16,1,24,1536]{3,2,0,1:T(8,128)(2,1)S(1)} %bitcast.225), channel_id=1, source_target_pairs={{0,1},{1,0},{2,3},{3,2},{4,5},{5,4},{6,7},{7,6},{8,9},{9,8},{10,11... | collective-permute-start | bytes 3538952 | tf_op jit(solution)/shard_map/ppermute | solution.py:18
  122.7 5.1 %slice-start.8 = ((s8[6291456]{0:T(1024)(128)(4,1)}), s8[4194304]{0:T(1024)(128)(4,1)S(1)}, s32[]{:S(2)}) async-start(s8[6291456]{0:T(1024)(128)(4,1)} %bitcast.252), calls=%async_computation.14 | async-start | bytes 8388608
  131.4 2.9 %collective-permute-start.10 = (bf16[16,1,24,1536]{3,2,0,1:T(8,128)(2,1)S(1)}, bf16[16,1,24,1536]{3,2,0,1:T(8,128)(2,1)S(1)}, u32[]{:S(2)}, u32[]{:S(2)}) collective-permute-start(bf16[16,1,24,1536]{3,2,0,1:T(8,128)(2,1)S(1)} %select_convert_fusion.1), channel_id=1, source_target_pairs={{0,1},{1,0},{2,3},{3,2},{4,5},{5,4},{6,7},{7,6},{8,9},{9,8},{10,11... | collective-permute-start | bytes 3538952 | tf_op jit(solution)/shard_map/ppermute | solution.py:18
  135.8 24.0 %all-to-all-start.3 = ((bf16[16,1,24,1536]{3,2,1,0:T(8,128)(2,1)}), bf16[16,1,24,1536]{3,2,1,0:T(8,128)(2,1)S(1)}, u32[]{:S(2)}, u32[]{:S(2)}) async-start(bf16[16,1,24,1536]{3,2,1,0:T(8,128)(2,1)} %fusion.61), calls=%async_computation.3 | async-start | bytes 2359296 | tf_op jit(solution)/shard_map/all_to_all | solution.py:124
  162.6 5.8 %collective-permute-start.11 = (f32[64,768]{1,0:T(8,128)S(1)}, f32[64,768]{1,0:T(8,128)S(1)}, u32[]{:S(2)}, u32[]{:S(2)}) collective-permute-start(f32[64,768]{1,0:T(8,128)S(1)} %slice_select_fusion.2), channel_id=1, source_target_pairs={{0,2},{1,3},{2,0},{3,1},{4,6},{5,7},{6,4},{7,5},{8,10},{9,11},{10,... | collective-permute-start | bytes 589832 | tf_op jit(solution)/shard_map/ppermute | solution.py:18
  168.5 8.0 %collective-permute-start.12 = (bf16[64,768]{1,0:T(8,128)(2,1)S(1)}, bf16[64,768]{1,0:T(8,128)(2,1)S(1)}, u32[]{:S(2)}, u32[]{:S(2)}) collective-permute-start(bf16[64,768]{1,0:T(8,128)(2,1)S(1)} %add_convert_fusion.4), channel_id=1, source_target_pairs={{0,64},{1,65},{2,66},{3,67},{4,68},{5,69},{6,70},{7,71},{8,72},{9,... | collective-permute-start | bytes 294920 | tf_op jit(solution)/shard_map/ppermute | solution.py:13
  169.8 7.8 %collective-permute-start.13 = (bf16[64,768]{1,0:T(8,128)(2,1)S(1)}, bf16[64,768]{1,0:T(8,128)(2,1)S(1)}, u32[]{:S(2)}, u32[]{:S(2)}) collective-permute-start(bf16[64,768]{1,0:T(8,128)(2,1)S(1)} %add_convert_fusion.4), channel_id=1, source_target_pairs={{0,66},{1,67},{2,64},{3,65},{4,70},{5,71},{6,68},{7,69},{8,74},{9,... | collective-permute-start | bytes 294920 | tf_op jit(solution)/shard_map/ppermute | solution.py:142
  201.3 2.8 %collective-permute-start.14 = (bf16[16,1,24,1536]{3,2,0,1:T(8,128)(2,1)S(1)}, bf16[16,1,24,1536]{3,2,0,1:T(8,128)(2,1)S(1)}, u32[]{:S(2)}, u32[]{:S(2)}) collective-permute-start(bf16[16,1,24,1536]{3,2,0,1:T(8,128)(2,1)S(1)} %bitcast.226), channel_id=1, source_target_pairs={{0,1},{1,0},{2,3},{3,2},{4,5},{5,4},{6,7},{7,6},{8,9},{9,8},{10,11... | collective-permute-start | bytes 3538952 | tf_op jit(solution)/shard_map/ppermute | solution.py:18
  204.4 5.3 %slice-start.10 = ((s8[6291456]{0:T(1024)(128)(4,1)}), s8[4194304]{0:T(1024)(128)(4,1)S(1)}, s32[]{:S(2)}) async-start(s8[6291456]{0:T(1024)(128)(4,1)} %bitcast.254), calls=%async_computation.16 | async-start | bytes 8388608
  213.3 2.9 %collective-permute-start.15 = (bf16[16,1,24,1536]{3,2,0,1:T(8,128)(2,1)S(1)}, bf16[16,1,24,1536]{3,2,0,1:T(8,128)(2,1)S(1)}, u32[]{:S(2)}, u32[]{:S(2)}) collective-permute-start(bf16[16,1,24,1536]{3,2,0,1:T(8,128)(2,1)S(1)} %select_convert_fusion), channel_id=1, source_target_pairs={{0,1},{1,0},{2,3},{3,2},{4,5},{5,4},{6,7},{7,6},{8,9},{9,8},{10,11... | collective-permute-start | bytes 3538952 | tf_op jit(solution)/shard_map/ppermute | solution.py:18
  217.6 24.0 %all-to-all-start.5 = ((bf16[16,1,24,1536]{3,2,1,0:T(8,128)(2,1)}), bf16[16,1,24,1536]{3,2,1,0:T(8,128)(2,1)S(1)}, u32[]{:S(2)}, u32[]{:S(2)}) async-start(bf16[16,1,24,1536]{3,2,1,0:T(8,128)(2,1)} %fusion.62), calls=%async_computation.5 | async-start | bytes 2359296 | tf_op jit(solution)/shard_map/all_to_all | solution.py:124
  244.5 5.8 %collective-permute-start.16 = (f32[64,768]{1,0:T(8,128)S(1)}, f32[64,768]{1,0:T(8,128)S(1)}, u32[]{:S(2)}, u32[]{:S(2)}) collective-permute-start(f32[64,768]{1,0:T(8,128)S(1)} %slice_select_fusion.1), channel_id=1, source_target_pairs={{0,2},{1,3},{2,0},{3,1},{4,6},{5,7},{6,4},{7,5},{8,10},{9,11},{10,... | collective-permute-start | bytes 589832 | tf_op jit(solution)/shard_map/ppermute | solution.py:18
  (10 other events, 27.0 us)

commit v5 on v4

--- a/solution.py
+++ b/solution.py
@@ -72,11 +72,12 @@
     cross_route = [
         (s * n_t + t, (s + 1) * n_t + (t ^ 2)) for s in range(segments - 1) for t in range(n_t)
     ]
-    carried = jnp.zeros((rows_here, 2 * quarter), jnp.bfloat16)
-    for step in range(total_steps):
+    def layer_step(step, carried, collected):
         which = step - segment_pos
         which_safe = jnp.clip(which, 0, micro - 1)
-        entering = tokens_half[min(step, micro - 1)]
+        entering = lax.dynamic_index_in_dim(
+            tokens_half, jnp.minimum(step, micro - 1), 0, keepdims=False
+        )
         half_rows = jnp.where(segment_pos == 0, entering, carried)
         weights = lax.dynamic_index_in_dim(gate_weights[0], which_safe, 0, keepdims=False)
         dest = lax.dynamic_index_in_dim(dest_all, which_safe, 0, keepdims=False)
@@ -136,11 +137,20 @@
         produced = mixed.astype(jnp.bfloat16)
         chosen = (jnp.arange(micro, dtype=jnp.int32) == which)[:, None, None]
         collected = jnp.where(chosen, produced[None], collected)
-        if step + 1 < total_steps:
-            carried = to_half(
-                from_behind(produced, "section", 1),
-                lax.ppermute(produced, ("section", "tensor"), cross_route),
-            )
+        return produced, collected
+
+    def looped(step, state):
+        carried, collected = state
+        produced, collected = layer_step(step, carried, collected)
+        carried = to_half(
+            from_behind(produced, "section", 1),
+            lax.ppermute(produced, ("section", "tensor"), cross_route),
+        )
+        return carried, collected
+
+    carried = jnp.zeros((rows_here, 2 * quarter), jnp.bfloat16)
+    carried, collected = lax.fori_loop(0, total_steps - 1, looped, (carried, collected))
+    _, collected = layer_step(total_steps - 1, carried, collected)
     return collected[None]
 
 

time: 252 us -> 251 us (level)
  blocking collectives: 70.2 us -> 67.6 us
    ppermute x2, waiting for transfers between devices: 10.8 us -> 3.19 us  [from_behind(): return lax.ppermute(block, axis, route)]
    ppermute x2, waiting for transfers between devices: 2.7 us -> 10 us  [looped(): lax.ppermute(produced, ('section', 'tensor'), cross_route)]
    while x0 -> x20, local copies, waits for them, and re-layouts: none -> 3.55 us
    unnamed x29 -> x15, local copies, waits for them, and re-layouts: 6.06 us -> 2.56 us
    all_to_all x3, blocking collectives: 70.2 us -> 67.6 us  [layer_step(): lax.all_to_all(outgoing, 'expert', split_axis=0, concat_axis=0, tiled=True)]
  transfers between devices with their start and end apart: 20 -> 20, of which waited for: 19 -> 17; matrix products, arithmetic and copies ran while one was open for 2% -> 2% of each run, Pallas kernels for 0% -> 0%
where the time goes in v5:
time: 251 us
  waiting for transfers between devices  107 us (43%)
  blocking collectives  67.6 us (27%)
  starting transfers between devices  22.6 us (9%)
  local copies, waits for them, and re-layouts  18.6 us (7%)
  other arithmetic  17.7 us (7%)
  matrix products  16.7 us (7%)
    all_to_all x3, blocking collectives, layer_step(): lax.all_to_all(outgoing, 'expert', split_axis=0, concat_axis=0, tiled=True)  67.6 us
    all_to_all x3, waiting for transfers between devices, layer_step(): lax.all_to_all(chip_sum, 'expert', split_axis=0, concat_axis=0, tiled=True)  60.6 us
    ppermute x13, waiting for transfers between devices, swap(): return lax.ppermute(block, axis, [(i, i ^ bit) for i in range(n)])  32.7 us
    all_to_all x3, starting transfers between devices, layer_step(): lax.all_to_all(chip_sum, 'expert', split_axis=0, concat_axis=0, tiled=True)  11.5 us
    ppermute x2, waiting for transfers between devices, looped(): lax.ppermute(produced, ('section', 'tensor'), cross_route)  10 us
    dot_general x3, matrix products, layer_step(): jnp.einsum('sekd,edf->sekf', normed, up_local, preferred_element_type=jnp...  8.6 us
    dot_general x3, matrix products, layer_step(): jnp.einsum('sekf,efd->sekd', hidden, down_local, preferred_element_type=j...  8.13 us
    ppermute x13, starting transfers between devices, swap(): return lax.ppermute(block, axis, [(i, i ^ bit) for i in range(n)])  5.89 us
  transfers between devices with their start and end apart: 20, of which 17 were waited for; matrix products, arithmetic and copies ran while one was open for 2% of the time, Pallas kernels for 0%

profile of v5, /device:TPU:6, one launch (start us, length us, event | category | flops | bytes accessed | tf_op | source)
XLA Modules:
  0.0 250.6 jit_solution(13372573798339192182)
XLA Ops:
  11.2 167.1 %while.17 = (s32[]{:T(128)}, bf16[64,1536]{1,0:T(8,128)(2,1)S(1)}, bf16[2,64,768]{2,1,0:T(8,128)(2,1)S(1)}, pred[]{:T(512)}, pred[]{:T(512)}, /*index=5*/bf16[2,...) while((s32[]{:T(128)}, bf16[64,1536]{1,0:T(8,128)(2,1)S(1)}, ...), condition=%wide.region_8.11_spmd.clone, body=%wide.region_4.10_spmd.clone.sunk | while | flops 4872197120 | bytes 129411200 | solution.py:152
  12.7 26.1 %all_to_all.35 = bf16[16,1,24,1536]{3,2,1,0:T(8,128)(2,1)S(1)} all-to-all(bf16[16,1,24,1536]{3,2,1,0:T(8,128)(2,1)S(1)} %bitcast.195), channel_id=1, replica_groups=mesh['section'=2,'expert'=16,'tensor'=4] {'expert'}, dimensions={0} | all-to-all | bytes 2359296 | tf_op jit(solution)/shard_map/while/body/eval_jaxpr/all_to_all | solution.py:95
  38.8 2.8 %collective-permute-done = bf16[16,1,24,1536]{3,2,0,1:T(8,128)(2,1)S(1)} collective-permute-done((bf16[16,1,24,1536]{3,2,0,1:T(8,128)(2,1)S(1)}, bf16[16,1,24,1536]{3,2,0,1:T(8,128)(2,1)S(1)}, u32[]{:S(2)}, u32[]{:S(2)}) %collective-permute-start) | collective-permute-done | bytes 1179680 | tf_op jit(solution)/shard_map/while/body/eval_jaxpr/ppermute | solution.py:18
  44.5 2.9 %fusion.80 = f32[16,24,1024]{2,1,0:T(8,128)S(1)} fusion(bf16[1,3072,1024]{2,1,0:T(8,128)(2,1)S(1)} %bitcast.212, bf16[16,24,768]{2,1,0:T(8,128)(2,1)S(1)} %get-tuple-element.505, bf16[16,24,768]{2,1,0:T(8,128)(2,1)S(1)} %get-tuple-element.506, bf16[16,24,768]{2,1,0:T(8,128)(2,1)S(1)} %get-tuple-element.507, ...), kind=kOutput, calls=%fused_computation.8.clone.1 | convolution fusion | flops 2428895232 | bytes 10237440 | tf_op jit(solution)/shard_map/while/body/eval_jaxpr/sekd,edf->sekf/dot_general | solution.py:105
  55.2 3.8 %all-to-all-start.1 = ((bf16[16,1,24,1536]{3,2,1,0:T(8,128)(2,1)}), bf16[16,1,24,1536]{3,2,1,0:T(8,128)(2,1)S(1)}, u32[]{:S(2)}, u32[]{:S(2)}) async-start(bf16[16,1,24,1536]{3,2,1,0:T(8,128)(2,1)} %fusion.83), calls=%async_computation.1 | async-start | bytes 2359296 | tf_op jit(solution)/shard_map/while/body/eval_jaxpr/all_to_all | solution.py:125
  59.2 20.2 %all-to-all-done.1 = bf16[16,1,24,1536]{3,2,1,0:T(8,128)(2,1)S(1)} async-done(((bf16[16,1,24,1536]{3,2,1,0:T(8,128)(2,1)}), bf16[16,1,24,1536]{3,2,1,0:T(8,128)(2,1)S(1)}, u32[]{:S(2)}, u32[]{:S(2)}) %all-to-all-start.1) | async-done | bytes 1179680 | tf_op jit(solution)/shard_map/while/body/eval_jaxpr/all_to_all | solution.py:125
  83.1 4.9 %collective-permute-done.2 = f32[64,768]{1,0:T(8,128)S(1)} collective-permute-done((f32[64,768]{1,0:T(8,128)S(1)}, f32[64,768]{1,0:T(8,128)S(1)}, u32[]{:S(2)}, u32[]{:S(2)}) %collective-permute-start.2) | collective-permute-done | bytes 196640 | tf_op jit(solution)/shard_map/while/body/eval_jaxpr/ppermute | solution.py:18
  90.8 5.0 %collective-permute-done.3 = bf16[64,768]{1,0:T(8,128)(2,1)S(1)} collective-permute-done((bf16[64,768]{1,0:T(8,128)(2,1)S(1)}, bf16[64,768]{1,0:T(8,128)(2,1)S(1)}, u32[]{:S(2)}, u32[]{:S(2)}) %collective-permute-start.3) | collective-permute-done | bytes 98336 | tf_op jit(solution)/shard_map/while/body/eval_jaxpr/ppermute | solution.py:147
  98.9 20.7 %all_to_all.35 = bf16[16,1,24,1536]{3,2,1,0:T(8,128)(2,1)S(1)} all-to-all(bf16[16,1,24,1536]{3,2,1,0:T(8,128)(2,1)S(1)} %bitcast.195), channel_id=1, replica_groups=mesh['section'=2,'expert'=16,'tensor'=4] {'expert'}, dimensions={0} | all-to-all | bytes 2359296 | tf_op jit(solution)/shard_map/while/body/eval_jaxpr/all_to_all | solution.py:95
  119.6 2.8 %collective-permute-done = bf16[16,1,24,1536]{3,2,0,1:T(8,128)(2,1)S(1)} collective-permute-done((bf16[16,1,24,1536]{3,2,0,1:T(8,128)(2,1)S(1)}, bf16[16,1,24,1536]{3,2,0,1:T(8,128)(2,1)S(1)}, u32[]{:S(2)}, u32[]{:S(2)}) %collective-permute-start) | collective-permute-done | bytes 1179680 | tf_op jit(solution)/shard_map/while/body/eval_jaxpr/ppermute | solution.py:18
  125.4 2.9 %fusion.80 = f32[16,24,1024]{2,1,0:T(8,128)S(1)} fusion(bf16[1,3072,1024]{2,1,0:T(8,128)(2,1)S(1)} %bitcast.212, bf16[16,24,768]{2,1,0:T(8,128)(2,1)S(1)} %get-tuple-element.505, bf16[16,24,768]{2,1,0:T(8,128)(2,1)S(1)} %get-tuple-element.506, bf16[16,24,768]{2,1,0:T(8,128)(2,1)S(1)} %get-tuple-element.507, ...), kind=kOutput, calls=%fused_computation.8.clone.1 | convolution fusion | flops 2428895232 | bytes 10237440 | tf_op jit(solution)/shard_map/while/body/eval_jaxpr/sekd,edf->sekf/dot_general | solution.py:105
  128.3 2.7 %fusion.81 = f32[16,1,24,3072]{3,2,0,1:T(8,128)S(1)} fusion(bf16[1,1024,3072]{2,1,0:T(8,128)(2,1)S(1)} %bitcast.218, f32[16,24,1024]{2,1,0:T(8,128)S(1)} %fusion.80), kind=kOutput, calls=%fused_computation.12.clone.1 | convolution fusion | flops 2417885184 | bytes 12582912 | tf_op jit(solution)/shard_map/while/body/eval_jaxpr/sekf,efd->sekd/dot_general | solution.py:109
  132.0 2.7 %collective-permute-done.1 = bf16[16,1,24,1536]{3,2,0,1:T(8,128)(2,1)S(1)} collective-permute-done((bf16[16,1,24,1536]{3,2,0,1:T(8,128)(2,1)S(1)}, bf16[16,1,24,1536]{3,2,0,1:T(8,128)(2,1)S(1)}, u32[]{:S(2)}, u32[]{:S(2)}) %collective-permute-start.1) | collective-permute-done | bytes 1179680 | tf_op jit(solution)/shard_map/while/body/eval_jaxpr/ppermute | solution.py:18
  136.1 3.8 %all-to-all-start.1 = ((bf16[16,1,24,1536]{3,2,1,0:T(8,128)(2,1)}), bf16[16,1,24,1536]{3,2,1,0:T(8,128)(2,1)S(1)}, u32[]{:S(2)}, u32[]{:S(2)}) async-start(bf16[16,1,24,1536]{3,2,1,0:T(8,128)(2,1)} %fusion.83), calls=%async_computation.1 | async-start | bytes 2359296 | tf_op jit(solution)/shard_map/while/body/eval_jaxpr/all_to_all | solution.py:125
  140.1 20.2 %all-to-all-done.1 = bf16[16,1,24,1536]{3,2,1,0:T(8,128)(2,1)S(1)} async-done(((bf16[16,1,24,1536]{3,2,1,0:T(8,128)(2,1)}), bf16[16,1,24,1536]{3,2,1,0:T(8,128)(2,1)S(1)}, u32[]{:S(2)}, u32[]{:S(2)}) %all-to-all-start.1) | async-done | bytes 1179680 | tf_op jit(solution)/shard_map/while/body/eval_jaxpr/all_to_all | solution.py:125
  163.9 5.0 %collective-permute-done.2 = f32[64,768]{1,0:T(8,128)S(1)} collective-permute-done((f32[64,768]{1,0:T(8,128)S(1)}, f32[64,768]{1,0:T(8,128)S(1)}, u32[]{:S(2)}, u32[]{:S(2)}) %collective-permute-start.2) | collective-permute-done | bytes 196640 | tf_op jit(solution)/shard_map/while/body/eval_jaxpr/ppermute | solution.py:18
  171.6 5.0 %collective-permute-done.3 = bf16[64,768]{1,0:T(8,128)(2,1)S(1)} collective-permute-done((bf16[64,768]{1,0:T(8,128)(2,1)S(1)}, bf16[64,768]{1,0:T(8,128)(2,1)S(1)}, u32[]{:S(2)}, u32[]{:S(2)}) %collective-permute-start.3) | collective-permute-done | bytes 98336 | tf_op jit(solution)/shard_map/while/body/eval_jaxpr/ppermute | solution.py:147
  179.8 20.8 %all_to_all.34 = bf16[16,1,24,1536]{3,2,1,0:T(8,128)(2,1)S(1)} all-to-all(bf16[16,1,24,1536]{3,2,1,0:T(8,128)(2,1)S(1)} %bitcast.200), channel_id=1, replica_groups=mesh['section'=2,'expert'=16,'tensor'=4] {'expert'}, dimensions={0} | all-to-all | bytes 2359296 | tf_op jit(solution)/shard_map/all_to_all | solution.py:95
  200.6 2.8 %collective-permute-done.9 = bf16[16,1,24,1536]{3,2,0,1:T(8,128)(2,1)S(1)} collective-permute-done((bf16[16,1,24,1536]{3,2,0,1:T(8,128)(2,1)S(1)}, bf16[16,1,24,1536]{3,2,0,1:T(8,128)(2,1)S(1)}, u32[]{:S(2)}, u32[]{:S(2)}) %collective-permute-start.9) | collective-permute-done | bytes 1179680 | tf_op jit(solution)/shard_map/ppermute | solution.py:18
  206.3 2.9 %fusion.28 = f32[16,24,1024]{2,1,0:T(8,128)S(1)} fusion(bf16[1,1,3072,1024]{3,2,1,0:T(8,128)(2,1)S(1)} %bitcast.215, bf16[16,24,768]{2,1,0:T(8,128)(2,1)S(1)} %get-tuple-element.399, bf16[16,24,768]{2,1,0:T(8,128)(2,1)S(1)} %get-tuple-element.386, bf16[16,24,768]{2,1,0:T(8,128)(2,1)S(1)} %get-tuple-element.400, ...), kind=kOutput, calls=%fused_computation.68 | convolution fusion | flops 2428895232 | bytes 10237440 | tf_op jit(solution)/shard_map/sekd,edf->sekf/dot_general | solution.py:105
  212.9 2.7 %collective-permute-done.10 = bf16[16,1,24,1536]{3,2,0,1:T(8,128)(2,1)S(1)} collective-permute-done((bf16[16,1,24,1536]{3,2,0,1:T(8,128)(2,1)S(1)}, bf16[16,1,24,1536]{3,2,0,1:T(8,128)(2,1)S(1)}, u32[]{:S(2)}, u32[]{:S(2)}) %collective-permute-start.10) | collective-permute-done | bytes 1179680 | tf_op jit(solution)/shard_map/ppermute | solution.py:18
  217.0 3.8 %all-to-all-start.3 = ((bf16[16,1,24,1536]{3,2,1,0:T(8,128)(2,1)}), bf16[16,1,24,1536]{3,2,1,0:T(8,128)(2,1)S(1)}, u32[]{:S(2)}, u32[]{:S(2)}) async-start(bf16[16,1,24,1536]{3,2,1,0:T(8,128)(2,1)} %fusion.46), calls=%async_computation.3 | async-start | bytes 2359296 | tf_op jit(solution)/shard_map/all_to_all | solution.py:125
  221.0 20.2 %all-to-all-done.3 = bf16[16,1,24,1536]{3,2,1,0:T(8,128)(2,1)S(1)} async-done(((bf16[16,1,24,1536]{3,2,1,0:T(8,128)(2,1)}), bf16[16,1,24,1536]{3,2,1,0:T(8,128)(2,1)S(1)}, u32[]{:S(2)}, u32[]{:S(2)}) %all-to-all-start.3) | async-done | bytes 1179680 | tf_op jit(solution)/shard_map/all_to_all | solution.py:125
  244.8 5.0 %collective-permute-done.11 = f32[64,768]{1,0:T(8,128)S(1)} collective-permute-done((f32[64,768]{1,0:T(8,128)S(1)}, f32[64,768]{1,0:T(8,128)S(1)}, u32[]{:S(2)}, u32[]{:S(2)}) %collective-permute-start.11) | collective-permute-done | bytes 196640 | tf_op jit(solution)/shard_map/ppermute | solution.py:18
  (172 shorter events, 59.8 us)
Async XLA Ops:
  0.7 8.1 %collective-permute-start.6 = (f32[768]{0:T(1024)S(1)}, f32[768]{0:T(1024)S(1)}, u32[]{:S(2)}, u32[]{:S(2)}) collective-permute-start(f32[768]{0:T(1024)S(1)} %reduce.6), channel_id=1, source_target_pairs={{0,1},{1,0},{2,3},{3,2},{4,5},{5,4},{6,7},{7,6},{8,9},{9,8},{10,11... | collective-permute-start | bytes 9224 | tf_op jit(solution)/shard_map/ppermute | solution.py:18
  0.8 8.0 %collective-permute-start.7 = (f32[768]{0:T(1024)S(1)}, f32[768]{0:T(1024)S(1)}, u32[]{:S(2)}, u32[]{:S(2)}) collective-permute-start(f32[768]{0:T(1024)S(1)} %reduce.6), channel_id=1, source_target_pairs={{0,2},{1,3},{2,0},{3,1},{4,6},{5,7},{6,4},{7,5},{8,10},{9,11},{10,... | collective-permute-start | bytes 9224 | tf_op jit(solution)/shard_map/ppermute | solution.py:18
  1.7 7.2 %collective-permute-start.8 = (f32[768]{0:T(1024)S(1)}, f32[768]{0:T(1024)S(1)}, u32[]{:S(2)}, u32[]{:S(2)}) collective-permute-start(f32[768]{0:T(1024)S(1)} %reduce.6), channel_id=1, source_target_pairs={{0,3},{1,2},{2,1},{3,0},{4,7},{5,6},{6,5},{7,4},{8,11},{9,10},{10,... | collective-permute-start | bytes 9224 | tf_op jit(solution)/shard_map/ppermute | solution.py:18
  2.6 7.4 %collective-permute-start.5 = (bf16[2,64,768]{2,1,0:T(8,128)(2,1)}, bf16[2,64,768]{2,1,0:T(8,128)(2,1)S(1)}, u32[]{:S(2)}, u32[]{:S(2)}) collective-permute-start(bf16[2,64,768]{2,1,0:T(8,128)(2,1)} %param.12), channel_id=1, source_target_pairs={{0,2},{1,3},{2,0},{3,1},{4,6},{5,7},{6,4},{7,5},{8,10},{9,11},{10,... | collective-permute-start | bytes 589832 | tf_op jit(solution)/shard_map/ppermute | solution.py:18
  38.7 2.8 %collective-permute-start = (bf16[16,1,24,1536]{3,2,0,1:T(8,128)(2,1)S(1)}, bf16[16,1,24,1536]{3,2,0,1:T(8,128)(2,1)S(1)}, u32[]{:S(2)}, u32[]{:S(2)}) collective-permute-start(bf16[16,1,24,1536]{3,2,0,1:T(8,128)(2,1)S(1)} %bitcast.193), channel_id=1, source_target_pairs={{0,1},{1,0},{2,3},{3,2},{4,5},{5,4},{6,7},{7,6},{8,9},{9,8},{10,11... | collective-permute-start | bytes 3538952 | tf_op jit(solution)/shard_map/while/body/eval_jaxpr/ppermute | solution.py:18
  42.1 5.3 %slice-start.4 = ((s8[6291456]{0:T(1024)(128)(4,1)}), s8[4194304]{0:T(1024)(128)(4,1)S(1)}, s32[]{:S(2)}) async-start(s8[6291456]{0:T(1024)(128)(4,1)} %bitcast.217), calls=%async_computation.8 | async-start | bytes 8388608 | tf_op jit(solution)/shard_map/while
  50.9 2.9 %collective-permute-start.1 = (bf16[16,1,24,1536]{3,2,0,1:T(8,128)(2,1)S(1)}, bf16[16,1,24,1536]{3,2,0,1:T(8,128)(2,1)S(1)}, u32[]{:S(2)}, u32[]{:S(2)}) collective-permute-start(bf16[16,1,24,1536]{3,2,0,1:T(8,128)(2,1)S(1)} %select_convert_fusion.3), channel_id=1, source_target_pairs={{0,1},{1,0},{2,3},{3,2},{4,5},{5,4},{6,7},{7,6},{8,9},{9,8},{10,11... | collective-permute-start | bytes 3538952 | tf_op jit(solution)/shard_map/while/body/eval_jaxpr/ppermute | solution.py:18
  55.2 3.8 %copy-start = (f32[1,2,64,2]{2,3,1,0:T(2,128)S(1)}, f32[1,2,64,2]{2,3,1,0:T(2,128)}, u32[]{:S(2)}) copy-start(f32[1,2,64,2]{2,3,1,0:T(2,128)} %get-tuple-element.566) | copy-start | bytes 3076 | tf_op jit(solution)/shard_map/while
  55.2 24.2 %all-to-all-start.1 = ((bf16[16,1,24,1536]{3,2,1,0:T(8,128)(2,1)}), bf16[16,1,24,1536]{3,2,1,0:T(8,128)(2,1)S(1)}, u32[]{:S(2)}, u32[]{:S(2)}) async-start(bf16[16,1,24,1536]{3,2,1,0:T(8,128)(2,1)} %fusion.83), calls=%async_computation.1 | async-start | bytes 2359296 | tf_op jit(solution)/shard_map/while/body/eval_jaxpr/all_to_all | solution.py:125
  82.2 5.8 %collective-permute-start.2 = (f32[64,768]{1,0:T(8,128)S(1)}, f32[64,768]{1,0:T(8,128)S(1)}, u32[]{:S(2)}, u32[]{:S(2)}) collective-permute-start(f32[64,768]{1,0:T(8,128)S(1)} %slice_select_fusion.5), channel_id=1, source_target_pairs={{0,2},{1,3},{2,0},{3,1},{4,6},{5,7},{6,4},{7,5},{8,10},{9,11},{10,... | collective-permute-start | bytes 589832 | tf_op jit(solution)/shard_map/while/body/eval_jaxpr/ppermute | solution.py:18
  88.1 7.7 %collective-permute-start.3 = (bf16[64,768]{1,0:T(8,128)(2,1)S(1)}, bf16[64,768]{1,0:T(8,128)(2,1)S(1)}, u32[]{:S(2)}, u32[]{:S(2)}) collective-permute-start(bf16[64,768]{1,0:T(8,128)(2,1)S(1)} %add_convert_fusion.5), channel_id=1, source_target_pairs={{0,66},{1,67},{2,64},{3,65},{4,70},{5,71},{6,68},{7,69},{8,74},{9,... | collective-permute-start | bytes 294920 | tf_op jit(solution)/shard_map/while/body/eval_jaxpr/ppermute | solution.py:147
  89.4 8.0 %collective-permute-start.4 = (bf16[64,768]{1,0:T(8,128)(2,1)S(1)}, bf16[64,768]{1,0:T(8,128)(2,1)S(1)}, u32[]{:S(2)}, u32[]{:S(2)}) collective-permute-start(bf16[64,768]{1,0:T(8,128)(2,1)S(1)} %add_convert_fusion.5), channel_id=1, source_target_pairs={{0,64},{1,65},{2,66},{3,67},{4,68},{5,69},{6,70},{7,71},{8,72},{9,... | collective-permute-start | bytes 294920 | tf_op jit(solution)/shard_map/while/body/eval_jaxpr/ppermute | solution.py:13
  119.6 2.8 %collective-permute-start = (bf16[16,1,24,1536]{3,2,0,1:T(8,128)(2,1)S(1)}, bf16[16,1,24,1536]{3,2,0,1:T(8,128)(2,1)S(1)}, u32[]{:S(2)}, u32[]{:S(2)}) collective-permute-start(bf16[16,1,24,1536]{3,2,0,1:T(8,128)(2,1)S(1)} %bitcast.193), channel_id=1, source_target_pairs={{0,1},{1,0},{2,3},{3,2},{4,5},{5,4},{6,7},{7,6},{8,9},{9,8},{10,11... | collective-permute-start | bytes 3538952 | tf_op jit(solution)/shard_map/while/body/eval_jaxpr/ppermute | solution.py:18
  123.0 5.3 %slice-start.4 = ((s8[6291456]{0:T(1024)(128)(4,1)}), s8[4194304]{0:T(1024)(128)(4,1)S(1)}, s32[]{:S(2)}) async-start(s8[6291456]{0:T(1024)(128)(4,1)} %bitcast.217), calls=%async_computation.8 | async-start | bytes 8388608 | tf_op jit(solution)/shard_map/while
  131.8 2.9 %collective-permute-start.1 = (bf16[16,1,24,1536]{3,2,0,1:T(8,128)(2,1)S(1)}, bf16[16,1,24,1536]{3,2,0,1:T(8,128)(2,1)S(1)}, u32[]{:S(2)}, u32[]{:S(2)}) collective-permute-start(bf16[16,1,24,1536]{3,2,0,1:T(8,128)(2,1)S(1)} %select_convert_fusion.3), channel_id=1, source_target_pairs={{0,1},{1,0},{2,3},{3,2},{4,5},{5,4},{6,7},{7,6},{8,9},{9,8},{10,11... | collective-permute-start | bytes 3538952 | tf_op jit(solution)/shard_map/while/body/eval_jaxpr/ppermute | solution.py:18
  136.1 24.2 %all-to-all-start.1 = ((bf16[16,1,24,1536]{3,2,1,0:T(8,128)(2,1)}), bf16[16,1,24,1536]{3,2,1,0:T(8,128)(2,1)S(1)}, u32[]{:S(2)}, u32[]{:S(2)}) async-start(bf16[16,1,24,1536]{3,2,1,0:T(8,128)(2,1)} %fusion.83), calls=%async_computation.1 | async-start | bytes 2359296 | tf_op jit(solution)/shard_map/while/body/eval_jaxpr/all_to_all | solution.py:125
  163.1 5.8 %collective-permute-start.2 = (f32[64,768]{1,0:T(8,128)S(1)}, f32[64,768]{1,0:T(8,128)S(1)}, u32[]{:S(2)}, u32[]{:S(2)}) collective-permute-start(f32[64,768]{1,0:T(8,128)S(1)} %slice_select_fusion.5), channel_id=1, source_target_pairs={{0,2},{1,3},{2,0},{3,1},{4,6},{5,7},{6,4},{7,5},{8,10},{9,11},{10,... | collective-permute-start | bytes 589832 | tf_op jit(solution)/shard_map/while/body/eval_jaxpr/ppermute | solution.py:18
  168.9 7.7 %collective-permute-start.3 = (bf16[64,768]{1,0:T(8,128)(2,1)S(1)}, bf16[64,768]{1,0:T(8,128)(2,1)S(1)}, u32[]{:S(2)}, u32[]{:S(2)}) collective-permute-start(bf16[64,768]{1,0:T(8,128)(2,1)S(1)} %add_convert_fusion.5), channel_id=1, source_target_pairs={{0,66},{1,67},{2,64},{3,65},{4,70},{5,71},{6,68},{7,69},{8,74},{9,... | collective-permute-start | bytes 294920 | tf_op jit(solution)/shard_map/while/body/eval_jaxpr/ppermute | solution.py:147
  170.2 8.0 %collective-permute-start.4 = (bf16[64,768]{1,0:T(8,128)(2,1)S(1)}, bf16[64,768]{1,0:T(8,128)(2,1)S(1)}, u32[]{:S(2)}, u32[]{:S(2)}) collective-permute-start(bf16[64,768]{1,0:T(8,128)(2,1)S(1)} %add_convert_fusion.5), channel_id=1, source_target_pairs={{0,64},{1,65},{2,66},{3,67},{4,68},{5,69},{6,70},{7,71},{8,72},{9,... | collective-permute-start | bytes 294920 | tf_op jit(solution)/shard_map/while/body/eval_jaxpr/ppermute | solution.py:13
  200.6 2.8 %collective-permute-start.9 = (bf16[16,1,24,1536]{3,2,0,1:T(8,128)(2,1)S(1)}, bf16[16,1,24,1536]{3,2,0,1:T(8,128)(2,1)S(1)}, u32[]{:S(2)}, u32[]{:S(2)}) collective-permute-start(bf16[16,1,24,1536]{3,2,0,1:T(8,128)(2,1)S(1)} %bitcast.198), channel_id=1, source_target_pairs={{0,1},{1,0},{2,3},{3,2},{4,5},{5,4},{6,7},{7,6},{8,9},{9,8},{10,11... | collective-permute-start | bytes 3538952 | tf_op jit(solution)/shard_map/ppermute | solution.py:18
  203.9 5.3 %slice-start.6 = ((s8[6291456]{0:T(1024)(128)(4,1)}), s8[4194304]{0:T(1024)(128)(4,1)S(1)}, s32[]{:S(2)}) async-start(s8[6291456]{0:T(1024)(128)(4,1)} %bitcast.219), calls=%async_computation.10 | async-start | bytes 8388608
  212.7 2.9 %collective-permute-start.10 = (bf16[16,1,24,1536]{3,2,0,1:T(8,128)(2,1)S(1)}, bf16[16,1,24,1536]{3,2,0,1:T(8,128)(2,1)S(1)}, u32[]{:S(2)}, u32[]{:S(2)}) collective-permute-start(bf16[16,1,24,1536]{3,2,0,1:T(8,128)(2,1)S(1)} %select_convert_fusion.1), channel_id=1, source_target_pairs={{0,1},{1,0},{2,3},{3,2},{4,5},{5,4},{6,7},{7,6},{8,9},{9,8},{10,11... | collective-permute-start | bytes 3538952 | tf_op jit(solution)/shard_map/ppermute | solution.py:18
  217.0 24.2 %all-to-all-start.3 = ((bf16[16,1,24,1536]{3,2,1,0:T(8,128)(2,1)}), bf16[16,1,24,1536]{3,2,1,0:T(8,128)(2,1)S(1)}, u32[]{:S(2)}, u32[]{:S(2)}) async-start(bf16[16,1,24,1536]{3,2,1,0:T(8,128)(2,1)} %fusion.46), calls=%async_computation.3 | async-start | bytes 2359296 | tf_op jit(solution)/shard_map/all_to_all | solution.py:125
  244.0 5.8 %collective-permute-start.11 = (f32[64,768]{1,0:T(8,128)S(1)}, f32[64,768]{1,0:T(8,128)S(1)}, u32[]{:S(2)}, u32[]{:S(2)}) collective-permute-start(f32[64,768]{1,0:T(8,128)S(1)} %slice_select_fusion.2), channel_id=1, source_target_pairs={{0,2},{1,3},{2,0},{3,1},{4,6},{5,7},{6,4},{7,5},{8,10},{9,11},{10,... | collective-permute-start | bytes 589832 | tf_op jit(solution)/shard_map/ppermute | solution.py:18
  (13 other events, 33.6 us)

commit v6 on v5

--- a/solution.py
+++ b/solution.py
@@ -108,7 +108,7 @@
         hidden = jax.nn.silu(summed_up).astype(jnp.bfloat16)
         partial_out = jnp.einsum(
             "sekf,efd->sekd", hidden, down_local, preferred_element_type=jnp.float32
-        )
+        ).astype(jnp.bfloat16)
         pq = [partial_out[..., q * quarter:(q + 1) * quarter] for q in range(4)]
         keep = jnp.where(
             core_first,
@@ -120,8 +120,8 @@
             jnp.concatenate([pq[1], pq[3]], axis=-1),
             jnp.concatenate([pq[0], pq[2]], axis=-1),
         )
-        got = swap(give.astype(jnp.bfloat16), "tensor", 1)
-        chip_sum = (keep + got.astype(jnp.float32)).astype(jnp.bfloat16)
+        got = swap(give, "tensor", 1)
+        chip_sum = (keep.astype(jnp.float32) + got.astype(jnp.float32)).astype(jnp.bfloat16)
         returned = lax.all_to_all(chip_sum, "expert", split_axis=0, concat_axis=0, tiled=True)
         summed = jnp.sum(
             returned.reshape(EXPERTS, copies, capacity, 2 * quarter).astype(jnp.float32), axis=1
@@ -131,7 +131,7 @@
         y_half = jnp.sum(picked * weights[:, :, None], axis=1)
         y_keep = jnp.where(x_first, y_half[:, :quarter], y_half[:, quarter:])
         y_give = jnp.where(x_first, y_half[:, quarter:], y_half[:, :quarter])
-        y_got = swap(y_give, "tensor", 2)
+        y_got = swap(y_give.astype(jnp.bfloat16), "tensor", 2).astype(jnp.float32)
         xf = jnp.where(x_first, half_rows[:, :quarter], half_rows[:, quarter:]).astype(jnp.float32)
         mixed = xf + (y_keep + y_got)
         produced = mixed.astype(jnp.bfloat16)

time: 251 us -> 246 us (0.980)
  no operation moved by 1% of the time
where the time goes in v6:
time: 246 us
  waiting for transfers between devices  105 us (43%)
  blocking collectives  65.6 us (27%)
  starting transfers between devices  22.7 us (9%)
  matrix products  17.9 us (7%)
  local copies, waits for them, and re-layouts  17.6 us (7%)
  other arithmetic  16.2 us (7%)
    all_to_all x3, blocking collectives, layer_step(): lax.all_to_all(outgoing, 'expert', split_axis=0, concat_axis=0, tiled=True)  65.6 us
    all_to_all x3, waiting for transfers between devices, layer_step(): lax.all_to_all(chip_sum, 'expert', split_axis=0, concat_axis=0, tiled=True)  60.6 us
    ppermute x13, waiting for transfers between devices, swap(): return lax.ppermute(block, axis, [(i, i ^ bit) for i in range(n)])  30.9 us
    all_to_all x3, starting transfers between devices, layer_step(): lax.all_to_all(chip_sum, 'expert', split_axis=0, concat_axis=0, tiled=True)  11.5 us
    ppermute x2, waiting for transfers between devices, looped(): lax.ppermute(produced, ('section', 'tensor'), cross_route)  10 us
    dot_general x3, matrix products, layer_step(): jnp.einsum('sekf,efd->sekd', hidden, down_local, preferred_element_type=j...  9.28 us
    dot_general x3, matrix products, layer_step(): jnp.einsum('sekd,edf->sekf', normed, up_local, preferred_element_type=jnp...  8.61 us
    ppermute x13, starting transfers between devices, swap(): return lax.ppermute(block, axis, [(i, i ^ bit) for i in range(n)])  5.99 us
  transfers between devices with their start and end apart: 20, of which 17 were waited for; matrix products, arithmetic and copies ran while one was open for 2% of the time, Pallas kernels for 0%

profile of v6, /device:TPU:6, one launch (start us, length us, event | category | flops | bytes accessed | tf_op | source)
XLA Modules:
  0.0 245.5 jit_solution(10997880646614422871)
XLA Ops:
  11.2 164.2 %while.17 = (s32[]{:T(128)}, bf16[64,1536]{1,0:T(8,128)(2,1)S(1)}, bf16[2,64,768]{2,1,0:T(8,128)(2,1)S(1)}, pred[]{:T(512)}, pred[]{:T(512)}, /*index=5*/bf16[2,...) while((s32[]{:T(128)}, bf16[64,1536]{1,0:T(8,128)(2,1)S(1)}, ...), condition=%wide.region_8.11_spmd.clone, body=%wide.region_4.10_spmd.clone.sunk | while | flops 4877554688 | bytes 116828288 | solution.py:152
  12.6 26.1 %all_to_all.35 = bf16[16,1,24,1536]{3,2,1,0:T(8,128)(2,1)S(1)} all-to-all(bf16[16,1,24,1536]{3,2,1,0:T(8,128)(2,1)S(1)} %bitcast.199), channel_id=1, replica_groups=mesh['section'=2,'expert'=16,'tensor'=4] {'expert'}, dimensions={0} | all-to-all | bytes 2359296 | tf_op jit(solution)/shard_map/while/body/eval_jaxpr/all_to_all | solution.py:95
  38.7 2.8 %collective-permute-done = bf16[16,1,24,1536]{3,2,0,1:T(8,128)(2,1)S(1)} collective-permute-done((bf16[16,1,24,1536]{3,2,0,1:T(8,128)(2,1)S(1)}, bf16[16,1,24,1536]{3,2,0,1:T(8,128)(2,1)S(1)}, u32[]{:S(2)}, u32[]{:S(2)}) %collective-permute-start) | collective-permute-done | bytes 1179680 | tf_op jit(solution)/shard_map/while/body/eval_jaxpr/ppermute | solution.py:18
  44.5 2.9 %fusion.86 = f32[16,24,1024]{2,1,0:T(8,128)S(1)} fusion(bf16[1,3072,1024]{2,1,0:T(8,128)(2,1)S(1)} %bitcast.216, bf16[16,24,768]{2,1,0:T(8,128)(2,1)S(1)} %get-tuple-element.505, bf16[16,24,768]{2,1,0:T(8,128)(2,1)S(1)} %get-tuple-element.506, bf16[16,24,768]{2,1,0:T(8,128)(2,1)S(1)} %get-tuple-element.507, ...), kind=kOutput, calls=%fused_computation.8.clone.1 | convolution fusion | flops 2428895232 | bytes 10237440 | tf_op jit(solution)/shard_map/while/body/eval_jaxpr/sekd,edf->sekf/dot_general | solution.py:105
  47.4 3.1 %fusion.87 = bf16[16,1,24,3072]{3,2,0,1:T(8,128)(2,1)S(1)} fusion(bf16[1,1024,3072]{2,1,0:T(8,128)(2,1)S(1)} %bitcast.222, f32[16,24,1024]{2,1,0:T(8,128)S(1)} %fusion.86), kind=kOutput, calls=%fused_computation.13.clone.1 | convolution fusion | flops 2419064832 | bytes 10223616 | tf_op jit(solution)/shard_map/while/body/eval_jaxpr/sekf,efd->sekd/dot_general | solution.py:109
  55.3 3.8 %all-to-all-start.1 = ((bf16[16,1,24,1536]{3,2,1,0:T(8,128)(2,1)}), bf16[16,1,24,1536]{3,2,1,0:T(8,128)(2,1)S(1)}, u32[]{:S(2)}, u32[]{:S(2)}) async-start(bf16[16,1,24,1536]{3,2,1,0:T(8,128)(2,1)} %fusion.89), calls=%async_computation.1 | async-start | bytes 2359296 | tf_op jit(solution)/shard_map/while/body/eval_jaxpr/all_to_all | solution.py:125
  59.3 20.2 %all-to-all-done.1 = bf16[16,1,24,1536]{3,2,1,0:T(8,128)(2,1)S(1)} async-done(((bf16[16,1,24,1536]{3,2,1,0:T(8,128)(2,1)}), bf16[16,1,24,1536]{3,2,1,0:T(8,128)(2,1)S(1)}, u32[]{:S(2)}, u32[]{:S(2)}) %all-to-all-start.1) | async-done | bytes 1179680 | tf_op jit(solution)/shard_map/while/body/eval_jaxpr/all_to_all | solution.py:125
  83.2 3.8 %collective-permute-done.2 = bf16[64,768]{1,0:T(8,128)(2,1)S(1)} collective-permute-done((bf16[64,768]{1,0:T(8,128)(2,1)S(1)}, bf16[64,768]{1,0:T(8,128)(2,1)S(1)}, u32[]{:S(2)}, u32[]{:S(2)}) %collective-permute-start.2) | collective-permute-done | bytes 98336 | tf_op jit(solution)/shard_map/while/body/eval_jaxpr/ppermute | solution.py:18
  89.7 5.0 %collective-permute-done.3 = bf16[64,768]{1,0:T(8,128)(2,1)S(1)} collective-permute-done((bf16[64,768]{1,0:T(8,128)(2,1)S(1)}, bf16[64,768]{1,0:T(8,128)(2,1)S(1)}, u32[]{:S(2)}, u32[]{:S(2)}) %collective-permute-start.3) | collective-permute-done | bytes 98336 | tf_op jit(solution)/shard_map/while/body/eval_jaxpr/ppermute | solution.py:147
  97.9 19.7 %all_to_all.35 = bf16[16,1,24,1536]{3,2,1,0:T(8,128)(2,1)S(1)} all-to-all(bf16[16,1,24,1536]{3,2,1,0:T(8,128)(2,1)S(1)} %bitcast.199), channel_id=1, replica_groups=mesh['section'=2,'expert'=16,'tensor'=4] {'expert'}, dimensions={0} | all-to-all | bytes 2359296 | tf_op jit(solution)/shard_map/while/body/eval_jaxpr/all_to_all | solution.py:95
  117.6 2.8 %collective-permute-done = bf16[16,1,24,1536]{3,2,0,1:T(8,128)(2,1)S(1)} collective-permute-done((bf16[16,1,24,1536]{3,2,0,1:T(8,128)(2,1)S(1)}, bf16[16,1,24,1536]{3,2,0,1:T(8,128)(2,1)S(1)}, u32[]{:S(2)}, u32[]{:S(2)}) %collective-permute-start) | collective-permute-done | bytes 1179680 | tf_op jit(solution)/shard_map/while/body/eval_jaxpr/ppermute | solution.py:18
  123.4 2.9 %fusion.86 = f32[16,24,1024]{2,1,0:T(8,128)S(1)} fusion(bf16[1,3072,1024]{2,1,0:T(8,128)(2,1)S(1)} %bitcast.216, bf16[16,24,768]{2,1,0:T(8,128)(2,1)S(1)} %get-tuple-element.505, bf16[16,24,768]{2,1,0:T(8,128)(2,1)S(1)} %get-tuple-element.506, bf16[16,24,768]{2,1,0:T(8,128)(2,1)S(1)} %get-tuple-element.507, ...), kind=kOutput, calls=%fused_computation.8.clone.1 | convolution fusion | flops 2428895232 | bytes 10237440 | tf_op jit(solution)/shard_map/while/body/eval_jaxpr/sekd,edf->sekf/dot_general | solution.py:105
  126.3 3.1 %fusion.87 = bf16[16,1,24,3072]{3,2,0,1:T(8,128)(2,1)S(1)} fusion(bf16[1,1024,3072]{2,1,0:T(8,128)(2,1)S(1)} %bitcast.222, f32[16,24,1024]{2,1,0:T(8,128)S(1)} %fusion.86), kind=kOutput, calls=%fused_computation.13.clone.1 | convolution fusion | flops 2419064832 | bytes 10223616 | tf_op jit(solution)/shard_map/while/body/eval_jaxpr/sekf,efd->sekd/dot_general | solution.py:109
  134.2 3.8 %all-to-all-start.1 = ((bf16[16,1,24,1536]{3,2,1,0:T(8,128)(2,1)}), bf16[16,1,24,1536]{3,2,1,0:T(8,128)(2,1)S(1)}, u32[]{:S(2)}, u32[]{:S(2)}) async-start(bf16[16,1,24,1536]{3,2,1,0:T(8,128)(2,1)} %fusion.89), calls=%async_computation.1 | async-start | bytes 2359296 | tf_op jit(solution)/shard_map/while/body/eval_jaxpr/all_to_all | solution.py:125
  138.2 20.2 %all-to-all-done.1 = bf16[16,1,24,1536]{3,2,1,0:T(8,128)(2,1)S(1)} async-done(((bf16[16,1,24,1536]{3,2,1,0:T(8,128)(2,1)}), bf16[16,1,24,1536]{3,2,1,0:T(8,128)(2,1)S(1)}, u32[]{:S(2)}, u32[]{:S(2)}) %all-to-all-start.1) | async-done | bytes 1179680 | tf_op jit(solution)/shard_map/while/body/eval_jaxpr/all_to_all | solution.py:125
  162.1 3.8 %collective-permute-done.2 = bf16[64,768]{1,0:T(8,128)(2,1)S(1)} collective-permute-done((bf16[64,768]{1,0:T(8,128)(2,1)S(1)}, bf16[64,768]{1,0:T(8,128)(2,1)S(1)}, u32[]{:S(2)}, u32[]{:S(2)}) %collective-permute-start.2) | collective-permute-done | bytes 98336 | tf_op jit(solution)/shard_map/while/body/eval_jaxpr/ppermute | solution.py:18
  168.6 5.0 %collective-permute-done.3 = bf16[64,768]{1,0:T(8,128)(2,1)S(1)} collective-permute-done((bf16[64,768]{1,0:T(8,128)(2,1)S(1)}, bf16[64,768]{1,0:T(8,128)(2,1)S(1)}, u32[]{:S(2)}, u32[]{:S(2)}) %collective-permute-start.3) | collective-permute-done | bytes 98336 | tf_op jit(solution)/shard_map/while/body/eval_jaxpr/ppermute | solution.py:147
  176.7 19.7 %all_to_all.34 = bf16[16,1,24,1536]{3,2,1,0:T(8,128)(2,1)S(1)} all-to-all(bf16[16,1,24,1536]{3,2,1,0:T(8,128)(2,1)S(1)} %bitcast.204), channel_id=1, replica_groups=mesh['section'=2,'expert'=16,'tensor'=4] {'expert'}, dimensions={0} | all-to-all | bytes 2359296 | tf_op jit(solution)/shard_map/all_to_all | solution.py:95
  196.4 2.8 %collective-permute-done.9 = bf16[16,1,24,1536]{3,2,0,1:T(8,128)(2,1)S(1)} collective-permute-done((bf16[16,1,24,1536]{3,2,0,1:T(8,128)(2,1)S(1)}, bf16[16,1,24,1536]{3,2,0,1:T(8,128)(2,1)S(1)}, u32[]{:S(2)}, u32[]{:S(2)}) %collective-permute-start.9) | collective-permute-done | bytes 1179680 | tf_op jit(solution)/shard_map/ppermute | solution.py:18
  202.2 2.9 %fusion.31 = f32[16,24,1024]{2,1,0:T(8,128)S(1)} fusion(bf16[1,1,3072,1024]{3,2,1,0:T(8,128)(2,1)S(1)} %bitcast.219, bf16[16,24,768]{2,1,0:T(8,128)(2,1)S(1)} %get-tuple-element.399, bf16[16,24,768]{2,1,0:T(8,128)(2,1)S(1)} %get-tuple-element.386, bf16[16,24,768]{2,1,0:T(8,128)(2,1)S(1)} %get-tuple-element.400, ...), kind=kOutput, calls=%fused_computation.69 | convolution fusion | flops 2428895232 | bytes 10237440 | tf_op jit(solution)/shard_map/sekd,edf->sekf/dot_general | solution.py:105
  205.1 3.1 %fusion.36 = bf16[16,1,24,3072]{3,2,0,1:T(8,128)(2,1)S(1)} fusion(bf16[1,1,1024,3072]{3,2,1,0:T(8,128)(2,1)S(1)} %bitcast.225, f32[16,24,1024]{2,1,0:T(8,128)S(1)} %fusion.31), kind=kOutput, calls=%fused_computation.74 | convolution fusion | flops 2419064832 | bytes 10223616 | tf_op jit(solution)/shard_map/sekf,efd->sekd/dot_general | solution.py:109
  213.0 3.8 %all-to-all-start.3 = ((bf16[16,1,24,1536]{3,2,1,0:T(8,128)(2,1)}), bf16[16,1,24,1536]{3,2,1,0:T(8,128)(2,1)S(1)}, u32[]{:S(2)}, u32[]{:S(2)}) async-start(bf16[16,1,24,1536]{3,2,1,0:T(8,128)(2,1)} %fusion.52), calls=%async_computation.3 | async-start | bytes 2359296 | tf_op jit(solution)/shard_map/all_to_all | solution.py:125
  217.0 20.2 %all-to-all-done.3 = bf16[16,1,24,1536]{3,2,1,0:T(8,128)(2,1)S(1)} async-done(((bf16[16,1,24,1536]{3,2,1,0:T(8,128)(2,1)}), bf16[16,1,24,1536]{3,2,1,0:T(8,128)(2,1)S(1)}, u32[]{:S(2)}, u32[]{:S(2)}) %all-to-all-start.3) | async-done | bytes 1179680 | tf_op jit(solution)/shard_map/all_to_all | solution.py:125
  240.8 3.9 %collective-permute-done.11 = bf16[64,768]{1,0:T(8,128)(2,1)S(1)} collective-permute-done((bf16[64,768]{1,0:T(8,128)(2,1)S(1)}, bf16[64,768]{1,0:T(8,128)(2,1)S(1)}, u32[]{:S(2)}, u32[]{:S(2)}) %collective-permute-start.11) | collective-permute-done | bytes 98336 | tf_op jit(solution)/shard_map/ppermute | solution.py:18
  (168 shorter events, 59.0 us)
Async XLA Ops:
  0.7 6.6 %collective-permute-start.6 = (f32[768]{0:T(1024)S(1)}, f32[768]{0:T(1024)S(1)}, u32[]{:S(2)}, u32[]{:S(2)}) collective-permute-start(f32[768]{0:T(1024)S(1)} %reduce.6), channel_id=1, source_target_pairs={{0,1},{1,0},{2,3},{3,2},{4,5},{5,4},{6,7},{7,6},{8,9},{9,8},{10,11... | collective-permute-start | bytes 9224 | tf_op jit(solution)/shard_map/ppermute | solution.py:18
  0.8 6.5 %collective-permute-start.7 = (f32[768]{0:T(1024)S(1)}, f32[768]{0:T(1024)S(1)}, u32[]{:S(2)}, u32[]{:S(2)}) collective-permute-start(f32[768]{0:T(1024)S(1)} %reduce.6), channel_id=1, source_target_pairs={{0,2},{1,3},{2,0},{3,1},{4,6},{5,7},{6,4},{7,5},{8,10},{9,11},{10,... | collective-permute-start | bytes 9224 | tf_op jit(solution)/shard_map/ppermute | solution.py:18
  1.7 5.6 %collective-permute-start.8 = (f32[768]{0:T(1024)S(1)}, f32[768]{0:T(1024)S(1)}, u32[]{:S(2)}, u32[]{:S(2)}) collective-permute-start(f32[768]{0:T(1024)S(1)} %reduce.6), channel_id=1, source_target_pairs={{0,3},{1,2},{2,1},{3,0},{4,7},{5,6},{6,5},{7,4},{8,11},{9,10},{10,... | collective-permute-start | bytes 9224 | tf_op jit(solution)/shard_map/ppermute | solution.py:18
  2.6 7.4 %collective-permute-start.5 = (bf16[2,64,768]{2,1,0:T(8,128)(2,1)}, bf16[2,64,768]{2,1,0:T(8,128)(2,1)S(1)}, u32[]{:S(2)}, u32[]{:S(2)}) collective-permute-start(bf16[2,64,768]{2,1,0:T(8,128)(2,1)} %param.12), channel_id=1, source_target_pairs={{0,2},{1,3},{2,0},{3,1},{4,6},{5,7},{6,4},{7,5},{8,10},{9,11},{10,... | collective-permute-start | bytes 589832 | tf_op jit(solution)/shard_map/ppermute | solution.py:18
  38.7 2.8 %collective-permute-start = (bf16[16,1,24,1536]{3,2,0,1:T(8,128)(2,1)S(1)}, bf16[16,1,24,1536]{3,2,0,1:T(8,128)(2,1)S(1)}, u32[]{:S(2)}, u32[]{:S(2)}) collective-permute-start(bf16[16,1,24,1536]{3,2,0,1:T(8,128)(2,1)S(1)} %bitcast.197), channel_id=1, source_target_pairs={{0,1},{1,0},{2,3},{3,2},{4,5},{5,4},{6,7},{7,6},{8,9},{9,8},{10,11... | collective-permute-start | bytes 3538952 | tf_op jit(solution)/shard_map/while/body/eval_jaxpr/ppermute | solution.py:18
  42.1 5.3 %slice-start.4 = ((s8[6291456]{0:T(1024)(128)(4,1)}), s8[4194304]{0:T(1024)(128)(4,1)S(1)}, s32[]{:S(2)}) async-start(s8[6291456]{0:T(1024)(128)(4,1)} %bitcast.221), calls=%async_computation.8 | async-start | bytes 8388608 | tf_op jit(solution)/shard_map/while
  50.9 2.9 %collective-permute-start.1 = (bf16[16,1,24,1536]{3,2,0,1:T(8,128)(2,1)S(1)}, bf16[16,1,24,1536]{3,2,0,1:T(8,128)(2,1)S(1)}, u32[]{:S(2)}, u32[]{:S(2)}) collective-permute-start(bf16[16,1,24,1536]{3,2,0,1:T(8,128)(2,1)S(1)} %broadcast_select_fusion.12), channel_id=1, source_target_pairs={{0,1},{1,0},{2,3},{3,2},{4,5},{5,4},{6,7},{7,6},{8,9},{9,8},{10,11... | collective-permute-start | bytes 3538952 | tf_op jit(solution)/shard_map/while/body/eval_jaxpr/ppermute | solution.py:18
  55.3 24.2 %all-to-all-start.1 = ((bf16[16,1,24,1536]{3,2,1,0:T(8,128)(2,1)}), bf16[16,1,24,1536]{3,2,1,0:T(8,128)(2,1)S(1)}, u32[]{:S(2)}, u32[]{:S(2)}) async-start(bf16[16,1,24,1536]{3,2,1,0:T(8,128)(2,1)} %fusion.89), calls=%async_computation.1 | async-start | bytes 2359296 | tf_op jit(solution)/shard_map/while/body/eval_jaxpr/all_to_all | solution.py:125
  82.3 4.7 %collective-permute-start.2 = (bf16[64,768]{1,0:T(8,128)(2,1)S(1)}, bf16[64,768]{1,0:T(8,128)(2,1)S(1)}, u32[]{:S(2)}, u32[]{:S(2)}) collective-permute-start(bf16[64,768]{1,0:T(8,128)(2,1)S(1)} %select_convert_fusion.3), channel_id=1, source_target_pairs={{0,2},{1,3},{2,0},{3,1},{4,6},{5,7},{6,4},{7,5},{8,10},{9,11},{10,... | collective-permute-start | bytes 294920 | tf_op jit(solution)/shard_map/while/body/eval_jaxpr/ppermute | solution.py:18
  87.0 7.7 %collective-permute-start.3 = (bf16[64,768]{1,0:T(8,128)(2,1)S(1)}, bf16[64,768]{1,0:T(8,128)(2,1)S(1)}, u32[]{:S(2)}, u32[]{:S(2)}) collective-permute-start(bf16[64,768]{1,0:T(8,128)(2,1)S(1)} %add_convert_fusion.5), channel_id=1, source_target_pairs={{0,66},{1,67},{2,64},{3,65},{4,70},{5,71},{6,68},{7,69},{8,74},{9,... | collective-permute-start | bytes 294920 | tf_op jit(solution)/shard_map/while/body/eval_jaxpr/ppermute | solution.py:147
  88.3 8.0 %collective-permute-start.4 = (bf16[64,768]{1,0:T(8,128)(2,1)S(1)}, bf16[64,768]{1,0:T(8,128)(2,1)S(1)}, u32[]{:S(2)}, u32[]{:S(2)}) collective-permute-start(bf16[64,768]{1,0:T(8,128)(2,1)S(1)} %add_convert_fusion.5), channel_id=1, source_target_pairs={{0,64},{1,65},{2,66},{3,67},{4,68},{5,69},{6,70},{7,71},{8,72},{9,... | collective-permute-start | bytes 294920 | tf_op jit(solution)/shard_map/while/body/eval_jaxpr/ppermute | solution.py:13
  117.6 2.8 %collective-permute-start = (bf16[16,1,24,1536]{3,2,0,1:T(8,128)(2,1)S(1)}, bf16[16,1,24,1536]{3,2,0,1:T(8,128)(2,1)S(1)}, u32[]{:S(2)}, u32[]{:S(2)}) collective-permute-start(bf16[16,1,24,1536]{3,2,0,1:T(8,128)(2,1)S(1)} %bitcast.197), channel_id=1, source_target_pairs={{0,1},{1,0},{2,3},{3,2},{4,5},{5,4},{6,7},{7,6},{8,9},{9,8},{10,11... | collective-permute-start | bytes 3538952 | tf_op jit(solution)/shard_map/while/body/eval_jaxpr/ppermute | solution.py:18
  121.0 5.3 %slice-start.4 = ((s8[6291456]{0:T(1024)(128)(4,1)}), s8[4194304]{0:T(1024)(128)(4,1)S(1)}, s32[]{:S(2)}) async-start(s8[6291456]{0:T(1024)(128)(4,1)} %bitcast.221), calls=%async_computation.8 | async-start | bytes 8388608 | tf_op jit(solution)/shard_map/while
  129.9 2.9 %collective-permute-start.1 = (bf16[16,1,24,1536]{3,2,0,1:T(8,128)(2,1)S(1)}, bf16[16,1,24,1536]{3,2,0,1:T(8,128)(2,1)S(1)}, u32[]{:S(2)}, u32[]{:S(2)}) collective-permute-start(bf16[16,1,24,1536]{3,2,0,1:T(8,128)(2,1)S(1)} %broadcast_select_fusion.12), channel_id=1, source_target_pairs={{0,1},{1,0},{2,3},{3,2},{4,5},{5,4},{6,7},{7,6},{8,9},{9,8},{10,11... | collective-permute-start | bytes 3538952 | tf_op jit(solution)/shard_map/while/body/eval_jaxpr/ppermute | solution.py:18
  134.2 24.2 %all-to-all-start.1 = ((bf16[16,1,24,1536]{3,2,1,0:T(8,128)(2,1)}), bf16[16,1,24,1536]{3,2,1,0:T(8,128)(2,1)S(1)}, u32[]{:S(2)}, u32[]{:S(2)}) async-start(bf16[16,1,24,1536]{3,2,1,0:T(8,128)(2,1)} %fusion.89), calls=%async_computation.1 | async-start | bytes 2359296 | tf_op jit(solution)/shard_map/while/body/eval_jaxpr/all_to_all | solution.py:125
  161.2 4.7 %collective-permute-start.2 = (bf16[64,768]{1,0:T(8,128)(2,1)S(1)}, bf16[64,768]{1,0:T(8,128)(2,1)S(1)}, u32[]{:S(2)}, u32[]{:S(2)}) collective-permute-start(bf16[64,768]{1,0:T(8,128)(2,1)S(1)} %select_convert_fusion.3), channel_id=1, source_target_pairs={{0,2},{1,3},{2,0},{3,1},{4,6},{5,7},{6,4},{7,5},{8,10},{9,11},{10,... | collective-permute-start | bytes 294920 | tf_op jit(solution)/shard_map/while/body/eval_jaxpr/ppermute | solution.py:18
  165.9 7.7 %collective-permute-start.3 = (bf16[64,768]{1,0:T(8,128)(2,1)S(1)}, bf16[64,768]{1,0:T(8,128)(2,1)S(1)}, u32[]{:S(2)}, u32[]{:S(2)}) collective-permute-start(bf16[64,768]{1,0:T(8,128)(2,1)S(1)} %add_convert_fusion.5), channel_id=1, source_target_pairs={{0,66},{1,67},{2,64},{3,65},{4,70},{5,71},{6,68},{7,69},{8,74},{9,... | collective-permute-start | bytes 294920 | tf_op jit(solution)/shard_map/while/body/eval_jaxpr/ppermute | solution.py:147
  167.2 8.0 %collective-permute-start.4 = (bf16[64,768]{1,0:T(8,128)(2,1)S(1)}, bf16[64,768]{1,0:T(8,128)(2,1)S(1)}, u32[]{:S(2)}, u32[]{:S(2)}) collective-permute-start(bf16[64,768]{1,0:T(8,128)(2,1)S(1)} %add_convert_fusion.5), channel_id=1, source_target_pairs={{0,64},{1,65},{2,66},{3,67},{4,68},{5,69},{6,70},{7,71},{8,72},{9,... | collective-permute-start | bytes 294920 | tf_op jit(solution)/shard_map/while/body/eval_jaxpr/ppermute | solution.py:13
  196.4 2.8 %collective-permute-start.9 = (bf16[16,1,24,1536]{3,2,0,1:T(8,128)(2,1)S(1)}, bf16[16,1,24,1536]{3,2,0,1:T(8,128)(2,1)S(1)}, u32[]{:S(2)}, u32[]{:S(2)}) collective-permute-start(bf16[16,1,24,1536]{3,2,0,1:T(8,128)(2,1)S(1)} %bitcast.202), channel_id=1, source_target_pairs={{0,1},{1,0},{2,3},{3,2},{4,5},{5,4},{6,7},{7,6},{8,9},{9,8},{10,11... | collective-permute-start | bytes 3538952 | tf_op jit(solution)/shard_map/ppermute | solution.py:18
  199.8 5.3 %slice-start.6 = ((s8[6291456]{0:T(1024)(128)(4,1)}), s8[4194304]{0:T(1024)(128)(4,1)S(1)}, s32[]{:S(2)}) async-start(s8[6291456]{0:T(1024)(128)(4,1)} %bitcast.223), calls=%async_computation.10 | async-start | bytes 8388608
  208.7 2.9 %collective-permute-start.10 = (bf16[16,1,24,1536]{3,2,0,1:T(8,128)(2,1)S(1)}, bf16[16,1,24,1536]{3,2,0,1:T(8,128)(2,1)S(1)}, u32[]{:S(2)}, u32[]{:S(2)}) collective-permute-start(bf16[16,1,24,1536]{3,2,0,1:T(8,128)(2,1)S(1)} %broadcast_select_fusion.4), channel_id=1, source_target_pairs={{0,1},{1,0},{2,3},{3,2},{4,5},{5,4},{6,7},{7,6},{8,9},{9,8},{10,11... | collective-permute-start | bytes 3538952 | tf_op jit(solution)/shard_map/ppermute | solution.py:18
  213.0 3.8 %copy-start.1 = (f32[1,2,64,2]{2,3,1,0:T(2,128)S(1)}, f32[1,2,64,2]{2,3,1,0:T(2,128)}, u32[]{:S(2)}) copy-start(f32[1,2,64,2]{2,3,1,0:T(2,128)} %get-tuple-element.592) | copy-start | bytes 3076
  213.0 24.2 %all-to-all-start.3 = ((bf16[16,1,24,1536]{3,2,1,0:T(8,128)(2,1)}), bf16[16,1,24,1536]{3,2,1,0:T(8,128)(2,1)S(1)}, u32[]{:S(2)}, u32[]{:S(2)}) async-start(bf16[16,1,24,1536]{3,2,1,0:T(8,128)(2,1)} %fusion.52), calls=%async_computation.3 | async-start | bytes 2359296 | tf_op jit(solution)/shard_map/all_to_all | solution.py:125
  240.0 4.7 %collective-permute-start.11 = (bf16[64,768]{1,0:T(8,128)(2,1)S(1)}, bf16[64,768]{1,0:T(8,128)(2,1)S(1)}, u32[]{:S(2)}, u32[]{:S(2)}) collective-permute-start(bf16[64,768]{1,0:T(8,128)(2,1)S(1)} %select_convert_fusion.1), channel_id=1, source_target_pairs={{0,2},{1,3},{2,0},{3,1},{4,6},{5,7},{6,4},{7,5},{8,10},{9,11},{10,... | collective-permute-start | bytes 294920 | tf_op jit(solution)/shard_map/ppermute | solution.py:18
  (11 other events, 31.2 us)

commit v7 on v6

--- a/solution.py
+++ b/solution.py
@@ -72,6 +72,12 @@
     cross_route = [
         (s * n_t + t, (s + 1) * n_t + (t ^ 2)) for s in range(segments - 1) for t in range(n_t)
     ]
+    down_q = [down_local[..., q * quarter:(q + 1) * quarter] for q in range(4)]
+    down_even = jnp.concatenate([down_q[0], down_q[2]], axis=-1)
+    down_odd = jnp.concatenate([down_q[1], down_q[3]], axis=-1)
+    down_keep = jnp.where(core_first, down_even, down_odd)
+    down_give = jnp.where(core_first, down_odd, down_even)
+
     def layer_step(step, carried, collected):
         which = step - segment_pos
         which_safe = jnp.clip(which, 0, micro - 1)
@@ -106,22 +112,14 @@
             "sekd,edf->sekf", normed, up_local, preferred_element_type=jnp.float32
         )
         hidden = jax.nn.silu(summed_up).astype(jnp.bfloat16)
-        partial_out = jnp.einsum(
-            "sekf,efd->sekd", hidden, down_local, preferred_element_type=jnp.float32
+        give = jnp.einsum(
+            "sekf,efd->sekd", hidden, down_give, preferred_element_type=jnp.float32
         ).astype(jnp.bfloat16)
-        pq = [partial_out[..., q * quarter:(q + 1) * quarter] for q in range(4)]
-        keep = jnp.where(
-            core_first,
-            jnp.concatenate([pq[0], pq[2]], axis=-1),
-            jnp.concatenate([pq[1], pq[3]], axis=-1),
+        got = swap(give, "tensor", 1)
+        keep = jnp.einsum(
+            "sekf,efd->sekd", hidden, down_keep, preferred_element_type=jnp.float32
         )
-        give = jnp.where(
-            core_first,
-            jnp.concatenate([pq[1], pq[3]], axis=-1),
-            jnp.concatenate([pq[0], pq[2]], axis=-1),
-        )
-        got = swap(give, "tensor", 1)
-        chip_sum = (keep.astype(jnp.float32) + got.astype(jnp.float32)).astype(jnp.bfloat16)
+        chip_sum = (keep + got.astype(jnp.float32)).astype(jnp.bfloat16)
         returned = lax.all_to_all(chip_sum, "expert", split_axis=0, concat_axis=0, tiled=True)
         summed = jnp.sum(
             returned.reshape(EXPERTS, copies, capacity, 2 * quarter).astype(jnp.float32), axis=1

time: 246 us -> 252 us (1.024)
  matrix products: 17.9 us -> 24.5 us
  local copies, waits for them, and re-layouts: 17.6 us -> 21.9 us
  waiting for transfers between devices: 105 us -> 101 us
  other arithmetic: 16.2 us -> 13.5 us
    dot_general x3 -> x6, matrix products: 9.28 us -> 14.8 us  [the longest x3 8.93 us: layer_step(): jnp.einsum('sekf,efd->sekd', hidden, down_keep, preferred_element_type=jn...]
    concatenate x0 -> x1, local copies, waits for them, and re-layouts: none -> 4.67 us  [shards(): down_even = jnp.concatenate([down_q[0], down_q[2]], axis=-1)]
    convert_element_type x3 -> x0, other arithmetic: 4.35 us -> none  [layer_step(): (keep.astype(jnp.float32) + got.astype(jnp.float32)).astype(jnp.bfloat16)]
    ppermute x13, waiting for transfers between devices: 30.9 us -> 26.9 us  [swap(): return lax.ppermute(block, axis, [(i, i ^ bit) for i in range(n)])]
    select_n x3 -> x4, other arithmetic: 0.87 us -> 3.61 us  [the longest x1 3.24 us: shards(): down_give = jnp.where(core_first, down_odd, down_even)]
  transfers between devices with their start and end apart: 20 -> 20, of which waited for: 17 -> 16; matrix products, arithmetic and copies ran while one was open for 2% -> 5% of each run, Pallas kernels for 0% -> 0%
where the time goes in v7:
time: 252 us; the launch traced here: 251 us
  waiting for transfers between devices  101 us (40%)
  blocking collectives  66.2 us (26%)
  matrix products  24.5 us (10%)
  starting transfers between devices  23.5 us (9%)
  local copies, waits for them, and re-layouts  21.9 us (9%)
  other arithmetic  13.5 us (5%)
    all_to_all x3, blocking collectives, layer_step(): lax.all_to_all(outgoing, 'expert', split_axis=0, concat_axis=0, tiled=True)  66.2 us
    all_to_all x3, waiting for transfers between devices, layer_step(): lax.all_to_all(chip_sum, 'expert', split_axis=0, concat_axis=0, tiled=True)  60.5 us
    ppermute x13, waiting for transfers between devices, swap(): return lax.ppermute(block, axis, [(i, i ^ bit) for i in range(n)])  26.9 us
    all_to_all x3, starting transfers between devices, layer_step(): lax.all_to_all(chip_sum, 'expert', split_axis=0, concat_axis=0, tiled=True)  11.1 us
    ppermute x2, waiting for transfers between devices, looped(): lax.ppermute(produced, ('section', 'tensor'), cross_route)  10 us
    dot_general x3, matrix products, layer_step(): jnp.einsum('sekd,edf->sekf', normed, up_local, preferred_element_type=jnp...  9.7 us
    dot_general x3, matrix products, layer_step(): jnp.einsum('sekf,efd->sekd', hidden, down_keep, preferred_element_type=jn...  8.93 us
    ppermute x13, starting transfers between devices, swap(): return lax.ppermute(block, axis, [(i, i ^ bit) for i in range(n)])  7.25 us
  transfers between devices with their start and end apart: 20, of which 16 were waited for; matrix products, arithmetic and copies ran while one was open for 5% of the time, Pallas kernels for 0%

profile of v7, /device:TPU:6, one launch (start us, length us, event | category | flops | bytes accessed | tf_op | source)
XLA Modules:
  0.0 251.2 jit_solution(8979251103081957079)
XLA Ops:
  7.2 4.7 %slice_bitcast_fusion.16 = (bf16[1024,768]{1,0:T(8,128)(2,1)}, bf16[1024,768]{1,0:T(8,128)(2,1)}, bf16[1024,768]{1,0:T(8,128)(2,1)}, bf16[1024,768]{1,0:T(8,128)...) fusion(bf16[1,1024,3072]{2,1,0:T(8,128)(2,1)} %bitcast.278), kind=kLoop, calls=%fused_computation.172 | loop fusion | bytes 18874368 | tf_op jit(solution)/shard_map/concatenate | solution.py:76
  11.9 3.2 %broadcast_select_fusion.2 = (bf16[1,1024,1536]{2,1,0:T(8,128)(2,1)}, bf16[1,1024,1536]{2,1,0:T(8,128)(2,1)}) fusion(pred[]{:T(512)} %eq.98, bf16[1,1024,768]{2,1,0:T(8,128)(2,1)S(1)} %get-tuple-element.400, bf16[1,1024,768]{2,1,0:T(8,128)(2,1)S(1)} %get-tuple-element.401, bf16[1,1024,768]{2,1,0:T(8,128)(2,1)S(1)} %get-tuple-element.402, ...), kind=kLoop, calls=%fused_computation.85 | loop fusion | flops 15728640 | bytes 12582913 | tf_op jit(solution)/shard_map/jit(_where)/select_n | solution.py:79
  15.4 163.3 %while.17 = (s32[]{:T(128)}, bf16[64,1536]{1,0:T(8,128)(2,1)S(1)}, bf16[2,64,768]{2,1,0:T(8,128)(2,1)S(1)}, pred[]{:T(512)}, pred[]{:T(512)}, /*index=5*/bf16[2,...) while((s32[]{:T(128)}, bf16[64,1536]{1,0:T(8,128)(2,1)S(1)}, ...), condition=%wide.region_8.11_spmd.clone, body=%wide.region_4.10_spmd.clone.sunk | while | flops 4865758208 | bytes 112892008 | solution.py:150
  16.9 26.7 %all_to_all.35 = bf16[16,1,24,1536]{3,2,1,0:T(8,128)(2,1)S(1)} all-to-all(bf16[16,1,24,1536]{3,2,1,0:T(8,128)(2,1)S(1)} %bitcast.274), channel_id=1, replica_groups=mesh['section'=2,'expert'=16,'tensor'=4] {'expert'}, dimensions={0} | all-to-all | bytes 2359296 | tf_op jit(solution)/shard_map/while/body/eval_jaxpr/all_to_all | solution.py:101
  43.5 2.8 %collective-permute-done = bf16[16,1,24,1536]{3,2,0,1:T(8,128)(2,1)S(1)} collective-permute-done((bf16[16,1,24,1536]{3,2,0,1:T(8,128)(2,1)S(1)}, bf16[16,1,24,1536]{3,2,0,1:T(8,128)(2,1)S(1)}, u32[]{:S(2)}, u32[]{:S(2)}) %collective-permute-start) | collective-permute-done | bytes 1179680 | tf_op jit(solution)/shard_map/while/body/eval_jaxpr/ppermute | solution.py:18
  49.4 3.2 %fusion.113 = bf16[16,1,24,1024]{3,2,0,1:T(8,128)(2,1)S(1)} fusion(bf16[1,3072,1024]{2,1,0:T(8,128)(2,1)S(1)} %bitcast.294, bf16[16,24,768]{2,1,0:T(8,128)(2,1)S(1)} %get-tuple-element.525, bf16[16,24,768]{2,1,0:T(8,128)(2,1)S(1)} %get-tuple-element.526, bf16[16,24,768]{2,1,0:T(8,128)(2,1)S(1)} %get-tuple-element.527, ...), kind=kOutput, calls=%fused_computation.34.clone.1 | convolution fusion | flops 2430861312 | bytes 9451008 | tf_op jit(solution)/shard_map/while/body/eval_jaxpr/sekd,edf->sekf/dot_general | solution.py:111
  59.6 3.7 %all-to-all-start.1 = ((bf16[16,1,24,1536]{3,2,1,0:T(8,128)(2,1)}), bf16[16,1,24,1536]{3,2,1,0:T(8,128)(2,1)S(1)}, u32[]{:S(2)}, u32[]{:S(2)}) async-start(bf16[16,1,24,1536]{3,2,1,0:T(8,128)(2,1)} %fusion.115), calls=%async_computation.1 | async-start | bytes 2359296 | tf_op jit(solution)/shard_map/while/body/eval_jaxpr/all_to_all | solution.py:123
  63.4 20.1 %all-to-all-done.1 = bf16[16,1,24,1536]{3,2,1,0:T(8,128)(2,1)S(1)} async-done(((bf16[16,1,24,1536]{3,2,1,0:T(8,128)(2,1)}), bf16[16,1,24,1536]{3,2,1,0:T(8,128)(2,1)S(1)}, u32[]{:S(2)}, u32[]{:S(2)}) %all-to-all-start.1) | async-done | bytes 1179680 | tf_op jit(solution)/shard_map/while/body/eval_jaxpr/all_to_all | solution.py:123
  87.7 3.3 %collective-permute-done.2 = bf16[64,768]{1,0:T(8,128)(2,1)S(1)} collective-permute-done((bf16[64,768]{1,0:T(8,128)(2,1)S(1)}, bf16[64,768]{1,0:T(8,128)(2,1)S(1)}, u32[]{:S(2)}, u32[]{:S(2)}) %collective-permute-start.2) | collective-permute-done | bytes 98336 | tf_op jit(solution)/shard_map/while/body/eval_jaxpr/ppermute | solution.py:18
  93.8 5.0 %collective-permute-done.3 = bf16[64,768]{1,0:T(8,128)(2,1)S(1)} collective-permute-done((bf16[64,768]{1,0:T(8,128)(2,1)S(1)}, bf16[64,768]{1,0:T(8,128)(2,1)S(1)}, u32[]{:S(2)}, u32[]{:S(2)}) %collective-permute-start.3) | collective-permute-done | bytes 98336 | tf_op jit(solution)/shard_map/while/body/eval_jaxpr/ppermute | solution.py:145
  101.9 19.8 %all_to_all.35 = bf16[16,1,24,1536]{3,2,1,0:T(8,128)(2,1)S(1)} all-to-all(bf16[16,1,24,1536]{3,2,1,0:T(8,128)(2,1)S(1)} %bitcast.274), channel_id=1, replica_groups=mesh['section'=2,'expert'=16,'tensor'=4] {'expert'}, dimensions={0} | all-to-all | bytes 2359296 | tf_op jit(solution)/shard_map/while/body/eval_jaxpr/all_to_all | solution.py:101
  121.7 2.8 %collective-permute-done = bf16[16,1,24,1536]{3,2,0,1:T(8,128)(2,1)S(1)} collective-permute-done((bf16[16,1,24,1536]{3,2,0,1:T(8,128)(2,1)S(1)}, bf16[16,1,24,1536]{3,2,0,1:T(8,128)(2,1)S(1)}, u32[]{:S(2)}, u32[]{:S(2)}) %collective-permute-start) | collective-permute-done | bytes 1179680 | tf_op jit(solution)/shard_map/while/body/eval_jaxpr/ppermute | solution.py:18
  127.6 3.2 %fusion.113 = bf16[16,1,24,1024]{3,2,0,1:T(8,128)(2,1)S(1)} fusion(bf16[1,3072,1024]{2,1,0:T(8,128)(2,1)S(1)} %bitcast.294, bf16[16,24,768]{2,1,0:T(8,128)(2,1)S(1)} %get-tuple-element.525, bf16[16,24,768]{2,1,0:T(8,128)(2,1)S(1)} %get-tuple-element.526, bf16[16,24,768]{2,1,0:T(8,128)(2,1)S(1)} %get-tuple-element.527, ...), kind=kOutput, calls=%fused_computation.34.clone.1 | convolution fusion | flops 2430861312 | bytes 9451008 | tf_op jit(solution)/shard_map/while/body/eval_jaxpr/sekd,edf->sekf/dot_general | solution.py:111
  137.7 3.7 %all-to-all-start.1 = ((bf16[16,1,24,1536]{3,2,1,0:T(8,128)(2,1)}), bf16[16,1,24,1536]{3,2,1,0:T(8,128)(2,1)S(1)}, u32[]{:S(2)}, u32[]{:S(2)}) async-start(bf16[16,1,24,1536]{3,2,1,0:T(8,128)(2,1)} %fusion.115), calls=%async_computation.1 | async-start | bytes 2359296 | tf_op jit(solution)/shard_map/while/body/eval_jaxpr/all_to_all | solution.py:123
  141.5 20.2 %all-to-all-done.1 = bf16[16,1,24,1536]{3,2,1,0:T(8,128)(2,1)S(1)} async-done(((bf16[16,1,24,1536]{3,2,1,0:T(8,128)(2,1)}), bf16[16,1,24,1536]{3,2,1,0:T(8,128)(2,1)S(1)}, u32[]{:S(2)}, u32[]{:S(2)}) %all-to-all-start.1) | async-done | bytes 1179680 | tf_op jit(solution)/shard_map/while/body/eval_jaxpr/all_to_all | solution.py:123
  165.8 3.5 %collective-permute-done.2 = bf16[64,768]{1,0:T(8,128)(2,1)S(1)} collective-permute-done((bf16[64,768]{1,0:T(8,128)(2,1)S(1)}, bf16[64,768]{1,0:T(8,128)(2,1)S(1)}, u32[]{:S(2)}, u32[]{:S(2)}) %collective-permute-start.2) | collective-permute-done | bytes 98336 | tf_op jit(solution)/shard_map/while/body/eval_jaxpr/ppermute | solution.py:18
  172.0 5.0 %collective-permute-done.3 = bf16[64,768]{1,0:T(8,128)(2,1)S(1)} collective-permute-done((bf16[64,768]{1,0:T(8,128)(2,1)S(1)}, bf16[64,768]{1,0:T(8,128)(2,1)S(1)}, u32[]{:S(2)}, u32[]{:S(2)}) %collective-permute-start.3) | collective-permute-done | bytes 98336 | tf_op jit(solution)/shard_map/while/body/eval_jaxpr/ppermute | solution.py:145
  180.1 19.7 %all_to_all.34 = bf16[16,1,24,1536]{3,2,1,0:T(8,128)(2,1)S(1)} all-to-all(bf16[16,1,24,1536]{3,2,1,0:T(8,128)(2,1)S(1)} %bitcast.282), channel_id=1, replica_groups=mesh['section'=2,'expert'=16,'tensor'=4] {'expert'}, dimensions={0} | all-to-all | bytes 2359296 | tf_op jit(solution)/shard_map/all_to_all | solution.py:101
  205.7 3.2 %fusion.75 = bf16[16,1,24,1024]{3,2,0,1:T(8,128)(2,1)S(1)} fusion(bf16[1,1,3072,1024]{3,2,1,0:T(8,128)(2,1)S(1)} %bitcast.297, bf16[16,24,768]{2,1,0:T(8,128)(2,1)S(1)} %get-tuple-element.422, bf16[16,24,768]{2,1,0:T(8,128)(2,1)S(1)} %get-tuple-element.411, bf16[16,24,768]{2,1,0:T(8,128)(2,1)S(1)} %get-tuple-element.409, ...), kind=kOutput, calls=%fused_computation.108 | convolution fusion | flops 2430861312 | bytes 9451008 | tf_op jit(solution)/shard_map/sekd,edf->sekf/dot_general | solution.py:111
  209.0 3.1 %fusion.55 = bf16[16,1,24,1536]{3,2,0,1:T(8,128)(2,1)S(1)} fusion(pred[]{:T(512)} %eq.98, bf16[1024,768]{1,0:T(8,128)(2,1)S(1)} %copy-done.5, bf16[1024,768]{1,0:T(8,128)(2,1)S(1)} %copy-done.4, bf16[1024,768]{1,0:T(8,128)(2,1)S(1)} %copy-done.3, bf16[1024,768]{1,0:T(8,128)(2,1)S(1)} %copy-done.2, bf16[16,1,24,1024]{3,2,0,1:T(8,128)(2,1)S(1)} %fusion.75), kind=kOutput, calls=%fused_computation.89 | convolution fusion | flops 1222705152 | bytes 8257537 | tf_op jit(solution)/shard_map/sekf,efd->sekd/dot_general | solution.py:115
  215.0 3.9 %fusion.69 = bf16[16,1,24,1536]{3,2,1,0:T(8,128)(2,1)} fusion(bf16[16,1,24,1536]{3,2,0,1:T(8,128)(2,1)S(1)} %collective-permute-done.10, pred[]{:T(512)} %eq.98, bf16[1024,768]{1,0:T(8,128)(2,1)S(1)} %copy-done.5, bf16[1024,768]{1,0:T(8,128)(2,1)S(1)} %copy-done.4, bf16[1024,768]{1,0:T(8,128)(2,1)S(1)} %copy-done.3, bf16[1024,768]{1,0:T(8,128)(2,1)S(1)} %copy-done.2, ...), kind=kOutput, calls=%fused_computation.102 | convolution fusion | flops 1223884800 | bytes 9437185 | tf_op jit(solution)/shard_map/sekf,efd->sekd/dot_general | solution.py:119
  218.9 3.7 %all-to-all-start.3 = ((bf16[16,1,24,1536]{3,2,1,0:T(8,128)(2,1)}), bf16[16,1,24,1536]{3,2,1,0:T(8,128)(2,1)S(1)}, u32[]{:S(2)}, u32[]{:S(2)}) async-start(bf16[16,1,24,1536]{3,2,1,0:T(8,128)(2,1)} %fusion.69), calls=%async_computation.3 | async-start | bytes 2359296 | tf_op jit(solution)/shard_map/all_to_all | solution.py:123
  222.7 20.2 %all-to-all-done.3 = bf16[16,1,24,1536]{3,2,1,0:T(8,128)(2,1)S(1)} async-done(((bf16[16,1,24,1536]{3,2,1,0:T(8,128)(2,1)}), bf16[16,1,24,1536]{3,2,1,0:T(8,128)(2,1)S(1)}, u32[]{:S(2)}, u32[]{:S(2)}) %all-to-all-start.3) | async-done | bytes 1179680 | tf_op jit(solution)/shard_map/all_to_all | solution.py:123
  247.0 3.5 %collective-permute-done.11 = bf16[64,768]{1,0:T(8,128)(2,1)S(1)} collective-permute-done((bf16[64,768]{1,0:T(8,128)(2,1)S(1)}, bf16[64,768]{1,0:T(8,128)(2,1)S(1)}, u32[]{:S(2)}, u32[]{:S(2)}) %collective-permute-start.11) | collective-permute-done | bytes 98336 | tf_op jit(solution)/shard_map/ppermute | solution.py:18
  (169 shorter events, 61.9 us)
Async XLA Ops:
  0.7 14.5 %collective-permute-start.6 = (f32[768]{0:T(1024)S(1)}, f32[768]{0:T(1024)S(1)}, u32[]{:S(2)}, u32[]{:S(2)}) collective-permute-start(f32[768]{0:T(1024)S(1)} %reduce.6), channel_id=1, source_target_pairs={{0,1},{1,0},{2,3},{3,2},{4,5},{5,4},{6,7},{7,6},{8,9},{9,8},{10,11... | collective-permute-start | bytes 9224 | tf_op jit(solution)/shard_map/ppermute | solution.py:18
  0.8 14.4 %collective-permute-start.7 = (f32[768]{0:T(1024)S(1)}, f32[768]{0:T(1024)S(1)}, u32[]{:S(2)}, u32[]{:S(2)}) collective-permute-start(f32[768]{0:T(1024)S(1)} %reduce.6), channel_id=1, source_target_pairs={{0,2},{1,3},{2,0},{3,1},{4,6},{5,7},{6,4},{7,5},{8,10},{9,11},{10,... | collective-permute-start | bytes 9224 | tf_op jit(solution)/shard_map/ppermute | solution.py:18
  1.7 13.5 %collective-permute-start.8 = (f32[768]{0:T(1024)S(1)}, f32[768]{0:T(1024)S(1)}, u32[]{:S(2)}, u32[]{:S(2)}) collective-permute-start(f32[768]{0:T(1024)S(1)} %reduce.6), channel_id=1, source_target_pairs={{0,3},{1,2},{2,1},{3,0},{4,7},{5,6},{6,5},{7,4},{8,11},{9,10},{10,... | collective-permute-start | bytes 9224 | tf_op jit(solution)/shard_map/ppermute | solution.py:18
  2.6 12.6 %collective-permute-start.5 = (bf16[2,64,768]{2,1,0:T(8,128)(2,1)}, bf16[2,64,768]{2,1,0:T(8,128)(2,1)S(1)}, u32[]{:S(2)}, u32[]{:S(2)}) collective-permute-start(bf16[2,64,768]{2,1,0:T(8,128)(2,1)} %param.12), channel_id=1, source_target_pairs={{0,2},{1,3},{2,0},{3,1},{4,6},{5,7},{6,4},{7,5},{8,10},{9,11},{10,... | collective-permute-start | bytes 589832 | tf_op jit(solution)/shard_map/ppermute | solution.py:18
  11.8 3.4 %copy-start.6 = (bf16[2,64,768]{2,1,0:T(8,128)(2,1)S(1)}, bf16[2,64,768]{2,1,0:T(8,128)(2,1)}, u32[]{:S(2)}) copy-start(bf16[2,64,768]{2,1,0:T(8,128)(2,1)} %param.12) | copy-start | bytes 589828
  11.8 3.5 %copy-start.7 = (f32[1,2,64,2]{2,3,1,0:T(2,128)S(1)}, f32[1,2,64,2]{2,3,1,0:T(2,128)}, u32[]{:S(2)}) copy-start(f32[1,2,64,2]{2,3,1,0:T(2,128)} %param.15) | copy-start | bytes 3076
  43.5 2.8 %collective-permute-start = (bf16[16,1,24,1536]{3,2,0,1:T(8,128)(2,1)S(1)}, bf16[16,1,24,1536]{3,2,0,1:T(8,128)(2,1)S(1)}, u32[]{:S(2)}, u32[]{:S(2)}) collective-permute-start(bf16[16,1,24,1536]{3,2,0,1:T(8,128)(2,1)S(1)} %bitcast.270), channel_id=1, source_target_pairs={{0,1},{1,0},{2,3},{3,2},{4,5},{5,4},{6,7},{7,6},{8,9},{9,8},{10,11... | collective-permute-start | bytes 3538952 | tf_op jit(solution)/shard_map/while/body/eval_jaxpr/ppermute | solution.py:18
  52.7 4.3 %copy-start.1 = (bf16[1,1024,1536]{2,1,0:T(8,128)(2,1)S(1)}, bf16[1,1024,1536]{2,1,0:T(8,128)(2,1)}, u32[]{:S(2)}) copy-start(bf16[1,1024,1536]{2,1,0:T(8,128)(2,1)} %get-tuple-element.582) | copy-start | bytes 9437188 | tf_op jit(solution)/shard_map/while
  54.1 2.9 %collective-permute-start.1 = (bf16[16,1,24,1536]{3,2,0,1:T(8,128)(2,1)S(1)}, bf16[16,1,24,1536]{3,2,0,1:T(8,128)(2,1)S(1)}, u32[]{:S(2)}, u32[]{:S(2)}) collective-permute-start(bf16[16,1,24,1536]{3,2,0,1:T(8,128)(2,1)S(1)} %fusion.114), channel_id=1, source_target_pairs={{0,1},{1,0},{2,3},{3,2},{4,5},{5,4},{6,7},{7,6},{8,9},{9,8},{10,11... | collective-permute-start | bytes 3538952 | tf_op jit(solution)/shard_map/while/body/eval_jaxpr/ppermute | solution.py:18
  59.6 24.0 %all-to-all-start.1 = ((bf16[16,1,24,1536]{3,2,1,0:T(8,128)(2,1)}), bf16[16,1,24,1536]{3,2,1,0:T(8,128)(2,1)S(1)}, u32[]{:S(2)}, u32[]{:S(2)}) async-start(bf16[16,1,24,1536]{3,2,1,0:T(8,128)(2,1)} %fusion.115), calls=%async_computation.1 | async-start | bytes 2359296 | tf_op jit(solution)/shard_map/while/body/eval_jaxpr/all_to_all | solution.py:123
  86.3 4.7 %collective-permute-start.2 = (bf16[64,768]{1,0:T(8,128)(2,1)S(1)}, bf16[64,768]{1,0:T(8,128)(2,1)S(1)}, u32[]{:S(2)}, u32[]{:S(2)}) collective-permute-start(bf16[64,768]{1,0:T(8,128)(2,1)S(1)} %select_convert_fusion.3), channel_id=1, source_target_pairs={{0,2},{1,3},{2,0},{3,1},{4,6},{5,7},{6,4},{7,5},{8,10},{9,11},{10,... | collective-permute-start | bytes 294920 | tf_op jit(solution)/shard_map/while/body/eval_jaxpr/ppermute | solution.py:18
  91.1 7.7 %collective-permute-start.3 = (bf16[64,768]{1,0:T(8,128)(2,1)S(1)}, bf16[64,768]{1,0:T(8,128)(2,1)S(1)}, u32[]{:S(2)}, u32[]{:S(2)}) collective-permute-start(bf16[64,768]{1,0:T(8,128)(2,1)S(1)} %add_convert_fusion.5), channel_id=1, source_target_pairs={{0,66},{1,67},{2,64},{3,65},{4,70},{5,71},{6,68},{7,69},{8,74},{9,... | collective-permute-start | bytes 294920 | tf_op jit(solution)/shard_map/while/body/eval_jaxpr/ppermute | solution.py:145
  92.4 8.0 %collective-permute-start.4 = (bf16[64,768]{1,0:T(8,128)(2,1)S(1)}, bf16[64,768]{1,0:T(8,128)(2,1)S(1)}, u32[]{:S(2)}, u32[]{:S(2)}) collective-permute-start(bf16[64,768]{1,0:T(8,128)(2,1)S(1)} %add_convert_fusion.5), channel_id=1, source_target_pairs={{0,64},{1,65},{2,66},{3,67},{4,68},{5,69},{6,70},{7,71},{8,72},{9,... | collective-permute-start | bytes 294920 | tf_op jit(solution)/shard_map/while/body/eval_jaxpr/ppermute | solution.py:13
  121.7 2.8 %collective-permute-start = (bf16[16,1,24,1536]{3,2,0,1:T(8,128)(2,1)S(1)}, bf16[16,1,24,1536]{3,2,0,1:T(8,128)(2,1)S(1)}, u32[]{:S(2)}, u32[]{:S(2)}) collective-permute-start(bf16[16,1,24,1536]{3,2,0,1:T(8,128)(2,1)S(1)} %bitcast.270), channel_id=1, source_target_pairs={{0,1},{1,0},{2,3},{3,2},{4,5},{5,4},{6,7},{7,6},{8,9},{9,8},{10,11... | collective-permute-start | bytes 3538952 | tf_op jit(solution)/shard_map/while/body/eval_jaxpr/ppermute | solution.py:18
  130.9 4.3 %copy-start.1 = (bf16[1,1024,1536]{2,1,0:T(8,128)(2,1)S(1)}, bf16[1,1024,1536]{2,1,0:T(8,128)(2,1)}, u32[]{:S(2)}) copy-start(bf16[1,1024,1536]{2,1,0:T(8,128)(2,1)} %get-tuple-element.582) | copy-start | bytes 9437188 | tf_op jit(solution)/shard_map/while
  132.3 2.9 %collective-permute-start.1 = (bf16[16,1,24,1536]{3,2,0,1:T(8,128)(2,1)S(1)}, bf16[16,1,24,1536]{3,2,0,1:T(8,128)(2,1)S(1)}, u32[]{:S(2)}, u32[]{:S(2)}) collective-permute-start(bf16[16,1,24,1536]{3,2,0,1:T(8,128)(2,1)S(1)} %fusion.114), channel_id=1, source_target_pairs={{0,1},{1,0},{2,3},{3,2},{4,5},{5,4},{6,7},{7,6},{8,9},{9,8},{10,11... | collective-permute-start | bytes 3538952 | tf_op jit(solution)/shard_map/while/body/eval_jaxpr/ppermute | solution.py:18
  137.7 24.0 %all-to-all-start.1 = ((bf16[16,1,24,1536]{3,2,1,0:T(8,128)(2,1)}), bf16[16,1,24,1536]{3,2,1,0:T(8,128)(2,1)S(1)}, u32[]{:S(2)}, u32[]{:S(2)}) async-start(bf16[16,1,24,1536]{3,2,1,0:T(8,128)(2,1)} %fusion.115), calls=%async_computation.1 | async-start | bytes 2359296 | tf_op jit(solution)/shard_map/while/body/eval_jaxpr/all_to_all | solution.py:123
  164.5 4.7 %collective-permute-start.2 = (bf16[64,768]{1,0:T(8,128)(2,1)S(1)}, bf16[64,768]{1,0:T(8,128)(2,1)S(1)}, u32[]{:S(2)}, u32[]{:S(2)}) collective-permute-start(bf16[64,768]{1,0:T(8,128)(2,1)S(1)} %select_convert_fusion.3), channel_id=1, source_target_pairs={{0,2},{1,3},{2,0},{3,1},{4,6},{5,7},{6,4},{7,5},{8,10},{9,11},{10,... | collective-permute-start | bytes 294920 | tf_op jit(solution)/shard_map/while/body/eval_jaxpr/ppermute | solution.py:18
  169.3 7.7 %collective-permute-start.3 = (bf16[64,768]{1,0:T(8,128)(2,1)S(1)}, bf16[64,768]{1,0:T(8,128)(2,1)S(1)}, u32[]{:S(2)}, u32[]{:S(2)}) collective-permute-start(bf16[64,768]{1,0:T(8,128)(2,1)S(1)} %add_convert_fusion.5), channel_id=1, source_target_pairs={{0,66},{1,67},{2,64},{3,65},{4,70},{5,71},{6,68},{7,69},{8,74},{9,... | collective-permute-start | bytes 294920 | tf_op jit(solution)/shard_map/while/body/eval_jaxpr/ppermute | solution.py:145
  170.6 8.0 %collective-permute-start.4 = (bf16[64,768]{1,0:T(8,128)(2,1)S(1)}, bf16[64,768]{1,0:T(8,128)(2,1)S(1)}, u32[]{:S(2)}, u32[]{:S(2)}) collective-permute-start(bf16[64,768]{1,0:T(8,128)(2,1)S(1)} %add_convert_fusion.5), channel_id=1, source_target_pairs={{0,64},{1,65},{2,66},{3,67},{4,68},{5,69},{6,70},{7,71},{8,72},{9,... | collective-permute-start | bytes 294920 | tf_op jit(solution)/shard_map/while/body/eval_jaxpr/ppermute | solution.py:13
  199.8 2.8 %collective-permute-start.9 = (bf16[16,1,24,1536]{3,2,0,1:T(8,128)(2,1)S(1)}, bf16[16,1,24,1536]{3,2,0,1:T(8,128)(2,1)S(1)}, u32[]{:S(2)}, u32[]{:S(2)}) collective-permute-start(bf16[16,1,24,1536]{3,2,0,1:T(8,128)(2,1)S(1)} %bitcast.277), channel_id=1, source_target_pairs={{0,1},{1,0},{2,3},{3,2},{4,5},{5,4},{6,7},{7,6},{8,9},{9,8},{10,11... | collective-permute-start | bytes 3538952 | tf_op jit(solution)/shard_map/ppermute | solution.py:18
  212.0 2.9 %collective-permute-start.10 = (bf16[16,1,24,1536]{3,2,0,1:T(8,128)(2,1)S(1)}, bf16[16,1,24,1536]{3,2,0,1:T(8,128)(2,1)S(1)}, u32[]{:S(2)}, u32[]{:S(2)}) collective-permute-start(bf16[16,1,24,1536]{3,2,0,1:T(8,128)(2,1)S(1)} %fusion.55), channel_id=1, source_target_pairs={{0,1},{1,0},{2,3},{3,2},{4,5},{5,4},{6,7},{7,6},{8,9},{9,8},{10,11... | collective-permute-start | bytes 3538952 | tf_op jit(solution)/shard_map/ppermute | solution.py:18
  218.9 24.1 %all-to-all-start.3 = ((bf16[16,1,24,1536]{3,2,1,0:T(8,128)(2,1)}), bf16[16,1,24,1536]{3,2,1,0:T(8,128)(2,1)S(1)}, u32[]{:S(2)}, u32[]{:S(2)}) async-start(bf16[16,1,24,1536]{3,2,1,0:T(8,128)(2,1)} %fusion.69), calls=%async_computation.3 | async-start | bytes 2359296 | tf_op jit(solution)/shard_map/all_to_all | solution.py:123
  245.7 4.7 %collective-permute-start.11 = (bf16[64,768]{1,0:T(8,128)(2,1)S(1)}, bf16[64,768]{1,0:T(8,128)(2,1)S(1)}, u32[]{:S(2)}, u32[]{:S(2)}) collective-permute-start(bf16[64,768]{1,0:T(8,128)(2,1)S(1)} %select_convert_fusion.1), channel_id=1, source_target_pairs={{0,2},{1,3},{2,0},{3,1},{4,6},{5,7},{6,4},{7,5},{8,10},{9,11},{10,... | collective-permute-start | bytes 294920 | tf_op jit(solution)/shard_map/ppermute | solution.py:18
  (12 other events, 34.4 us)

commit v8 on v7

--- a/solution.py
+++ b/solution.py
@@ -72,12 +72,6 @@
     cross_route = [
         (s * n_t + t, (s + 1) * n_t + (t ^ 2)) for s in range(segments - 1) for t in range(n_t)
     ]
-    down_q = [down_local[..., q * quarter:(q + 1) * quarter] for q in range(4)]
-    down_even = jnp.concatenate([down_q[0], down_q[2]], axis=-1)
-    down_odd = jnp.concatenate([down_q[1], down_q[3]], axis=-1)
-    down_keep = jnp.where(core_first, down_even, down_odd)
-    down_give = jnp.where(core_first, down_odd, down_even)
-
     def layer_step(step, carried, collected):
         which = step - segment_pos
         which_safe = jnp.clip(which, 0, micro - 1)
@@ -99,27 +93,42 @@
             n_exp, local_count, capacity, 2 * quarter
         )
         mine = lax.all_to_all(outgoing, "expert", split_axis=0, concat_axis=0, tiled=True)
-        theirs = swap(mine, "tensor", 1)
-        lo_q = lambda a: a[..., :quarter]
-        hi_q = lambda a: a[..., quarter:]
-        first = jnp.where(core_first, mine, theirs)
-        second = jnp.where(core_first, theirs, mine)
-        rows = jnp.concatenate([lo_q(first), lo_q(second), hi_q(first), hi_q(second)], axis=-1)
-        rf = rows.astype(jnp.float32)
-        sums = jnp.sum(rf * rf, axis=-1)
-        normed = (rf * lax.rsqrt(sums / D + 1e-05)[..., None] * gain_full).astype(jnp.bfloat16)
-        summed_up = jnp.einsum(
-            "sekd,edf->sekf", normed, up_local, preferred_element_type=jnp.float32
+        def expert_rows(mine):
+            theirs = swap(mine, "tensor", 1)
+            lo_q = lambda a: a[..., :quarter]
+            hi_q = lambda a: a[..., quarter:]
+            first = jnp.where(core_first, mine, theirs)
+            second = jnp.where(core_first, theirs, mine)
+            rows = jnp.concatenate([lo_q(first), lo_q(second), hi_q(first), hi_q(second)], axis=-1)
+            rf = rows.astype(jnp.float32)
+            sums = jnp.sum(rf * rf, axis=-1)
+            normed = (rf * lax.rsqrt(sums / D + 1e-05)[..., None] * gain_full).astype(jnp.bfloat16)
+            summed_up = jnp.einsum(
+                "sekd,edf->sekf", normed, up_local, preferred_element_type=jnp.float32
+            )
+            hidden = jax.nn.silu(summed_up).astype(jnp.bfloat16)
+            partial_out = jnp.einsum(
+                "sekf,efd->sekd", hidden, down_local, preferred_element_type=jnp.float32
+            ).astype(jnp.bfloat16)
+            pq = [partial_out[..., q * quarter:(q + 1) * quarter] for q in range(4)]
+            keep = jnp.where(
+                core_first,
+                jnp.concatenate([pq[0], pq[2]], axis=-1),
+                jnp.concatenate([pq[1], pq[3]], axis=-1),
+            )
+            give = jnp.where(
+                core_first,
+                jnp.concatenate([pq[1], pq[3]], axis=-1),
+                jnp.concatenate([pq[0], pq[2]], axis=-1),
+            )
+            got = swap(give, "tensor", 1)
+            chip_sum = (keep.astype(jnp.float32) + got.astype(jnp.float32)).astype(jnp.bfloat16)
+            return chip_sum
+
+        half_src = n_exp // 2
+        chip_sum = jnp.concatenate(
+            [expert_rows(mine[:half_src]), expert_rows(mine[half_src:])], axis=0
         )
-        hidden = jax.nn.silu(summed_up).astype(jnp.bfloat16)
-        give = jnp.einsum(
-            "sekf,efd->sekd", hidden, down_give, preferred_element_type=jnp.float32
-        ).astype(jnp.bfloat16)
-        got = swap(give, "tensor", 1)
-        keep = jnp.einsum(
-            "sekf,efd->sekd", hidden, down_keep, preferred_element_type=jnp.float32
-        )
-        chip_sum = (keep + got.astype(jnp.float32)).astype(jnp.bfloat16)
         returned = lax.all_to_all(chip_sum, "expert", split_axis=0, concat_axis=0, tiled=True)
         summed = jnp.sum(
             returned.reshape(EXPERTS, copies, capacity, 2 * quarter).astype(jnp.float32), axis=1

time: 252 us -> 290 us (1.15)
  matrix products: 24.5 us -> 50.8 us
  other arithmetic: 13.5 us -> 26.8 us
  waiting for transfers between devices: 101 us -> 97.5 us
    dot_general x9 -> x6, matrix products: 24.5 us -> 50.8 us  [expert_rows(): jnp.einsum('sekf,efd->sekd', hidden, down_local, preferred_element_type=j...]
    slice x6 -> x15, local copies, waits for them, and re-layouts: 0.93 us -> 11.2 us  [the longest x6 7.86 us: expert_rows(): pq = [partial_out[..., q * quarter:(q + 1) * quarter] for q in range(4)]]
    select_n x7 -> x12, other arithmetic: 3.98 us -> 9.83 us  [the longest x6 6.44 us: expert_rows(): first = jnp.where(core_first, mine, theirs)]
    concatenate x1 -> x0, local copies, waits for them, and re-layouts: 4.67 us -> none  [shards(): down_even = jnp.concatenate([down_q[0], down_q[2]], axis=-1)]
    concatenate x0 -> x3, other arithmetic: none -> 3.36 us  [layer_step(): jnp.concatenate([expert_rows(mine[:half_src]), expert_rows(mine[half_src:...]
    ppermute x13 -> x19, waiting for transfers between devices: 26.9 us -> 23.7 us  [swap(): return lax.ppermute(block, axis, [(i, i ^ bit) for i in range(n)])]
    ppermute x13 -> x19, starting transfers between devices: 7.25 us -> 7.76 us  [swap(): return lax.ppermute(block, axis, [(i, i ^ bit) for i in range(n)])]
  transfers between devices with their start and end apart: 20 -> 26, of which waited for: 16 -> 17; matrix products, arithmetic and copies ran while one was open for 5% -> 27% of each run, Pallas kernels for 0% -> 0%
where the time goes in v8:
time: 290 us; the launch traced here: 289 us
  waiting for transfers between devices  97.5 us (34%)
  blocking collectives  65.6 us (23%)
  matrix products  50.8 us (18%)
  other arithmetic  26.8 us (9%)
  starting transfers between devices  24 us (8%)
  local copies, waits for them, and re-layouts  23.4 us (8%)
    all_to_all x3, blocking collectives, layer_step(): lax.all_to_all(outgoing, 'expert', split_axis=0, concat_axis=0, tiled=True)  65.6 us
    all_to_all x3, waiting for transfers between devices, layer_step(): lax.all_to_all(chip_sum, 'expert', split_axis=0, concat_axis=0, tiled=True)  60.6 us
    dot_general x6, matrix products, expert_rows(): jnp.einsum('sekf,efd->sekd', hidden, down_local, preferred_element_type=j...  50.8 us
    ppermute x19, waiting for transfers between devices, swap(): return lax.ppermute(block, axis, [(i, i ^ bit) for i in range(n)])  23.7 us
    all_to_all x3, starting transfers between devices, layer_step(): lax.all_to_all(chip_sum, 'expert', split_axis=0, concat_axis=0, tiled=True)  11.1 us
    ppermute x2, waiting for transfers between devices, looped(): lax.ppermute(produced, ('section', 'tensor'), cross_route)  10 us
    slice x6, local copies, waits for them, and re-layouts, expert_rows(): pq = [partial_out[..., q * quarter:(q + 1) * quarter] for q in range(4)]  7.86 us
    ppermute x19, starting transfers between devices, swap(): return lax.ppermute(block, axis, [(i, i ^ bit) for i in range(n)])  7.76 us
  transfers between devices with their start and end apart: 26, of which 17 were waited for; matrix products, arithmetic and copies ran while one was open for 27% of the time, Pallas kernels for 0%

profile of v8, /device:TPU:6, one launch (start us, length us, event | category | flops | bytes accessed | tf_op | source)
XLA Modules:
  0.0 289.4 jit_solution(11640160368596076562)
XLA Ops:
  11.2 193.7 %while.17 = (s32[]{:T(128)}, bf16[64,1536]{1,0:T(8,128)(2,1)S(1)}, bf16[2,64,768]{2,1,0:T(8,128)(2,1)}, pred[]{:T(512)}, pred[]{:T(512)}, /*index=5*/bf16[2,64,1...) while((s32[]{:T(128)}, bf16[64,1536]{1,0:T(8,128)(2,1)S(1)}, ...), condition=%wide.region_9.12_spmd.clone, body=%wide.region_4.11_spmd.clone.sunk | while | flops 4878144512 | bytes 97962184 | solution.py:159
  13.5 26.1 %all_to_all.35 = bf16[16,1,24,1536]{3,2,1,0:T(8,128)(2,1)S(1)} all-to-all(bf16[16,1,24,1536]{3,2,1,0:T(8,128)(2,1)S(1)} %bitcast.297), channel_id=1, replica_groups=mesh['section'=2,'expert'=16,'tensor'=4] {'expert'}, dimensions={0} | all-to-all | bytes 2359296 | tf_op jit(solution)/shard_map/while/body/eval_jaxpr/all_to_all | solution.py:95
  39.8 2.0 collective-permute-done
  43.4 8.4 %fusion.174 = bf16[8,1,24,3072]{3,2,0,1:T(8,128)(2,1)} fusion(bf16[1,1024,3072]{2,1,0:T(8,128)(2,1)} %get-tuple-element.632, bf16[1,3072,1024]{2,1,0:T(8,128)(2,1)} %get-tuple-element.631, bf16[8,24,768]{2,1,0:T(8,128)(2,1)S(1)} %get-tuple-element.573, bf16[8,24,768]{2,1,0:T(8,128)(2,1)S(1)} %get-tuple-element.574, ...), kind=kOutput, calls=%fused_computation.17.clone.1 | convolution fusion | flops 2423980032 | bytes 14955264 | tf_op jit(solution)/shard_map/while/body/eval_jaxpr/sekf,efd->sekd/dot_general | solution.py:110
  56.8 8.5 %fusion.171 = bf16[8,1,24,3072]{3,2,0,1:T(8,128)(2,1)} fusion(bf16[1,1024,3072]{2,1,0:T(8,128)(2,1)} %get-tuple-element.632, bf16[1,3072,1024]{2,1,0:T(8,128)(2,1)} %get-tuple-element.631, bf16[8,24,768]{2,1,0:T(8,128)(2,1)S(1)} %get-tuple-element.559, bf16[8,24,768]{2,1,0:T(8,128)(2,1)S(1)} %get-tuple-element.560, ...), kind=kOutput, calls=%fused_computation.16.clone.1 | convolution fusion | flops 2423980032 | bytes 14955264 | tf_op jit(solution)/shard_map/while/body/eval_jaxpr/sekf,efd->sekd/dot_general | solution.py:110
  70.2 3.7 %all-to-all-start.1 = ((bf16[16,1,24,1536]{3,2,1,0:T(8,128)(2,1)}), bf16[16,1,24,1536]{3,2,1,0:T(8,128)(2,1)S(1)}, u32[]{:S(2)}, u32[]{:S(2)}) async-start(bf16[16,1,24,1536]{3,2,1,0:T(8,128)(2,1)} %maximum_bitcast_fusion.3), calls=%async_computation.1 | async-start | bytes 2359296 | tf_op jit(solution)/shard_map/while/body/eval_jaxpr/all_to_all | solution.py:132
  74.0 20.2 %all-to-all-done.1 = bf16[16,1,24,1536]{3,2,1,0:T(8,128)(2,1)S(1)} async-done(((bf16[16,1,24,1536]{3,2,1,0:T(8,128)(2,1)}), bf16[16,1,24,1536]{3,2,1,0:T(8,128)(2,1)S(1)}, u32[]{:S(2)}, u32[]{:S(2)}) %all-to-all-start.1) | async-done | bytes 1179680 | tf_op jit(solution)/shard_map/while/body/eval_jaxpr/all_to_all | solution.py:132
  98.0 3.8 %collective-permute-done.4 = bf16[64,768]{1,0:T(8,128)(2,1)S(1)} collective-permute-done((bf16[64,768]{1,0:T(8,128)(2,1)S(1)}, bf16[64,768]{1,0:T(8,128)(2,1)S(1)}, u32[]{:S(2)}, u32[]{:S(2)}) %collective-permute-start.4) | collective-permute-done | bytes 98336 | tf_op jit(solution)/shard_map/while/body/eval_jaxpr/ppermute | solution.py:18
  104.5 5.0 %collective-permute-done.5 = bf16[64,768]{1,0:T(8,128)(2,1)S(1)} collective-permute-done((bf16[64,768]{1,0:T(8,128)(2,1)S(1)}, bf16[64,768]{1,0:T(8,128)(2,1)S(1)}, u32[]{:S(2)}, u32[]{:S(2)}) %collective-permute-start.5) | collective-permute-done | bytes 98336 | tf_op jit(solution)/shard_map/while/body/eval_jaxpr/ppermute | solution.py:154
  113.4 19.7 %all_to_all.35 = bf16[16,1,24,1536]{3,2,1,0:T(8,128)(2,1)S(1)} all-to-all(bf16[16,1,24,1536]{3,2,1,0:T(8,128)(2,1)S(1)} %bitcast.297), channel_id=1, replica_groups=mesh['section'=2,'expert'=16,'tensor'=4] {'expert'}, dimensions={0} | all-to-all | bytes 2359296 | tf_op jit(solution)/shard_map/while/body/eval_jaxpr/all_to_all | solution.py:95
  133.2 2.0 collective-permute-done
  136.8 8.4 %fusion.174 = bf16[8,1,24,3072]{3,2,0,1:T(8,128)(2,1)} fusion(bf16[1,1024,3072]{2,1,0:T(8,128)(2,1)} %get-tuple-element.632, bf16[1,3072,1024]{2,1,0:T(8,128)(2,1)} %get-tuple-element.631, bf16[8,24,768]{2,1,0:T(8,128)(2,1)S(1)} %get-tuple-element.573, bf16[8,24,768]{2,1,0:T(8,128)(2,1)S(1)} %get-tuple-element.574, ...), kind=kOutput, calls=%fused_computation.17.clone.1 | convolution fusion | flops 2423980032 | bytes 14955264 | tf_op jit(solution)/shard_map/while/body/eval_jaxpr/sekf,efd->sekd/dot_general | solution.py:110
  150.3 8.5 %fusion.171 = bf16[8,1,24,3072]{3,2,0,1:T(8,128)(2,1)} fusion(bf16[1,1024,3072]{2,1,0:T(8,128)(2,1)} %get-tuple-element.632, bf16[1,3072,1024]{2,1,0:T(8,128)(2,1)} %get-tuple-element.631, bf16[8,24,768]{2,1,0:T(8,128)(2,1)S(1)} %get-tuple-element.559, bf16[8,24,768]{2,1,0:T(8,128)(2,1)S(1)} %get-tuple-element.560, ...), kind=kOutput, calls=%fused_computation.16.clone.1 | convolution fusion | flops 2423980032 | bytes 14955264 | tf_op jit(solution)/shard_map/while/body/eval_jaxpr/sekf,efd->sekd/dot_general | solution.py:110
  163.7 3.7 %all-to-all-start.1 = ((bf16[16,1,24,1536]{3,2,1,0:T(8,128)(2,1)}), bf16[16,1,24,1536]{3,2,1,0:T(8,128)(2,1)S(1)}, u32[]{:S(2)}, u32[]{:S(2)}) async-start(bf16[16,1,24,1536]{3,2,1,0:T(8,128)(2,1)} %maximum_bitcast_fusion.3), calls=%async_computation.1 | async-start | bytes 2359296 | tf_op jit(solution)/shard_map/while/body/eval_jaxpr/all_to_all | solution.py:132
  167.5 20.2 %all-to-all-done.1 = bf16[16,1,24,1536]{3,2,1,0:T(8,128)(2,1)S(1)} async-done(((bf16[16,1,24,1536]{3,2,1,0:T(8,128)(2,1)}), bf16[16,1,24,1536]{3,2,1,0:T(8,128)(2,1)S(1)}, u32[]{:S(2)}, u32[]{:S(2)}) %all-to-all-start.1) | async-done | bytes 1179680 | tf_op jit(solution)/shard_map/while/body/eval_jaxpr/all_to_all | solution.py:132
  191.4 3.8 %collective-permute-done.4 = bf16[64,768]{1,0:T(8,128)(2,1)S(1)} collective-permute-done((bf16[64,768]{1,0:T(8,128)(2,1)S(1)}, bf16[64,768]{1,0:T(8,128)(2,1)S(1)}, u32[]{:S(2)}, u32[]{:S(2)}) %collective-permute-start.4) | collective-permute-done | bytes 98336 | tf_op jit(solution)/shard_map/while/body/eval_jaxpr/ppermute | solution.py:18
  198.0 5.0 %collective-permute-done.5 = bf16[64,768]{1,0:T(8,128)(2,1)S(1)} collective-permute-done((bf16[64,768]{1,0:T(8,128)(2,1)S(1)}, bf16[64,768]{1,0:T(8,128)(2,1)S(1)}, u32[]{:S(2)}, u32[]{:S(2)}) %collective-permute-start.5) | collective-permute-done | bytes 98336 | tf_op jit(solution)/shard_map/while/body/eval_jaxpr/ppermute | solution.py:154
  206.4 19.7 %all_to_all.34 = bf16[16,1,24,1536]{3,2,1,0:T(8,128)(2,1)S(1)} all-to-all(bf16[16,1,24,1536]{3,2,1,0:T(8,128)(2,1)S(1)} %bitcast.304), channel_id=1, replica_groups=mesh['section'=2,'expert'=16,'tensor'=4] {'expert'}, dimensions={0} | all-to-all | bytes 2359296 | tf_op jit(solution)/shard_map/all_to_all | solution.py:95
  226.3 2.0 collective-permute-done.11
  229.9 8.4 %fusion.84 = bf16[8,1,24,3072]{3,2,0,1:T(8,128)(2,1)} fusion(bf16[1,1,1024,3072]{3,2,1,0:T(8,128)(2,1)} %bitcast.318, bf16[1,1,3072,1024]{3,2,1,0:T(8,128)(2,1)} %bitcast.315, bf16[8,24,768]{2,1,0:T(8,128)(2,1)S(1)} %get-tuple-element.433, bf16[8,24,768]{2,1,0:T(8,128)(2,1)S(1)} %get-tuple-element.412, bf16[8,24,768]{2,1,0:T(8,128)(2,1)S(1)} %get-tuple-element.434, ...), kind=kOutput, calls=%fused_computation.109 | convolution fusion | flops 2423980032 | bytes 14955264 | tf_op jit(solution)/shard_map/sekf,efd->sekd/dot_general | solution.py:110
  243.5 8.7 %fusion.81 = bf16[8,1,24,3072]{3,2,0,1:T(8,128)(2,1)} fusion(bf16[1,1,1024,3072]{3,2,1,0:T(8,128)(2,1)} %bitcast.319, bf16[1,1,3072,1024]{3,2,1,0:T(8,128)(2,1)} %bitcast.316, bf16[8,24,768]{2,1,0:T(8,128)(2,1)} %get-tuple-element.437, bf16[8,24,768]{2,1,0:T(8,128)(2,1)} %get-tuple-element.420, bf16[8,24,768]{2,1,0:T(8,128)(2,1)} %get-tuple-element.438, ...), kind=kOutput, calls=%fused_computation.108 | convolution fusion | flops 2423980032 | bytes 14955264 | tf_op jit(solution)/shard_map/sekf,efd->sekd/dot_general | solution.py:110
  257.0 3.7 %all-to-all-start.3 = ((bf16[16,1,24,1536]{3,2,1,0:T(8,128)(2,1)}), bf16[16,1,24,1536]{3,2,1,0:T(8,128)(2,1)S(1)}, u32[]{:S(2)}, u32[]{:S(2)}) async-start(bf16[16,1,24,1536]{3,2,1,0:T(8,128)(2,1)} %maximum_bitcast_fusion.1), calls=%async_computation.3 | async-start | bytes 2359296 | tf_op jit(solution)/shard_map/all_to_all | solution.py:132
  260.9 20.2 %all-to-all-done.3 = bf16[16,1,24,1536]{3,2,1,0:T(8,128)(2,1)S(1)} async-done(((bf16[16,1,24,1536]{3,2,1,0:T(8,128)(2,1)}), bf16[16,1,24,1536]{3,2,1,0:T(8,128)(2,1)S(1)}, u32[]{:S(2)}, u32[]{:S(2)}) %all-to-all-start.3) | async-done | bytes 1179680 | tf_op jit(solution)/shard_map/all_to_all | solution.py:132
  284.7 3.9 %collective-permute-done.15 = bf16[64,768]{1,0:T(8,128)(2,1)S(1)} collective-permute-done((bf16[64,768]{1,0:T(8,128)(2,1)S(1)}, bf16[64,768]{1,0:T(8,128)(2,1)S(1)}, u32[]{:S(2)}, u32[]{:S(2)}) %collective-permute-start.15) | collective-permute-done | bytes 98336 | tf_op jit(solution)/shard_map/ppermute | solution.py:18
  (195 shorter events, 72.5 us)
Async XLA Ops:
  0.7 8.0 %collective-permute-start.8 = (f32[768]{0:T(1024)S(1)}, f32[768]{0:T(1024)S(1)}, u32[]{:S(2)}, u32[]{:S(2)}) collective-permute-start(f32[768]{0:T(1024)S(1)} %reduce.11), channel_id=1, source_target_pairs={{0,1},{1,0},{2,3},{3,2},{4,5},{5,4},{6,7},{7,6},{8,9},{9,8},{10,11... | collective-permute-start | bytes 9224 | tf_op jit(solution)/shard_map/ppermute | solution.py:18
  0.8 7.9 %collective-permute-start.9 = (f32[768]{0:T(1024)S(1)}, f32[768]{0:T(1024)S(1)}, u32[]{:S(2)}, u32[]{:S(2)}) collective-permute-start(f32[768]{0:T(1024)S(1)} %reduce.11), channel_id=1, source_target_pairs={{0,2},{1,3},{2,0},{3,1},{4,6},{5,7},{6,4},{7,5},{8,10},{9,11},{10,... | collective-permute-start | bytes 9224 | tf_op jit(solution)/shard_map/ppermute | solution.py:18
  1.7 7.0 %collective-permute-start.10 = (f32[768]{0:T(1024)S(1)}, f32[768]{0:T(1024)S(1)}, u32[]{:S(2)}, u32[]{:S(2)}) collective-permute-start(f32[768]{0:T(1024)S(1)} %reduce.11), channel_id=1, source_target_pairs={{0,3},{1,2},{2,1},{3,0},{4,7},{5,6},{6,5},{7,4},{8,11},{9,10},{10,... | collective-permute-start | bytes 9224 | tf_op jit(solution)/shard_map/ppermute | solution.py:18
  2.7 7.4 %collective-permute-start.7 = (bf16[2,64,768]{2,1,0:T(8,128)(2,1)}, bf16[2,64,768]{2,1,0:T(8,128)(2,1)S(1)}, u32[]{:S(2)}, u32[]{:S(2)}) collective-permute-start(bf16[2,64,768]{2,1,0:T(8,128)(2,1)} %param.12), channel_id=1, source_target_pairs={{0,2},{1,3},{2,0},{3,1},{4,6},{5,7},{6,4},{7,5},{8,10},{9,11},{10,... | collective-permute-start | bytes 589832 | tf_op jit(solution)/shard_map/ppermute | solution.py:18
  39.7 2.1 collective-permute-start
  42.8 11.7 %collective-permute-start.1 = (bf16[8,1,24,1536]{3,2,0,1:T(8,128)(2,1)}, bf16[8,1,24,1536]{3,2,0,1:T(8,128)(2,1)}, u32[]{:S(2)}, u32[]{:S(2)}) collective-permute-start(bf16[8,1,24,1536]{3,2,0,1:T(8,128)(2,1)} %get-tuple-element.556), channel_id=1, source_target_pairs={{0,1},{1,0},{2,3},{3,2},{4,5},{5,4},{6,7},{7,6},{8,9},{9,8},{10,11... | collective-permute-start | bytes 1769480 | tf_op jit(solution)/shard_map/while/body/eval_jaxpr/ppermute | solution.py:18
  54.1 12.9 %collective-permute-start.3 = (bf16[8,1,24,1536]{3,2,0,1:T(8,128)(2,1)}, bf16[8,1,24,1536]{3,2,0,1:T(8,128)(2,1)S(1)}, u32[]{:S(2)}, u32[]{:S(2)}) collective-permute-start(bf16[8,1,24,1536]{3,2,0,1:T(8,128)(2,1)} %broadcast_select_fusion.22), channel_id=1, source_target_pairs={{0,1},{1,0},{2,3},{3,2},{4,5},{5,4},{6,7},{7,6},{8,9},{9,8},{10,11... | collective-permute-start | bytes 1769480 | tf_op jit(solution)/shard_map/while/body/eval_jaxpr/ppermute | solution.py:18
  66.7 2.1 collective-permute-start.2
  70.2 24.0 %all-to-all-start.1 = ((bf16[16,1,24,1536]{3,2,1,0:T(8,128)(2,1)}), bf16[16,1,24,1536]{3,2,1,0:T(8,128)(2,1)S(1)}, u32[]{:S(2)}, u32[]{:S(2)}) async-start(bf16[16,1,24,1536]{3,2,1,0:T(8,128)(2,1)} %maximum_bitcast_fusion.3), calls=%async_computation.1 | async-start | bytes 2359296 | tf_op jit(solution)/shard_map/while/body/eval_jaxpr/all_to_all | solution.py:132
  97.1 4.7 %collective-permute-start.4 = (bf16[64,768]{1,0:T(8,128)(2,1)S(1)}, bf16[64,768]{1,0:T(8,128)(2,1)S(1)}, u32[]{:S(2)}, u32[]{:S(2)}) collective-permute-start(bf16[64,768]{1,0:T(8,128)(2,1)S(1)} %select_convert_fusion.3), channel_id=1, source_target_pairs={{0,2},{1,3},{2,0},{3,1},{4,6},{5,7},{6,4},{7,5},{8,10},{9,11},{10,... | collective-permute-start | bytes 294920 | tf_op jit(solution)/shard_map/while/body/eval_jaxpr/ppermute | solution.py:18
  101.8 7.7 %collective-permute-start.5 = (bf16[64,768]{1,0:T(8,128)(2,1)S(1)}, bf16[64,768]{1,0:T(8,128)(2,1)S(1)}, u32[]{:S(2)}, u32[]{:S(2)}) collective-permute-start(bf16[64,768]{1,0:T(8,128)(2,1)S(1)} %add_convert_fusion.11), channel_id=1, source_target_pairs={{0,66},{1,67},{2,64},{3,65},{4,70},{5,71},{6,68},{7,69},{8,74},{9,... | collective-permute-start | bytes 294920 | tf_op jit(solution)/shard_map/while/body/eval_jaxpr/ppermute | solution.py:154
  103.1 8.0 %collective-permute-start.6 = (bf16[64,768]{1,0:T(8,128)(2,1)S(1)}, bf16[64,768]{1,0:T(8,128)(2,1)S(1)}, u32[]{:S(2)}, u32[]{:S(2)}) collective-permute-start(bf16[64,768]{1,0:T(8,128)(2,1)S(1)} %add_convert_fusion.11), channel_id=1, source_target_pairs={{0,64},{1,65},{2,66},{3,67},{4,68},{5,69},{6,70},{7,71},{8,72},{9,... | collective-permute-start | bytes 294920 | tf_op jit(solution)/shard_map/while/body/eval_jaxpr/ppermute | solution.py:13
  133.1 2.1 collective-permute-start
  136.2 11.7 %collective-permute-start.1 = (bf16[8,1,24,1536]{3,2,0,1:T(8,128)(2,1)}, bf16[8,1,24,1536]{3,2,0,1:T(8,128)(2,1)}, u32[]{:S(2)}, u32[]{:S(2)}) collective-permute-start(bf16[8,1,24,1536]{3,2,0,1:T(8,128)(2,1)} %get-tuple-element.556), channel_id=1, source_target_pairs={{0,1},{1,0},{2,3},{3,2},{4,5},{5,4},{6,7},{7,6},{8,9},{9,8},{10,11... | collective-permute-start | bytes 1769480 | tf_op jit(solution)/shard_map/while/body/eval_jaxpr/ppermute | solution.py:18
  147.5 12.9 %collective-permute-start.3 = (bf16[8,1,24,1536]{3,2,0,1:T(8,128)(2,1)}, bf16[8,1,24,1536]{3,2,0,1:T(8,128)(2,1)S(1)}, u32[]{:S(2)}, u32[]{:S(2)}) collective-permute-start(bf16[8,1,24,1536]{3,2,0,1:T(8,128)(2,1)} %broadcast_select_fusion.22), channel_id=1, source_target_pairs={{0,1},{1,0},{2,3},{3,2},{4,5},{5,4},{6,7},{7,6},{8,9},{9,8},{10,11... | collective-permute-start | bytes 1769480 | tf_op jit(solution)/shard_map/while/body/eval_jaxpr/ppermute | solution.py:18
  160.2 2.1 collective-permute-start.2
  163.7 24.0 %all-to-all-start.1 = ((bf16[16,1,24,1536]{3,2,1,0:T(8,128)(2,1)}), bf16[16,1,24,1536]{3,2,1,0:T(8,128)(2,1)S(1)}, u32[]{:S(2)}, u32[]{:S(2)}) async-start(bf16[16,1,24,1536]{3,2,1,0:T(8,128)(2,1)} %maximum_bitcast_fusion.3), calls=%async_computation.1 | async-start | bytes 2359296 | tf_op jit(solution)/shard_map/while/body/eval_jaxpr/all_to_all | solution.py:132
  190.5 4.7 %collective-permute-start.4 = (bf16[64,768]{1,0:T(8,128)(2,1)S(1)}, bf16[64,768]{1,0:T(8,128)(2,1)S(1)}, u32[]{:S(2)}, u32[]{:S(2)}) collective-permute-start(bf16[64,768]{1,0:T(8,128)(2,1)S(1)} %select_convert_fusion.3), channel_id=1, source_target_pairs={{0,2},{1,3},{2,0},{3,1},{4,6},{5,7},{6,4},{7,5},{8,10},{9,11},{10,... | collective-permute-start | bytes 294920 | tf_op jit(solution)/shard_map/while/body/eval_jaxpr/ppermute | solution.py:18
  195.3 7.7 %collective-permute-start.5 = (bf16[64,768]{1,0:T(8,128)(2,1)S(1)}, bf16[64,768]{1,0:T(8,128)(2,1)S(1)}, u32[]{:S(2)}, u32[]{:S(2)}) collective-permute-start(bf16[64,768]{1,0:T(8,128)(2,1)S(1)} %add_convert_fusion.11), channel_id=1, source_target_pairs={{0,66},{1,67},{2,64},{3,65},{4,70},{5,71},{6,68},{7,69},{8,74},{9,... | collective-permute-start | bytes 294920 | tf_op jit(solution)/shard_map/while/body/eval_jaxpr/ppermute | solution.py:154
  196.6 8.0 %collective-permute-start.6 = (bf16[64,768]{1,0:T(8,128)(2,1)S(1)}, bf16[64,768]{1,0:T(8,128)(2,1)S(1)}, u32[]{:S(2)}, u32[]{:S(2)}) collective-permute-start(bf16[64,768]{1,0:T(8,128)(2,1)S(1)} %add_convert_fusion.11), channel_id=1, source_target_pairs={{0,64},{1,65},{2,66},{3,67},{4,68},{5,69},{6,70},{7,71},{8,72},{9,... | collective-permute-start | bytes 294920 | tf_op jit(solution)/shard_map/while/body/eval_jaxpr/ppermute | solution.py:13
  229.3 11.7 %collective-permute-start.13 = (bf16[8,1,24,1536]{3,2,0,1:T(8,128)(2,1)}, bf16[8,1,24,1536]{3,2,0,1:T(8,128)(2,1)}, u32[]{:S(2)}, u32[]{:S(2)}) collective-permute-start(bf16[8,1,24,1536]{3,2,0,1:T(8,128)(2,1)} %get-tuple-element.405), channel_id=1, source_target_pairs={{0,1},{1,0},{2,3},{3,2},{4,5},{5,4},{6,7},{7,6},{8,9},{9,8},{10,11... | collective-permute-start | bytes 1769480 | tf_op jit(solution)/shard_map/ppermute | solution.py:18
  240.6 13.2 %collective-permute-start.12 = (bf16[8,1,24,1536]{3,2,0,1:T(8,128)(2,1)}, bf16[8,1,24,1536]{3,2,0,1:T(8,128)(2,1)S(1)}, u32[]{:S(2)}, u32[]{:S(2)}) collective-permute-start(bf16[8,1,24,1536]{3,2,0,1:T(8,128)(2,1)} %broadcast_select_fusion.10), channel_id=1, source_target_pairs={{0,1},{1,0},{2,3},{3,2},{4,5},{5,4},{6,7},{7,6},{8,9},{9,8},{10,11... | collective-permute-start | bytes 1769480 | tf_op jit(solution)/shard_map/ppermute | solution.py:18
  257.0 24.0 %all-to-all-start.3 = ((bf16[16,1,24,1536]{3,2,1,0:T(8,128)(2,1)}), bf16[16,1,24,1536]{3,2,1,0:T(8,128)(2,1)S(1)}, u32[]{:S(2)}, u32[]{:S(2)}) async-start(bf16[16,1,24,1536]{3,2,1,0:T(8,128)(2,1)} %maximum_bitcast_fusion.1), calls=%async_computation.3 | async-start | bytes 2359296 | tf_op jit(solution)/shard_map/all_to_all | solution.py:132
  283.9 4.7 %collective-permute-start.15 = (bf16[64,768]{1,0:T(8,128)(2,1)S(1)}, bf16[64,768]{1,0:T(8,128)(2,1)S(1)}, u32[]{:S(2)}, u32[]{:S(2)}) collective-permute-start(bf16[64,768]{1,0:T(8,128)(2,1)S(1)} %select_convert_fusion.1), channel_id=1, source_target_pairs={{0,2},{1,3},{2,0},{3,1},{4,6},{5,7},{6,4},{7,5},{8,10},{9,11},{10,... | collective-permute-start | bytes 294920 | tf_op jit(solution)/shard_map/ppermute | solution.py:18
  (14 other events, 84.0 us)

commit v9 on v6

--- a/solution.py
+++ b/solution.py
@@ -98,16 +98,16 @@
         hi_q = lambda a: a[..., quarter:]
         first = jnp.where(core_first, mine, theirs)
         second = jnp.where(core_first, theirs, mine)
-        rows = jnp.concatenate([lo_q(first), lo_q(second), hi_q(first), hi_q(second)], axis=-1)
+        rows = jnp.concatenate(
+            [lo_q(first), lo_q(second), hi_q(first), hi_q(second)], axis=-1
+        ).reshape(-1, D)
         rf = rows.astype(jnp.float32)
         sums = jnp.sum(rf * rf, axis=-1)
         normed = (rf * lax.rsqrt(sums / D + 1e-05)[..., None] * gain_full).astype(jnp.bfloat16)
-        summed_up = jnp.einsum(
-            "sekd,edf->sekf", normed, up_local, preferred_element_type=jnp.float32
-        )
+        summed_up = jnp.dot(normed, up_local[0], preferred_element_type=jnp.float32)
         hidden = jax.nn.silu(summed_up).astype(jnp.bfloat16)
-        partial_out = jnp.einsum(
-            "sekf,efd->sekd", hidden, down_local, preferred_element_type=jnp.float32
+        partial_out = jnp.dot(
+            hidden, down_local[0], preferred_element_type=jnp.float32
         ).astype(jnp.bfloat16)
         pq = [partial_out[..., q * quarter:(q + 1) * quarter] for q in range(4)]
         keep = jnp.where(
@@ -122,6 +122,7 @@
         )
         got = swap(give, "tensor", 1)
         chip_sum = (keep.astype(jnp.float32) + got.astype(jnp.float32)).astype(jnp.bfloat16)
+        chip_sum = chip_sum.reshape(mine.shape)
         returned = lax.all_to_all(chip_sum, "expert", split_axis=0, concat_axis=0, tiled=True)
         summed = jnp.sum(
             returned.reshape(EXPERTS, copies, capacity, 2 * quarter).astype(jnp.float32), axis=1

time: 246 us -> 256 us (1.041)
  matrix products: 17.9 us -> 33.5 us
  local copies, waits for them, and re-layouts: 17.6 us -> 12.2 us
    dot_general x6, matrix products: 17.9 us -> 33.5 us  [the longest x3 17.2 us: layer_step(): jnp.dot(hidden, down_local[0], preferred_element_type=jnp.float32)]
    while x20 -> x4, local copies, waits for them, and re-layouts: 3.55 us -> 0.01 us
where the time goes in v9:
time: 256 us
  waiting for transfers between devices  105 us (41%)
  blocking collectives  65.6 us (26%)
  matrix products  33.5 us (13%)
  starting transfers between devices  22.6 us (9%)
  other arithmetic  16.1 us (6%)
  local copies, waits for them, and re-layouts  12.2 us (5%)
    all_to_all x3, blocking collectives, layer_step(): lax.all_to_all(outgoing, 'expert', split_axis=0, concat_axis=0, tiled=True)  65.6 us
    all_to_all x3, waiting for transfers between devices, layer_step(): lax.all_to_all(chip_sum, 'expert', split_axis=0, concat_axis=0, tiled=True)  60.6 us
    ppermute x13, waiting for transfers between devices, swap(): return lax.ppermute(block, axis, [(i, i ^ bit) for i in range(n)])  30.9 us
    dot_general x3, matrix products, layer_step(): jnp.dot(hidden, down_local[0], preferred_element_type=jnp.float32)  17.2 us
    dot_general x3, matrix products, layer_step(): summed_up = jnp.dot(normed, up_local[0], preferred_element_type=jnp.float32)  16.3 us
    all_to_all x3, starting transfers between devices, layer_step(): lax.all_to_all(chip_sum, 'expert', split_axis=0, concat_axis=0, tiled=True)  11.5 us
    ppermute x2, waiting for transfers between devices, looped(): lax.ppermute(produced, ('section', 'tensor'), cross_route)  10 us
    ppermute x13, starting transfers between devices, swap(): return lax.ppermute(block, axis, [(i, i ^ bit) for i in range(n)])  5.98 us
  transfers between devices with their start and end apart: 20, of which 17 were waited for; matrix products, arithmetic and copies ran while one was open for 2% of the time, Pallas kernels for 0%

profile of v9, /device:TPU:6, one launch (start us, length us, event | category | flops | bytes accessed | tf_op | source)
XLA Modules:
  0.0 255.5 jit_solution(13862384583276511403)
XLA Ops:
  11.2 170.8 %while.17 = (s32[]{:T(128)}, bf16[64,1536]{1,0:T(8,128)(2,1)S(1)}, bf16[2,64,768]{2,1,0:T(8,128)(2,1)S(1)}, pred[]{:T(512)}, pred[]{:T(512)}, /*index=5*/bf16[2,...) while((s32[]{:T(128)}, bf16[64,1536]{1,0:T(8,128)(2,1)S(1)}, ...), condition=%wide.region_8.11_spmd.clone, body=%wide.region_4.10_spmd.clone.sunk | while | flops 4877554688 | bytes 76723232 | solution.py:153
  12.6 26.1 %all_to_all.35 = bf16[16,1,24,1536]{3,2,1,0:T(8,128)(2,1)S(1)} all-to-all(bf16[16,1,24,1536]{3,2,1,0:T(8,128)(2,1)S(1)} %bitcast.110), channel_id=1, replica_groups=mesh['section'=2,'expert'=16,'tensor'=4] {'expert'}, dimensions={0} | all-to-all | bytes 2359296 | tf_op jit(solution)/shard_map/while/body/eval_jaxpr/all_to_all | solution.py:95
  38.7 2.8 %collective-permute-done = bf16[16,1,24,1536]{3,2,1,0:T(8,128)(2,1)S(1)} collective-permute-done((bf16[16,1,24,1536]{3,2,1,0:T(8,128)(2,1)S(1)}, bf16[16,1,24,1536]{3,2,1,0:T(8,128)(2,1)S(1)}, u32[]{:S(2)}, u32[]{:S(2)}) %collective-permute-start) | collective-permute-done | bytes 1179680 | tf_op jit(solution)/shard_map/while/body/eval_jaxpr/ppermute | solution.py:18
  42.7 5.4 %fusion.65 = f32[384,1024]{1,0:T(8,128)S(1)} fusion(bf16[1,1,3072,1024]{3,2,1,0:T(8,128)(2,1)} %get-tuple-element.543, bf16[384,768]{1,0:T(8,128)(2,1)S(1)} %bitcast.113, bf16[384,768]{1,0:T(8,128)(2,1)S(1)} %bitcast.112, bf16[384,768]{1,0:T(8,128)(2,1)S(1)} %bitcast.114, bf16[384,768]{1,0:T(8,128)(2,1)S(1)} %bitcast.111, ...), kind=kOutput, calls=%fused_computation.8.clone.1 | convolution fusion | flops 2428895232 | bytes 10237440 | tf_op jit(solution)/shard_map/while/body/eval_jaxpr/dot_general | solution.py:107
  48.1 5.7 %fusion.66 = bf16[384,3072]{1,0:T(8,128)(2,1)S(1)} fusion(bf16[1,1,1024,3072]{3,2,1,0:T(8,128)(2,1)} %get-tuple-element.544, f32[384,1024]{1,0:T(8,128)S(1)} %fusion.65), kind=kOutput, calls=%fused_computation.12.clone.1 | convolution fusion | flops 2419064832 | bytes 10223616 | tf_op jit(solution)/shard_map/while/body/eval_jaxpr/dot_general | solution.py:109
  58.6 3.8 %all-to-all-start.1 = ((bf16[16,1,24,1536]{3,2,1,0:T(8,128)(2,1)}), bf16[16,1,24,1536]{3,2,1,0:T(8,128)(2,1)S(1)}, u32[]{:S(2)}, u32[]{:S(2)}) async-start(bf16[16,1,24,1536]{3,2,1,0:T(8,128)(2,1)} %bitcast.105), calls=%async_computation.1 | async-start | bytes 2359296 | tf_op jit(solution)/shard_map/while/body/eval_jaxpr/all_to_all | solution.py:126
  62.6 20.2 %all-to-all-done.1 = bf16[16,1,24,1536]{3,2,1,0:T(8,128)(2,1)S(1)} async-done(((bf16[16,1,24,1536]{3,2,1,0:T(8,128)(2,1)}), bf16[16,1,24,1536]{3,2,1,0:T(8,128)(2,1)S(1)}, u32[]{:S(2)}, u32[]{:S(2)}) %all-to-all-start.1) | async-done | bytes 1179680 | tf_op jit(solution)/shard_map/while/body/eval_jaxpr/all_to_all | solution.py:126
  86.5 3.8 %collective-permute-done.2 = bf16[64,768]{1,0:T(8,128)(2,1)S(1)} collective-permute-done((bf16[64,768]{1,0:T(8,128)(2,1)S(1)}, bf16[64,768]{1,0:T(8,128)(2,1)S(1)}, u32[]{:S(2)}, u32[]{:S(2)}) %collective-permute-start.2) | collective-permute-done | bytes 98336 | tf_op jit(solution)/shard_map/while/body/eval_jaxpr/ppermute | solution.py:18
  93.1 5.0 %collective-permute-done.3 = bf16[64,768]{1,0:T(8,128)(2,1)S(1)} collective-permute-done((bf16[64,768]{1,0:T(8,128)(2,1)S(1)}, bf16[64,768]{1,0:T(8,128)(2,1)S(1)}, u32[]{:S(2)}, u32[]{:S(2)}) %collective-permute-start.3) | collective-permute-done | bytes 98336 | tf_op jit(solution)/shard_map/while/body/eval_jaxpr/ppermute | solution.py:148
  101.2 19.7 %all_to_all.35 = bf16[16,1,24,1536]{3,2,1,0:T(8,128)(2,1)S(1)} all-to-all(bf16[16,1,24,1536]{3,2,1,0:T(8,128)(2,1)S(1)} %bitcast.110), channel_id=1, replica_groups=mesh['section'=2,'expert'=16,'tensor'=4] {'expert'}, dimensions={0} | all-to-all | bytes 2359296 | tf_op jit(solution)/shard_map/while/body/eval_jaxpr/all_to_all | solution.py:95
  121.0 2.8 %collective-permute-done = bf16[16,1,24,1536]{3,2,1,0:T(8,128)(2,1)S(1)} collective-permute-done((bf16[16,1,24,1536]{3,2,1,0:T(8,128)(2,1)S(1)}, bf16[16,1,24,1536]{3,2,1,0:T(8,128)(2,1)S(1)}, u32[]{:S(2)}, u32[]{:S(2)}) %collective-permute-start) | collective-permute-done | bytes 1179680 | tf_op jit(solution)/shard_map/while/body/eval_jaxpr/ppermute | solution.py:18
  124.9 5.4 %fusion.65 = f32[384,1024]{1,0:T(8,128)S(1)} fusion(bf16[1,1,3072,1024]{3,2,1,0:T(8,128)(2,1)} %get-tuple-element.543, bf16[384,768]{1,0:T(8,128)(2,1)S(1)} %bitcast.113, bf16[384,768]{1,0:T(8,128)(2,1)S(1)} %bitcast.112, bf16[384,768]{1,0:T(8,128)(2,1)S(1)} %bitcast.114, bf16[384,768]{1,0:T(8,128)(2,1)S(1)} %bitcast.111, ...), kind=kOutput, calls=%fused_computation.8.clone.1 | convolution fusion | flops 2428895232 | bytes 10237440 | tf_op jit(solution)/shard_map/while/body/eval_jaxpr/dot_general | solution.py:107
  130.3 5.7 %fusion.66 = bf16[384,3072]{1,0:T(8,128)(2,1)S(1)} fusion(bf16[1,1,1024,3072]{3,2,1,0:T(8,128)(2,1)} %get-tuple-element.544, f32[384,1024]{1,0:T(8,128)S(1)} %fusion.65), kind=kOutput, calls=%fused_computation.12.clone.1 | convolution fusion | flops 2419064832 | bytes 10223616 | tf_op jit(solution)/shard_map/while/body/eval_jaxpr/dot_general | solution.py:109
  140.9 3.8 %all-to-all-start.1 = ((bf16[16,1,24,1536]{3,2,1,0:T(8,128)(2,1)}), bf16[16,1,24,1536]{3,2,1,0:T(8,128)(2,1)S(1)}, u32[]{:S(2)}, u32[]{:S(2)}) async-start(bf16[16,1,24,1536]{3,2,1,0:T(8,128)(2,1)} %bitcast.105), calls=%async_computation.1 | async-start | bytes 2359296 | tf_op jit(solution)/shard_map/while/body/eval_jaxpr/all_to_all | solution.py:126
  144.9 20.2 %all-to-all-done.1 = bf16[16,1,24,1536]{3,2,1,0:T(8,128)(2,1)S(1)} async-done(((bf16[16,1,24,1536]{3,2,1,0:T(8,128)(2,1)}), bf16[16,1,24,1536]{3,2,1,0:T(8,128)(2,1)S(1)}, u32[]{:S(2)}, u32[]{:S(2)}) %all-to-all-start.1) | async-done | bytes 1179680 | tf_op jit(solution)/shard_map/while/body/eval_jaxpr/all_to_all | solution.py:126
  168.7 3.8 %collective-permute-done.2 = bf16[64,768]{1,0:T(8,128)(2,1)S(1)} collective-permute-done((bf16[64,768]{1,0:T(8,128)(2,1)S(1)}, bf16[64,768]{1,0:T(8,128)(2,1)S(1)}, u32[]{:S(2)}, u32[]{:S(2)}) %collective-permute-start.2) | collective-permute-done | bytes 98336 | tf_op jit(solution)/shard_map/while/body/eval_jaxpr/ppermute | solution.py:18
  175.3 5.0 %collective-permute-done.3 = bf16[64,768]{1,0:T(8,128)(2,1)S(1)} collective-permute-done((bf16[64,768]{1,0:T(8,128)(2,1)S(1)}, bf16[64,768]{1,0:T(8,128)(2,1)S(1)}, u32[]{:S(2)}, u32[]{:S(2)}) %collective-permute-start.3) | collective-permute-done | bytes 98336 | tf_op jit(solution)/shard_map/while/body/eval_jaxpr/ppermute | solution.py:148
  183.3 19.7 %all_to_all.34 = bf16[16,1,24,1536]{3,2,1,0:T(8,128)(2,1)S(1)} all-to-all(bf16[16,1,24,1536]{3,2,1,0:T(8,128)(2,1)S(1)} %bitcast.118), channel_id=1, replica_groups=mesh['section'=2,'expert'=16,'tensor'=4] {'expert'}, dimensions={0} | all-to-all | bytes 2359296 | tf_op jit(solution)/shard_map/all_to_all | solution.py:95
  203.1 2.8 %collective-permute-done.9 = bf16[16,1,24,1536]{3,2,1,0:T(8,128)(2,1)S(1)} collective-permute-done((bf16[16,1,24,1536]{3,2,1,0:T(8,128)(2,1)S(1)}, bf16[16,1,24,1536]{3,2,1,0:T(8,128)(2,1)S(1)}, u32[]{:S(2)}, u32[]{:S(2)}) %collective-permute-start.9) | collective-permute-done | bytes 1179680 | tf_op jit(solution)/shard_map/ppermute | solution.py:18
  207.0 5.4 %fusion.22 = f32[384,1024]{1,0:T(8,128)S(1)} fusion(bf16[1,1,3072,1024]{3,2,1,0:T(8,128)(2,1)} %get-tuple-element.580, bf16[384,768]{1,0:T(8,128)(2,1)S(1)} %bitcast.121, bf16[384,768]{1,0:T(8,128)(2,1)S(1)} %bitcast.120, bf16[384,768]{1,0:T(8,128)(2,1)S(1)} %bitcast.122, bf16[384,768]{1,0:T(8,128)(2,1)S(1)} %bitcast.119, f32[3072]{0:T(1024)S(1)} %get-tuple-element.576, ...), kind=kOutput, calls=%fused_computation.58 | convolution fusion | flops 2428895232 | bytes 10237440 | tf_op jit(solution)/shard_map/dot_general | solution.py:107
  212.5 5.7 %fusion.24 = bf16[384,3072]{1,0:T(8,128)(2,1)S(1)} fusion(bf16[1,1,1024,3072]{3,2,1,0:T(8,128)(2,1)} %get-tuple-element.581, f32[384,1024]{1,0:T(8,128)S(1)} %fusion.22), kind=kOutput, calls=%fused_computation.62 | convolution fusion | flops 2419064832 | bytes 10223616 | tf_op jit(solution)/shard_map/dot_general | solution.py:109
  223.0 3.8 %all-to-all-start.3 = ((bf16[16,1,24,1536]{3,2,1,0:T(8,128)(2,1)}), bf16[16,1,24,1536]{3,2,1,0:T(8,128)(2,1)S(1)}, u32[]{:S(2)}, u32[]{:S(2)}) async-start(bf16[16,1,24,1536]{3,2,1,0:T(8,128)(2,1)} %bitcast.18), calls=%async_computation.3 | async-start | bytes 2359296 | tf_op jit(solution)/shard_map/all_to_all | solution.py:126
  227.0 20.2 %all-to-all-done.3 = bf16[16,1,24,1536]{3,2,1,0:T(8,128)(2,1)S(1)} async-done(((bf16[16,1,24,1536]{3,2,1,0:T(8,128)(2,1)}), bf16[16,1,24,1536]{3,2,1,0:T(8,128)(2,1)S(1)}, u32[]{:S(2)}, u32[]{:S(2)}) %all-to-all-start.3) | async-done | bytes 1179680 | tf_op jit(solution)/shard_map/all_to_all | solution.py:126
  250.8 3.9 %collective-permute-done.11 = bf16[64,768]{1,0:T(8,128)(2,1)S(1)} collective-permute-done((bf16[64,768]{1,0:T(8,128)(2,1)S(1)}, bf16[64,768]{1,0:T(8,128)(2,1)S(1)}, u32[]{:S(2)}, u32[]{:S(2)}) %collective-permute-start.11) | collective-permute-done | bytes 98336 | tf_op jit(solution)/shard_map/ppermute | solution.py:18
  (141 shorter events, 53.5 us)
Async XLA Ops:
  0.7 6.6 %collective-permute-start.6 = (f32[768]{0:T(1024)S(1)}, f32[768]{0:T(1024)S(1)}, u32[]{:S(2)}, u32[]{:S(2)}) collective-permute-start(f32[768]{0:T(1024)S(1)} %reduce.8), channel_id=1, source_target_pairs={{0,1},{1,0},{2,3},{3,2},{4,5},{5,4},{6,7},{7,6},{8,9},{9,8},{10,11... | collective-permute-start | bytes 9224 | tf_op jit(solution)/shard_map/ppermute | solution.py:18
  0.8 6.5 %collective-permute-start.7 = (f32[768]{0:T(1024)S(1)}, f32[768]{0:T(1024)S(1)}, u32[]{:S(2)}, u32[]{:S(2)}) collective-permute-start(f32[768]{0:T(1024)S(1)} %reduce.8), channel_id=1, source_target_pairs={{0,2},{1,3},{2,0},{3,1},{4,6},{5,7},{6,4},{7,5},{8,10},{9,11},{10,... | collective-permute-start | bytes 9224 | tf_op jit(solution)/shard_map/ppermute | solution.py:18
  1.7 5.6 %collective-permute-start.8 = (f32[768]{0:T(1024)S(1)}, f32[768]{0:T(1024)S(1)}, u32[]{:S(2)}, u32[]{:S(2)}) collective-permute-start(f32[768]{0:T(1024)S(1)} %reduce.8), channel_id=1, source_target_pairs={{0,3},{1,2},{2,1},{3,0},{4,7},{5,6},{6,5},{7,4},{8,11},{9,10},{10,... | collective-permute-start | bytes 9224 | tf_op jit(solution)/shard_map/ppermute | solution.py:18
  2.6 7.4 %collective-permute-start.5 = (bf16[2,64,768]{2,1,0:T(8,128)(2,1)}, bf16[2,64,768]{2,1,0:T(8,128)(2,1)S(1)}, u32[]{:S(2)}, u32[]{:S(2)}) collective-permute-start(bf16[2,64,768]{2,1,0:T(8,128)(2,1)} %param.12), channel_id=1, source_target_pairs={{0,2},{1,3},{2,0},{3,1},{4,6},{5,7},{6,4},{7,5},{8,10},{9,11},{10,... | collective-permute-start | bytes 589832 | tf_op jit(solution)/shard_map/ppermute | solution.py:18
  38.7 2.8 %collective-permute-start = (bf16[16,1,24,1536]{3,2,1,0:T(8,128)(2,1)S(1)}, bf16[16,1,24,1536]{3,2,1,0:T(8,128)(2,1)S(1)}, u32[]{:S(2)}, u32[]{:S(2)}) collective-permute-start(bf16[16,1,24,1536]{3,2,1,0:T(8,128)(2,1)S(1)} %all_to_all.35), channel_id=1, source_target_pairs={{0,1},{1,0},{2,3},{3,2},{4,5},{5,4},{6,7},{7,6},{8,9},{9,8},{10,11... | collective-permute-start | bytes 3538952 | tf_op jit(solution)/shard_map/while/body/eval_jaxpr/ppermute | solution.py:18
  54.3 2.9 %collective-permute-start.1 = (bf16[384,1536]{1,0:T(8,128)(2,1)S(1)}, bf16[384,1536]{1,0:T(8,128)(2,1)S(1)}, u32[]{:S(2)}, u32[]{:S(2)}) collective-permute-start(bf16[384,1536]{1,0:T(8,128)(2,1)S(1)} %broadcast_select_fusion.12), channel_id=1, source_target_pairs={{0,1},{1,0},{2,3},{3,2},{4,5},{5,4},{6,7},{7,6},{8,9},{9,8},{10,11... | collective-permute-start | bytes 3538952 | tf_op jit(solution)/shard_map/while/body/eval_jaxpr/ppermute | solution.py:18
  58.6 3.8 %copy-start = (f32[1,2,64,2]{2,3,1,0:T(2,128)S(1)}, f32[1,2,64,2]{2,3,1,0:T(2,128)}, u32[]{:S(2)}) copy-start(f32[1,2,64,2]{2,3,1,0:T(2,128)} %get-tuple-element.546) | copy-start | bytes 3076 | tf_op jit(solution)/shard_map/while
  58.6 24.2 %all-to-all-start.1 = ((bf16[16,1,24,1536]{3,2,1,0:T(8,128)(2,1)}), bf16[16,1,24,1536]{3,2,1,0:T(8,128)(2,1)S(1)}, u32[]{:S(2)}, u32[]{:S(2)}) async-start(bf16[16,1,24,1536]{3,2,1,0:T(8,128)(2,1)} %bitcast.105), calls=%async_computation.1 | async-start | bytes 2359296 | tf_op jit(solution)/shard_map/while/body/eval_jaxpr/all_to_all | solution.py:126
  85.6 4.7 %collective-permute-start.2 = (bf16[64,768]{1,0:T(8,128)(2,1)S(1)}, bf16[64,768]{1,0:T(8,128)(2,1)S(1)}, u32[]{:S(2)}, u32[]{:S(2)}) collective-permute-start(bf16[64,768]{1,0:T(8,128)(2,1)S(1)} %select_convert_fusion.3), channel_id=1, source_target_pairs={{0,2},{1,3},{2,0},{3,1},{4,6},{5,7},{6,4},{7,5},{8,10},{9,11},{10,... | collective-permute-start | bytes 294920 | tf_op jit(solution)/shard_map/while/body/eval_jaxpr/ppermute | solution.py:18
  90.4 7.7 %collective-permute-start.3 = (bf16[64,768]{1,0:T(8,128)(2,1)S(1)}, bf16[64,768]{1,0:T(8,128)(2,1)S(1)}, u32[]{:S(2)}, u32[]{:S(2)}) collective-permute-start(bf16[64,768]{1,0:T(8,128)(2,1)S(1)} %add_convert_fusion.7), channel_id=1, source_target_pairs={{0,66},{1,67},{2,64},{3,65},{4,70},{5,71},{6,68},{7,69},{8,74},{9,... | collective-permute-start | bytes 294920 | tf_op jit(solution)/shard_map/while/body/eval_jaxpr/ppermute | solution.py:148
  91.7 8.0 %collective-permute-start.4 = (bf16[64,768]{1,0:T(8,128)(2,1)S(1)}, bf16[64,768]{1,0:T(8,128)(2,1)S(1)}, u32[]{:S(2)}, u32[]{:S(2)}) collective-permute-start(bf16[64,768]{1,0:T(8,128)(2,1)S(1)} %add_convert_fusion.7), channel_id=1, source_target_pairs={{0,64},{1,65},{2,66},{3,67},{4,68},{5,69},{6,70},{7,71},{8,72},{9,... | collective-permute-start | bytes 294920 | tf_op jit(solution)/shard_map/while/body/eval_jaxpr/ppermute | solution.py:13
  121.0 2.8 %collective-permute-start = (bf16[16,1,24,1536]{3,2,1,0:T(8,128)(2,1)S(1)}, bf16[16,1,24,1536]{3,2,1,0:T(8,128)(2,1)S(1)}, u32[]{:S(2)}, u32[]{:S(2)}) collective-permute-start(bf16[16,1,24,1536]{3,2,1,0:T(8,128)(2,1)S(1)} %all_to_all.35), channel_id=1, source_target_pairs={{0,1},{1,0},{2,3},{3,2},{4,5},{5,4},{6,7},{7,6},{8,9},{9,8},{10,11... | collective-permute-start | bytes 3538952 | tf_op jit(solution)/shard_map/while/body/eval_jaxpr/ppermute | solution.py:18
  136.5 2.9 %collective-permute-start.1 = (bf16[384,1536]{1,0:T(8,128)(2,1)S(1)}, bf16[384,1536]{1,0:T(8,128)(2,1)S(1)}, u32[]{:S(2)}, u32[]{:S(2)}) collective-permute-start(bf16[384,1536]{1,0:T(8,128)(2,1)S(1)} %broadcast_select_fusion.12), channel_id=1, source_target_pairs={{0,1},{1,0},{2,3},{3,2},{4,5},{5,4},{6,7},{7,6},{8,9},{9,8},{10,11... | collective-permute-start | bytes 3538952 | tf_op jit(solution)/shard_map/while/body/eval_jaxpr/ppermute | solution.py:18
  140.9 3.8 %copy-start = (f32[1,2,64,2]{2,3,1,0:T(2,128)S(1)}, f32[1,2,64,2]{2,3,1,0:T(2,128)}, u32[]{:S(2)}) copy-start(f32[1,2,64,2]{2,3,1,0:T(2,128)} %get-tuple-element.546) | copy-start | bytes 3076 | tf_op jit(solution)/shard_map/while
  140.9 24.2 %all-to-all-start.1 = ((bf16[16,1,24,1536]{3,2,1,0:T(8,128)(2,1)}), bf16[16,1,24,1536]{3,2,1,0:T(8,128)(2,1)S(1)}, u32[]{:S(2)}, u32[]{:S(2)}) async-start(bf16[16,1,24,1536]{3,2,1,0:T(8,128)(2,1)} %bitcast.105), calls=%async_computation.1 | async-start | bytes 2359296 | tf_op jit(solution)/shard_map/while/body/eval_jaxpr/all_to_all | solution.py:126
  167.8 4.7 %collective-permute-start.2 = (bf16[64,768]{1,0:T(8,128)(2,1)S(1)}, bf16[64,768]{1,0:T(8,128)(2,1)S(1)}, u32[]{:S(2)}, u32[]{:S(2)}) collective-permute-start(bf16[64,768]{1,0:T(8,128)(2,1)S(1)} %select_convert_fusion.3), channel_id=1, source_target_pairs={{0,2},{1,3},{2,0},{3,1},{4,6},{5,7},{6,4},{7,5},{8,10},{9,11},{10,... | collective-permute-start | bytes 294920 | tf_op jit(solution)/shard_map/while/body/eval_jaxpr/ppermute | solution.py:18
  172.6 7.7 %collective-permute-start.3 = (bf16[64,768]{1,0:T(8,128)(2,1)S(1)}, bf16[64,768]{1,0:T(8,128)(2,1)S(1)}, u32[]{:S(2)}, u32[]{:S(2)}) collective-permute-start(bf16[64,768]{1,0:T(8,128)(2,1)S(1)} %add_convert_fusion.7), channel_id=1, source_target_pairs={{0,66},{1,67},{2,64},{3,65},{4,70},{5,71},{6,68},{7,69},{8,74},{9,... | collective-permute-start | bytes 294920 | tf_op jit(solution)/shard_map/while/body/eval_jaxpr/ppermute | solution.py:148
  173.9 8.0 %collective-permute-start.4 = (bf16[64,768]{1,0:T(8,128)(2,1)S(1)}, bf16[64,768]{1,0:T(8,128)(2,1)S(1)}, u32[]{:S(2)}, u32[]{:S(2)}) collective-permute-start(bf16[64,768]{1,0:T(8,128)(2,1)S(1)} %add_convert_fusion.7), channel_id=1, source_target_pairs={{0,64},{1,65},{2,66},{3,67},{4,68},{5,69},{6,70},{7,71},{8,72},{9,... | collective-permute-start | bytes 294920 | tf_op jit(solution)/shard_map/while/body/eval_jaxpr/ppermute | solution.py:13
  203.1 2.8 %collective-permute-start.9 = (bf16[16,1,24,1536]{3,2,1,0:T(8,128)(2,1)S(1)}, bf16[16,1,24,1536]{3,2,1,0:T(8,128)(2,1)S(1)}, u32[]{:S(2)}, u32[]{:S(2)}) collective-permute-start(bf16[16,1,24,1536]{3,2,1,0:T(8,128)(2,1)S(1)} %all_to_all.34), channel_id=1, source_target_pairs={{0,1},{1,0},{2,3},{3,2},{4,5},{5,4},{6,7},{7,6},{8,9},{9,8},{10,11... | collective-permute-start | bytes 3538952 | tf_op jit(solution)/shard_map/ppermute | solution.py:18
  218.7 2.9 %collective-permute-start.10 = (bf16[384,1536]{1,0:T(8,128)(2,1)S(1)}, bf16[384,1536]{1,0:T(8,128)(2,1)S(1)}, u32[]{:S(2)}, u32[]{:S(2)}) collective-permute-start(bf16[384,1536]{1,0:T(8,128)(2,1)S(1)} %broadcast_select_fusion.6), channel_id=1, source_target_pairs={{0,1},{1,0},{2,3},{3,2},{4,5},{5,4},{6,7},{7,6},{8,9},{9,8},{10,11... | collective-permute-start | bytes 3538952 | tf_op jit(solution)/shard_map/ppermute | solution.py:18
  223.0 3.8 %copy-start.1 = (f32[1,2,64,2]{2,3,1,0:T(2,128)S(1)}, f32[1,2,64,2]{2,3,1,0:T(2,128)}, u32[]{:S(2)}) copy-start(f32[1,2,64,2]{2,3,1,0:T(2,128)} %get-tuple-element.572) | copy-start | bytes 3076
  223.0 24.2 %all-to-all-start.3 = ((bf16[16,1,24,1536]{3,2,1,0:T(8,128)(2,1)}), bf16[16,1,24,1536]{3,2,1,0:T(8,128)(2,1)S(1)}, u32[]{:S(2)}, u32[]{:S(2)}) async-start(bf16[16,1,24,1536]{3,2,1,0:T(8,128)(2,1)} %bitcast.18), calls=%async_computation.3 | async-start | bytes 2359296 | tf_op jit(solution)/shard_map/all_to_all | solution.py:126
  250.0 4.7 %collective-permute-start.11 = (bf16[64,768]{1,0:T(8,128)(2,1)S(1)}, bf16[64,768]{1,0:T(8,128)(2,1)S(1)}, u32[]{:S(2)}, u32[]{:S(2)}) collective-permute-start(bf16[64,768]{1,0:T(8,128)(2,1)S(1)} %select_convert_fusion.1), channel_id=1, source_target_pairs={{0,2},{1,3},{2,0},{3,1},{4,6},{5,7},{6,4},{7,5},{8,10},{9,11},{10,... | collective-permute-start | bytes 294920 | tf_op jit(solution)/shard_map/ppermute | solution.py:18

commit v10 on v5

--- a/solution.py
+++ b/solution.py
@@ -55,7 +55,9 @@
             jnp.concatenate([other, own], axis=-1),
         )
 
-    tokens_half = to_half(tokens, swap(tokens, "tensor", 2))
+    tokens_half = jnp.stack(
+        [to_half(tokens[m], swap(tokens[m], "tensor", 2)) for m in range(micro)]
+    )
     routes_all = expert_ids[0].reshape(micro, -1)
     onehot_all = (routes_all[..., None] == jnp.arange(EXPERTS, dtype=jnp.int32)).astype(jnp.int32)
     slot_all = jnp.sum((jnp.cumsum(onehot_all, axis=1) - onehot_all) * onehot_all, axis=2)
@@ -131,7 +133,7 @@
         y_half = jnp.sum(picked * weights[:, :, None], axis=1)
         y_keep = jnp.where(x_first, y_half[:, :quarter], y_half[:, quarter:])
         y_give = jnp.where(x_first, y_half[:, quarter:], y_half[:, :quarter])
-        y_got = swap(y_give, "tensor", 2)
+        y_got = swap(y_give.astype(jnp.bfloat16), "tensor", 2).astype(jnp.float32)
         xf = jnp.where(x_first, half_rows[:, :quarter], half_rows[:, quarter:]).astype(jnp.float32)
         mixed = xf + (y_keep + y_got)
         produced = mixed.astype(jnp.bfloat16)

time: 251 us -> 251 us (level)
  waiting for transfers between devices: 107 us -> 104 us
    ppermute x13 -> x14, starting transfers between devices: 5.89 us -> 8.62 us  [swap(): return lax.ppermute(block, axis, [(i, i ^ bit) for i in range(n)])]
    ppermute x13 -> x14, waiting for transfers between devices: 32.7 us -> 30.6 us  [swap(): return lax.ppermute(block, axis, [(i, i ^ bit) for i in range(n)])]
  transfers between devices with their start and end apart: 20 -> 21, of which waited for: 17 -> 17; matrix products, arithmetic and copies ran while one was open for 2% -> 3% of each run, Pallas kernels for 0% -> 0%
where the time goes in v10:
time: 251 us; the launch traced here: 250 us
  waiting for transfers between devices  104 us (41%)
  blocking collectives  65.3 us (26%)
  starting transfers between devices  24.9 us (10%)
  local copies, waits for them, and re-layouts  19.9 us (8%)
  other arithmetic  17.9 us (7%)
  matrix products  16.9 us (7%)
    all_to_all x3, blocking collectives, layer_step(): lax.all_to_all(outgoing, 'expert', split_axis=0, concat_axis=0, tiled=True)  65.3 us
    all_to_all x3, waiting for transfers between devices, layer_step(): lax.all_to_all(chip_sum, 'expert', split_axis=0, concat_axis=0, tiled=True)  60.6 us
    ppermute x14, waiting for transfers between devices, swap(): return lax.ppermute(block, axis, [(i, i ^ bit) for i in range(n)])  30.6 us
    all_to_all x3, starting transfers between devices, layer_step(): lax.all_to_all(chip_sum, 'expert', split_axis=0, concat_axis=0, tiled=True)  11.1 us
    ppermute x2, waiting for transfers between devices, looped(): lax.ppermute(produced, ('section', 'tensor'), cross_route)  10 us
    dot_general x3, matrix products, layer_step(): jnp.einsum('sekd,edf->sekf', normed, up_local, preferred_element_type=jnp...  8.63 us
    ppermute x14, starting transfers between devices, swap(): return lax.ppermute(block, axis, [(i, i ^ bit) for i in range(n)])  8.62 us
    dot_general x3, matrix products, layer_step(): jnp.einsum('sekf,efd->sekd', hidden, down_local, preferred_element_type=j...  8.29 us
  transfers between devices with their start and end apart: 21, of which 17 were waited for; matrix products, arithmetic and copies ran while one was open for 3% of the time, Pallas kernels for 0%

profile of v10, /device:TPU:6, one launch (start us, length us, event | category | flops | bytes accessed | tf_op | source)
XLA Modules:
  0.0 250.2 jit_solution(8942413128797960636)
XLA Ops:
  11.3 3.5 %collective-permute-done.5 = bf16[64,768]{1,0:T(8,128)(2,1)S(1)} collective-permute-done((bf16[64,768]{1,0:T(8,128)(2,1)S(1)}, bf16[64,768]{1,0:T(8,128)(2,1)S(1)}, u32[]{:S(2)}, u32[]{:S(2)}) %collective-permute-start.5) | collective-permute-done | bytes 98336 | tf_op jit(solution)/shard_map/ppermute | solution.py:18
  15.4 163.6 %while.17 = (s32[]{:T(128)}, bf16[64,1536]{1,0:T(8,128)(2,1)S(1)}, bf16[2,64,768]{2,1,0:T(8,128)(2,1)S(1)}, pred[]{:T(512)}, pred[]{:T(512)}, /*index=5*/bf16[2,...) while((s32[]{:T(128)}, bf16[64,1536]{1,0:T(8,128)(2,1)S(1)}, ...), condition=%wide.region_8.11_spmd.clone, body=%wide.region_4.10_spmd.clone.sunk | while | flops 4872246272 | bytes 128620640 | solution.py:154
  16.8 25.9 %all_to_all.35 = bf16[16,1,24,1536]{3,2,1,0:T(8,128)(2,1)S(1)} all-to-all(bf16[16,1,24,1536]{3,2,1,0:T(8,128)(2,1)S(1)} %bitcast.197), channel_id=1, replica_groups=mesh['section'=2,'expert'=16,'tensor'=4] {'expert'}, dimensions={0} | all-to-all | bytes 2359296 | tf_op jit(solution)/shard_map/while/body/eval_jaxpr/all_to_all | solution.py:97
  42.7 2.8 %collective-permute-done = bf16[16,1,24,1536]{3,2,0,1:T(8,128)(2,1)S(1)} collective-permute-done((bf16[16,1,24,1536]{3,2,0,1:T(8,128)(2,1)S(1)}, bf16[16,1,24,1536]{3,2,0,1:T(8,128)(2,1)S(1)}, u32[]{:S(2)}, u32[]{:S(2)}) %collective-permute-start) | collective-permute-done | bytes 1179680 | tf_op jit(solution)/shard_map/while/body/eval_jaxpr/ppermute | solution.py:18
  48.5 2.9 %fusion.81 = f32[16,24,1024]{2,1,0:T(8,128)S(1)} fusion(bf16[1,3072,1024]{2,1,0:T(8,128)(2,1)S(1)} %bitcast.216, bf16[16,24,768]{2,1,0:T(8,128)(2,1)S(1)} %get-tuple-element.509, bf16[16,24,768]{2,1,0:T(8,128)(2,1)S(1)} %get-tuple-element.510, bf16[16,24,768]{2,1,0:T(8,128)(2,1)S(1)} %get-tuple-element.511, ...), kind=kOutput, calls=%fused_computation.8.clone.1 | convolution fusion | flops 2428895232 | bytes 10237440 | tf_op jit(solution)/shard_map/while/body/eval_jaxpr/sekd,edf->sekf/dot_general | solution.py:107
  59.2 3.7 %all-to-all-start.1 = ((bf16[16,1,24,1536]{3,2,1,0:T(8,128)(2,1)}), bf16[16,1,24,1536]{3,2,1,0:T(8,128)(2,1)S(1)}, u32[]{:S(2)}, u32[]{:S(2)}) async-start(bf16[16,1,24,1536]{3,2,1,0:T(8,128)(2,1)} %fusion.84), calls=%async_computation.1 | async-start | bytes 2359296 | tf_op jit(solution)/shard_map/while/body/eval_jaxpr/all_to_all | solution.py:127
  63.1 20.2 %all-to-all-done.1 = bf16[16,1,24,1536]{3,2,1,0:T(8,128)(2,1)S(1)} async-done(((bf16[16,1,24,1536]{3,2,1,0:T(8,128)(2,1)}), bf16[16,1,24,1536]{3,2,1,0:T(8,128)(2,1)S(1)}, u32[]{:S(2)}, u32[]{:S(2)}) %all-to-all-start.1) | async-done | bytes 1179680 | tf_op jit(solution)/shard_map/while/body/eval_jaxpr/all_to_all | solution.py:127
  87.4 3.4 %collective-permute-done.2 = bf16[64,768]{1,0:T(8,128)(2,1)S(1)} collective-permute-done((bf16[64,768]{1,0:T(8,128)(2,1)S(1)}, bf16[64,768]{1,0:T(8,128)(2,1)S(1)}, u32[]{:S(2)}, u32[]{:S(2)}) %collective-permute-start.2) | collective-permute-done | bytes 98336 | tf_op jit(solution)/shard_map/while/body/eval_jaxpr/ppermute | solution.py:18
  93.5 5.0 %collective-permute-done.3 = bf16[64,768]{1,0:T(8,128)(2,1)S(1)} collective-permute-done((bf16[64,768]{1,0:T(8,128)(2,1)S(1)}, bf16[64,768]{1,0:T(8,128)(2,1)S(1)}, u32[]{:S(2)}, u32[]{:S(2)}) %collective-permute-start.3) | collective-permute-done | bytes 98336 | tf_op jit(solution)/shard_map/while/body/eval_jaxpr/ppermute | solution.py:149
  101.7 19.7 %all_to_all.35 = bf16[16,1,24,1536]{3,2,1,0:T(8,128)(2,1)S(1)} all-to-all(bf16[16,1,24,1536]{3,2,1,0:T(8,128)(2,1)S(1)} %bitcast.197), channel_id=1, replica_groups=mesh['section'=2,'expert'=16,'tensor'=4] {'expert'}, dimensions={0} | all-to-all | bytes 2359296 | tf_op jit(solution)/shard_map/while/body/eval_jaxpr/all_to_all | solution.py:97
  121.4 2.8 %collective-permute-done = bf16[16,1,24,1536]{3,2,0,1:T(8,128)(2,1)S(1)} collective-permute-done((bf16[16,1,24,1536]{3,2,0,1:T(8,128)(2,1)S(1)}, bf16[16,1,24,1536]{3,2,0,1:T(8,128)(2,1)S(1)}, u32[]{:S(2)}, u32[]{:S(2)}) %collective-permute-start) | collective-permute-done | bytes 1179680 | tf_op jit(solution)/shard_map/while/body/eval_jaxpr/ppermute | solution.py:18
  127.2 2.9 %fusion.81 = f32[16,24,1024]{2,1,0:T(8,128)S(1)} fusion(bf16[1,3072,1024]{2,1,0:T(8,128)(2,1)S(1)} %bitcast.216, bf16[16,24,768]{2,1,0:T(8,128)(2,1)S(1)} %get-tuple-element.509, bf16[16,24,768]{2,1,0:T(8,128)(2,1)S(1)} %get-tuple-element.510, bf16[16,24,768]{2,1,0:T(8,128)(2,1)S(1)} %get-tuple-element.511, ...), kind=kOutput, calls=%fused_computation.8.clone.1 | convolution fusion | flops 2428895232 | bytes 10237440 | tf_op jit(solution)/shard_map/while/body/eval_jaxpr/sekd,edf->sekf/dot_general | solution.py:107
  130.1 2.8 %fusion.82 = f32[16,1,24,3072]{3,2,0,1:T(8,128)S(1)} fusion(bf16[1,1024,3072]{2,1,0:T(8,128)(2,1)S(1)} %bitcast.222, f32[16,24,1024]{2,1,0:T(8,128)S(1)} %fusion.81), kind=kOutput, calls=%fused_computation.12.clone.1 | convolution fusion | flops 2417885184 | bytes 12582912 | tf_op jit(solution)/shard_map/while/body/eval_jaxpr/sekf,efd->sekd/dot_general | solution.py:111
  137.9 3.7 %all-to-all-start.1 = ((bf16[16,1,24,1536]{3,2,1,0:T(8,128)(2,1)}), bf16[16,1,24,1536]{3,2,1,0:T(8,128)(2,1)S(1)}, u32[]{:S(2)}, u32[]{:S(2)}) async-start(bf16[16,1,24,1536]{3,2,1,0:T(8,128)(2,1)} %fusion.84), calls=%async_computation.1 | async-start | bytes 2359296 | tf_op jit(solution)/shard_map/while/body/eval_jaxpr/all_to_all | solution.py:127
  141.8 20.2 %all-to-all-done.1 = bf16[16,1,24,1536]{3,2,1,0:T(8,128)(2,1)S(1)} async-done(((bf16[16,1,24,1536]{3,2,1,0:T(8,128)(2,1)}), bf16[16,1,24,1536]{3,2,1,0:T(8,128)(2,1)S(1)}, u32[]{:S(2)}, u32[]{:S(2)}) %all-to-all-start.1) | async-done | bytes 1179680 | tf_op jit(solution)/shard_map/while/body/eval_jaxpr/all_to_all | solution.py:127
  166.0 3.5 %collective-permute-done.2 = bf16[64,768]{1,0:T(8,128)(2,1)S(1)} collective-permute-done((bf16[64,768]{1,0:T(8,128)(2,1)S(1)}, bf16[64,768]{1,0:T(8,128)(2,1)S(1)}, u32[]{:S(2)}, u32[]{:S(2)}) %collective-permute-start.2) | collective-permute-done | bytes 98336 | tf_op jit(solution)/shard_map/while/body/eval_jaxpr/ppermute | solution.py:18
  172.3 5.0 %collective-permute-done.3 = bf16[64,768]{1,0:T(8,128)(2,1)S(1)} collective-permute-done((bf16[64,768]{1,0:T(8,128)(2,1)S(1)}, bf16[64,768]{1,0:T(8,128)(2,1)S(1)}, u32[]{:S(2)}, u32[]{:S(2)}) %collective-permute-start.3) | collective-permute-done | bytes 98336 | tf_op jit(solution)/shard_map/while/body/eval_jaxpr/ppermute | solution.py:149
  181.6 19.7 %all_to_all.34 = bf16[16,1,24,1536]{3,2,1,0:T(8,128)(2,1)S(1)} all-to-all(bf16[16,1,24,1536]{3,2,1,0:T(8,128)(2,1)S(1)} %bitcast.202), channel_id=1, replica_groups=mesh['section'=2,'expert'=16,'tensor'=4] {'expert'}, dimensions={0} | all-to-all | bytes 2359296 | tf_op jit(solution)/shard_map/all_to_all | solution.py:97
  201.3 2.8 %collective-permute-done.10 = bf16[16,1,24,1536]{3,2,0,1:T(8,128)(2,1)S(1)} collective-permute-done((bf16[16,1,24,1536]{3,2,0,1:T(8,128)(2,1)S(1)}, bf16[16,1,24,1536]{3,2,0,1:T(8,128)(2,1)S(1)}, u32[]{:S(2)}, u32[]{:S(2)}) %collective-permute-start.10) | collective-permute-done | bytes 1179680 | tf_op jit(solution)/shard_map/ppermute | solution.py:18
  207.1 2.9 %fusion.28 = f32[16,24,1024]{2,1,0:T(8,128)S(1)} fusion(bf16[1,1,3072,1024]{3,2,1,0:T(8,128)(2,1)S(1)} %bitcast.219, bf16[16,24,768]{2,1,0:T(8,128)(2,1)S(1)} %get-tuple-element.403, bf16[16,24,768]{2,1,0:T(8,128)(2,1)S(1)} %get-tuple-element.386, bf16[16,24,768]{2,1,0:T(8,128)(2,1)S(1)} %get-tuple-element.404, ...), kind=kOutput, calls=%fused_computation.68 | convolution fusion | flops 2428895232 | bytes 10237440 | tf_op jit(solution)/shard_map/sekd,edf->sekf/dot_general | solution.py:107
  210.0 2.8 %fusion.30 = f32[16,1,24,3072]{3,2,0,1:T(8,128)S(1)} fusion(bf16[1,1,1024,3072]{3,2,1,0:T(8,128)(2,1)S(1)} %bitcast.225, f32[16,24,1024]{2,1,0:T(8,128)S(1)} %fusion.28), kind=kOutput, calls=%fused_computation.72 | convolution fusion | flops 2417885184 | bytes 12582912 | tf_op jit(solution)/shard_map/sekf,efd->sekd/dot_general | solution.py:111
  217.8 3.7 %all-to-all-start.3 = ((bf16[16,1,24,1536]{3,2,1,0:T(8,128)(2,1)}), bf16[16,1,24,1536]{3,2,1,0:T(8,128)(2,1)S(1)}, u32[]{:S(2)}, u32[]{:S(2)}) async-start(bf16[16,1,24,1536]{3,2,1,0:T(8,128)(2,1)} %fusion.46), calls=%async_computation.3 | async-start | bytes 2359296 | tf_op jit(solution)/shard_map/all_to_all | solution.py:127
  221.7 20.2 %all-to-all-done.3 = bf16[16,1,24,1536]{3,2,1,0:T(8,128)(2,1)S(1)} async-done(((bf16[16,1,24,1536]{3,2,1,0:T(8,128)(2,1)}), bf16[16,1,24,1536]{3,2,1,0:T(8,128)(2,1)S(1)}, u32[]{:S(2)}, u32[]{:S(2)}) %all-to-all-start.3) | async-done | bytes 1179680 | tf_op jit(solution)/shard_map/all_to_all | solution.py:127
  245.9 3.5 %collective-permute-done.12 = bf16[64,768]{1,0:T(8,128)(2,1)S(1)} collective-permute-done((bf16[64,768]{1,0:T(8,128)(2,1)S(1)}, bf16[64,768]{1,0:T(8,128)(2,1)S(1)}, u32[]{:S(2)}, u32[]{:S(2)}) %collective-permute-start.12) | collective-permute-done | bytes 98336 | tf_op jit(solution)/shard_map/ppermute | solution.py:18
  (177 shorter events, 65.7 us)
Async XLA Ops:
  0.0 14.9 %copy-start.2 = (f32[1,2,64,2]{2,3,1,0:T(2,128)S(1)}, f32[1,2,64,2]{2,3,1,0:T(2,128)}, u32[]{:S(2)}) copy-start(f32[1,2,64,2]{2,3,1,0:T(2,128)} %param.15) | copy-start | bytes 3076
  0.7 10.4 %collective-permute-start.7 = (f32[768]{0:T(1024)S(1)}, f32[768]{0:T(1024)S(1)}, u32[]{:S(2)}, u32[]{:S(2)}) collective-permute-start(f32[768]{0:T(1024)S(1)} %reduce.6), channel_id=1, source_target_pairs={{0,1},{1,0},{2,3},{3,2},{4,5},{5,4},{6,7},{7,6},{8,9},{9,8},{10,11... | collective-permute-start | bytes 9224 | tf_op jit(solution)/shard_map/ppermute | solution.py:18
  0.8 10.4 %collective-permute-start.8 = (f32[768]{0:T(1024)S(1)}, f32[768]{0:T(1024)S(1)}, u32[]{:S(2)}, u32[]{:S(2)}) collective-permute-start(f32[768]{0:T(1024)S(1)} %reduce.6), channel_id=1, source_target_pairs={{0,2},{1,3},{2,0},{3,1},{4,6},{5,7},{6,4},{7,5},{8,10},{9,11},{10,... | collective-permute-start | bytes 9224 | tf_op jit(solution)/shard_map/ppermute | solution.py:18
  1.7 9.5 %collective-permute-start.9 = (f32[768]{0:T(1024)S(1)}, f32[768]{0:T(1024)S(1)}, u32[]{:S(2)}, u32[]{:S(2)}) collective-permute-start(f32[768]{0:T(1024)S(1)} %reduce.6), channel_id=1, source_target_pairs={{0,3},{1,2},{2,1},{3,0},{4,7},{5,6},{6,5},{7,4},{8,11},{9,10},{10,... | collective-permute-start | bytes 9224 | tf_op jit(solution)/shard_map/ppermute | solution.py:18
  3.6 11.2 %copy-start = (bf16[64,768]{1,0:T(8,128)(2,1)}, bf16[64,768]{1,0:T(8,128)(2,1)S(1)}, u32[]{:S(2)}) copy-start(bf16[64,768]{1,0:T(8,128)(2,1)S(1)} %get-tuple-element.393) | copy-start | bytes 294916
  3.6 7.6 %collective-permute-start.6 = (bf16[64,768]{1,0:T(8,128)(2,1)S(1)}, bf16[64,768]{1,0:T(8,128)(2,1)S(1)}, u32[]{:S(2)}, u32[]{:S(2)}) collective-permute-start(bf16[64,768]{1,0:T(8,128)(2,1)S(1)} %get-tuple-element.394), channel_id=1, source_target_pairs={{0,2},{1,3},{2,0},{3,1},{4,6},{5,7},{6,4},{7,5},{8,10},{9,11},{10,... | collective-permute-start | bytes 294920 | tf_op jit(solution)/shard_map/ppermute | solution.py:18
  9.7 5.1 %collective-permute-start.5 = (bf16[64,768]{1,0:T(8,128)(2,1)S(1)}, bf16[64,768]{1,0:T(8,128)(2,1)S(1)}, u32[]{:S(2)}, u32[]{:S(2)}) collective-permute-start(bf16[64,768]{1,0:T(8,128)(2,1)S(1)} %get-tuple-element.393), channel_id=1, source_target_pairs={{0,2},{1,3},{2,0},{3,1},{4,6},{5,7},{6,4},{7,5},{8,10},{9,11},{10,... | collective-permute-start | bytes 294920 | tf_op jit(solution)/shard_map/ppermute | solution.py:18
  42.7 2.8 %collective-permute-start = (bf16[16,1,24,1536]{3,2,0,1:T(8,128)(2,1)S(1)}, bf16[16,1,24,1536]{3,2,0,1:T(8,128)(2,1)S(1)}, u32[]{:S(2)}, u32[]{:S(2)}) collective-permute-start(bf16[16,1,24,1536]{3,2,0,1:T(8,128)(2,1)S(1)} %bitcast.195), channel_id=1, source_target_pairs={{0,1},{1,0},{2,3},{3,2},{4,5},{5,4},{6,7},{7,6},{8,9},{9,8},{10,11... | collective-permute-start | bytes 3538952 | tf_op jit(solution)/shard_map/while/body/eval_jaxpr/ppermute | solution.py:18
  46.0 5.3 %slice-start.4 = ((s8[6291456]{0:T(1024)(128)(4,1)}), s8[4194304]{0:T(1024)(128)(4,1)S(1)}, s32[]{:S(2)}) async-start(s8[6291456]{0:T(1024)(128)(4,1)} %bitcast.221), calls=%async_computation.8 | async-start | bytes 8388608 | tf_op jit(solution)/shard_map/while
  54.9 2.9 %collective-permute-start.1 = (bf16[16,1,24,1536]{3,2,0,1:T(8,128)(2,1)S(1)}, bf16[16,1,24,1536]{3,2,0,1:T(8,128)(2,1)S(1)}, u32[]{:S(2)}, u32[]{:S(2)}) collective-permute-start(bf16[16,1,24,1536]{3,2,0,1:T(8,128)(2,1)S(1)} %select_convert_fusion.6), channel_id=1, source_target_pairs={{0,1},{1,0},{2,3},{3,2},{4,5},{5,4},{6,7},{7,6},{8,9},{9,8},{10,11... | collective-permute-start | bytes 3538952 | tf_op jit(solution)/shard_map/while/body/eval_jaxpr/ppermute | solution.py:18
  59.2 24.0 %all-to-all-start.1 = ((bf16[16,1,24,1536]{3,2,1,0:T(8,128)(2,1)}), bf16[16,1,24,1536]{3,2,1,0:T(8,128)(2,1)S(1)}, u32[]{:S(2)}, u32[]{:S(2)}) async-start(bf16[16,1,24,1536]{3,2,1,0:T(8,128)(2,1)} %fusion.84), calls=%async_computation.1 | async-start | bytes 2359296 | tf_op jit(solution)/shard_map/while/body/eval_jaxpr/all_to_all | solution.py:127
  86.1 4.7 %collective-permute-start.2 = (bf16[64,768]{1,0:T(8,128)(2,1)S(1)}, bf16[64,768]{1,0:T(8,128)(2,1)S(1)}, u32[]{:S(2)}, u32[]{:S(2)}) collective-permute-start(bf16[64,768]{1,0:T(8,128)(2,1)S(1)} %select_convert_fusion.7), channel_id=1, source_target_pairs={{0,2},{1,3},{2,0},{3,1},{4,6},{5,7},{6,4},{7,5},{8,10},{9,11},{10,... | collective-permute-start | bytes 294920 | tf_op jit(solution)/shard_map/while/body/eval_jaxpr/ppermute | solution.py:18
  90.8 7.7 %collective-permute-start.3 = (bf16[64,768]{1,0:T(8,128)(2,1)S(1)}, bf16[64,768]{1,0:T(8,128)(2,1)S(1)}, u32[]{:S(2)}, u32[]{:S(2)}) collective-permute-start(bf16[64,768]{1,0:T(8,128)(2,1)S(1)} %add_convert_fusion.5), channel_id=1, source_target_pairs={{0,66},{1,67},{2,64},{3,65},{4,70},{5,71},{6,68},{7,69},{8,74},{9,... | collective-permute-start | bytes 294920 | tf_op jit(solution)/shard_map/while/body/eval_jaxpr/ppermute | solution.py:149
  92.1 8.0 %collective-permute-start.4 = (bf16[64,768]{1,0:T(8,128)(2,1)S(1)}, bf16[64,768]{1,0:T(8,128)(2,1)S(1)}, u32[]{:S(2)}, u32[]{:S(2)}) collective-permute-start(bf16[64,768]{1,0:T(8,128)(2,1)S(1)} %add_convert_fusion.5), channel_id=1, source_target_pairs={{0,64},{1,65},{2,66},{3,67},{4,68},{5,69},{6,70},{7,71},{8,72},{9,... | collective-permute-start | bytes 294920 | tf_op jit(solution)/shard_map/while/body/eval_jaxpr/ppermute | solution.py:13
  121.4 2.8 %collective-permute-start = (bf16[16,1,24,1536]{3,2,0,1:T(8,128)(2,1)S(1)}, bf16[16,1,24,1536]{3,2,0,1:T(8,128)(2,1)S(1)}, u32[]{:S(2)}, u32[]{:S(2)}) collective-permute-start(bf16[16,1,24,1536]{3,2,0,1:T(8,128)(2,1)S(1)} %bitcast.195), channel_id=1, source_target_pairs={{0,1},{1,0},{2,3},{3,2},{4,5},{5,4},{6,7},{7,6},{8,9},{9,8},{10,11... | collective-permute-start | bytes 3538952 | tf_op jit(solution)/shard_map/while/body/eval_jaxpr/ppermute | solution.py:18
  133.6 2.9 %collective-permute-start.1 = (bf16[16,1,24,1536]{3,2,0,1:T(8,128)(2,1)S(1)}, bf16[16,1,24,1536]{3,2,0,1:T(8,128)(2,1)S(1)}, u32[]{:S(2)}, u32[]{:S(2)}) collective-permute-start(bf16[16,1,24,1536]{3,2,0,1:T(8,128)(2,1)S(1)} %select_convert_fusion.6), channel_id=1, source_target_pairs={{0,1},{1,0},{2,3},{3,2},{4,5},{5,4},{6,7},{7,6},{8,9},{9,8},{10,11... | collective-permute-start | bytes 3538952 | tf_op jit(solution)/shard_map/while/body/eval_jaxpr/ppermute | solution.py:18
  137.9 24.0 %all-to-all-start.1 = ((bf16[16,1,24,1536]{3,2,1,0:T(8,128)(2,1)}), bf16[16,1,24,1536]{3,2,1,0:T(8,128)(2,1)S(1)}, u32[]{:S(2)}, u32[]{:S(2)}) async-start(bf16[16,1,24,1536]{3,2,1,0:T(8,128)(2,1)} %fusion.84), calls=%async_computation.1 | async-start | bytes 2359296 | tf_op jit(solution)/shard_map/while/body/eval_jaxpr/all_to_all | solution.py:127
  164.8 4.7 %collective-permute-start.2 = (bf16[64,768]{1,0:T(8,128)(2,1)S(1)}, bf16[64,768]{1,0:T(8,128)(2,1)S(1)}, u32[]{:S(2)}, u32[]{:S(2)}) collective-permute-start(bf16[64,768]{1,0:T(8,128)(2,1)S(1)} %select_convert_fusion.7), channel_id=1, source_target_pairs={{0,2},{1,3},{2,0},{3,1},{4,6},{5,7},{6,4},{7,5},{8,10},{9,11},{10,... | collective-permute-start | bytes 294920 | tf_op jit(solution)/shard_map/while/body/eval_jaxpr/ppermute | solution.py:18
  169.6 7.7 %collective-permute-start.3 = (bf16[64,768]{1,0:T(8,128)(2,1)S(1)}, bf16[64,768]{1,0:T(8,128)(2,1)S(1)}, u32[]{:S(2)}, u32[]{:S(2)}) collective-permute-start(bf16[64,768]{1,0:T(8,128)(2,1)S(1)} %add_convert_fusion.5), channel_id=1, source_target_pairs={{0,66},{1,67},{2,64},{3,65},{4,70},{5,71},{6,68},{7,69},{8,74},{9,... | collective-permute-start | bytes 294920 | tf_op jit(solution)/shard_map/while/body/eval_jaxpr/ppermute | solution.py:149
  170.9 8.0 %collective-permute-start.4 = (bf16[64,768]{1,0:T(8,128)(2,1)S(1)}, bf16[64,768]{1,0:T(8,128)(2,1)S(1)}, u32[]{:S(2)}, u32[]{:S(2)}) collective-permute-start(bf16[64,768]{1,0:T(8,128)(2,1)S(1)} %add_convert_fusion.5), channel_id=1, source_target_pairs={{0,64},{1,65},{2,66},{3,67},{4,68},{5,69},{6,70},{7,71},{8,72},{9,... | collective-permute-start | bytes 294920 | tf_op jit(solution)/shard_map/while/body/eval_jaxpr/ppermute | solution.py:13
  201.3 2.8 %collective-permute-start.10 = (bf16[16,1,24,1536]{3,2,0,1:T(8,128)(2,1)S(1)}, bf16[16,1,24,1536]{3,2,0,1:T(8,128)(2,1)S(1)}, u32[]{:S(2)}, u32[]{:S(2)}) collective-permute-start(bf16[16,1,24,1536]{3,2,0,1:T(8,128)(2,1)S(1)} %bitcast.200), channel_id=1, source_target_pairs={{0,1},{1,0},{2,3},{3,2},{4,5},{5,4},{6,7},{7,6},{8,9},{9,8},{10,11... | collective-permute-start | bytes 3538952 | tf_op jit(solution)/shard_map/ppermute | solution.py:18
  213.5 2.9 %collective-permute-start.11 = (bf16[16,1,24,1536]{3,2,0,1:T(8,128)(2,1)S(1)}, bf16[16,1,24,1536]{3,2,0,1:T(8,128)(2,1)S(1)}, u32[]{:S(2)}, u32[]{:S(2)}) collective-permute-start(bf16[16,1,24,1536]{3,2,0,1:T(8,128)(2,1)S(1)} %select_convert_fusion.2), channel_id=1, source_target_pairs={{0,1},{1,0},{2,3},{3,2},{4,5},{5,4},{6,7},{7,6},{8,9},{9,8},{10,11... | collective-permute-start | bytes 3538952 | tf_op jit(solution)/shard_map/ppermute | solution.py:18
  217.8 24.0 %all-to-all-start.3 = ((bf16[16,1,24,1536]{3,2,1,0:T(8,128)(2,1)}), bf16[16,1,24,1536]{3,2,1,0:T(8,128)(2,1)S(1)}, u32[]{:S(2)}, u32[]{:S(2)}) async-start(bf16[16,1,24,1536]{3,2,1,0:T(8,128)(2,1)} %fusion.46), calls=%async_computation.3 | async-start | bytes 2359296 | tf_op jit(solution)/shard_map/all_to_all | solution.py:127
  244.7 4.7 %collective-permute-start.12 = (bf16[64,768]{1,0:T(8,128)(2,1)S(1)}, bf16[64,768]{1,0:T(8,128)(2,1)S(1)}, u32[]{:S(2)}, u32[]{:S(2)}) collective-permute-start(bf16[64,768]{1,0:T(8,128)(2,1)S(1)} %select_convert_fusion.3), channel_id=1, source_target_pairs={{0,2},{1,3},{2,0},{3,1},{4,6},{5,7},{6,4},{7,5},{8,10},{9,11},{10,... | collective-permute-start | bytes 294920 | tf_op jit(solution)/shard_map/ppermute | solution.py:18
  (14 other events, 37.2 us)

commit v11 on v5

--- a/solution.py
+++ b/solution.py
@@ -131,7 +131,7 @@
         y_half = jnp.sum(picked * weights[:, :, None], axis=1)
         y_keep = jnp.where(x_first, y_half[:, :quarter], y_half[:, quarter:])
         y_give = jnp.where(x_first, y_half[:, quarter:], y_half[:, :quarter])
-        y_got = swap(y_give, "tensor", 2)
+        y_got = swap(y_give.astype(jnp.bfloat16), "tensor", 2).astype(jnp.float32)
         xf = jnp.where(x_first, half_rows[:, :quarter], half_rows[:, quarter:]).astype(jnp.float32)
         mixed = xf + (y_keep + y_got)
         produced = mixed.astype(jnp.bfloat16)

time: 251 us -> 246 us (0.980)
  waiting for transfers between devices: 107 us -> 103 us
    ppermute x13, waiting for transfers between devices: 32.7 us -> 29.4 us  [swap(): return lax.ppermute(block, axis, [(i, i ^ bit) for i in range(n)])]
where the time goes in v11:
time: 246 us; the launch traced here: 245 us
  waiting for transfers between devices  103 us (42%)
  blocking collectives  65.6 us (27%)
  starting transfers between devices  22.6 us (9%)
  local copies, waits for them, and re-layouts  18.6 us (8%)
  other arithmetic  17.7 us (7%)
  matrix products  16.7 us (7%)
    all_to_all x3, blocking collectives, layer_step(): lax.all_to_all(outgoing, 'expert', split_axis=0, concat_axis=0, tiled=True)  65.6 us
    all_to_all x3, waiting for transfers between devices, layer_step(): lax.all_to_all(chip_sum, 'expert', split_axis=0, concat_axis=0, tiled=True)  60.6 us
    ppermute x13, waiting for transfers between devices, swap(): return lax.ppermute(block, axis, [(i, i ^ bit) for i in range(n)])  29.4 us
    all_to_all x3, starting transfers between devices, layer_step(): lax.all_to_all(chip_sum, 'expert', split_axis=0, concat_axis=0, tiled=True)  11.5 us
    ppermute x2, waiting for transfers between devices, looped(): lax.ppermute(produced, ('section', 'tensor'), cross_route)  10 us
    dot_general x3, matrix products, layer_step(): jnp.einsum('sekd,edf->sekf', normed, up_local, preferred_element_type=jnp...  8.6 us
    dot_general x3, matrix products, layer_step(): jnp.einsum('sekf,efd->sekd', hidden, down_local, preferred_element_type=j...  8.11 us
    ppermute x13, starting transfers between devices, swap(): return lax.ppermute(block, axis, [(i, i ^ bit) for i in range(n)])  5.94 us
  transfers between devices with their start and end apart: 20, of which 17 were waited for; matrix products, arithmetic and copies ran while one was open for 2% of the time, Pallas kernels for 0%

profile of v11, /device:TPU:6, one launch (start us, length us, event | category | flops | bytes accessed | tf_op | source)
XLA Modules:
  0.0 245.3 jit_solution(140767157897510750)
XLA Ops:
  11.2 163.9 %while.17 = (s32[]{:T(128)}, bf16[64,1536]{1,0:T(8,128)(2,1)S(1)}, bf16[2,64,768]{2,1,0:T(8,128)(2,1)S(1)}, pred[]{:T(512)}, pred[]{:T(512)}, /*index=5*/bf16[2,...) while((s32[]{:T(128)}, bf16[64,1536]{1,0:T(8,128)(2,1)S(1)}, ...), condition=%wide.region_8.11_spmd.clone, body=%wide.region_4.10_spmd.clone.sunk | while | flops 4872246272 | bytes 128624768 | solution.py:152
  12.7 26.1 %all_to_all.35 = bf16[16,1,24,1536]{3,2,1,0:T(8,128)(2,1)S(1)} all-to-all(bf16[16,1,24,1536]{3,2,1,0:T(8,128)(2,1)S(1)} %bitcast.195), channel_id=1, replica_groups=mesh['section'=2,'expert'=16,'tensor'=4] {'expert'}, dimensions={0} | all-to-all | bytes 2359296 | tf_op jit(solution)/shard_map/while/body/eval_jaxpr/all_to_all | solution.py:95
  38.8 2.8 %collective-permute-done = bf16[16,1,24,1536]{3,2,0,1:T(8,128)(2,1)S(1)} collective-permute-done((bf16[16,1,24,1536]{3,2,0,1:T(8,128)(2,1)S(1)}, bf16[16,1,24,1536]{3,2,0,1:T(8,128)(2,1)S(1)}, u32[]{:S(2)}, u32[]{:S(2)}) %collective-permute-start) | collective-permute-done | bytes 1179680 | tf_op jit(solution)/shard_map/while/body/eval_jaxpr/ppermute | solution.py:18
  44.5 2.9 %fusion.80 = f32[16,24,1024]{2,1,0:T(8,128)S(1)} fusion(bf16[1,3072,1024]{2,1,0:T(8,128)(2,1)S(1)} %bitcast.212, bf16[16,24,768]{2,1,0:T(8,128)(2,1)S(1)} %get-tuple-element.505, bf16[16,24,768]{2,1,0:T(8,128)(2,1)S(1)} %get-tuple-element.506, bf16[16,24,768]{2,1,0:T(8,128)(2,1)S(1)} %get-tuple-element.507, ...), kind=kOutput, calls=%fused_computation.8.clone.1 | convolution fusion | flops 2428895232 | bytes 10237440 | tf_op jit(solution)/shard_map/while/body/eval_jaxpr/sekd,edf->sekf/dot_general | solution.py:105
  55.2 3.8 %all-to-all-start.1 = ((bf16[16,1,24,1536]{3,2,1,0:T(8,128)(2,1)}), bf16[16,1,24,1536]{3,2,1,0:T(8,128)(2,1)S(1)}, u32[]{:S(2)}, u32[]{:S(2)}) async-start(bf16[16,1,24,1536]{3,2,1,0:T(8,128)(2,1)} %fusion.83), calls=%async_computation.1 | async-start | bytes 2359296 | tf_op jit(solution)/shard_map/while/body/eval_jaxpr/all_to_all | solution.py:125
  59.2 20.2 %all-to-all-done.1 = bf16[16,1,24,1536]{3,2,1,0:T(8,128)(2,1)S(1)} async-done(((bf16[16,1,24,1536]{3,2,1,0:T(8,128)(2,1)}), bf16[16,1,24,1536]{3,2,1,0:T(8,128)(2,1)S(1)}, u32[]{:S(2)}, u32[]{:S(2)}) %all-to-all-start.1) | async-done | bytes 1179680 | tf_op jit(solution)/shard_map/while/body/eval_jaxpr/all_to_all | solution.py:125
  83.1 3.8 %collective-permute-done.2 = bf16[64,768]{1,0:T(8,128)(2,1)S(1)} collective-permute-done((bf16[64,768]{1,0:T(8,128)(2,1)S(1)}, bf16[64,768]{1,0:T(8,128)(2,1)S(1)}, u32[]{:S(2)}, u32[]{:S(2)}) %collective-permute-start.2) | collective-permute-done | bytes 98336 | tf_op jit(solution)/shard_map/while/body/eval_jaxpr/ppermute | solution.py:18
  89.6 5.0 %collective-permute-done.3 = bf16[64,768]{1,0:T(8,128)(2,1)S(1)} collective-permute-done((bf16[64,768]{1,0:T(8,128)(2,1)S(1)}, bf16[64,768]{1,0:T(8,128)(2,1)S(1)}, u32[]{:S(2)}, u32[]{:S(2)}) %collective-permute-start.3) | collective-permute-done | bytes 98336 | tf_op jit(solution)/shard_map/while/body/eval_jaxpr/ppermute | solution.py:147
  97.8 19.7 %all_to_all.35 = bf16[16,1,24,1536]{3,2,1,0:T(8,128)(2,1)S(1)} all-to-all(bf16[16,1,24,1536]{3,2,1,0:T(8,128)(2,1)S(1)} %bitcast.195), channel_id=1, replica_groups=mesh['section'=2,'expert'=16,'tensor'=4] {'expert'}, dimensions={0} | all-to-all | bytes 2359296 | tf_op jit(solution)/shard_map/while/body/eval_jaxpr/all_to_all | solution.py:95
  117.5 2.8 %collective-permute-done = bf16[16,1,24,1536]{3,2,0,1:T(8,128)(2,1)S(1)} collective-permute-done((bf16[16,1,24,1536]{3,2,0,1:T(8,128)(2,1)S(1)}, bf16[16,1,24,1536]{3,2,0,1:T(8,128)(2,1)S(1)}, u32[]{:S(2)}, u32[]{:S(2)}) %collective-permute-start) | collective-permute-done | bytes 1179680 | tf_op jit(solution)/shard_map/while/body/eval_jaxpr/ppermute | solution.py:18
  123.3 2.9 %fusion.80 = f32[16,24,1024]{2,1,0:T(8,128)S(1)} fusion(bf16[1,3072,1024]{2,1,0:T(8,128)(2,1)S(1)} %bitcast.212, bf16[16,24,768]{2,1,0:T(8,128)(2,1)S(1)} %get-tuple-element.505, bf16[16,24,768]{2,1,0:T(8,128)(2,1)S(1)} %get-tuple-element.506, bf16[16,24,768]{2,1,0:T(8,128)(2,1)S(1)} %get-tuple-element.507, ...), kind=kOutput, calls=%fused_computation.8.clone.1 | convolution fusion | flops 2428895232 | bytes 10237440 | tf_op jit(solution)/shard_map/while/body/eval_jaxpr/sekd,edf->sekf/dot_general | solution.py:105
  126.2 2.7 %fusion.81 = f32[16,1,24,3072]{3,2,0,1:T(8,128)S(1)} fusion(bf16[1,1024,3072]{2,1,0:T(8,128)(2,1)S(1)} %bitcast.218, f32[16,24,1024]{2,1,0:T(8,128)S(1)} %fusion.80), kind=kOutput, calls=%fused_computation.12.clone.1 | convolution fusion | flops 2417885184 | bytes 12582912 | tf_op jit(solution)/shard_map/while/body/eval_jaxpr/sekf,efd->sekd/dot_general | solution.py:109
  129.9 2.7 %collective-permute-done.1 = bf16[16,1,24,1536]{3,2,0,1:T(8,128)(2,1)S(1)} collective-permute-done((bf16[16,1,24,1536]{3,2,0,1:T(8,128)(2,1)S(1)}, bf16[16,1,24,1536]{3,2,0,1:T(8,128)(2,1)S(1)}, u32[]{:S(2)}, u32[]{:S(2)}) %collective-permute-start.1) | collective-permute-done | bytes 1179680 | tf_op jit(solution)/shard_map/while/body/eval_jaxpr/ppermute | solution.py:18
  134.0 3.8 %all-to-all-start.1 = ((bf16[16,1,24,1536]{3,2,1,0:T(8,128)(2,1)}), bf16[16,1,24,1536]{3,2,1,0:T(8,128)(2,1)S(1)}, u32[]{:S(2)}, u32[]{:S(2)}) async-start(bf16[16,1,24,1536]{3,2,1,0:T(8,128)(2,1)} %fusion.83), calls=%async_computation.1 | async-start | bytes 2359296 | tf_op jit(solution)/shard_map/while/body/eval_jaxpr/all_to_all | solution.py:125
  137.9 20.2 %all-to-all-done.1 = bf16[16,1,24,1536]{3,2,1,0:T(8,128)(2,1)S(1)} async-done(((bf16[16,1,24,1536]{3,2,1,0:T(8,128)(2,1)}), bf16[16,1,24,1536]{3,2,1,0:T(8,128)(2,1)S(1)}, u32[]{:S(2)}, u32[]{:S(2)}) %all-to-all-start.1) | async-done | bytes 1179680 | tf_op jit(solution)/shard_map/while/body/eval_jaxpr/all_to_all | solution.py:125
  161.8 3.9 %collective-permute-done.2 = bf16[64,768]{1,0:T(8,128)(2,1)S(1)} collective-permute-done((bf16[64,768]{1,0:T(8,128)(2,1)S(1)}, bf16[64,768]{1,0:T(8,128)(2,1)S(1)}, u32[]{:S(2)}, u32[]{:S(2)}) %collective-permute-start.2) | collective-permute-done | bytes 98336 | tf_op jit(solution)/shard_map/while/body/eval_jaxpr/ppermute | solution.py:18
  168.4 5.0 %collective-permute-done.3 = bf16[64,768]{1,0:T(8,128)(2,1)S(1)} collective-permute-done((bf16[64,768]{1,0:T(8,128)(2,1)S(1)}, bf16[64,768]{1,0:T(8,128)(2,1)S(1)}, u32[]{:S(2)}, u32[]{:S(2)}) %collective-permute-start.3) | collective-permute-done | bytes 98336 | tf_op jit(solution)/shard_map/while/body/eval_jaxpr/ppermute | solution.py:147
  176.6 19.7 %all_to_all.34 = bf16[16,1,24,1536]{3,2,1,0:T(8,128)(2,1)S(1)} all-to-all(bf16[16,1,24,1536]{3,2,1,0:T(8,128)(2,1)S(1)} %bitcast.200), channel_id=1, replica_groups=mesh['section'=2,'expert'=16,'tensor'=4] {'expert'}, dimensions={0} | all-to-all | bytes 2359296 | tf_op jit(solution)/shard_map/all_to_all | solution.py:95
  196.4 2.8 %collective-permute-done.9 = bf16[16,1,24,1536]{3,2,0,1:T(8,128)(2,1)S(1)} collective-permute-done((bf16[16,1,24,1536]{3,2,0,1:T(8,128)(2,1)S(1)}, bf16[16,1,24,1536]{3,2,0,1:T(8,128)(2,1)S(1)}, u32[]{:S(2)}, u32[]{:S(2)}) %collective-permute-start.9) | collective-permute-done | bytes 1179680 | tf_op jit(solution)/shard_map/ppermute | solution.py:18
  202.1 2.9 %fusion.28 = f32[16,24,1024]{2,1,0:T(8,128)S(1)} fusion(bf16[1,1,3072,1024]{3,2,1,0:T(8,128)(2,1)S(1)} %bitcast.215, bf16[16,24,768]{2,1,0:T(8,128)(2,1)S(1)} %get-tuple-element.399, bf16[16,24,768]{2,1,0:T(8,128)(2,1)S(1)} %get-tuple-element.386, bf16[16,24,768]{2,1,0:T(8,128)(2,1)S(1)} %get-tuple-element.400, ...), kind=kOutput, calls=%fused_computation.68 | convolution fusion | flops 2428895232 | bytes 10237440 | tf_op jit(solution)/shard_map/sekd,edf->sekf/dot_general | solution.py:105
  208.7 2.7 %collective-permute-done.10 = bf16[16,1,24,1536]{3,2,0,1:T(8,128)(2,1)S(1)} collective-permute-done((bf16[16,1,24,1536]{3,2,0,1:T(8,128)(2,1)S(1)}, bf16[16,1,24,1536]{3,2,0,1:T(8,128)(2,1)S(1)}, u32[]{:S(2)}, u32[]{:S(2)}) %collective-permute-start.10) | collective-permute-done | bytes 1179680 | tf_op jit(solution)/shard_map/ppermute | solution.py:18
  212.8 3.8 %all-to-all-start.3 = ((bf16[16,1,24,1536]{3,2,1,0:T(8,128)(2,1)}), bf16[16,1,24,1536]{3,2,1,0:T(8,128)(2,1)S(1)}, u32[]{:S(2)}, u32[]{:S(2)}) async-start(bf16[16,1,24,1536]{3,2,1,0:T(8,128)(2,1)} %fusion.46), calls=%async_computation.3 | async-start | bytes 2359296 | tf_op jit(solution)/shard_map/all_to_all | solution.py:125
  216.8 20.2 %all-to-all-done.3 = bf16[16,1,24,1536]{3,2,1,0:T(8,128)(2,1)S(1)} async-done(((bf16[16,1,24,1536]{3,2,1,0:T(8,128)(2,1)}), bf16[16,1,24,1536]{3,2,1,0:T(8,128)(2,1)S(1)}, u32[]{:S(2)}, u32[]{:S(2)}) %all-to-all-start.3) | async-done | bytes 1179680 | tf_op jit(solution)/shard_map/all_to_all | solution.py:125
  240.6 3.9 %collective-permute-done.11 = bf16[64,768]{1,0:T(8,128)(2,1)S(1)} collective-permute-done((bf16[64,768]{1,0:T(8,128)(2,1)S(1)}, bf16[64,768]{1,0:T(8,128)(2,1)S(1)}, u32[]{:S(2)}, u32[]{:S(2)}) %collective-permute-start.11) | collective-permute-done | bytes 98336 | tf_op jit(solution)/shard_map/ppermute | solution.py:18
  (172 shorter events, 59.8 us)
Async XLA Ops:
  0.7 8.1 %collective-permute-start.6 = (f32[768]{0:T(1024)S(1)}, f32[768]{0:T(1024)S(1)}, u32[]{:S(2)}, u32[]{:S(2)}) collective-permute-start(f32[768]{0:T(1024)S(1)} %reduce.6), channel_id=1, source_target_pairs={{0,1},{1,0},{2,3},{3,2},{4,5},{5,4},{6,7},{7,6},{8,9},{9,8},{10,11... | collective-permute-start | bytes 9224 | tf_op jit(solution)/shard_map/ppermute | solution.py:18
  0.8 8.0 %collective-permute-start.7 = (f32[768]{0:T(1024)S(1)}, f32[768]{0:T(1024)S(1)}, u32[]{:S(2)}, u32[]{:S(2)}) collective-permute-start(f32[768]{0:T(1024)S(1)} %reduce.6), channel_id=1, source_target_pairs={{0,2},{1,3},{2,0},{3,1},{4,6},{5,7},{6,4},{7,5},{8,10},{9,11},{10,... | collective-permute-start | bytes 9224 | tf_op jit(solution)/shard_map/ppermute | solution.py:18
  1.7 7.2 %collective-permute-start.8 = (f32[768]{0:T(1024)S(1)}, f32[768]{0:T(1024)S(1)}, u32[]{:S(2)}, u32[]{:S(2)}) collective-permute-start(f32[768]{0:T(1024)S(1)} %reduce.6), channel_id=1, source_target_pairs={{0,3},{1,2},{2,1},{3,0},{4,7},{5,6},{6,5},{7,4},{8,11},{9,10},{10,... | collective-permute-start | bytes 9224 | tf_op jit(solution)/shard_map/ppermute | solution.py:18
  2.6 7.4 %collective-permute-start.5 = (bf16[2,64,768]{2,1,0:T(8,128)(2,1)}, bf16[2,64,768]{2,1,0:T(8,128)(2,1)S(1)}, u32[]{:S(2)}, u32[]{:S(2)}) collective-permute-start(bf16[2,64,768]{2,1,0:T(8,128)(2,1)} %param.12), channel_id=1, source_target_pairs={{0,2},{1,3},{2,0},{3,1},{4,6},{5,7},{6,4},{7,5},{8,10},{9,11},{10,... | collective-permute-start | bytes 589832 | tf_op jit(solution)/shard_map/ppermute | solution.py:18
  38.7 2.8 %collective-permute-start = (bf16[16,1,24,1536]{3,2,0,1:T(8,128)(2,1)S(1)}, bf16[16,1,24,1536]{3,2,0,1:T(8,128)(2,1)S(1)}, u32[]{:S(2)}, u32[]{:S(2)}) collective-permute-start(bf16[16,1,24,1536]{3,2,0,1:T(8,128)(2,1)S(1)} %bitcast.193), channel_id=1, source_target_pairs={{0,1},{1,0},{2,3},{3,2},{4,5},{5,4},{6,7},{7,6},{8,9},{9,8},{10,11... | collective-permute-start | bytes 3538952 | tf_op jit(solution)/shard_map/while/body/eval_jaxpr/ppermute | solution.py:18
  42.1 5.3 %slice-start.4 = ((s8[6291456]{0:T(1024)(128)(4,1)}), s8[4194304]{0:T(1024)(128)(4,1)S(1)}, s32[]{:S(2)}) async-start(s8[6291456]{0:T(1024)(128)(4,1)} %bitcast.217), calls=%async_computation.8 | async-start | bytes 8388608 | tf_op jit(solution)/shard_map/while
  50.9 2.9 %collective-permute-start.1 = (bf16[16,1,24,1536]{3,2,0,1:T(8,128)(2,1)S(1)}, bf16[16,1,24,1536]{3,2,0,1:T(8,128)(2,1)S(1)}, u32[]{:S(2)}, u32[]{:S(2)}) collective-permute-start(bf16[16,1,24,1536]{3,2,0,1:T(8,128)(2,1)S(1)} %select_convert_fusion.6), channel_id=1, source_target_pairs={{0,1},{1,0},{2,3},{3,2},{4,5},{5,4},{6,7},{7,6},{8,9},{9,8},{10,11... | collective-permute-start | bytes 3538952 | tf_op jit(solution)/shard_map/while/body/eval_jaxpr/ppermute | solution.py:18
  55.2 3.8 %copy-start = (f32[1,2,64,2]{2,3,1,0:T(2,128)S(1)}, f32[1,2,64,2]{2,3,1,0:T(2,128)}, u32[]{:S(2)}) copy-start(f32[1,2,64,2]{2,3,1,0:T(2,128)} %get-tuple-element.566) | copy-start | bytes 3076 | tf_op jit(solution)/shard_map/while
  55.2 24.2 %all-to-all-start.1 = ((bf16[16,1,24,1536]{3,2,1,0:T(8,128)(2,1)}), bf16[16,1,24,1536]{3,2,1,0:T(8,128)(2,1)S(1)}, u32[]{:S(2)}, u32[]{:S(2)}) async-start(bf16[16,1,24,1536]{3,2,1,0:T(8,128)(2,1)} %fusion.83), calls=%async_computation.1 | async-start | bytes 2359296 | tf_op jit(solution)/shard_map/while/body/eval_jaxpr/all_to_all | solution.py:125
  82.2 4.7 %collective-permute-start.2 = (bf16[64,768]{1,0:T(8,128)(2,1)S(1)}, bf16[64,768]{1,0:T(8,128)(2,1)S(1)}, u32[]{:S(2)}, u32[]{:S(2)}) collective-permute-start(bf16[64,768]{1,0:T(8,128)(2,1)S(1)} %select_convert_fusion.7), channel_id=1, source_target_pairs={{0,2},{1,3},{2,0},{3,1},{4,6},{5,7},{6,4},{7,5},{8,10},{9,11},{10,... | collective-permute-start | bytes 294920 | tf_op jit(solution)/shard_map/while/body/eval_jaxpr/ppermute | solution.py:18
  86.9 7.7 %collective-permute-start.3 = (bf16[64,768]{1,0:T(8,128)(2,1)S(1)}, bf16[64,768]{1,0:T(8,128)(2,1)S(1)}, u32[]{:S(2)}, u32[]{:S(2)}) collective-permute-start(bf16[64,768]{1,0:T(8,128)(2,1)S(1)} %add_convert_fusion.5), channel_id=1, source_target_pairs={{0,66},{1,67},{2,64},{3,65},{4,70},{5,71},{6,68},{7,69},{8,74},{9,... | collective-permute-start | bytes 294920 | tf_op jit(solution)/shard_map/while/body/eval_jaxpr/ppermute | solution.py:147
  88.2 8.0 %collective-permute-start.4 = (bf16[64,768]{1,0:T(8,128)(2,1)S(1)}, bf16[64,768]{1,0:T(8,128)(2,1)S(1)}, u32[]{:S(2)}, u32[]{:S(2)}) collective-permute-start(bf16[64,768]{1,0:T(8,128)(2,1)S(1)} %add_convert_fusion.5), channel_id=1, source_target_pairs={{0,64},{1,65},{2,66},{3,67},{4,68},{5,69},{6,70},{7,71},{8,72},{9,... | collective-permute-start | bytes 294920 | tf_op jit(solution)/shard_map/while/body/eval_jaxpr/ppermute | solution.py:13
  117.5 2.8 %collective-permute-start = (bf16[16,1,24,1536]{3,2,0,1:T(8,128)(2,1)S(1)}, bf16[16,1,24,1536]{3,2,0,1:T(8,128)(2,1)S(1)}, u32[]{:S(2)}, u32[]{:S(2)}) collective-permute-start(bf16[16,1,24,1536]{3,2,0,1:T(8,128)(2,1)S(1)} %bitcast.193), channel_id=1, source_target_pairs={{0,1},{1,0},{2,3},{3,2},{4,5},{5,4},{6,7},{7,6},{8,9},{9,8},{10,11... | collective-permute-start | bytes 3538952 | tf_op jit(solution)/shard_map/while/body/eval_jaxpr/ppermute | solution.py:18
  120.9 5.3 %slice-start.4 = ((s8[6291456]{0:T(1024)(128)(4,1)}), s8[4194304]{0:T(1024)(128)(4,1)S(1)}, s32[]{:S(2)}) async-start(s8[6291456]{0:T(1024)(128)(4,1)} %bitcast.217), calls=%async_computation.8 | async-start | bytes 8388608 | tf_op jit(solution)/shard_map/while
  129.7 2.9 %collective-permute-start.1 = (bf16[16,1,24,1536]{3,2,0,1:T(8,128)(2,1)S(1)}, bf16[16,1,24,1536]{3,2,0,1:T(8,128)(2,1)S(1)}, u32[]{:S(2)}, u32[]{:S(2)}) collective-permute-start(bf16[16,1,24,1536]{3,2,0,1:T(8,128)(2,1)S(1)} %select_convert_fusion.6), channel_id=1, source_target_pairs={{0,1},{1,0},{2,3},{3,2},{4,5},{5,4},{6,7},{7,6},{8,9},{9,8},{10,11... | collective-permute-start | bytes 3538952 | tf_op jit(solution)/shard_map/while/body/eval_jaxpr/ppermute | solution.py:18
  134.0 24.2 %all-to-all-start.1 = ((bf16[16,1,24,1536]{3,2,1,0:T(8,128)(2,1)}), bf16[16,1,24,1536]{3,2,1,0:T(8,128)(2,1)S(1)}, u32[]{:S(2)}, u32[]{:S(2)}) async-start(bf16[16,1,24,1536]{3,2,1,0:T(8,128)(2,1)} %fusion.83), calls=%async_computation.1 | async-start | bytes 2359296 | tf_op jit(solution)/shard_map/while/body/eval_jaxpr/all_to_all | solution.py:125
  160.9 4.7 %collective-permute-start.2 = (bf16[64,768]{1,0:T(8,128)(2,1)S(1)}, bf16[64,768]{1,0:T(8,128)(2,1)S(1)}, u32[]{:S(2)}, u32[]{:S(2)}) collective-permute-start(bf16[64,768]{1,0:T(8,128)(2,1)S(1)} %select_convert_fusion.7), channel_id=1, source_target_pairs={{0,2},{1,3},{2,0},{3,1},{4,6},{5,7},{6,4},{7,5},{8,10},{9,11},{10,... | collective-permute-start | bytes 294920 | tf_op jit(solution)/shard_map/while/body/eval_jaxpr/ppermute | solution.py:18
  165.7 7.7 %collective-permute-start.3 = (bf16[64,768]{1,0:T(8,128)(2,1)S(1)}, bf16[64,768]{1,0:T(8,128)(2,1)S(1)}, u32[]{:S(2)}, u32[]{:S(2)}) collective-permute-start(bf16[64,768]{1,0:T(8,128)(2,1)S(1)} %add_convert_fusion.5), channel_id=1, source_target_pairs={{0,66},{1,67},{2,64},{3,65},{4,70},{5,71},{6,68},{7,69},{8,74},{9,... | collective-permute-start | bytes 294920 | tf_op jit(solution)/shard_map/while/body/eval_jaxpr/ppermute | solution.py:147
  167.0 8.0 %collective-permute-start.4 = (bf16[64,768]{1,0:T(8,128)(2,1)S(1)}, bf16[64,768]{1,0:T(8,128)(2,1)S(1)}, u32[]{:S(2)}, u32[]{:S(2)}) collective-permute-start(bf16[64,768]{1,0:T(8,128)(2,1)S(1)} %add_convert_fusion.5), channel_id=1, source_target_pairs={{0,64},{1,65},{2,66},{3,67},{4,68},{5,69},{6,70},{7,71},{8,72},{9,... | collective-permute-start | bytes 294920 | tf_op jit(solution)/shard_map/while/body/eval_jaxpr/ppermute | solution.py:13
  196.4 2.8 %collective-permute-start.9 = (bf16[16,1,24,1536]{3,2,0,1:T(8,128)(2,1)S(1)}, bf16[16,1,24,1536]{3,2,0,1:T(8,128)(2,1)S(1)}, u32[]{:S(2)}, u32[]{:S(2)}) collective-permute-start(bf16[16,1,24,1536]{3,2,0,1:T(8,128)(2,1)S(1)} %bitcast.198), channel_id=1, source_target_pairs={{0,1},{1,0},{2,3},{3,2},{4,5},{5,4},{6,7},{7,6},{8,9},{9,8},{10,11... | collective-permute-start | bytes 3538952 | tf_op jit(solution)/shard_map/ppermute | solution.py:18
  199.7 5.3 %slice-start.6 = ((s8[6291456]{0:T(1024)(128)(4,1)}), s8[4194304]{0:T(1024)(128)(4,1)S(1)}, s32[]{:S(2)}) async-start(s8[6291456]{0:T(1024)(128)(4,1)} %bitcast.219), calls=%async_computation.10 | async-start | bytes 8388608
  208.5 2.9 %collective-permute-start.10 = (bf16[16,1,24,1536]{3,2,0,1:T(8,128)(2,1)S(1)}, bf16[16,1,24,1536]{3,2,0,1:T(8,128)(2,1)S(1)}, u32[]{:S(2)}, u32[]{:S(2)}) collective-permute-start(bf16[16,1,24,1536]{3,2,0,1:T(8,128)(2,1)S(1)} %select_convert_fusion.2), channel_id=1, source_target_pairs={{0,1},{1,0},{2,3},{3,2},{4,5},{5,4},{6,7},{7,6},{8,9},{9,8},{10,11... | collective-permute-start | bytes 3538952 | tf_op jit(solution)/shard_map/ppermute | solution.py:18
  212.8 24.2 %all-to-all-start.3 = ((bf16[16,1,24,1536]{3,2,1,0:T(8,128)(2,1)}), bf16[16,1,24,1536]{3,2,1,0:T(8,128)(2,1)S(1)}, u32[]{:S(2)}, u32[]{:S(2)}) async-start(bf16[16,1,24,1536]{3,2,1,0:T(8,128)(2,1)} %fusion.46), calls=%async_computation.3 | async-start | bytes 2359296 | tf_op jit(solution)/shard_map/all_to_all | solution.py:125
  239.8 4.7 %collective-permute-start.11 = (bf16[64,768]{1,0:T(8,128)(2,1)S(1)}, bf16[64,768]{1,0:T(8,128)(2,1)S(1)}, u32[]{:S(2)}, u32[]{:S(2)}) collective-permute-start(bf16[64,768]{1,0:T(8,128)(2,1)S(1)} %select_convert_fusion.3), channel_id=1, source_target_pairs={{0,2},{1,3},{2,0},{3,1},{4,6},{5,7},{6,4},{7,5},{8,10},{9,11},{10,... | collective-permute-start | bytes 294920 | tf_op jit(solution)/shard_map/ppermute | solution.py:18
  (13 other events, 33.6 us)

commit v12 on v11

--- a/solution.py
+++ b/solution.py
@@ -129,23 +129,21 @@
         picked = jnp.take(summed.reshape(-1, 2 * quarter), dest, axis=0)
         picked = picked.reshape(rows_here, 2, 2 * quarter)
         y_half = jnp.sum(picked * weights[:, :, None], axis=1)
-        y_keep = jnp.where(x_first, y_half[:, :quarter], y_half[:, quarter:])
-        y_give = jnp.where(x_first, y_half[:, quarter:], y_half[:, :quarter])
-        y_got = swap(y_give.astype(jnp.bfloat16), "tensor", 2).astype(jnp.float32)
-        xf = jnp.where(x_first, half_rows[:, :quarter], half_rows[:, quarter:]).astype(jnp.float32)
-        mixed = xf + (y_keep + y_got)
-        produced = mixed.astype(jnp.bfloat16)
+        y_mine = y_half.astype(jnp.bfloat16)
+        y_other = swap(y_mine, "tensor", 2)
+        full_half = (
+            half_rows.astype(jnp.float32)
+            + (y_mine.astype(jnp.float32) + y_other.astype(jnp.float32))
+        ).astype(jnp.bfloat16)
+        produced = jnp.where(x_first, full_half[:, :quarter], full_half[:, quarter:])
         chosen = (jnp.arange(micro, dtype=jnp.int32) == which)[:, None, None]
         collected = jnp.where(chosen, produced[None], collected)
-        return produced, collected
+        return full_half, collected
 
     def looped(step, state):
         carried, collected = state
-        produced, collected = layer_step(step, carried, collected)
-        carried = to_half(
-            from_behind(produced, "section", 1),
-            lax.ppermute(produced, ("section", "tensor"), cross_route),
-        )
+        full_half, collected = layer_step(step, carried, collected)
+        carried = lax.ppermute(full_half, ("section", "tensor"), cross_route)
         return carried, collected
 
     carried = jnp.zeros((rows_here, 2 * quarter), jnp.bfloat16)

time: 246 us -> 252 us (1.024)
  waiting for transfers between devices: 103 us -> 110 us
  starting transfers between devices: 22.6 us -> 18.6 us
  blocking collectives: 65.6 us -> 69.2 us
    ppermute x13, waiting for transfers between devices: 29.4 us -> 34.5 us  [swap(): return lax.ppermute(block, axis, [(i, i ^ bit) for i in range(n)])]
    all_to_all x3, blocking collectives: 65.6 us -> 69.2 us  [layer_step(): lax.all_to_all(outgoing, 'expert', split_axis=0, concat_axis=0, tiled=True)]
    ppermute x4 -> x2, starting transfers between devices: 5.17 us -> 2.58 us  [looped(): carried = lax.ppermute(full_half, ('section', 'tensor'), cross_route)]
    ppermute x4 -> x2, waiting for transfers between devices: 13.2 us -> 14.7 us  [looped(): carried = lax.ppermute(full_half, ('section', 'tensor'), cross_route)]
  transfers between devices with their start and end apart: 20 -> 18, of which waited for: 17 -> 15; matrix products, arithmetic and copies ran while one was open for 2% -> 2% of each run, Pallas kernels for 0% -> 0%
where the time goes in v12:
time: 252 us; the launch traced here: 251 us
  waiting for transfers between devices  110 us (44%)
  blocking collectives  69.2 us (27%)
  starting transfers between devices  18.6 us (7%)
  local copies, waits for them, and re-layouts  18.5 us (7%)
  other arithmetic  17.1 us (7%)
  matrix products  16.9 us (7%)
    all_to_all x3, blocking collectives, layer_step(): lax.all_to_all(outgoing, 'expert', split_axis=0, concat_axis=0, tiled=True)  69.2 us
    all_to_all x3, waiting for transfers between devices, layer_step(): lax.all_to_all(chip_sum, 'expert', split_axis=0, concat_axis=0, tiled=True)  60.6 us
    ppermute x13, waiting for transfers between devices, swap(): return lax.ppermute(block, axis, [(i, i ^ bit) for i in range(n)])  34.5 us
    ppermute x2, waiting for transfers between devices, looped(): carried = lax.ppermute(full_half, ('section', 'tensor'), cross_route)  14.7 us
    all_to_all x3, starting transfers between devices, layer_step(): lax.all_to_all(chip_sum, 'expert', split_axis=0, concat_axis=0, tiled=True)  11.5 us
    dot_general x3, matrix products, layer_step(): jnp.einsum('sekd,edf->sekf', normed, up_local, preferred_element_type=jnp...  8.63 us
    dot_general x3, matrix products, layer_step(): jnp.einsum('sekf,efd->sekd', hidden, down_local, preferred_element_type=j...  8.29 us
  transfers between devices with their start and end apart: 18, of which 15 were waited for; matrix products, arithmetic and copies ran while one was open for 2% of the time, Pallas kernels for 0%

profile of v12, /device:TPU:6, one launch (start us, length us, event | category | flops | bytes accessed | tf_op | source)
XLA Modules:
  0.0 251.0 jit_solution(6242873185719770420)
XLA Ops:
  11.2 166.8 %while.17 = (s32[]{:T(128)}, bf16[64,1536]{1,0:T(8,128)(2,1)S(1)}, bf16[2,64,768]{2,1,0:T(8,128)(2,1)S(1)}, pred[]{:T(512)}, bf16[2,64,1536]{2,1,0:T(8,128)(2,1)...) while((s32[]{:T(128)}, bf16[64,1536]{1,0:T(8,128)(2,1)S(1)}, ...), condition=%wide.region_8.11_spmd.clone, body=%wide.region_4.10_spmd.clone.sunk | while | flops 4871508992 | bytes 128428112 | solution.py:150
  12.7 26.1 %all_to_all.35 = bf16[16,1,24,1536]{3,2,1,0:T(8,128)(2,1)S(1)} all-to-all(bf16[16,1,24,1536]{3,2,1,0:T(8,128)(2,1)S(1)} %bitcast.195), channel_id=1, replica_groups=mesh['section'=2,'expert'=16,'tensor'=4] {'expert'}, dimensions={0} | all-to-all | bytes 2359296 | tf_op jit(solution)/shard_map/while/body/eval_jaxpr/all_to_all | solution.py:95
  38.8 2.8 %collective-permute-done = bf16[16,1,24,1536]{3,2,0,1:T(8,128)(2,1)S(1)} collective-permute-done((bf16[16,1,24,1536]{3,2,0,1:T(8,128)(2,1)S(1)}, bf16[16,1,24,1536]{3,2,0,1:T(8,128)(2,1)S(1)}, u32[]{:S(2)}, u32[]{:S(2)}) %collective-permute-start) | collective-permute-done | bytes 1179680 | tf_op jit(solution)/shard_map/while/body/eval_jaxpr/ppermute | solution.py:18
  44.5 2.9 %fusion.80 = f32[16,24,1024]{2,1,0:T(8,128)S(1)} fusion(bf16[1,3072,1024]{2,1,0:T(8,128)(2,1)S(1)} %bitcast.212, bf16[16,24,768]{2,1,0:T(8,128)(2,1)S(1)} %get-tuple-element.505, bf16[16,24,768]{2,1,0:T(8,128)(2,1)S(1)} %get-tuple-element.506, bf16[16,24,768]{2,1,0:T(8,128)(2,1)S(1)} %get-tuple-element.507, ...), kind=kOutput, calls=%fused_computation.8.clone.1 | convolution fusion | flops 2428895232 | bytes 10237440 | tf_op jit(solution)/shard_map/while/body/eval_jaxpr/sekd,edf->sekf/dot_general | solution.py:105
  47.4 2.8 %fusion.81 = f32[16,1,24,3072]{3,2,0,1:T(8,128)S(1)} fusion(bf16[1,1024,3072]{2,1,0:T(8,128)(2,1)S(1)} %bitcast.218, f32[16,24,1024]{2,1,0:T(8,128)S(1)} %fusion.80), kind=kOutput, calls=%fused_computation.12.clone.1 | convolution fusion | flops 2417885184 | bytes 12582912 | tf_op jit(solution)/shard_map/while/body/eval_jaxpr/sekf,efd->sekd/dot_general | solution.py:109
  55.3 3.8 %all-to-all-start.1 = ((bf16[16,1,24,1536]{3,2,1,0:T(8,128)(2,1)}), bf16[16,1,24,1536]{3,2,1,0:T(8,128)(2,1)S(1)}, u32[]{:S(2)}, u32[]{:S(2)}) async-start(bf16[16,1,24,1536]{3,2,1,0:T(8,128)(2,1)} %fusion.83), calls=%async_computation.1 | async-start | bytes 2359296 | tf_op jit(solution)/shard_map/while/body/eval_jaxpr/all_to_all | solution.py:125
  59.2 20.2 %all-to-all-done.1 = bf16[16,1,24,1536]{3,2,1,0:T(8,128)(2,1)S(1)} async-done(((bf16[16,1,24,1536]{3,2,1,0:T(8,128)(2,1)}), bf16[16,1,24,1536]{3,2,1,0:T(8,128)(2,1)S(1)}, u32[]{:S(2)}, u32[]{:S(2)}) %all-to-all-start.1) | async-done | bytes 1179680 | tf_op jit(solution)/shard_map/while/body/eval_jaxpr/all_to_all | solution.py:125
  83.1 4.9 %collective-permute-done.2 = bf16[64,1536]{1,0:T(8,128)(2,1)S(1)} collective-permute-done((bf16[64,1536]{1,0:T(8,128)(2,1)S(1)}, bf16[64,1536]{1,0:T(8,128)(2,1)S(1)}, u32[]{:S(2)}, u32[]{:S(2)}) %collective-permute-start.2) | collective-permute-done | bytes 196640 | tf_op jit(solution)/shard_map/while/body/eval_jaxpr/ppermute | solution.py:18
  89.5 7.4 %collective-permute-done.3 = bf16[64,1536]{1,0:T(8,128)(2,1)S(1)} collective-permute-done((bf16[64,1536]{1,0:T(8,128)(2,1)S(1)}, bf16[64,1536]{1,0:T(8,128)(2,1)S(1)}, u32[]{:S(2)}, u32[]{:S(2)}) %collective-permute-start.3) | collective-permute-done | bytes 196640 | tf_op jit(solution)/shard_map/while/body/eval_jaxpr/ppermute | solution.py:146
  98.3 21.6 %all_to_all.35 = bf16[16,1,24,1536]{3,2,1,0:T(8,128)(2,1)S(1)} all-to-all(bf16[16,1,24,1536]{3,2,1,0:T(8,128)(2,1)S(1)} %bitcast.195), channel_id=1, replica_groups=mesh['section'=2,'expert'=16,'tensor'=4] {'expert'}, dimensions={0} | all-to-all | bytes 2359296 | tf_op jit(solution)/shard_map/while/body/eval_jaxpr/all_to_all | solution.py:95
  119.9 2.8 %collective-permute-done = bf16[16,1,24,1536]{3,2,0,1:T(8,128)(2,1)S(1)} collective-permute-done((bf16[16,1,24,1536]{3,2,0,1:T(8,128)(2,1)S(1)}, bf16[16,1,24,1536]{3,2,0,1:T(8,128)(2,1)S(1)}, u32[]{:S(2)}, u32[]{:S(2)}) %collective-permute-start) | collective-permute-done | bytes 1179680 | tf_op jit(solution)/shard_map/while/body/eval_jaxpr/ppermute | solution.py:18
  125.6 2.9 %fusion.80 = f32[16,24,1024]{2,1,0:T(8,128)S(1)} fusion(bf16[1,3072,1024]{2,1,0:T(8,128)(2,1)S(1)} %bitcast.212, bf16[16,24,768]{2,1,0:T(8,128)(2,1)S(1)} %get-tuple-element.505, bf16[16,24,768]{2,1,0:T(8,128)(2,1)S(1)} %get-tuple-element.506, bf16[16,24,768]{2,1,0:T(8,128)(2,1)S(1)} %get-tuple-element.507, ...), kind=kOutput, calls=%fused_computation.8.clone.1 | convolution fusion | flops 2428895232 | bytes 10237440 | tf_op jit(solution)/shard_map/while/body/eval_jaxpr/sekd,edf->sekf/dot_general | solution.py:105
  128.5 2.8 %fusion.81 = f32[16,1,24,3072]{3,2,0,1:T(8,128)S(1)} fusion(bf16[1,1024,3072]{2,1,0:T(8,128)(2,1)S(1)} %bitcast.218, f32[16,24,1024]{2,1,0:T(8,128)S(1)} %fusion.80), kind=kOutput, calls=%fused_computation.12.clone.1 | convolution fusion | flops 2417885184 | bytes 12582912 | tf_op jit(solution)/shard_map/while/body/eval_jaxpr/sekf,efd->sekd/dot_general | solution.py:109
  136.4 3.8 %all-to-all-start.1 = ((bf16[16,1,24,1536]{3,2,1,0:T(8,128)(2,1)}), bf16[16,1,24,1536]{3,2,1,0:T(8,128)(2,1)S(1)}, u32[]{:S(2)}, u32[]{:S(2)}) async-start(bf16[16,1,24,1536]{3,2,1,0:T(8,128)(2,1)} %fusion.83), calls=%async_computation.1 | async-start | bytes 2359296 | tf_op jit(solution)/shard_map/while/body/eval_jaxpr/all_to_all | solution.py:125
  140.3 20.2 %all-to-all-done.1 = bf16[16,1,24,1536]{3,2,1,0:T(8,128)(2,1)S(1)} async-done(((bf16[16,1,24,1536]{3,2,1,0:T(8,128)(2,1)}), bf16[16,1,24,1536]{3,2,1,0:T(8,128)(2,1)S(1)}, u32[]{:S(2)}, u32[]{:S(2)}) %all-to-all-start.1) | async-done | bytes 1179680 | tf_op jit(solution)/shard_map/while/body/eval_jaxpr/all_to_all | solution.py:125
  163.4 5.7 %collective-permute-done.2 = bf16[64,1536]{1,0:T(8,128)(2,1)S(1)} collective-permute-done((bf16[64,1536]{1,0:T(8,128)(2,1)S(1)}, bf16[64,1536]{1,0:T(8,128)(2,1)S(1)}, u32[]{:S(2)}, u32[]{:S(2)}) %collective-permute-start.2) | collective-permute-done | bytes 196640 | tf_op jit(solution)/shard_map/while/body/eval_jaxpr/ppermute | solution.py:18
  170.6 7.4 %collective-permute-done.3 = bf16[64,1536]{1,0:T(8,128)(2,1)S(1)} collective-permute-done((bf16[64,1536]{1,0:T(8,128)(2,1)S(1)}, bf16[64,1536]{1,0:T(8,128)(2,1)S(1)}, u32[]{:S(2)}, u32[]{:S(2)}) %collective-permute-start.3) | collective-permute-done | bytes 196640 | tf_op jit(solution)/shard_map/while/body/eval_jaxpr/ppermute | solution.py:146
  179.4 21.6 %all_to_all.34 = bf16[16,1,24,1536]{3,2,1,0:T(8,128)(2,1)S(1)} all-to-all(bf16[16,1,24,1536]{3,2,1,0:T(8,128)(2,1)S(1)} %bitcast.200), channel_id=1, replica_groups=mesh['section'=2,'expert'=16,'tensor'=4] {'expert'}, dimensions={0} | all-to-all | bytes 2359296 | tf_op jit(solution)/shard_map/all_to_all | solution.py:95
  200.9 2.8 %collective-permute-done.8 = bf16[16,1,24,1536]{3,2,0,1:T(8,128)(2,1)S(1)} collective-permute-done((bf16[16,1,24,1536]{3,2,0,1:T(8,128)(2,1)S(1)}, bf16[16,1,24,1536]{3,2,0,1:T(8,128)(2,1)S(1)}, u32[]{:S(2)}, u32[]{:S(2)}) %collective-permute-start.8) | collective-permute-done | bytes 1179680 | tf_op jit(solution)/shard_map/ppermute | solution.py:18
  206.7 2.9 %fusion.28 = f32[16,24,1024]{2,1,0:T(8,128)S(1)} fusion(bf16[1,1,3072,1024]{3,2,1,0:T(8,128)(2,1)S(1)} %bitcast.215, bf16[16,24,768]{2,1,0:T(8,128)(2,1)S(1)} %get-tuple-element.399, bf16[16,24,768]{2,1,0:T(8,128)(2,1)S(1)} %get-tuple-element.386, bf16[16,24,768]{2,1,0:T(8,128)(2,1)S(1)} %get-tuple-element.400, ...), kind=kOutput, calls=%fused_computation.66 | convolution fusion | flops 2428895232 | bytes 10237440 | tf_op jit(solution)/shard_map/sekd,edf->sekf/dot_general | solution.py:105
  209.6 2.8 %fusion.30 = f32[16,1,24,3072]{3,2,0,1:T(8,128)S(1)} fusion(bf16[1,1,1024,3072]{3,2,1,0:T(8,128)(2,1)S(1)} %bitcast.221, f32[16,24,1024]{2,1,0:T(8,128)S(1)} %fusion.28), kind=kOutput, calls=%fused_computation.70 | convolution fusion | flops 2417885184 | bytes 12582912 | tf_op jit(solution)/shard_map/sekf,efd->sekd/dot_general | solution.py:109
  217.4 3.8 %all-to-all-start.3 = ((bf16[16,1,24,1536]{3,2,1,0:T(8,128)(2,1)}), bf16[16,1,24,1536]{3,2,1,0:T(8,128)(2,1)S(1)}, u32[]{:S(2)}, u32[]{:S(2)}) async-start(bf16[16,1,24,1536]{3,2,1,0:T(8,128)(2,1)} %fusion.46), calls=%async_computation.3 | async-start | bytes 2359296 | tf_op jit(solution)/shard_map/all_to_all | solution.py:125
  221.4 20.2 %all-to-all-done.3 = bf16[16,1,24,1536]{3,2,1,0:T(8,128)(2,1)S(1)} async-done(((bf16[16,1,24,1536]{3,2,1,0:T(8,128)(2,1)}), bf16[16,1,24,1536]{3,2,1,0:T(8,128)(2,1)S(1)}, u32[]{:S(2)}, u32[]{:S(2)}) %all-to-all-start.3) | async-done | bytes 1179680 | tf_op jit(solution)/shard_map/all_to_all | solution.py:125
  244.5 5.7 %collective-permute-done.10 = bf16[64,1536]{1,0:T(8,128)(2,1)S(1)} collective-permute-done((bf16[64,1536]{1,0:T(8,128)(2,1)S(1)}, bf16[64,1536]{1,0:T(8,128)(2,1)S(1)}, u32[]{:S(2)}, u32[]{:S(2)}) %collective-permute-start.10) | collective-permute-done | bytes 196640 | tf_op jit(solution)/shard_map/ppermute | solution.py:18
  (166 shorter events, 52.4 us)
Async XLA Ops:
  0.7 7.6 %collective-permute-start.5 = (f32[768]{0:T(1024)S(1)}, f32[768]{0:T(1024)S(1)}, u32[]{:S(2)}, u32[]{:S(2)}) collective-permute-start(f32[768]{0:T(1024)S(1)} %reduce.6), channel_id=1, source_target_pairs={{0,1},{1,0},{2,3},{3,2},{4,5},{5,4},{6,7},{7,6},{8,9},{9,8},{10,11... | collective-permute-start | bytes 9224 | tf_op jit(solution)/shard_map/ppermute | solution.py:18
  0.8 7.6 %collective-permute-start.6 = (f32[768]{0:T(1024)S(1)}, f32[768]{0:T(1024)S(1)}, u32[]{:S(2)}, u32[]{:S(2)}) collective-permute-start(f32[768]{0:T(1024)S(1)} %reduce.6), channel_id=1, source_target_pairs={{0,2},{1,3},{2,0},{3,1},{4,6},{5,7},{6,4},{7,5},{8,10},{9,11},{10,... | collective-permute-start | bytes 9224 | tf_op jit(solution)/shard_map/ppermute | solution.py:18
  1.7 6.7 %collective-permute-start.7 = (f32[768]{0:T(1024)S(1)}, f32[768]{0:T(1024)S(1)}, u32[]{:S(2)}, u32[]{:S(2)}) collective-permute-start(f32[768]{0:T(1024)S(1)} %reduce.6), channel_id=1, source_target_pairs={{0,3},{1,2},{2,1},{3,0},{4,7},{5,6},{6,5},{7,4},{8,11},{9,10},{10,... | collective-permute-start | bytes 9224 | tf_op jit(solution)/shard_map/ppermute | solution.py:18
  2.6 7.4 %collective-permute-start.4 = (bf16[2,64,768]{2,1,0:T(8,128)(2,1)}, bf16[2,64,768]{2,1,0:T(8,128)(2,1)S(1)}, u32[]{:S(2)}, u32[]{:S(2)}) collective-permute-start(bf16[2,64,768]{2,1,0:T(8,128)(2,1)} %param.12), channel_id=1, source_target_pairs={{0,2},{1,3},{2,0},{3,1},{4,6},{5,7},{6,4},{7,5},{8,10},{9,11},{10,... | collective-permute-start | bytes 589832 | tf_op jit(solution)/shard_map/ppermute | solution.py:18
  38.8 2.8 %collective-permute-start = (bf16[16,1,24,1536]{3,2,0,1:T(8,128)(2,1)S(1)}, bf16[16,1,24,1536]{3,2,0,1:T(8,128)(2,1)S(1)}, u32[]{:S(2)}, u32[]{:S(2)}) collective-permute-start(bf16[16,1,24,1536]{3,2,0,1:T(8,128)(2,1)S(1)} %bitcast.193), channel_id=1, source_target_pairs={{0,1},{1,0},{2,3},{3,2},{4,5},{5,4},{6,7},{7,6},{8,9},{9,8},{10,11... | collective-permute-start | bytes 3538952 | tf_op jit(solution)/shard_map/while/body/eval_jaxpr/ppermute | solution.py:18
  42.1 5.3 %slice-start.4 = ((s8[6291456]{0:T(1024)(128)(4,1)}), s8[4194304]{0:T(1024)(128)(4,1)S(1)}, s32[]{:S(2)}) async-start(s8[6291456]{0:T(1024)(128)(4,1)} %bitcast.217), calls=%async_computation.8 | async-start | bytes 8388608 | tf_op jit(solution)/shard_map/while
  50.9 2.9 %collective-permute-start.1 = (bf16[16,1,24,1536]{3,2,0,1:T(8,128)(2,1)S(1)}, bf16[16,1,24,1536]{3,2,0,1:T(8,128)(2,1)S(1)}, u32[]{:S(2)}, u32[]{:S(2)}) collective-permute-start(bf16[16,1,24,1536]{3,2,0,1:T(8,128)(2,1)S(1)} %select_convert_fusion.3), channel_id=1, source_target_pairs={{0,1},{1,0},{2,3},{3,2},{4,5},{5,4},{6,7},{7,6},{8,9},{9,8},{10,11... | collective-permute-start | bytes 3538952 | tf_op jit(solution)/shard_map/while/body/eval_jaxpr/ppermute | solution.py:18
  55.3 3.8 %copy-start = (f32[1,2,64,2]{2,3,1,0:T(2,128)S(1)}, f32[1,2,64,2]{2,3,1,0:T(2,128)}, u32[]{:S(2)}) copy-start(f32[1,2,64,2]{2,3,1,0:T(2,128)} %get-tuple-element.565) | copy-start | bytes 3076 | tf_op jit(solution)/shard_map/while
  55.3 24.2 %all-to-all-start.1 = ((bf16[16,1,24,1536]{3,2,1,0:T(8,128)(2,1)}), bf16[16,1,24,1536]{3,2,1,0:T(8,128)(2,1)S(1)}, u32[]{:S(2)}, u32[]{:S(2)}) async-start(bf16[16,1,24,1536]{3,2,1,0:T(8,128)(2,1)} %fusion.83), calls=%async_computation.1 | async-start | bytes 2359296 | tf_op jit(solution)/shard_map/while/body/eval_jaxpr/all_to_all | solution.py:125
  82.2 5.8 %collective-permute-start.2 = (bf16[64,1536]{1,0:T(8,128)(2,1)S(1)}, bf16[64,1536]{1,0:T(8,128)(2,1)S(1)}, u32[]{:S(2)}, u32[]{:S(2)}) collective-permute-start(bf16[64,1536]{1,0:T(8,128)(2,1)S(1)} %multiply_reduce_fusion.7), channel_id=1, source_target_pairs={{0,2},{1,3},{2,0},{3,1},{4,6},{5,7},{6,4},{7,5},{8,10},{9,11},{10,... | collective-permute-start | bytes 589832 | tf_op jit(solution)/shard_map/while/body/eval_jaxpr/ppermute | solution.py:18
  88.1 8.8 %collective-permute-start.3 = (bf16[64,1536]{1,0:T(8,128)(2,1)S(1)}, bf16[64,1536]{1,0:T(8,128)(2,1)S(1)}, u32[]{:S(2)}, u32[]{:S(2)}) collective-permute-start(bf16[64,1536]{1,0:T(8,128)(2,1)S(1)} %add_convert_fusion.5), channel_id=1, source_target_pairs={{0,66},{1,67},{2,64},{3,65},{4,70},{5,71},{6,68},{7,69},{8,74},{9,... | collective-permute-start | bytes 589832 | tf_op jit(solution)/shard_map/while/body/eval_jaxpr/ppermute | solution.py:146
  119.9 2.8 %collective-permute-start = (bf16[16,1,24,1536]{3,2,0,1:T(8,128)(2,1)S(1)}, bf16[16,1,24,1536]{3,2,0,1:T(8,128)(2,1)S(1)}, u32[]{:S(2)}, u32[]{:S(2)}) collective-permute-start(bf16[16,1,24,1536]{3,2,0,1:T(8,128)(2,1)S(1)} %bitcast.193), channel_id=1, source_target_pairs={{0,1},{1,0},{2,3},{3,2},{4,5},{5,4},{6,7},{7,6},{8,9},{9,8},{10,11... | collective-permute-start | bytes 3538952 | tf_op jit(solution)/shard_map/while/body/eval_jaxpr/ppermute | solution.py:18
  123.2 5.3 %slice-start.4 = ((s8[6291456]{0:T(1024)(128)(4,1)}), s8[4194304]{0:T(1024)(128)(4,1)S(1)}, s32[]{:S(2)}) async-start(s8[6291456]{0:T(1024)(128)(4,1)} %bitcast.217), calls=%async_computation.8 | async-start | bytes 8388608 | tf_op jit(solution)/shard_map/while
  132.1 2.9 %collective-permute-start.1 = (bf16[16,1,24,1536]{3,2,0,1:T(8,128)(2,1)S(1)}, bf16[16,1,24,1536]{3,2,0,1:T(8,128)(2,1)S(1)}, u32[]{:S(2)}, u32[]{:S(2)}) collective-permute-start(bf16[16,1,24,1536]{3,2,0,1:T(8,128)(2,1)S(1)} %select_convert_fusion.3), channel_id=1, source_target_pairs={{0,1},{1,0},{2,3},{3,2},{4,5},{5,4},{6,7},{7,6},{8,9},{9,8},{10,11... | collective-permute-start | bytes 3538952 | tf_op jit(solution)/shard_map/while/body/eval_jaxpr/ppermute | solution.py:18
  136.4 3.8 %copy-start = (f32[1,2,64,2]{2,3,1,0:T(2,128)S(1)}, f32[1,2,64,2]{2,3,1,0:T(2,128)}, u32[]{:S(2)}) copy-start(f32[1,2,64,2]{2,3,1,0:T(2,128)} %get-tuple-element.565) | copy-start | bytes 3076 | tf_op jit(solution)/shard_map/while
  136.4 24.2 %all-to-all-start.1 = ((bf16[16,1,24,1536]{3,2,1,0:T(8,128)(2,1)}), bf16[16,1,24,1536]{3,2,1,0:T(8,128)(2,1)S(1)}, u32[]{:S(2)}, u32[]{:S(2)}) async-start(bf16[16,1,24,1536]{3,2,1,0:T(8,128)(2,1)} %fusion.83), calls=%async_computation.1 | async-start | bytes 2359296 | tf_op jit(solution)/shard_map/while/body/eval_jaxpr/all_to_all | solution.py:125
  163.3 5.8 %collective-permute-start.2 = (bf16[64,1536]{1,0:T(8,128)(2,1)S(1)}, bf16[64,1536]{1,0:T(8,128)(2,1)S(1)}, u32[]{:S(2)}, u32[]{:S(2)}) collective-permute-start(bf16[64,1536]{1,0:T(8,128)(2,1)S(1)} %multiply_reduce_fusion.7), channel_id=1, source_target_pairs={{0,2},{1,3},{2,0},{3,1},{4,6},{5,7},{6,4},{7,5},{8,10},{9,11},{10,... | collective-permute-start | bytes 589832 | tf_op jit(solution)/shard_map/while/body/eval_jaxpr/ppermute | solution.py:18
  169.2 8.8 %collective-permute-start.3 = (bf16[64,1536]{1,0:T(8,128)(2,1)S(1)}, bf16[64,1536]{1,0:T(8,128)(2,1)S(1)}, u32[]{:S(2)}, u32[]{:S(2)}) collective-permute-start(bf16[64,1536]{1,0:T(8,128)(2,1)S(1)} %add_convert_fusion.5), channel_id=1, source_target_pairs={{0,66},{1,67},{2,64},{3,65},{4,70},{5,71},{6,68},{7,69},{8,74},{9,... | collective-permute-start | bytes 589832 | tf_op jit(solution)/shard_map/while/body/eval_jaxpr/ppermute | solution.py:146
  200.9 2.8 %collective-permute-start.8 = (bf16[16,1,24,1536]{3,2,0,1:T(8,128)(2,1)S(1)}, bf16[16,1,24,1536]{3,2,0,1:T(8,128)(2,1)S(1)}, u32[]{:S(2)}, u32[]{:S(2)}) collective-permute-start(bf16[16,1,24,1536]{3,2,0,1:T(8,128)(2,1)S(1)} %bitcast.198), channel_id=1, source_target_pairs={{0,1},{1,0},{2,3},{3,2},{4,5},{5,4},{6,7},{7,6},{8,9},{9,8},{10,11... | collective-permute-start | bytes 3538952 | tf_op jit(solution)/shard_map/ppermute | solution.py:18
  204.3 5.3 %slice-start.6 = ((s8[6291456]{0:T(1024)(128)(4,1)}), s8[4194304]{0:T(1024)(128)(4,1)S(1)}, s32[]{:S(2)}) async-start(s8[6291456]{0:T(1024)(128)(4,1)} %bitcast.219), calls=%async_computation.10 | async-start | bytes 8388608
  213.1 2.9 %collective-permute-start.9 = (bf16[16,1,24,1536]{3,2,0,1:T(8,128)(2,1)S(1)}, bf16[16,1,24,1536]{3,2,0,1:T(8,128)(2,1)S(1)}, u32[]{:S(2)}, u32[]{:S(2)}) collective-permute-start(bf16[16,1,24,1536]{3,2,0,1:T(8,128)(2,1)S(1)} %select_convert_fusion.1), channel_id=1, source_target_pairs={{0,1},{1,0},{2,3},{3,2},{4,5},{5,4},{6,7},{7,6},{8,9},{9,8},{10,11... | collective-permute-start | bytes 3538952 | tf_op jit(solution)/shard_map/ppermute | solution.py:18
  217.4 3.8 %copy-start.1 = (f32[1,2,64,2]{2,3,1,0:T(2,128)S(1)}, f32[1,2,64,2]{2,3,1,0:T(2,128)}, u32[]{:S(2)}) copy-start(f32[1,2,64,2]{2,3,1,0:T(2,128)} %get-tuple-element.590) | copy-start | bytes 3076
  217.4 24.2 %all-to-all-start.3 = ((bf16[16,1,24,1536]{3,2,1,0:T(8,128)(2,1)}), bf16[16,1,24,1536]{3,2,1,0:T(8,128)(2,1)S(1)}, u32[]{:S(2)}, u32[]{:S(2)}) async-start(bf16[16,1,24,1536]{3,2,1,0:T(8,128)(2,1)} %fusion.46), calls=%async_computation.3 | async-start | bytes 2359296 | tf_op jit(solution)/shard_map/all_to_all | solution.py:125
  244.4 5.8 %collective-permute-start.10 = (bf16[64,1536]{1,0:T(8,128)(2,1)S(1)}, bf16[64,1536]{1,0:T(8,128)(2,1)S(1)}, u32[]{:S(2)}, u32[]{:S(2)}) collective-permute-start(bf16[64,1536]{1,0:T(8,128)(2,1)S(1)} %multiply_reduce_fusion.3), channel_id=1, source_target_pairs={{0,2},{1,3},{2,0},{3,1},{4,6},{5,7},{6,4},{7,5},{8,10},{9,11},{10,... | collective-permute-start | bytes 589832 | tf_op jit(solution)/shard_map/ppermute | solution.py:18
  (11 other events, 25.7 us)

commit v13 on v11

--- a/solution.py
+++ b/solution.py
@@ -70,7 +70,7 @@
     )
     n_t = lax.axis_size("tensor")
     cross_route = [
-        (s * n_t + t, (s + 1) * n_t + (t ^ 2)) for s in range(segments - 1) for t in range(n_t)
+        (s * n_t + t, ((s + 1) % segments) * n_t + (t ^ 2)) for s in range(segments) for t in range(n_t)
     ]
     def layer_step(step, carried, collected):
         which = step - segment_pos
@@ -143,7 +143,7 @@
         carried, collected = state
         produced, collected = layer_step(step, carried, collected)
         carried = to_half(
-            from_behind(produced, "section", 1),
+            lax.ppermute(produced, "section", [(i, (i + 1) % segments) for i in range(segments)]),
             lax.ppermute(produced, ("section", "tensor"), cross_route),
         )
         return carried, collected

time: 246 us -> 244 us (level)
    ppermute x2, waiting for transfers between devices: 10 us -> 7.55 us  [looped(): lax.ppermute(produced, ('section', 'tensor'), cross_route)]
  transfers between devices with their start and end apart: 20 -> 20, of which waited for: 17 -> 16; matrix products, arithmetic and copies ran while one was open for 2% -> 2% of each run, Pallas kernels for 0% -> 0%
where the time goes in v13:
time: 244 us; the launch traced here: 242 us
  waiting for transfers between devices  101 us (41%)
  blocking collectives  66.1 us (27%)
  starting transfers between devices  21.1 us (9%)
  local copies, waits for them, and re-layouts  18.4 us (8%)
  other arithmetic  17.7 us (7%)
  matrix products  16.7 us (7%)
    all_to_all x3, blocking collectives, layer_step(): lax.all_to_all(outgoing, 'expert', split_axis=0, concat_axis=0, tiled=True)  66.1 us
    all_to_all x3, waiting for transfers between devices, layer_step(): lax.all_to_all(chip_sum, 'expert', split_axis=0, concat_axis=0, tiled=True)  60.6 us
    ppermute x13, waiting for transfers between devices, swap(): return lax.ppermute(block, axis, [(i, i ^ bit) for i in range(n)])  31 us
    all_to_all x3, starting transfers between devices, layer_step(): lax.all_to_all(chip_sum, 'expert', split_axis=0, concat_axis=0, tiled=True)  11.5 us
    dot_general x3, matrix products, layer_step(): jnp.einsum('sekd,edf->sekf', normed, up_local, preferred_element_type=jnp...  8.6 us
    dot_general x3, matrix products, layer_step(): jnp.einsum('sekf,efd->sekd', hidden, down_local, preferred_element_type=j...  8.12 us
    ppermute x2, waiting for transfers between devices, looped(): lax.ppermute(produced, ('section', 'tensor'), cross_route)  7.55 us
  transfers between devices with their start and end apart: 20, of which 16 were waited for; matrix products, arithmetic and copies ran while one was open for 2% of the time, Pallas kernels for 0%

profile of v13, /device:TPU:6, one launch (start us, length us, event | category | flops | bytes accessed | tf_op | source)
XLA Modules:
  0.0 241.9 jit_solution(3224543651604832071)
XLA Ops:
  11.2 160.8 %while.17 = (s32[]{:T(128)}, bf16[64,1536]{1,0:T(8,128)(2,1)S(1)}, bf16[2,64,768]{2,1,0:T(8,128)(2,1)S(1)}, pred[]{:T(512)}, pred[]{:T(512)}, /*index=5*/bf16[2,...) while((s32[]{:T(128)}, bf16[64,1536]{1,0:T(8,128)(2,1)S(1)}, ...), condition=%wide.region_8.11_spmd.clone, body=%wide.region_4.10_spmd.clone.sunk | while | flops 4872246272 | bytes 128624768 | solution.py:152
  12.8 26.1 %all_to_all.35 = bf16[16,1,24,1536]{3,2,1,0:T(8,128)(2,1)S(1)} all-to-all(bf16[16,1,24,1536]{3,2,1,0:T(8,128)(2,1)S(1)} %bitcast.195), channel_id=1, replica_groups=mesh['section'=2,'expert'=16,'tensor'=4] {'expert'}, dimensions={0} | all-to-all | bytes 2359296 | tf_op jit(solution)/shard_map/while/body/eval_jaxpr/all_to_all | solution.py:95
  38.9 2.8 %collective-permute-done = bf16[16,1,24,1536]{3,2,0,1:T(8,128)(2,1)S(1)} collective-permute-done((bf16[16,1,24,1536]{3,2,0,1:T(8,128)(2,1)S(1)}, bf16[16,1,24,1536]{3,2,0,1:T(8,128)(2,1)S(1)}, u32[]{:S(2)}, u32[]{:S(2)}) %collective-permute-start) | collective-permute-done | bytes 1179680 | tf_op jit(solution)/shard_map/while/body/eval_jaxpr/ppermute | solution.py:18
  44.7 2.9 %fusion.80 = f32[16,24,1024]{2,1,0:T(8,128)S(1)} fusion(bf16[1,3072,1024]{2,1,0:T(8,128)(2,1)S(1)} %bitcast.212, bf16[16,24,768]{2,1,0:T(8,128)(2,1)S(1)} %get-tuple-element.505, bf16[16,24,768]{2,1,0:T(8,128)(2,1)S(1)} %get-tuple-element.506, bf16[16,24,768]{2,1,0:T(8,128)(2,1)S(1)} %get-tuple-element.507, ...), kind=kOutput, calls=%fused_computation.8.clone.1 | convolution fusion | flops 2428895232 | bytes 10237440 | tf_op jit(solution)/shard_map/while/body/eval_jaxpr/sekd,edf->sekf/dot_general | solution.py:105
  47.6 2.7 %fusion.81 = f32[16,1,24,3072]{3,2,0,1:T(8,128)S(1)} fusion(bf16[1,1024,3072]{2,1,0:T(8,128)(2,1)S(1)} %bitcast.218, f32[16,24,1024]{2,1,0:T(8,128)S(1)} %fusion.80), kind=kOutput, calls=%fused_computation.12.clone.1 | convolution fusion | flops 2417885184 | bytes 12582912 | tf_op jit(solution)/shard_map/while/body/eval_jaxpr/sekf,efd->sekd/dot_general | solution.py:109
  51.3 2.7 %collective-permute-done.1 = bf16[16,1,24,1536]{3,2,0,1:T(8,128)(2,1)S(1)} collective-permute-done((bf16[16,1,24,1536]{3,2,0,1:T(8,128)(2,1)S(1)}, bf16[16,1,24,1536]{3,2,0,1:T(8,128)(2,1)S(1)}, u32[]{:S(2)}, u32[]{:S(2)}) %collective-permute-start.1) | collective-permute-done | bytes 1179680 | tf_op jit(solution)/shard_map/while/body/eval_jaxpr/ppermute | solution.py:18
  55.4 3.8 %all-to-all-start.1 = ((bf16[16,1,24,1536]{3,2,1,0:T(8,128)(2,1)}), bf16[16,1,24,1536]{3,2,1,0:T(8,128)(2,1)S(1)}, u32[]{:S(2)}, u32[]{:S(2)}) async-start(bf16[16,1,24,1536]{3,2,1,0:T(8,128)(2,1)} %fusion.83), calls=%async_computation.1 | async-start | bytes 2359296 | tf_op jit(solution)/shard_map/while/body/eval_jaxpr/all_to_all | solution.py:125
  59.3 20.2 %all-to-all-done.1 = bf16[16,1,24,1536]{3,2,1,0:T(8,128)(2,1)S(1)} async-done(((bf16[16,1,24,1536]{3,2,1,0:T(8,128)(2,1)}), bf16[16,1,24,1536]{3,2,1,0:T(8,128)(2,1)S(1)}, u32[]{:S(2)}, u32[]{:S(2)}) %all-to-all-start.1) | async-done | bytes 1179680 | tf_op jit(solution)/shard_map/while/body/eval_jaxpr/all_to_all | solution.py:125
  83.2 3.8 %collective-permute-done.2 = bf16[64,768]{1,0:T(8,128)(2,1)S(1)} collective-permute-done((bf16[64,768]{1,0:T(8,128)(2,1)S(1)}, bf16[64,768]{1,0:T(8,128)(2,1)S(1)}, u32[]{:S(2)}, u32[]{:S(2)}) %collective-permute-start.2) | collective-permute-done | bytes 98336 | tf_op jit(solution)/shard_map/while/body/eval_jaxpr/ppermute | solution.py:18
  90.2 3.9 %collective-permute-done.3 = bf16[64,768]{1,0:T(8,128)(2,1)S(1)} collective-permute-done((bf16[64,768]{1,0:T(8,128)(2,1)S(1)}, bf16[64,768]{1,0:T(8,128)(2,1)S(1)}, u32[]{:S(2)}, u32[]{:S(2)}) %collective-permute-start.3) | collective-permute-done | bytes 98336 | tf_op jit(solution)/shard_map/while/body/eval_jaxpr/ppermute | solution.py:147
  95.6 20.5 %all_to_all.35 = bf16[16,1,24,1536]{3,2,1,0:T(8,128)(2,1)S(1)} all-to-all(bf16[16,1,24,1536]{3,2,1,0:T(8,128)(2,1)S(1)} %bitcast.195), channel_id=1, replica_groups=mesh['section'=2,'expert'=16,'tensor'=4] {'expert'}, dimensions={0} | all-to-all | bytes 2359296 | tf_op jit(solution)/shard_map/while/body/eval_jaxpr/all_to_all | solution.py:95
  116.2 2.8 %collective-permute-done = bf16[16,1,24,1536]{3,2,0,1:T(8,128)(2,1)S(1)} collective-permute-done((bf16[16,1,24,1536]{3,2,0,1:T(8,128)(2,1)S(1)}, bf16[16,1,24,1536]{3,2,0,1:T(8,128)(2,1)S(1)}, u32[]{:S(2)}, u32[]{:S(2)}) %collective-permute-start) | collective-permute-done | bytes 1179680 | tf_op jit(solution)/shard_map/while/body/eval_jaxpr/ppermute | solution.py:18
  121.9 2.9 %fusion.80 = f32[16,24,1024]{2,1,0:T(8,128)S(1)} fusion(bf16[1,3072,1024]{2,1,0:T(8,128)(2,1)S(1)} %bitcast.212, bf16[16,24,768]{2,1,0:T(8,128)(2,1)S(1)} %get-tuple-element.505, bf16[16,24,768]{2,1,0:T(8,128)(2,1)S(1)} %get-tuple-element.506, bf16[16,24,768]{2,1,0:T(8,128)(2,1)S(1)} %get-tuple-element.507, ...), kind=kOutput, calls=%fused_computation.8.clone.1 | convolution fusion | flops 2428895232 | bytes 10237440 | tf_op jit(solution)/shard_map/while/body/eval_jaxpr/sekd,edf->sekf/dot_general | solution.py:105
  128.5 2.7 %collective-permute-done.1 = bf16[16,1,24,1536]{3,2,0,1:T(8,128)(2,1)S(1)} collective-permute-done((bf16[16,1,24,1536]{3,2,0,1:T(8,128)(2,1)S(1)}, bf16[16,1,24,1536]{3,2,0,1:T(8,128)(2,1)S(1)}, u32[]{:S(2)}, u32[]{:S(2)}) %collective-permute-start.1) | collective-permute-done | bytes 1179680 | tf_op jit(solution)/shard_map/while/body/eval_jaxpr/ppermute | solution.py:18
  132.6 3.8 %all-to-all-start.1 = ((bf16[16,1,24,1536]{3,2,1,0:T(8,128)(2,1)}), bf16[16,1,24,1536]{3,2,1,0:T(8,128)(2,1)S(1)}, u32[]{:S(2)}, u32[]{:S(2)}) async-start(bf16[16,1,24,1536]{3,2,1,0:T(8,128)(2,1)} %fusion.83), calls=%async_computation.1 | async-start | bytes 2359296 | tf_op jit(solution)/shard_map/while/body/eval_jaxpr/all_to_all | solution.py:125
  136.6 20.2 %all-to-all-done.1 = bf16[16,1,24,1536]{3,2,1,0:T(8,128)(2,1)S(1)} async-done(((bf16[16,1,24,1536]{3,2,1,0:T(8,128)(2,1)}), bf16[16,1,24,1536]{3,2,1,0:T(8,128)(2,1)S(1)}, u32[]{:S(2)}, u32[]{:S(2)}) %all-to-all-start.1) | async-done | bytes 1179680 | tf_op jit(solution)/shard_map/while/body/eval_jaxpr/all_to_all | solution.py:125
  159.6 4.6 %collective-permute-done.2 = bf16[64,768]{1,0:T(8,128)(2,1)S(1)} collective-permute-done((bf16[64,768]{1,0:T(8,128)(2,1)S(1)}, bf16[64,768]{1,0:T(8,128)(2,1)S(1)}, u32[]{:S(2)}, u32[]{:S(2)}) %collective-permute-start.2) | collective-permute-done | bytes 98336 | tf_op jit(solution)/shard_map/while/body/eval_jaxpr/ppermute | solution.py:18
  166.6 3.7 %collective-permute-done.3 = bf16[64,768]{1,0:T(8,128)(2,1)S(1)} collective-permute-done((bf16[64,768]{1,0:T(8,128)(2,1)S(1)}, bf16[64,768]{1,0:T(8,128)(2,1)S(1)}, u32[]{:S(2)}, u32[]{:S(2)}) %collective-permute-start.3) | collective-permute-done | bytes 98336 | tf_op jit(solution)/shard_map/while/body/eval_jaxpr/ppermute | solution.py:147
  173.5 19.4 %all_to_all.34 = bf16[16,1,24,1536]{3,2,1,0:T(8,128)(2,1)S(1)} all-to-all(bf16[16,1,24,1536]{3,2,1,0:T(8,128)(2,1)S(1)} %bitcast.200), channel_id=1, replica_groups=mesh['section'=2,'expert'=16,'tensor'=4] {'expert'}, dimensions={0} | all-to-all | bytes 2359296 | tf_op jit(solution)/shard_map/all_to_all | solution.py:95
  192.9 2.8 %collective-permute-done.9 = bf16[16,1,24,1536]{3,2,0,1:T(8,128)(2,1)S(1)} collective-permute-done((bf16[16,1,24,1536]{3,2,0,1:T(8,128)(2,1)S(1)}, bf16[16,1,24,1536]{3,2,0,1:T(8,128)(2,1)S(1)}, u32[]{:S(2)}, u32[]{:S(2)}) %collective-permute-start.9) | collective-permute-done | bytes 1179680 | tf_op jit(solution)/shard_map/ppermute | solution.py:18
  198.7 2.9 %fusion.28 = f32[16,24,1024]{2,1,0:T(8,128)S(1)} fusion(bf16[1,1,3072,1024]{3,2,1,0:T(8,128)(2,1)S(1)} %bitcast.215, bf16[16,24,768]{2,1,0:T(8,128)(2,1)S(1)} %get-tuple-element.399, bf16[16,24,768]{2,1,0:T(8,128)(2,1)S(1)} %get-tuple-element.386, bf16[16,24,768]{2,1,0:T(8,128)(2,1)S(1)} %get-tuple-element.400, ...), kind=kOutput, calls=%fused_computation.68 | convolution fusion | flops 2428895232 | bytes 10237440 | tf_op jit(solution)/shard_map/sekd,edf->sekf/dot_general | solution.py:105
  209.3 3.8 %all-to-all-start.3 = ((bf16[16,1,24,1536]{3,2,1,0:T(8,128)(2,1)}), bf16[16,1,24,1536]{3,2,1,0:T(8,128)(2,1)S(1)}, u32[]{:S(2)}, u32[]{:S(2)}) async-start(bf16[16,1,24,1536]{3,2,1,0:T(8,128)(2,1)} %fusion.46), calls=%async_computation.3 | async-start | bytes 2359296 | tf_op jit(solution)/shard_map/all_to_all | solution.py:125
  213.3 20.2 %all-to-all-done.3 = bf16[16,1,24,1536]{3,2,1,0:T(8,128)(2,1)S(1)} async-done(((bf16[16,1,24,1536]{3,2,1,0:T(8,128)(2,1)}), bf16[16,1,24,1536]{3,2,1,0:T(8,128)(2,1)S(1)}, u32[]{:S(2)}, u32[]{:S(2)}) %all-to-all-start.3) | async-done | bytes 1179680 | tf_op jit(solution)/shard_map/all_to_all | solution.py:125
  236.4 4.6 %collective-permute-done.11 = bf16[64,768]{1,0:T(8,128)(2,1)S(1)} collective-permute-done((bf16[64,768]{1,0:T(8,128)(2,1)S(1)}, bf16[64,768]{1,0:T(8,128)(2,1)S(1)}, u32[]{:S(2)}, u32[]{:S(2)}) %collective-permute-start.11) | collective-permute-done | bytes 98336 | tf_op jit(solution)/shard_map/ppermute | solution.py:18
  (172 shorter events, 56.8 us)
Async XLA Ops:
  0.7 8.0 %collective-permute-start.6 = (f32[768]{0:T(1024)S(1)}, f32[768]{0:T(1024)S(1)}, u32[]{:S(2)}, u32[]{:S(2)}) collective-permute-start(f32[768]{0:T(1024)S(1)} %reduce.6), channel_id=1, source_target_pairs={{0,1},{1,0},{2,3},{3,2},{4,5},{5,4},{6,7},{7,6},{8,9},{9,8},{10,11... | collective-permute-start | bytes 9224 | tf_op jit(solution)/shard_map/ppermute | solution.py:18
  0.8 7.9 %collective-permute-start.7 = (f32[768]{0:T(1024)S(1)}, f32[768]{0:T(1024)S(1)}, u32[]{:S(2)}, u32[]{:S(2)}) collective-permute-start(f32[768]{0:T(1024)S(1)} %reduce.6), channel_id=1, source_target_pairs={{0,2},{1,3},{2,0},{3,1},{4,6},{5,7},{6,4},{7,5},{8,10},{9,11},{10,... | collective-permute-start | bytes 9224 | tf_op jit(solution)/shard_map/ppermute | solution.py:18
  1.7 7.0 %collective-permute-start.8 = (f32[768]{0:T(1024)S(1)}, f32[768]{0:T(1024)S(1)}, u32[]{:S(2)}, u32[]{:S(2)}) collective-permute-start(f32[768]{0:T(1024)S(1)} %reduce.6), channel_id=1, source_target_pairs={{0,3},{1,2},{2,1},{3,0},{4,7},{5,6},{6,5},{7,4},{8,11},{9,10},{10,... | collective-permute-start | bytes 9224 | tf_op jit(solution)/shard_map/ppermute | solution.py:18
  2.6 7.4 %collective-permute-start.5 = (bf16[2,64,768]{2,1,0:T(8,128)(2,1)}, bf16[2,64,768]{2,1,0:T(8,128)(2,1)S(1)}, u32[]{:S(2)}, u32[]{:S(2)}) collective-permute-start(bf16[2,64,768]{2,1,0:T(8,128)(2,1)} %param.12), channel_id=1, source_target_pairs={{0,2},{1,3},{2,0},{3,1},{4,6},{5,7},{6,4},{7,5},{8,10},{9,11},{10,... | collective-permute-start | bytes 589832 | tf_op jit(solution)/shard_map/ppermute | solution.py:18
  38.9 2.8 %collective-permute-start = (bf16[16,1,24,1536]{3,2,0,1:T(8,128)(2,1)S(1)}, bf16[16,1,24,1536]{3,2,0,1:T(8,128)(2,1)S(1)}, u32[]{:S(2)}, u32[]{:S(2)}) collective-permute-start(bf16[16,1,24,1536]{3,2,0,1:T(8,128)(2,1)S(1)} %bitcast.193), channel_id=1, source_target_pairs={{0,1},{1,0},{2,3},{3,2},{4,5},{5,4},{6,7},{7,6},{8,9},{9,8},{10,11... | collective-permute-start | bytes 3538952 | tf_op jit(solution)/shard_map/while/body/eval_jaxpr/ppermute | solution.py:18
  42.3 5.3 %slice-start.4 = ((s8[6291456]{0:T(1024)(128)(4,1)}), s8[4194304]{0:T(1024)(128)(4,1)S(1)}, s32[]{:S(2)}) async-start(s8[6291456]{0:T(1024)(128)(4,1)} %bitcast.217), calls=%async_computation.8 | async-start | bytes 8388608 | tf_op jit(solution)/shard_map/while
  51.0 2.9 %collective-permute-start.1 = (bf16[16,1,24,1536]{3,2,0,1:T(8,128)(2,1)S(1)}, bf16[16,1,24,1536]{3,2,0,1:T(8,128)(2,1)S(1)}, u32[]{:S(2)}, u32[]{:S(2)}) collective-permute-start(bf16[16,1,24,1536]{3,2,0,1:T(8,128)(2,1)S(1)} %select_convert_fusion.6), channel_id=1, source_target_pairs={{0,1},{1,0},{2,3},{3,2},{4,5},{5,4},{6,7},{7,6},{8,9},{9,8},{10,11... | collective-permute-start | bytes 3538952 | tf_op jit(solution)/shard_map/while/body/eval_jaxpr/ppermute | solution.py:18
  55.4 3.8 %copy-start = (f32[1,2,64,2]{2,3,1,0:T(2,128)S(1)}, f32[1,2,64,2]{2,3,1,0:T(2,128)}, u32[]{:S(2)}) copy-start(f32[1,2,64,2]{2,3,1,0:T(2,128)} %get-tuple-element.566) | copy-start | bytes 3076 | tf_op jit(solution)/shard_map/while
  55.4 24.2 %all-to-all-start.1 = ((bf16[16,1,24,1536]{3,2,1,0:T(8,128)(2,1)}), bf16[16,1,24,1536]{3,2,1,0:T(8,128)(2,1)S(1)}, u32[]{:S(2)}, u32[]{:S(2)}) async-start(bf16[16,1,24,1536]{3,2,1,0:T(8,128)(2,1)} %fusion.83), calls=%async_computation.1 | async-start | bytes 2359296 | tf_op jit(solution)/shard_map/while/body/eval_jaxpr/all_to_all | solution.py:125
  82.3 4.7 %collective-permute-start.2 = (bf16[64,768]{1,0:T(8,128)(2,1)S(1)}, bf16[64,768]{1,0:T(8,128)(2,1)S(1)}, u32[]{:S(2)}, u32[]{:S(2)}) collective-permute-start(bf16[64,768]{1,0:T(8,128)(2,1)S(1)} %select_convert_fusion.7), channel_id=1, source_target_pairs={{0,2},{1,3},{2,0},{3,1},{4,6},{5,7},{6,4},{7,5},{8,10},{9,11},{10,... | collective-permute-start | bytes 294920 | tf_op jit(solution)/shard_map/while/body/eval_jaxpr/ppermute | solution.py:18
  87.1 7.0 %collective-permute-start.3 = (bf16[64,768]{1,0:T(8,128)(2,1)S(1)}, bf16[64,768]{1,0:T(8,128)(2,1)S(1)}, u32[]{:S(2)}, u32[]{:S(2)}) collective-permute-start(bf16[64,768]{1,0:T(8,128)(2,1)S(1)} %add_convert_fusion.5), channel_id=1, source_target_pairs={{0,66},{1,67},{2,64},{3,65},{64,2},{65,3},{66,0},{67,1},{4,70},{5,... | collective-permute-start | bytes 294920 | tf_op jit(solution)/shard_map/while/body/eval_jaxpr/ppermute | solution.py:147
  87.6 6.4 %collective-permute-start.4 = (bf16[64,768]{1,0:T(8,128)(2,1)S(1)}, bf16[64,768]{1,0:T(8,128)(2,1)S(1)}, u32[]{:S(2)}, u32[]{:S(2)}) collective-permute-start(bf16[64,768]{1,0:T(8,128)(2,1)S(1)} %add_convert_fusion.5), channel_id=1, source_target_pairs={{0,64},{64,0},{1,65},{65,1},{2,66},{66,2},{3,67},{67,3},{4,68},{68... | collective-permute-start | bytes 294920 | tf_op jit(solution)/shard_map/while/body/eval_jaxpr/ppermute | solution.py:146
  116.1 2.8 %collective-permute-start = (bf16[16,1,24,1536]{3,2,0,1:T(8,128)(2,1)S(1)}, bf16[16,1,24,1536]{3,2,0,1:T(8,128)(2,1)S(1)}, u32[]{:S(2)}, u32[]{:S(2)}) collective-permute-start(bf16[16,1,24,1536]{3,2,0,1:T(8,128)(2,1)S(1)} %bitcast.193), channel_id=1, source_target_pairs={{0,1},{1,0},{2,3},{3,2},{4,5},{5,4},{6,7},{7,6},{8,9},{9,8},{10,11... | collective-permute-start | bytes 3538952 | tf_op jit(solution)/shard_map/while/body/eval_jaxpr/ppermute | solution.py:18
  119.5 5.3 %slice-start.4 = ((s8[6291456]{0:T(1024)(128)(4,1)}), s8[4194304]{0:T(1024)(128)(4,1)S(1)}, s32[]{:S(2)}) async-start(s8[6291456]{0:T(1024)(128)(4,1)} %bitcast.217), calls=%async_computation.8 | async-start | bytes 8388608 | tf_op jit(solution)/shard_map/while
  128.3 2.9 %collective-permute-start.1 = (bf16[16,1,24,1536]{3,2,0,1:T(8,128)(2,1)S(1)}, bf16[16,1,24,1536]{3,2,0,1:T(8,128)(2,1)S(1)}, u32[]{:S(2)}, u32[]{:S(2)}) collective-permute-start(bf16[16,1,24,1536]{3,2,0,1:T(8,128)(2,1)S(1)} %select_convert_fusion.6), channel_id=1, source_target_pairs={{0,1},{1,0},{2,3},{3,2},{4,5},{5,4},{6,7},{7,6},{8,9},{9,8},{10,11... | collective-permute-start | bytes 3538952 | tf_op jit(solution)/shard_map/while/body/eval_jaxpr/ppermute | solution.py:18
  132.6 24.2 %all-to-all-start.1 = ((bf16[16,1,24,1536]{3,2,1,0:T(8,128)(2,1)}), bf16[16,1,24,1536]{3,2,1,0:T(8,128)(2,1)S(1)}, u32[]{:S(2)}, u32[]{:S(2)}) async-start(bf16[16,1,24,1536]{3,2,1,0:T(8,128)(2,1)} %fusion.83), calls=%async_computation.1 | async-start | bytes 2359296 | tf_op jit(solution)/shard_map/while/body/eval_jaxpr/all_to_all | solution.py:125
  159.5 4.7 %collective-permute-start.2 = (bf16[64,768]{1,0:T(8,128)(2,1)S(1)}, bf16[64,768]{1,0:T(8,128)(2,1)S(1)}, u32[]{:S(2)}, u32[]{:S(2)}) collective-permute-start(bf16[64,768]{1,0:T(8,128)(2,1)S(1)} %select_convert_fusion.7), channel_id=1, source_target_pairs={{0,2},{1,3},{2,0},{3,1},{4,6},{5,7},{6,4},{7,5},{8,10},{9,11},{10,... | collective-permute-start | bytes 294920 | tf_op jit(solution)/shard_map/while/body/eval_jaxpr/ppermute | solution.py:18
  164.3 5.9 %collective-permute-start.3 = (bf16[64,768]{1,0:T(8,128)(2,1)S(1)}, bf16[64,768]{1,0:T(8,128)(2,1)S(1)}, u32[]{:S(2)}, u32[]{:S(2)}) collective-permute-start(bf16[64,768]{1,0:T(8,128)(2,1)S(1)} %add_convert_fusion.5), channel_id=1, source_target_pairs={{0,66},{1,67},{2,64},{3,65},{64,2},{65,3},{66,0},{67,1},{4,70},{5,... | collective-permute-start | bytes 294920 | tf_op jit(solution)/shard_map/while/body/eval_jaxpr/ppermute | solution.py:147
  165.8 6.1 %collective-permute-start.4 = (bf16[64,768]{1,0:T(8,128)(2,1)S(1)}, bf16[64,768]{1,0:T(8,128)(2,1)S(1)}, u32[]{:S(2)}, u32[]{:S(2)}) collective-permute-start(bf16[64,768]{1,0:T(8,128)(2,1)S(1)} %add_convert_fusion.5), channel_id=1, source_target_pairs={{0,64},{64,0},{1,65},{65,1},{2,66},{66,2},{3,67},{67,3},{4,68},{68... | collective-permute-start | bytes 294920 | tf_op jit(solution)/shard_map/while/body/eval_jaxpr/ppermute | solution.py:146
  192.9 2.8 %collective-permute-start.9 = (bf16[16,1,24,1536]{3,2,0,1:T(8,128)(2,1)S(1)}, bf16[16,1,24,1536]{3,2,0,1:T(8,128)(2,1)S(1)}, u32[]{:S(2)}, u32[]{:S(2)}) collective-permute-start(bf16[16,1,24,1536]{3,2,0,1:T(8,128)(2,1)S(1)} %bitcast.198), channel_id=1, source_target_pairs={{0,1},{1,0},{2,3},{3,2},{4,5},{5,4},{6,7},{7,6},{8,9},{9,8},{10,11... | collective-permute-start | bytes 3538952 | tf_op jit(solution)/shard_map/ppermute | solution.py:18
  196.3 5.3 %slice-start.6 = ((s8[6291456]{0:T(1024)(128)(4,1)}), s8[4194304]{0:T(1024)(128)(4,1)S(1)}, s32[]{:S(2)}) async-start(s8[6291456]{0:T(1024)(128)(4,1)} %bitcast.219), calls=%async_computation.10 | async-start | bytes 8388608
  205.0 2.9 %collective-permute-start.10 = (bf16[16,1,24,1536]{3,2,0,1:T(8,128)(2,1)S(1)}, bf16[16,1,24,1536]{3,2,0,1:T(8,128)(2,1)S(1)}, u32[]{:S(2)}, u32[]{:S(2)}) collective-permute-start(bf16[16,1,24,1536]{3,2,0,1:T(8,128)(2,1)S(1)} %select_convert_fusion.2), channel_id=1, source_target_pairs={{0,1},{1,0},{2,3},{3,2},{4,5},{5,4},{6,7},{7,6},{8,9},{9,8},{10,11... | collective-permute-start | bytes 3538952 | tf_op jit(solution)/shard_map/ppermute | solution.py:18
  209.3 24.2 %all-to-all-start.3 = ((bf16[16,1,24,1536]{3,2,1,0:T(8,128)(2,1)}), bf16[16,1,24,1536]{3,2,1,0:T(8,128)(2,1)S(1)}, u32[]{:S(2)}, u32[]{:S(2)}) async-start(bf16[16,1,24,1536]{3,2,1,0:T(8,128)(2,1)} %fusion.46), calls=%async_computation.3 | async-start | bytes 2359296 | tf_op jit(solution)/shard_map/all_to_all | solution.py:125
  236.3 4.7 %collective-permute-start.11 = (bf16[64,768]{1,0:T(8,128)(2,1)S(1)}, bf16[64,768]{1,0:T(8,128)(2,1)S(1)}, u32[]{:S(2)}, u32[]{:S(2)}) collective-permute-start(bf16[64,768]{1,0:T(8,128)(2,1)S(1)} %select_convert_fusion.3), channel_id=1, source_target_pairs={{0,2},{1,3},{2,0},{3,1},{4,6},{5,7},{6,4},{7,5},{8,10},{9,11},{10,... | collective-permute-start | bytes 294920 | tf_op jit(solution)/shard_map/ppermute | solution.py:18
  (13 other events, 33.6 us)

commit v14 on v13

--- a/solution.py
+++ b/solution.py
@@ -29,16 +29,6 @@
     rows_here = tokens.shape[1]
     quarter = tokens.shape[2]
     capacity = max(3 * rows_here // 8, 2 * rows_here // EXPERTS)
-    gain = norm_gain[0]
-    gain_from = [gain, swap(gain, "tensor", 1), swap(gain, "tensor", 2), swap(gain, "tensor", 3)]
-    gain_full = jnp.concatenate(
-        [
-            jnp.where(t_pos == q, gain_from[0],
-                      jnp.where(t_pos ^ 1 == q, gain_from[1],
-                                jnp.where(t_pos ^ 2 == q, gain_from[2], gain_from[3])))
-            for q in range(4)
-        ]
-    )
     up_local = w_up[0]
     down_local = w_down[0]
     local_count = up_local.shape[0]
@@ -56,6 +46,13 @@
         )
 
     tokens_half = to_half(tokens, swap(tokens, "tensor", 2))
+    gain_mine = to_half(norm_gain[0], swap(norm_gain[0], "tensor", 2))
+    gain_theirs = swap(gain_mine, "tensor", 1)
+    gain_first = jnp.where(core_first, gain_mine, gain_theirs)
+    gain_second = jnp.where(core_first, gain_theirs, gain_mine)
+    gain_full = jnp.concatenate(
+        [gain_first[:quarter], gain_second[:quarter], gain_first[quarter:], gain_second[quarter:]]
+    )
     routes_all = expert_ids[0].reshape(micro, -1)
     onehot_all = (routes_all[..., None] == jnp.arange(EXPERTS, dtype=jnp.int32)).astype(jnp.int32)
     slot_all = jnp.sum((jnp.cumsum(onehot_all, axis=1) - onehot_all) * onehot_all, axis=2)

time: 244 us -> 244 us (level)
    ppermute x13 -> x12, waiting for transfers between devices: 31 us -> 30.7 us  [swap(): return lax.ppermute(block, axis, [(i, i ^ bit) for i in range(n)])]
  transfers between devices with their start and end apart: 20 -> 19, of which waited for: 16 -> 16; matrix products, arithmetic and copies ran while one was open for 2% -> 2% of each run, Pallas kernels for 0% -> 0%
where the time goes in v14:
time: 244 us; the launch traced here: 242 us
  waiting for transfers between devices  101 us (41%)
  blocking collectives  66.7 us (27%)
  starting transfers between devices  20.6 us (8%)
  local copies, waits for them, and re-layouts  18.4 us (8%)
  other arithmetic  17.7 us (7%)
  matrix products  16.7 us (7%)
    all_to_all x3, blocking collectives, layer_step(): lax.all_to_all(outgoing, 'expert', split_axis=0, concat_axis=0, tiled=True)  66.7 us
    all_to_all x3, waiting for transfers between devices, layer_step(): lax.all_to_all(chip_sum, 'expert', split_axis=0, concat_axis=0, tiled=True)  60.6 us
    ppermute x12, waiting for transfers between devices, swap(): return lax.ppermute(block, axis, [(i, i ^ bit) for i in range(n)])  30.7 us
    all_to_all x3, starting transfers between devices, layer_step(): lax.all_to_all(chip_sum, 'expert', split_axis=0, concat_axis=0, tiled=True)  11.5 us
    dot_general x3, matrix products, layer_step(): jnp.einsum('sekd,edf->sekf', normed, up_local, preferred_element_type=jnp...  8.6 us
    dot_general x3, matrix products, layer_step(): jnp.einsum('sekf,efd->sekd', hidden, down_local, preferred_element_type=j...  8.11 us
    ppermute x2, waiting for transfers between devices, looped(): lax.ppermute(produced, ('section', 'tensor'), cross_route)  7.54 us
  transfers between devices with their start and end apart: 19, of which 16 were waited for; matrix products, arithmetic and copies ran while one was open for 2% of the time, Pallas kernels for 0%

profile of v14, /device:TPU:6, one launch (start us, length us, event | category | flops | bytes accessed | tf_op | source)
XLA Modules:
  0.0 241.7 jit_solution(2302758030978449337)
XLA Ops:
  10.4 161.4 %while.17 = (s32[]{:T(128)}, bf16[64,1536]{1,0:T(8,128)(2,1)S(1)}, bf16[2,64,768]{2,1,0:T(8,128)(2,1)S(1)}, pred[]{:T(512)}, pred[]{:T(512)}, /*index=5*/bf16[2,...) while((s32[]{:T(128)}, bf16[64,1536]{1,0:T(8,128)(2,1)S(1)}, ...), condition=%wide.region_8.11_spmd.clone, body=%wide.region_4.10_spmd.clone.sunk | while | flops 4872246272 | bytes 128624768 | solution.py:149
  12.0 26.7 %all_to_all.35 = bf16[16,1,24,1536]{3,2,1,0:T(8,128)(2,1)S(1)} all-to-all(bf16[16,1,24,1536]{3,2,1,0:T(8,128)(2,1)S(1)} %bitcast.195), channel_id=1, replica_groups=mesh['section'=2,'expert'=16,'tensor'=4] {'expert'}, dimensions={0} | all-to-all | bytes 2359296 | tf_op jit(solution)/shard_map/while/body/eval_jaxpr/all_to_all | solution.py:92
  38.8 2.8 %collective-permute-done = bf16[16,1,24,1536]{3,2,0,1:T(8,128)(2,1)S(1)} collective-permute-done((bf16[16,1,24,1536]{3,2,0,1:T(8,128)(2,1)S(1)}, bf16[16,1,24,1536]{3,2,0,1:T(8,128)(2,1)S(1)}, u32[]{:S(2)}, u32[]{:S(2)}) %collective-permute-start) | collective-permute-done | bytes 1179680 | tf_op jit(solution)/shard_map/while/body/eval_jaxpr/ppermute | solution.py:18
  44.5 2.9 %fusion.82 = f32[16,24,1024]{2,1,0:T(8,128)S(1)} fusion(bf16[1,3072,1024]{2,1,0:T(8,128)(2,1)S(1)} %bitcast.212, bf16[16,24,768]{2,1,0:T(8,128)(2,1)S(1)} %get-tuple-element.505, bf16[16,24,768]{2,1,0:T(8,128)(2,1)S(1)} %get-tuple-element.506, bf16[16,24,768]{2,1,0:T(8,128)(2,1)S(1)} %get-tuple-element.507, ...), kind=kOutput, calls=%fused_computation.8.clone.1 | convolution fusion | flops 2428895232 | bytes 10237440 | tf_op jit(solution)/shard_map/while/body/eval_jaxpr/sekd,edf->sekf/dot_general | solution.py:102
  51.1 2.7 %collective-permute-done.1 = bf16[16,1,24,1536]{3,2,0,1:T(8,128)(2,1)S(1)} collective-permute-done((bf16[16,1,24,1536]{3,2,0,1:T(8,128)(2,1)S(1)}, bf16[16,1,24,1536]{3,2,0,1:T(8,128)(2,1)S(1)}, u32[]{:S(2)}, u32[]{:S(2)}) %collective-permute-start.1) | collective-permute-done | bytes 1179680 | tf_op jit(solution)/shard_map/while/body/eval_jaxpr/ppermute | solution.py:18
  55.2 3.8 %all-to-all-start.1 = ((bf16[16,1,24,1536]{3,2,1,0:T(8,128)(2,1)}), bf16[16,1,24,1536]{3,2,1,0:T(8,128)(2,1)S(1)}, u32[]{:S(2)}, u32[]{:S(2)}) async-start(bf16[16,1,24,1536]{3,2,1,0:T(8,128)(2,1)} %fusion.85), calls=%async_computation.1 | async-start | bytes 2359296 | tf_op jit(solution)/shard_map/while/body/eval_jaxpr/all_to_all | solution.py:122
  59.2 20.2 %all-to-all-done.1 = bf16[16,1,24,1536]{3,2,1,0:T(8,128)(2,1)S(1)} async-done(((bf16[16,1,24,1536]{3,2,1,0:T(8,128)(2,1)}), bf16[16,1,24,1536]{3,2,1,0:T(8,128)(2,1)S(1)}, u32[]{:S(2)}, u32[]{:S(2)}) %all-to-all-start.1) | async-done | bytes 1179680 | tf_op jit(solution)/shard_map/while/body/eval_jaxpr/all_to_all | solution.py:122
  83.1 3.8 %collective-permute-done.2 = bf16[64,768]{1,0:T(8,128)(2,1)S(1)} collective-permute-done((bf16[64,768]{1,0:T(8,128)(2,1)S(1)}, bf16[64,768]{1,0:T(8,128)(2,1)S(1)}, u32[]{:S(2)}, u32[]{:S(2)}) %collective-permute-start.2) | collective-permute-done | bytes 98336 | tf_op jit(solution)/shard_map/while/body/eval_jaxpr/ppermute | solution.py:18
  90.0 3.9 %collective-permute-done.3 = bf16[64,768]{1,0:T(8,128)(2,1)S(1)} collective-permute-done((bf16[64,768]{1,0:T(8,128)(2,1)S(1)}, bf16[64,768]{1,0:T(8,128)(2,1)S(1)}, u32[]{:S(2)}, u32[]{:S(2)}) %collective-permute-start.3) | collective-permute-done | bytes 98336 | tf_op jit(solution)/shard_map/while/body/eval_jaxpr/ppermute | solution.py:144
  95.5 20.5 %all_to_all.35 = bf16[16,1,24,1536]{3,2,1,0:T(8,128)(2,1)S(1)} all-to-all(bf16[16,1,24,1536]{3,2,1,0:T(8,128)(2,1)S(1)} %bitcast.195), channel_id=1, replica_groups=mesh['section'=2,'expert'=16,'tensor'=4] {'expert'}, dimensions={0} | all-to-all | bytes 2359296 | tf_op jit(solution)/shard_map/while/body/eval_jaxpr/all_to_all | solution.py:92
  116.0 2.8 %collective-permute-done = bf16[16,1,24,1536]{3,2,0,1:T(8,128)(2,1)S(1)} collective-permute-done((bf16[16,1,24,1536]{3,2,0,1:T(8,128)(2,1)S(1)}, bf16[16,1,24,1536]{3,2,0,1:T(8,128)(2,1)S(1)}, u32[]{:S(2)}, u32[]{:S(2)}) %collective-permute-start) | collective-permute-done | bytes 1179680 | tf_op jit(solution)/shard_map/while/body/eval_jaxpr/ppermute | solution.py:18
  121.8 2.9 %fusion.82 = f32[16,24,1024]{2,1,0:T(8,128)S(1)} fusion(bf16[1,3072,1024]{2,1,0:T(8,128)(2,1)S(1)} %bitcast.212, bf16[16,24,768]{2,1,0:T(8,128)(2,1)S(1)} %get-tuple-element.505, bf16[16,24,768]{2,1,0:T(8,128)(2,1)S(1)} %get-tuple-element.506, bf16[16,24,768]{2,1,0:T(8,128)(2,1)S(1)} %get-tuple-element.507, ...), kind=kOutput, calls=%fused_computation.8.clone.1 | convolution fusion | flops 2428895232 | bytes 10237440 | tf_op jit(solution)/shard_map/while/body/eval_jaxpr/sekd,edf->sekf/dot_general | solution.py:102
  128.3 2.7 %collective-permute-done.1 = bf16[16,1,24,1536]{3,2,0,1:T(8,128)(2,1)S(1)} collective-permute-done((bf16[16,1,24,1536]{3,2,0,1:T(8,128)(2,1)S(1)}, bf16[16,1,24,1536]{3,2,0,1:T(8,128)(2,1)S(1)}, u32[]{:S(2)}, u32[]{:S(2)}) %collective-permute-start.1) | collective-permute-done | bytes 1179680 | tf_op jit(solution)/shard_map/while/body/eval_jaxpr/ppermute | solution.py:18
  132.4 3.8 %all-to-all-start.1 = ((bf16[16,1,24,1536]{3,2,1,0:T(8,128)(2,1)}), bf16[16,1,24,1536]{3,2,1,0:T(8,128)(2,1)S(1)}, u32[]{:S(2)}, u32[]{:S(2)}) async-start(bf16[16,1,24,1536]{3,2,1,0:T(8,128)(2,1)} %fusion.85), calls=%async_computation.1 | async-start | bytes 2359296 | tf_op jit(solution)/shard_map/while/body/eval_jaxpr/all_to_all | solution.py:122
  136.4 20.2 %all-to-all-done.1 = bf16[16,1,24,1536]{3,2,1,0:T(8,128)(2,1)S(1)} async-done(((bf16[16,1,24,1536]{3,2,1,0:T(8,128)(2,1)}), bf16[16,1,24,1536]{3,2,1,0:T(8,128)(2,1)S(1)}, u32[]{:S(2)}, u32[]{:S(2)}) %all-to-all-start.1) | async-done | bytes 1179680 | tf_op jit(solution)/shard_map/while/body/eval_jaxpr/all_to_all | solution.py:122
  159.5 4.6 %collective-permute-done.2 = bf16[64,768]{1,0:T(8,128)(2,1)S(1)} collective-permute-done((bf16[64,768]{1,0:T(8,128)(2,1)S(1)}, bf16[64,768]{1,0:T(8,128)(2,1)S(1)}, u32[]{:S(2)}, u32[]{:S(2)}) %collective-permute-start.2) | collective-permute-done | bytes 98336 | tf_op jit(solution)/shard_map/while/body/eval_jaxpr/ppermute | solution.py:18
  166.4 3.7 %collective-permute-done.3 = bf16[64,768]{1,0:T(8,128)(2,1)S(1)} collective-permute-done((bf16[64,768]{1,0:T(8,128)(2,1)S(1)}, bf16[64,768]{1,0:T(8,128)(2,1)S(1)}, u32[]{:S(2)}, u32[]{:S(2)}) %collective-permute-start.3) | collective-permute-done | bytes 98336 | tf_op jit(solution)/shard_map/while/body/eval_jaxpr/ppermute | solution.py:144
  173.4 19.4 %all_to_all.34 = bf16[16,1,24,1536]{3,2,1,0:T(8,128)(2,1)S(1)} all-to-all(bf16[16,1,24,1536]{3,2,1,0:T(8,128)(2,1)S(1)} %bitcast.200), channel_id=1, replica_groups=mesh['section'=2,'expert'=16,'tensor'=4] {'expert'}, dimensions={0} | all-to-all | bytes 2359296 | tf_op jit(solution)/shard_map/all_to_all | solution.py:92
  192.8 2.8 %collective-permute-done.8 = bf16[16,1,24,1536]{3,2,0,1:T(8,128)(2,1)S(1)} collective-permute-done((bf16[16,1,24,1536]{3,2,0,1:T(8,128)(2,1)S(1)}, bf16[16,1,24,1536]{3,2,0,1:T(8,128)(2,1)S(1)}, u32[]{:S(2)}, u32[]{:S(2)}) %collective-permute-start.8) | collective-permute-done | bytes 1179680 | tf_op jit(solution)/shard_map/ppermute | solution.py:18
  198.6 2.9 %fusion.28 = f32[16,24,1024]{2,1,0:T(8,128)S(1)} fusion(bf16[1,1,3072,1024]{3,2,1,0:T(8,128)(2,1)S(1)} %bitcast.215, bf16[16,24,768]{2,1,0:T(8,128)(2,1)S(1)} %get-tuple-element.390, bf16[16,24,768]{2,1,0:T(8,128)(2,1)S(1)} %get-tuple-element.386, bf16[16,24,768]{2,1,0:T(8,128)(2,1)S(1)} %get-tuple-element.389, ...), kind=kOutput, calls=%fused_computation.68 | convolution fusion | flops 2428895232 | bytes 10237440 | tf_op jit(solution)/shard_map/sekd,edf->sekf/dot_general | solution.py:102
  205.1 2.7 %collective-permute-done.9 = bf16[16,1,24,1536]{3,2,0,1:T(8,128)(2,1)S(1)} collective-permute-done((bf16[16,1,24,1536]{3,2,0,1:T(8,128)(2,1)S(1)}, bf16[16,1,24,1536]{3,2,0,1:T(8,128)(2,1)S(1)}, u32[]{:S(2)}, u32[]{:S(2)}) %collective-permute-start.9) | collective-permute-done | bytes 1179680 | tf_op jit(solution)/shard_map/ppermute | solution.py:18
  209.2 3.8 %all-to-all-start.3 = ((bf16[16,1,24,1536]{3,2,1,0:T(8,128)(2,1)}), bf16[16,1,24,1536]{3,2,1,0:T(8,128)(2,1)S(1)}, u32[]{:S(2)}, u32[]{:S(2)}) async-start(bf16[16,1,24,1536]{3,2,1,0:T(8,128)(2,1)} %fusion.46), calls=%async_computation.3 | async-start | bytes 2359296 | tf_op jit(solution)/shard_map/all_to_all | solution.py:122
  213.2 20.2 %all-to-all-done.3 = bf16[16,1,24,1536]{3,2,1,0:T(8,128)(2,1)S(1)} async-done(((bf16[16,1,24,1536]{3,2,1,0:T(8,128)(2,1)}), bf16[16,1,24,1536]{3,2,1,0:T(8,128)(2,1)S(1)}, u32[]{:S(2)}, u32[]{:S(2)}) %all-to-all-start.3) | async-done | bytes 1179680 | tf_op jit(solution)/shard_map/all_to_all | solution.py:122
  236.3 4.6 %collective-permute-done.10 = bf16[64,768]{1,0:T(8,128)(2,1)S(1)} collective-permute-done((bf16[64,768]{1,0:T(8,128)(2,1)S(1)}, bf16[64,768]{1,0:T(8,128)(2,1)S(1)}, u32[]{:S(2)}, u32[]{:S(2)}) %collective-permute-start.10) | collective-permute-done | bytes 98336 | tf_op jit(solution)/shard_map/ppermute | solution.py:18
  (173 shorter events, 56.1 us)
Async XLA Ops:
  0.7 7.2 %collective-permute-start.6 = (f32[768]{0:T(1024)S(1)}, f32[768]{0:T(1024)S(1)}, u32[]{:S(2)}, u32[]{:S(2)}) collective-permute-start(f32[768]{0:T(1024)S(1)} %reduce.6), channel_id=1, source_target_pairs={{0,2},{1,3},{2,0},{3,1},{4,6},{5,7},{6,4},{7,5},{8,10},{9,11},{10,... | collective-permute-start | bytes 9224 | tf_op jit(solution)/shard_map/ppermute | solution.py:18
  1.6 7.6 %collective-permute-start.5 = (bf16[2,64,768]{2,1,0:T(8,128)(2,1)}, bf16[2,64,768]{2,1,0:T(8,128)(2,1)S(1)}, u32[]{:S(2)}, u32[]{:S(2)}) collective-permute-start(bf16[2,64,768]{2,1,0:T(8,128)(2,1)} %param.12), channel_id=1, source_target_pairs={{0,2},{1,3},{2,0},{3,1},{4,6},{5,7},{6,4},{7,5},{8,10},{9,11},{10,... | collective-permute-start | bytes 589832 | tf_op jit(solution)/shard_map/ppermute | solution.py:18
  7.9 1.3 collective-permute-start.7
  38.8 2.8 %collective-permute-start = (bf16[16,1,24,1536]{3,2,0,1:T(8,128)(2,1)S(1)}, bf16[16,1,24,1536]{3,2,0,1:T(8,128)(2,1)S(1)}, u32[]{:S(2)}, u32[]{:S(2)}) collective-permute-start(bf16[16,1,24,1536]{3,2,0,1:T(8,128)(2,1)S(1)} %bitcast.193), channel_id=1, source_target_pairs={{0,1},{1,0},{2,3},{3,2},{4,5},{5,4},{6,7},{7,6},{8,9},{9,8},{10,11... | collective-permute-start | bytes 3538952 | tf_op jit(solution)/shard_map/while/body/eval_jaxpr/ppermute | solution.py:18
  42.1 5.3 %slice-start.4 = ((s8[6291456]{0:T(1024)(128)(4,1)}), s8[4194304]{0:T(1024)(128)(4,1)S(1)}, s32[]{:S(2)}) async-start(s8[6291456]{0:T(1024)(128)(4,1)} %bitcast.217), calls=%async_computation.8 | async-start | bytes 8388608 | tf_op jit(solution)/shard_map/while
  50.9 2.9 %collective-permute-start.1 = (bf16[16,1,24,1536]{3,2,0,1:T(8,128)(2,1)S(1)}, bf16[16,1,24,1536]{3,2,0,1:T(8,128)(2,1)S(1)}, u32[]{:S(2)}, u32[]{:S(2)}) collective-permute-start(bf16[16,1,24,1536]{3,2,0,1:T(8,128)(2,1)S(1)} %select_convert_fusion.6), channel_id=1, source_target_pairs={{0,1},{1,0},{2,3},{3,2},{4,5},{5,4},{6,7},{7,6},{8,9},{9,8},{10,11... | collective-permute-start | bytes 3538952 | tf_op jit(solution)/shard_map/while/body/eval_jaxpr/ppermute | solution.py:18
  55.2 3.8 %copy-start = (f32[1,2,64,2]{2,3,1,0:T(2,128)S(1)}, f32[1,2,64,2]{2,3,1,0:T(2,128)}, u32[]{:S(2)}) copy-start(f32[1,2,64,2]{2,3,1,0:T(2,128)} %get-tuple-element.566) | copy-start | bytes 3076 | tf_op jit(solution)/shard_map/while
  55.2 24.2 %all-to-all-start.1 = ((bf16[16,1,24,1536]{3,2,1,0:T(8,128)(2,1)}), bf16[16,1,24,1536]{3,2,1,0:T(8,128)(2,1)S(1)}, u32[]{:S(2)}, u32[]{:S(2)}) async-start(bf16[16,1,24,1536]{3,2,1,0:T(8,128)(2,1)} %fusion.85), calls=%async_computation.1 | async-start | bytes 2359296 | tf_op jit(solution)/shard_map/while/body/eval_jaxpr/all_to_all | solution.py:122
  82.2 4.7 %collective-permute-start.2 = (bf16[64,768]{1,0:T(8,128)(2,1)S(1)}, bf16[64,768]{1,0:T(8,128)(2,1)S(1)}, u32[]{:S(2)}, u32[]{:S(2)}) collective-permute-start(bf16[64,768]{1,0:T(8,128)(2,1)S(1)} %select_convert_fusion.7), channel_id=1, source_target_pairs={{0,2},{1,3},{2,0},{3,1},{4,6},{5,7},{6,4},{7,5},{8,10},{9,11},{10,... | collective-permute-start | bytes 294920 | tf_op jit(solution)/shard_map/while/body/eval_jaxpr/ppermute | solution.py:18
  87.0 7.0 %collective-permute-start.3 = (bf16[64,768]{1,0:T(8,128)(2,1)S(1)}, bf16[64,768]{1,0:T(8,128)(2,1)S(1)}, u32[]{:S(2)}, u32[]{:S(2)}) collective-permute-start(bf16[64,768]{1,0:T(8,128)(2,1)S(1)} %add_convert_fusion.5), channel_id=1, source_target_pairs={{0,66},{1,67},{2,64},{3,65},{64,2},{65,3},{66,0},{67,1},{4,70},{5,... | collective-permute-start | bytes 294920 | tf_op jit(solution)/shard_map/while/body/eval_jaxpr/ppermute | solution.py:144
  87.5 6.4 %collective-permute-start.4 = (bf16[64,768]{1,0:T(8,128)(2,1)S(1)}, bf16[64,768]{1,0:T(8,128)(2,1)S(1)}, u32[]{:S(2)}, u32[]{:S(2)}) collective-permute-start(bf16[64,768]{1,0:T(8,128)(2,1)S(1)} %add_convert_fusion.5), channel_id=1, source_target_pairs={{0,64},{64,0},{1,65},{65,1},{2,66},{66,2},{3,67},{67,3},{4,68},{68... | collective-permute-start | bytes 294920 | tf_op jit(solution)/shard_map/while/body/eval_jaxpr/ppermute | solution.py:143
  116.0 2.8 %collective-permute-start = (bf16[16,1,24,1536]{3,2,0,1:T(8,128)(2,1)S(1)}, bf16[16,1,24,1536]{3,2,0,1:T(8,128)(2,1)S(1)}, u32[]{:S(2)}, u32[]{:S(2)}) collective-permute-start(bf16[16,1,24,1536]{3,2,0,1:T(8,128)(2,1)S(1)} %bitcast.193), channel_id=1, source_target_pairs={{0,1},{1,0},{2,3},{3,2},{4,5},{5,4},{6,7},{7,6},{8,9},{9,8},{10,11... | collective-permute-start | bytes 3538952 | tf_op jit(solution)/shard_map/while/body/eval_jaxpr/ppermute | solution.py:18
  119.4 5.3 %slice-start.4 = ((s8[6291456]{0:T(1024)(128)(4,1)}), s8[4194304]{0:T(1024)(128)(4,1)S(1)}, s32[]{:S(2)}) async-start(s8[6291456]{0:T(1024)(128)(4,1)} %bitcast.217), calls=%async_computation.8 | async-start | bytes 8388608 | tf_op jit(solution)/shard_map/while
  128.1 2.9 %collective-permute-start.1 = (bf16[16,1,24,1536]{3,2,0,1:T(8,128)(2,1)S(1)}, bf16[16,1,24,1536]{3,2,0,1:T(8,128)(2,1)S(1)}, u32[]{:S(2)}, u32[]{:S(2)}) collective-permute-start(bf16[16,1,24,1536]{3,2,0,1:T(8,128)(2,1)S(1)} %select_convert_fusion.6), channel_id=1, source_target_pairs={{0,1},{1,0},{2,3},{3,2},{4,5},{5,4},{6,7},{7,6},{8,9},{9,8},{10,11... | collective-permute-start | bytes 3538952 | tf_op jit(solution)/shard_map/while/body/eval_jaxpr/ppermute | solution.py:18
  132.4 3.8 %copy-start = (f32[1,2,64,2]{2,3,1,0:T(2,128)S(1)}, f32[1,2,64,2]{2,3,1,0:T(2,128)}, u32[]{:S(2)}) copy-start(f32[1,2,64,2]{2,3,1,0:T(2,128)} %get-tuple-element.566) | copy-start | bytes 3076 | tf_op jit(solution)/shard_map/while
  132.4 24.2 %all-to-all-start.1 = ((bf16[16,1,24,1536]{3,2,1,0:T(8,128)(2,1)}), bf16[16,1,24,1536]{3,2,1,0:T(8,128)(2,1)S(1)}, u32[]{:S(2)}, u32[]{:S(2)}) async-start(bf16[16,1,24,1536]{3,2,1,0:T(8,128)(2,1)} %fusion.85), calls=%async_computation.1 | async-start | bytes 2359296 | tf_op jit(solution)/shard_map/while/body/eval_jaxpr/all_to_all | solution.py:122
  159.4 4.7 %collective-permute-start.2 = (bf16[64,768]{1,0:T(8,128)(2,1)S(1)}, bf16[64,768]{1,0:T(8,128)(2,1)S(1)}, u32[]{:S(2)}, u32[]{:S(2)}) collective-permute-start(bf16[64,768]{1,0:T(8,128)(2,1)S(1)} %select_convert_fusion.7), channel_id=1, source_target_pairs={{0,2},{1,3},{2,0},{3,1},{4,6},{5,7},{6,4},{7,5},{8,10},{9,11},{10,... | collective-permute-start | bytes 294920 | tf_op jit(solution)/shard_map/while/body/eval_jaxpr/ppermute | solution.py:18
  164.2 5.9 %collective-permute-start.3 = (bf16[64,768]{1,0:T(8,128)(2,1)S(1)}, bf16[64,768]{1,0:T(8,128)(2,1)S(1)}, u32[]{:S(2)}, u32[]{:S(2)}) collective-permute-start(bf16[64,768]{1,0:T(8,128)(2,1)S(1)} %add_convert_fusion.5), channel_id=1, source_target_pairs={{0,66},{1,67},{2,64},{3,65},{64,2},{65,3},{66,0},{67,1},{4,70},{5,... | collective-permute-start | bytes 294920 | tf_op jit(solution)/shard_map/while/body/eval_jaxpr/ppermute | solution.py:144
  165.6 6.1 %collective-permute-start.4 = (bf16[64,768]{1,0:T(8,128)(2,1)S(1)}, bf16[64,768]{1,0:T(8,128)(2,1)S(1)}, u32[]{:S(2)}, u32[]{:S(2)}) collective-permute-start(bf16[64,768]{1,0:T(8,128)(2,1)S(1)} %add_convert_fusion.5), channel_id=1, source_target_pairs={{0,64},{64,0},{1,65},{65,1},{2,66},{66,2},{3,67},{67,3},{4,68},{68... | collective-permute-start | bytes 294920 | tf_op jit(solution)/shard_map/while/body/eval_jaxpr/ppermute | solution.py:143
  192.8 2.8 %collective-permute-start.8 = (bf16[16,1,24,1536]{3,2,0,1:T(8,128)(2,1)S(1)}, bf16[16,1,24,1536]{3,2,0,1:T(8,128)(2,1)S(1)}, u32[]{:S(2)}, u32[]{:S(2)}) collective-permute-start(bf16[16,1,24,1536]{3,2,0,1:T(8,128)(2,1)S(1)} %bitcast.198), channel_id=1, source_target_pairs={{0,1},{1,0},{2,3},{3,2},{4,5},{5,4},{6,7},{7,6},{8,9},{9,8},{10,11... | collective-permute-start | bytes 3538952 | tf_op jit(solution)/shard_map/ppermute | solution.py:18
  196.2 5.3 %slice-start.6 = ((s8[6291456]{0:T(1024)(128)(4,1)}), s8[4194304]{0:T(1024)(128)(4,1)S(1)}, s32[]{:S(2)}) async-start(s8[6291456]{0:T(1024)(128)(4,1)} %bitcast.219), calls=%async_computation.10 | async-start | bytes 8388608
  204.9 2.9 %collective-permute-start.9 = (bf16[16,1,24,1536]{3,2,0,1:T(8,128)(2,1)S(1)}, bf16[16,1,24,1536]{3,2,0,1:T(8,128)(2,1)S(1)}, u32[]{:S(2)}, u32[]{:S(2)}) collective-permute-start(bf16[16,1,24,1536]{3,2,0,1:T(8,128)(2,1)S(1)} %select_convert_fusion.2), channel_id=1, source_target_pairs={{0,1},{1,0},{2,3},{3,2},{4,5},{5,4},{6,7},{7,6},{8,9},{9,8},{10,11... | collective-permute-start | bytes 3538952 | tf_op jit(solution)/shard_map/ppermute | solution.py:18
  209.2 24.2 %all-to-all-start.3 = ((bf16[16,1,24,1536]{3,2,1,0:T(8,128)(2,1)}), bf16[16,1,24,1536]{3,2,1,0:T(8,128)(2,1)S(1)}, u32[]{:S(2)}, u32[]{:S(2)}) async-start(bf16[16,1,24,1536]{3,2,1,0:T(8,128)(2,1)} %fusion.46), calls=%async_computation.3 | async-start | bytes 2359296 | tf_op jit(solution)/shard_map/all_to_all | solution.py:122
  236.2 4.7 %collective-permute-start.10 = (bf16[64,768]{1,0:T(8,128)(2,1)S(1)}, bf16[64,768]{1,0:T(8,128)(2,1)S(1)}, u32[]{:S(2)}, u32[]{:S(2)}) collective-permute-start(bf16[64,768]{1,0:T(8,128)(2,1)S(1)} %select_convert_fusion.3), channel_id=1, source_target_pairs={{0,2},{1,3},{2,0},{3,1},{4,6},{5,7},{6,4},{7,5},{8,10},{9,11},{10,... | collective-permute-start | bytes 294920 | tf_op jit(solution)/shard_map/ppermute | solution.py:18
  (12 other events, 29.8 us)

commit v15 on v13

--- a/solution.py
+++ b/solution.py
@@ -149,7 +149,8 @@
         return carried, collected
 
     carried = jnp.zeros((rows_here, 2 * quarter), jnp.bfloat16)
-    carried, collected = lax.fori_loop(0, total_steps - 1, looped, (carried, collected))
+    for step in range(total_steps - 1):
+        carried, collected = looped(step, (carried, collected))
     _, collected = layer_step(total_steps - 1, carried, collected)
     return collected[None]
 

time: 244 us -> 243 us (level)
  starting transfers between devices: 21.1 us -> 24.3 us
  waiting for transfers between devices: 101 us -> 98.4 us
    ppermute x2, waiting for transfers between devices: 7.55 us -> 2.07 us  [looped(): lax.ppermute(produced, ('section', 'tensor'), cross_route)]
    ppermute x2, waiting for transfers between devices: 1.67 us -> 5.72 us  [looped(): lax.ppermute(produced, 'section', [(i, (i + 1) % segments) for i in range...]
    while x20 -> x0, local copies, waits for them, and re-layouts: 3.55 us -> none
    unnamed x15 -> x29, local copies, waits for them, and re-layouts: 2.56 us -> 6.06 us
  transfers between devices with their start and end apart: 20 -> 20, of which waited for: 16 -> 19; matrix products, arithmetic and copies ran while one was open for 2% -> 2% of each run, Pallas kernels for 0% -> 0%
where the time goes in v15:
time: 243 us; the launch traced here: 242 us
  waiting for transfers between devices  98.4 us (40%)
  blocking collectives  68.3 us (28%)
  starting transfers between devices  24.3 us (10%)
  local copies, waits for them, and re-layouts  18.2 us (7%)
  matrix products  16.4 us (7%)
  other arithmetic  15.3 us (6%)
    all_to_all x3, blocking collectives, layer_step(): lax.all_to_all(outgoing, 'expert', split_axis=0, concat_axis=0, tiled=True)  68.3 us
    all_to_all x3, waiting for transfers between devices, layer_step(): lax.all_to_all(chip_sum, 'expert', split_axis=0, concat_axis=0, tiled=True)  59.9 us
    ppermute x13, waiting for transfers between devices, swap(): return lax.ppermute(block, axis, [(i, i ^ bit) for i in range(n)])  30.7 us
    all_to_all x3, starting transfers between devices, layer_step(): lax.all_to_all(chip_sum, 'expert', split_axis=0, concat_axis=0, tiled=True)  11.9 us
    dot_general x3, matrix products, layer_step(): jnp.einsum('sekf,efd->sekd', hidden, down_local, preferred_element_type=j...  8.36 us
    dot_general x3, matrix products, layer_step(): jnp.einsum('sekd,edf->sekf', normed, up_local, preferred_element_type=jnp...  8.07 us
    unnamed x29, local copies, waits for them, and re-layouts  6.06 us
    ppermute x2, waiting for transfers between devices, looped(): lax.ppermute(produced, 'section', [(i, (i + 1) % segments) for i in range...  5.72 us
  transfers between devices with their start and end apart: 20, of which 19 were waited for; matrix products, arithmetic and copies ran while one was open for 2% of the time, Pallas kernels for 0%

profile of v15, /device:TPU:6, one launch (start us, length us, event | category | flops | bytes accessed | tf_op | source)
XLA Modules:
  0.0 241.6 jit_solution(344302691871203717)
XLA Ops:
  9.4 25.6 %all_to_all.30 = bf16[16,1,24,1536]{3,2,1,0:T(8,128)(2,1)S(1)} all-to-all(bf16[16,1,24,1536]{3,2,1,0:T(8,128)(2,1)S(1)} %bitcast.230), channel_id=1, replica_groups=mesh['section'=2,'expert'=16,'tensor'=4] {'expert'}, dimensions={0} | all-to-all | bytes 2359296 | tf_op jit(solution)/shard_map/all_to_all | solution.py:95
  42.5 2.7 %fusion.10 = f32[16,24,1024]{2,1,0:T(8,128)S(1)} fusion(bf16[1,1,3072,1024]{3,2,1,0:T(8,128)(2,1)S(1)} %bitcast.245, bf16[16,24,768]{2,1,0:T(8,128)(2,1)S(1)} %get-tuple-element.81, bf16[16,24,768]{2,1,0:T(8,128)(2,1)S(1)} %get-tuple-element.55, bf16[16,24,768]{2,1,0:T(8,128)(2,1)S(1)} %get-tuple-element.82, ...), kind=kOutput, calls=%fused_computation.18 | convolution fusion | flops 2428895232 | bytes 10237440 | tf_op jit(solution)/shard_map/sekd,edf->sekf/dot_general | solution.py:105
  45.2 2.8 %fusion.12 = f32[16,1,24,3072]{3,2,0,1:T(8,128)S(1)} fusion(bf16[1,1,1024,3072]{3,2,1,0:T(8,128)(2,1)S(1)} %bitcast.251, f32[16,24,1024]{2,1,0:T(8,128)S(1)} %fusion.10), kind=kOutput, calls=%fused_computation.26 | convolution fusion | flops 2417885184 | bytes 12582912 | tf_op jit(solution)/shard_map/sekf,efd->sekd/dot_general | solution.py:109
  48.9 2.7 %collective-permute-done.5 = bf16[16,1,24,1536]{3,2,0,1:T(8,128)(2,1)S(1)} collective-permute-done((bf16[16,1,24,1536]{3,2,0,1:T(8,128)(2,1)S(1)}, bf16[16,1,24,1536]{3,2,0,1:T(8,128)(2,1)S(1)}, u32[]{:S(2)}, u32[]{:S(2)}) %collective-permute-start.5) | collective-permute-done | bytes 1179680 | tf_op jit(solution)/shard_map/ppermute | solution.py:18
  53.2 4.0 %all-to-all-start.1 = ((bf16[16,1,24,1536]{3,2,1,0:T(8,128)(2,1)}), bf16[16,1,24,1536]{3,2,1,0:T(8,128)(2,1)S(1)}, u32[]{:S(2)}, u32[]{:S(2)}) async-start(bf16[16,1,24,1536]{3,2,1,0:T(8,128)(2,1)} %fusion.60), calls=%async_computation.1 | async-start | bytes 2359296 | tf_op jit(solution)/shard_map/all_to_all | solution.py:125
  57.4 20.0 %all-to-all-done.1 = bf16[16,1,24,1536]{3,2,1,0:T(8,128)(2,1)S(1)} async-done(((bf16[16,1,24,1536]{3,2,1,0:T(8,128)(2,1)}), bf16[16,1,24,1536]{3,2,1,0:T(8,128)(2,1)S(1)}, u32[]{:S(2)}, u32[]{:S(2)}) %all-to-all-start.1) | async-done | bytes 1179680 | tf_op jit(solution)/shard_map/all_to_all | solution.py:125
  81.4 3.4 %collective-permute-done.6 = bf16[64,768]{1,0:T(8,128)(2,1)S(1)} collective-permute-done((bf16[64,768]{1,0:T(8,128)(2,1)S(1)}, bf16[64,768]{1,0:T(8,128)(2,1)S(1)}, u32[]{:S(2)}, u32[]{:S(2)}) %collective-permute-start.6) | collective-permute-done | bytes 98336 | tf_op jit(solution)/shard_map/ppermute | solution.py:18
  86.1 2.7 %collective-permute-start.8 = (bf16[64,768]{1,0:T(8,128)(2,1)S(1)}, bf16[64,768]{1,0:T(8,128)(2,1)S(1)}, u32[]{:S(2)}, u32[]{:S(2)}) collective-permute-start(bf16[64,768]{1,0:T(8,128)(2,1)S(1)} %add_convert_fusion.5), channel_id=1, source_target_pairs={{0,66},{1,67},{2,64},{3,65},{64,2},{65,3},{66,0},{67,1},{4,70},{5,... | collective-permute-start | bytes 294920 | tf_op jit(solution)/shard_map/ppermute | solution.py:147
  93.5 21.3 %all_to_all.31 = bf16[16,1,24,1536]{3,2,1,0:T(8,128)(2,1)S(1)} all-to-all(bf16[16,1,24,1536]{3,2,1,0:T(8,128)(2,1)S(1)} %bitcast.231), channel_id=1, replica_groups=mesh['section'=2,'expert'=16,'tensor'=4] {'expert'}, dimensions={0} | all-to-all | bytes 2359296 | tf_op jit(solution)/shard_map/all_to_all | solution.py:95
  114.8 2.8 %collective-permute-done.9 = bf16[16,1,24,1536]{3,2,0,1:T(8,128)(2,1)S(1)} collective-permute-done((bf16[16,1,24,1536]{3,2,0,1:T(8,128)(2,1)S(1)}, bf16[16,1,24,1536]{3,2,0,1:T(8,128)(2,1)S(1)}, u32[]{:S(2)}, u32[]{:S(2)}) %collective-permute-start.9) | collective-permute-done | bytes 1179680 | tf_op jit(solution)/shard_map/ppermute | solution.py:18
  120.6 2.7 %fusion.8 = f32[16,24,1024]{2,1,0:T(8,128)S(1)} fusion(bf16[1,1,3072,1024]{3,2,1,0:T(8,128)(2,1)S(1)} %bitcast.247, bf16[16,24,768]{2,1,0:T(8,128)(2,1)S(1)} %get-tuple-element.51, bf16[16,24,768]{2,1,0:T(8,128)(2,1)S(1)} %get-tuple-element.47, bf16[16,24,768]{2,1,0:T(8,128)(2,1)S(1)} %get-tuple-element.50, bf16[16,24,768]{2,1,0:T(8,128)(2,1)S(1)} %get-tuple-element.46, ...), kind=kOutput, calls=%fused_computation.16 | convolution fusion | flops 2428895232 | bytes 10237440 | tf_op jit(solution)/shard_map/sekd,edf->sekf/dot_general | solution.py:105
  123.3 2.8 %fusion.15 = f32[16,1,24,3072]{3,2,0,1:T(8,128)S(1)} fusion(bf16[1,1,1024,3072]{3,2,1,0:T(8,128)(2,1)S(1)} %bitcast.253, f32[16,24,1024]{2,1,0:T(8,128)S(1)} %fusion.8), kind=kOutput, calls=%fused_computation.27 | convolution fusion | flops 2417885184 | bytes 12582912 | tf_op jit(solution)/shard_map/sekf,efd->sekd/dot_general | solution.py:109
  127.0 2.7 %collective-permute-done.10 = bf16[16,1,24,1536]{3,2,0,1:T(8,128)(2,1)S(1)} collective-permute-done((bf16[16,1,24,1536]{3,2,0,1:T(8,128)(2,1)S(1)}, bf16[16,1,24,1536]{3,2,0,1:T(8,128)(2,1)S(1)}, u32[]{:S(2)}, u32[]{:S(2)}) %collective-permute-start.10) | collective-permute-done | bytes 1179680 | tf_op jit(solution)/shard_map/ppermute | solution.py:18
  131.3 3.9 %all-to-all-start.3 = ((bf16[16,1,24,1536]{3,2,1,0:T(8,128)(2,1)}), bf16[16,1,24,1536]{3,2,1,0:T(8,128)(2,1)S(1)}, u32[]{:S(2)}, u32[]{:S(2)}) async-start(bf16[16,1,24,1536]{3,2,1,0:T(8,128)(2,1)} %fusion.61), calls=%async_computation.3 | async-start | bytes 2359296 | tf_op jit(solution)/shard_map/all_to_all | solution.py:125
  135.3 20.0 %all-to-all-done.3 = bf16[16,1,24,1536]{3,2,1,0:T(8,128)(2,1)S(1)} async-done(((bf16[16,1,24,1536]{3,2,1,0:T(8,128)(2,1)}), bf16[16,1,24,1536]{3,2,1,0:T(8,128)(2,1)S(1)}, u32[]{:S(2)}, u32[]{:S(2)}) %all-to-all-start.3) | async-done | bytes 1179680 | tf_op jit(solution)/shard_map/all_to_all | solution.py:125
  158.2 4.6 %collective-permute-done.11 = bf16[64,768]{1,0:T(8,128)(2,1)S(1)} collective-permute-done((bf16[64,768]{1,0:T(8,128)(2,1)S(1)}, bf16[64,768]{1,0:T(8,128)(2,1)S(1)}, u32[]{:S(2)}, u32[]{:S(2)}) %collective-permute-start.11) | collective-permute-done | bytes 98336 | tf_op jit(solution)/shard_map/ppermute | solution.py:18
  165.6 3.5 %collective-permute-done.12 = bf16[64,768]{1,0:T(8,128)(2,1)S(1)} collective-permute-done((bf16[64,768]{1,0:T(8,128)(2,1)S(1)}, bf16[64,768]{1,0:T(8,128)(2,1)S(1)}, u32[]{:S(2)}, u32[]{:S(2)}) %collective-permute-start.12) | collective-permute-done | bytes 98336 | tf_op jit(solution)/shard_map/ppermute | solution.py:146
  171.5 21.4 %all_to_all.32 = bf16[16,1,24,1536]{3,2,1,0:T(8,128)(2,1)S(1)} all-to-all(bf16[16,1,24,1536]{3,2,1,0:T(8,128)(2,1)S(1)} %bitcast.232), channel_id=1, replica_groups=mesh['section'=2,'expert'=16,'tensor'=4] {'expert'}, dimensions={0} | all-to-all | bytes 2359296 | tf_op jit(solution)/shard_map/all_to_all | solution.py:95
  192.9 2.8 %collective-permute-done.14 = bf16[16,1,24,1536]{3,2,0,1:T(8,128)(2,1)S(1)} collective-permute-done((bf16[16,1,24,1536]{3,2,0,1:T(8,128)(2,1)S(1)}, bf16[16,1,24,1536]{3,2,0,1:T(8,128)(2,1)S(1)}, u32[]{:S(2)}, u32[]{:S(2)}) %collective-permute-start.14) | collective-permute-done | bytes 1179680 | tf_op jit(solution)/shard_map/ppermute | solution.py:18
  201.3 2.8 %fusion.18 = f32[16,1,24,3072]{3,2,0,1:T(8,128)S(1)} fusion(bf16[1,1,1024,3072]{3,2,1,0:T(8,128)(2,1)S(1)} %bitcast.255, f32[16,24,1024]{2,1,0:T(8,128)S(1)} %fusion.6), kind=kOutput, calls=%fused_computation.28 | convolution fusion | flops 2417885184 | bytes 12582912 | tf_op jit(solution)/shard_map/sekf,efd->sekd/dot_general | solution.py:109
  205.1 2.7 %collective-permute-done.15 = bf16[16,1,24,1536]{3,2,0,1:T(8,128)(2,1)S(1)} collective-permute-done((bf16[16,1,24,1536]{3,2,0,1:T(8,128)(2,1)S(1)}, bf16[16,1,24,1536]{3,2,0,1:T(8,128)(2,1)S(1)}, u32[]{:S(2)}, u32[]{:S(2)}) %collective-permute-start.15) | collective-permute-done | bytes 1179680 | tf_op jit(solution)/shard_map/ppermute | solution.py:18
  209.2 4.0 %all-to-all-start.5 = ((bf16[16,1,24,1536]{3,2,1,0:T(8,128)(2,1)}), bf16[16,1,24,1536]{3,2,1,0:T(8,128)(2,1)S(1)}, u32[]{:S(2)}, u32[]{:S(2)}) async-start(bf16[16,1,24,1536]{3,2,1,0:T(8,128)(2,1)} %fusion.62), calls=%async_computation.5 | async-start | bytes 2359296 | tf_op jit(solution)/shard_map/all_to_all | solution.py:125
  213.3 20.0 %all-to-all-done.5 = bf16[16,1,24,1536]{3,2,1,0:T(8,128)(2,1)S(1)} async-done(((bf16[16,1,24,1536]{3,2,1,0:T(8,128)(2,1)}), bf16[16,1,24,1536]{3,2,1,0:T(8,128)(2,1)S(1)}, u32[]{:S(2)}, u32[]{:S(2)}) %all-to-all-start.5) | async-done | bytes 1179680 | tf_op jit(solution)/shard_map/all_to_all | solution.py:125
  236.9 3.9 %collective-permute-done.16 = bf16[64,768]{1,0:T(8,128)(2,1)S(1)} collective-permute-done((bf16[64,768]{1,0:T(8,128)(2,1)S(1)}, bf16[64,768]{1,0:T(8,128)(2,1)S(1)}, u32[]{:S(2)}, u32[]{:S(2)}) %collective-permute-start.16) | collective-permute-done | bytes 98336 | tf_op jit(solution)/shard_map/ppermute | solution.py:18
  (152 shorter events, 55.1 us)
Async XLA Ops:
  0.0 6.9 %collective-permute-start = (bf16[2,64,768]{2,1,0:T(8,128)(2,1)}, bf16[2,64,768]{2,1,0:T(8,128)(2,1)S(1)}, u32[]{:S(2)}, u32[]{:S(2)}) collective-permute-start(bf16[2,64,768]{2,1,0:T(8,128)(2,1)} %param.10), channel_id=1, source_target_pairs={{0,2},{1,3},{2,0},{3,1},{4,6},{5,7},{6,4},{7,5},{8,10},{9,11},{10,... | collective-permute-start | bytes 589832 | tf_op jit(solution)/shard_map/ppermute | solution.py:18
  9.3 25.8 %copy-start.1 = (f32[1,768]{1,0:T(1,128)S(1)}, f32[1,768]{1,0:T(1,128)}, u32[]{:S(2)}) copy-start(f32[1,768]{1,0:T(1,128)} %param.11) | copy-start | bytes 9220
  35.0 4.5 %collective-permute-start.1 = (bf16[16,1,24,1536]{3,2,0,1:T(8,128)(2,1)S(1)}, bf16[16,1,24,1536]{3,2,0,1:T(8,128)(2,1)S(1)}, u32[]{:S(2)}, u32[]{:S(2)}) collective-permute-start(bf16[16,1,24,1536]{3,2,0,1:T(8,128)(2,1)S(1)} %bitcast.224), channel_id=1, source_target_pairs={{0,1},{1,0},{2,3},{3,2},{4,5},{5,4},{6,7},{7,6},{8,9},{9,8},{10,11... | collective-permute-start | bytes 3538952 | tf_op jit(solution)/shard_map/ppermute | solution.py:18
  35.0 2.8 %collective-permute-start.2 = (f32[768]{0:T(1024)S(1)}, f32[768]{0:T(1024)S(1)}, u32[]{:S(2)}, u32[]{:S(2)}) collective-permute-start(f32[768]{0:T(1024)S(1)} %reduce.4), channel_id=1, source_target_pairs={{0,1},{1,0},{2,3},{3,2},{4,5},{5,4},{6,7},{7,6},{8,9},{9,8},{10,11... | collective-permute-start | bytes 9224 | tf_op jit(solution)/shard_map/ppermute | solution.py:18
  35.6 3.6 %collective-permute-start.3 = (f32[768]{0:T(1024)S(1)}, f32[768]{0:T(1024)S(1)}, u32[]{:S(2)}, u32[]{:S(2)}) collective-permute-start(f32[768]{0:T(1024)S(1)} %reduce.4), channel_id=1, source_target_pairs={{0,2},{1,3},{2,0},{3,1},{4,6},{5,7},{6,4},{7,5},{8,10},{9,11},{10,... | collective-permute-start | bytes 9224 | tf_op jit(solution)/shard_map/ppermute | solution.py:18
  36.5 3.1 %collective-permute-start.4 = (f32[768]{0:T(1024)S(1)}, f32[768]{0:T(1024)S(1)}, u32[]{:S(2)}, u32[]{:S(2)}) collective-permute-start(f32[768]{0:T(1024)S(1)} %reduce.4), channel_id=1, source_target_pairs={{0,3},{1,2},{2,1},{3,0},{4,7},{5,6},{6,5},{7,4},{8,11},{9,10},{10,... | collective-permute-start | bytes 9224 | tf_op jit(solution)/shard_map/ppermute | solution.py:18
  40.1 5.1 %slice-start.6 = ((s8[6291456]{0:T(1024)(128)(4,1)}), s8[4194304]{0:T(1024)(128)(4,1)S(1)}, s32[]{:S(2)}) async-start(s8[6291456]{0:T(1024)(128)(4,1)} %bitcast.250), calls=%async_computation.12 | async-start | bytes 8388608
  48.7 2.9 %collective-permute-start.5 = (bf16[16,1,24,1536]{3,2,0,1:T(8,128)(2,1)S(1)}, bf16[16,1,24,1536]{3,2,0,1:T(8,128)(2,1)S(1)}, u32[]{:S(2)}, u32[]{:S(2)}) collective-permute-start(bf16[16,1,24,1536]{3,2,0,1:T(8,128)(2,1)S(1)} %select_convert_fusion.2), channel_id=1, source_target_pairs={{0,1},{1,0},{2,3},{3,2},{4,5},{5,4},{6,7},{7,6},{8,9},{9,8},{10,11... | collective-permute-start | bytes 3538952 | tf_op jit(solution)/shard_map/ppermute | solution.py:18
  53.2 24.2 %all-to-all-start.1 = ((bf16[16,1,24,1536]{3,2,1,0:T(8,128)(2,1)}), bf16[16,1,24,1536]{3,2,1,0:T(8,128)(2,1)S(1)}, u32[]{:S(2)}, u32[]{:S(2)}) async-start(bf16[16,1,24,1536]{3,2,1,0:T(8,128)(2,1)} %fusion.60), calls=%async_computation.1 | async-start | bytes 2359296 | tf_op jit(solution)/shard_map/all_to_all | solution.py:125
  80.1 4.7 %collective-permute-start.6 = (bf16[64,768]{1,0:T(8,128)(2,1)S(1)}, bf16[64,768]{1,0:T(8,128)(2,1)S(1)}, u32[]{:S(2)}, u32[]{:S(2)}) collective-permute-start(bf16[64,768]{1,0:T(8,128)(2,1)S(1)} %select_convert_fusion.5), channel_id=1, source_target_pairs={{0,2},{1,3},{2,0},{3,1},{4,6},{5,7},{6,4},{7,5},{8,10},{9,11},{10,... | collective-permute-start | bytes 294920 | tf_op jit(solution)/shard_map/ppermute | solution.py:18
  84.9 6.2 %collective-permute-start.7 = (bf16[64,768]{1,0:T(8,128)(2,1)S(1)}, bf16[64,768]{1,0:T(8,128)(2,1)S(1)}, u32[]{:S(2)}, u32[]{:S(2)}) collective-permute-start(bf16[64,768]{1,0:T(8,128)(2,1)S(1)} %add_convert_fusion.5), channel_id=1, source_target_pairs={{0,64},{64,0},{1,65},{65,1},{2,66},{66,2},{3,67},{67,3},{4,68},{68... | collective-permute-start | bytes 294920 | tf_op jit(solution)/shard_map/ppermute | solution.py:146
  86.1 6.0 %collective-permute-start.8 = (bf16[64,768]{1,0:T(8,128)(2,1)S(1)}, bf16[64,768]{1,0:T(8,128)(2,1)S(1)}, u32[]{:S(2)}, u32[]{:S(2)}) collective-permute-start(bf16[64,768]{1,0:T(8,128)(2,1)S(1)} %add_convert_fusion.5), channel_id=1, source_target_pairs={{0,66},{1,67},{2,64},{3,65},{64,2},{65,3},{66,0},{67,1},{4,70},{5,... | collective-permute-start | bytes 294920 | tf_op jit(solution)/shard_map/ppermute | solution.py:147
  114.8 2.8 %collective-permute-start.9 = (bf16[16,1,24,1536]{3,2,0,1:T(8,128)(2,1)S(1)}, bf16[16,1,24,1536]{3,2,0,1:T(8,128)(2,1)S(1)}, u32[]{:S(2)}, u32[]{:S(2)}) collective-permute-start(bf16[16,1,24,1536]{3,2,0,1:T(8,128)(2,1)S(1)} %bitcast.225), channel_id=1, source_target_pairs={{0,1},{1,0},{2,3},{3,2},{4,5},{5,4},{6,7},{7,6},{8,9},{9,8},{10,11... | collective-permute-start | bytes 3538952 | tf_op jit(solution)/shard_map/ppermute | solution.py:18
  118.2 5.1 %slice-start.8 = ((s8[6291456]{0:T(1024)(128)(4,1)}), s8[4194304]{0:T(1024)(128)(4,1)S(1)}, s32[]{:S(2)}) async-start(s8[6291456]{0:T(1024)(128)(4,1)} %bitcast.252), calls=%async_computation.14 | async-start | bytes 8388608
  126.8 2.9 %collective-permute-start.10 = (bf16[16,1,24,1536]{3,2,0,1:T(8,128)(2,1)S(1)}, bf16[16,1,24,1536]{3,2,0,1:T(8,128)(2,1)S(1)}, u32[]{:S(2)}, u32[]{:S(2)}) collective-permute-start(bf16[16,1,24,1536]{3,2,0,1:T(8,128)(2,1)S(1)} %select_convert_fusion.1), channel_id=1, source_target_pairs={{0,1},{1,0},{2,3},{3,2},{4,5},{5,4},{6,7},{7,6},{8,9},{9,8},{10,11... | collective-permute-start | bytes 3538952 | tf_op jit(solution)/shard_map/ppermute | solution.py:18
  131.3 24.0 %all-to-all-start.3 = ((bf16[16,1,24,1536]{3,2,1,0:T(8,128)(2,1)}), bf16[16,1,24,1536]{3,2,1,0:T(8,128)(2,1)S(1)}, u32[]{:S(2)}, u32[]{:S(2)}) async-start(bf16[16,1,24,1536]{3,2,1,0:T(8,128)(2,1)} %fusion.61), calls=%async_computation.3 | async-start | bytes 2359296 | tf_op jit(solution)/shard_map/all_to_all | solution.py:125
  158.1 4.7 %collective-permute-start.11 = (bf16[64,768]{1,0:T(8,128)(2,1)S(1)}, bf16[64,768]{1,0:T(8,128)(2,1)S(1)}, u32[]{:S(2)}, u32[]{:S(2)}) collective-permute-start(bf16[64,768]{1,0:T(8,128)(2,1)S(1)} %select_convert_fusion.4), channel_id=1, source_target_pairs={{0,2},{1,3},{2,0},{3,1},{4,6},{5,7},{6,4},{7,5},{8,10},{9,11},{10,... | collective-permute-start | bytes 294920 | tf_op jit(solution)/shard_map/ppermute | solution.py:18
  162.8 6.2 %collective-permute-start.12 = (bf16[64,768]{1,0:T(8,128)(2,1)S(1)}, bf16[64,768]{1,0:T(8,128)(2,1)S(1)}, u32[]{:S(2)}, u32[]{:S(2)}) collective-permute-start(bf16[64,768]{1,0:T(8,128)(2,1)S(1)} %add_convert_fusion.4), channel_id=1, source_target_pairs={{0,64},{64,0},{1,65},{65,1},{2,66},{66,2},{3,67},{67,3},{4,68},{68... | collective-permute-start | bytes 294920 | tf_op jit(solution)/shard_map/ppermute | solution.py:146
  164.1 6.0 %collective-permute-start.13 = (bf16[64,768]{1,0:T(8,128)(2,1)S(1)}, bf16[64,768]{1,0:T(8,128)(2,1)S(1)}, u32[]{:S(2)}, u32[]{:S(2)}) collective-permute-start(bf16[64,768]{1,0:T(8,128)(2,1)S(1)} %add_convert_fusion.4), channel_id=1, source_target_pairs={{0,66},{1,67},{2,64},{3,65},{64,2},{65,3},{66,0},{67,1},{4,70},{5,... | collective-permute-start | bytes 294920 | tf_op jit(solution)/shard_map/ppermute | solution.py:147
  192.9 2.8 %collective-permute-start.14 = (bf16[16,1,24,1536]{3,2,0,1:T(8,128)(2,1)S(1)}, bf16[16,1,24,1536]{3,2,0,1:T(8,128)(2,1)S(1)}, u32[]{:S(2)}, u32[]{:S(2)}) collective-permute-start(bf16[16,1,24,1536]{3,2,0,1:T(8,128)(2,1)S(1)} %bitcast.226), channel_id=1, source_target_pairs={{0,1},{1,0},{2,3},{3,2},{4,5},{5,4},{6,7},{7,6},{8,9},{9,8},{10,11... | collective-permute-start | bytes 3538952 | tf_op jit(solution)/shard_map/ppermute | solution.py:18
  196.0 5.3 %slice-start.10 = ((s8[6291456]{0:T(1024)(128)(4,1)}), s8[4194304]{0:T(1024)(128)(4,1)S(1)}, s32[]{:S(2)}) async-start(s8[6291456]{0:T(1024)(128)(4,1)} %bitcast.254), calls=%async_computation.16 | async-start | bytes 8388608
  204.9 2.9 %collective-permute-start.15 = (bf16[16,1,24,1536]{3,2,0,1:T(8,128)(2,1)S(1)}, bf16[16,1,24,1536]{3,2,0,1:T(8,128)(2,1)S(1)}, u32[]{:S(2)}, u32[]{:S(2)}) collective-permute-start(bf16[16,1,24,1536]{3,2,0,1:T(8,128)(2,1)S(1)} %select_convert_fusion), channel_id=1, source_target_pairs={{0,1},{1,0},{2,3},{3,2},{4,5},{5,4},{6,7},{7,6},{8,9},{9,8},{10,11... | collective-permute-start | bytes 3538952 | tf_op jit(solution)/shard_map/ppermute | solution.py:18
  209.2 24.0 %all-to-all-start.5 = ((bf16[16,1,24,1536]{3,2,1,0:T(8,128)(2,1)}), bf16[16,1,24,1536]{3,2,1,0:T(8,128)(2,1)S(1)}, u32[]{:S(2)}, u32[]{:S(2)}) async-start(bf16[16,1,24,1536]{3,2,1,0:T(8,128)(2,1)} %fusion.62), calls=%async_computation.5 | async-start | bytes 2359296 | tf_op jit(solution)/shard_map/all_to_all | solution.py:125
  236.0 4.7 %collective-permute-start.16 = (bf16[64,768]{1,0:T(8,128)(2,1)S(1)}, bf16[64,768]{1,0:T(8,128)(2,1)S(1)}, u32[]{:S(2)}, u32[]{:S(2)}) collective-permute-start(bf16[64,768]{1,0:T(8,128)(2,1)S(1)} %select_convert_fusion.3), channel_id=1, source_target_pairs={{0,2},{1,3},{2,0},{3,1},{4,6},{5,7},{6,4},{7,5},{8,10},{9,11},{10,... | collective-permute-start | bytes 294920 | tf_op jit(solution)/shard_map/ppermute | solution.py:18
  (10 other events, 27.0 us)
